TPU v7x, 256 devices: a whole 4x4x8 slice. The times are simulated.
256 devices in a mesh: mode: 16 (over y, x), slab: 16 (over z, core).
Axes of the slice: x: 4, y: 4, z: 8, core: 2. Of those that a mesh axis runs over, the one named last changes fastest.
Arguments:
- velocity: float32 [3, 64, 256, 128], P(None, 'mode', 'slab'), may hold values from -6 to 6
- vorticity: bfloat16 [3, 64, 256, 128], P(None, 'mode', 'slab'), may hold values from -1.5 to 1.5
- lift: bfloat16 [4096, 1920], P('slab'), may hold values from -0.125 to 0.125
- extend: bfloat16 [30720, 256], P('slab'), may hold values from -0.375 to 0.375
- interface_chain_factors: float32 [2, 64, 2048, 128], P(None, 'mode', 'slab'), may hold values from -1 to 1
- pivot_inverse: float32 [64, 2048, 128], P('mode', 'slab'), may hold values from -1 to 1
- interior_diag: float32 [240, 128], P('slab'), may hold values from 0.5 to 4
- node_map: int32 [16, 256], P('slab'), may hold values from 0 to 127, as said below
Outputs:
- new_velocity: float32 [3, 64, 256, 128], P(None, 'mode', 'slab')
Inputs may be any that keep to these rules, and one draw needn't show every extreme that they name: `node_map`: the first 128 and the last 128 entries of each row are each a permutation of 0 to 127.
All inputs are finite; a program needn't handle non-finite values.
Results may differ from a plain program's by a relative error of at most 0.0062.
Values may be sent and summed in bfloat16 or wider, within the bound.
No kernel may reach another device: no remote copies, remote signals or barrier semaphores. Data moves between devices by JAX's collectives and lax.ppermute only.
A program may use at most 128 MiB of HBM per device.

v0:
```python
import jax
import jax.numpy as jnp
from jax import lax
from jax.sharding import PartitionSpec as P

PLANES = 64


LAMBDA_TIMESTEP = 0.5
WAVE_BASE = 0.125


def prefix(value, axis, join, neutral, backward):
    count, mine = (lax.axis_size(axis), lax.axis_index(axis))
    pieces = jax.tree.map(lambda part: lax.all_gather(part, axis), value)
    if backward:
        pieces = jax.tree.map(lambda part: part[::-1], pieces)
        mine = count - 1 - mine
    subtotal = jax.tree.map(
        lambda part, zero: jnp.full_like(part, 0) + jnp.asarray(zero, part.dtype), value, neutral
    )

    def step(position, subtotal):
        longer = join(subtotal, jax.tree.map(lambda part: part[position], pieces))
        return jax.tree.map(lambda new, old: jnp.where(position < mine, new, old), longer, subtotal)

    return lax.fori_loop(0, count - 1, step, subtotal)


def plane_numbers(planes):
    index_plane = jnp.arange(planes, dtype=jnp.int32)
    return jnp.where(index_plane == 1, planes // 2, index_plane // 2)


def plane_shift(wavenum):
    return LAMBDA_TIMESTEP + (wavenum.astype(jnp.float32) * WAVE_BASE) ** 2


def spectral_tables(planes, quad_points):
    wavenum = plane_numbers(planes)
    station = jnp.arange(quad_points, dtype=jnp.int32)
    phases = station[:, None] * wavenum[None, :] % quad_points
    angles = phases.astype(jnp.float32) * (2.0 * jnp.pi / quad_points)
    index_plane = jnp.arange(planes, dtype=jnp.int32)
    odd_plane = (index_plane % 2 == 1) & (index_plane != 1)
    inverse = jnp.where(odd_plane[None, :], -jnp.sin(angles), jnp.cos(angles))
    weights = jnp.where(index_plane == 0, 1.0, 2.0).astype(jnp.float32) / quad_points
    forward = weights[:, None] * inverse.T
    return (inverse.astype(jnp.bfloat16), forward.astype(jnp.bfloat16))


def lamb_vector(velocity_phys, vorticity_phys):
    first = velocity_phys[1] * vorticity_phys[2] - velocity_phys[2] * vorticity_phys[1]
    second = velocity_phys[2] * vorticity_phys[0] - velocity_phys[0] * vorticity_phys[2]
    third = velocity_phys[0] * vorticity_phys[1] - velocity_phys[1] * vorticity_phys[0]
    return jnp.stack([first, second, third])


def mapping_application(matrix, vectors):
    return jnp.einsum("pab,pcb->pca", matrix, vectors, precision=lax.Precision.HIGHEST)


def chain_maps(earlier, later_one):
    early_matrix, early_offset = earlier
    late_matrix, late_offset = later_one
    joined = jnp.einsum("pab,pbd->pad", late_matrix, early_matrix, precision=lax.Precision.HIGHEST)
    return (joined, late_offset + mapping_application(late_matrix, early_offset))


def on_device(
    velocity,
    vorticity,
    lift,
    extend,
    interface_chain_factors,
    pivot_inverse,
    interior_diag,
    node_map,
):
    components, planes_dev, line_count, point_total = velocity.shape
    quad_points = 3 * PLANES // 2
    inverse, forward = spectral_tables(PLANES, quad_points)
    wavenum = lax.dynamic_slice_in_dim(
        plane_numbers(PLANES), lax.axis_index("mode") * planes_dev, planes_dev
    )
    shifts = plane_shift(wavenum)
    velocity_half = velocity.astype(jnp.bfloat16)
    vel_lines = lax.all_to_all(velocity_half, "mode", split_axis=2, concat_axis=1, tiled=True)
    vort_lines = lax.all_to_all(vorticity, "mode", split_axis=2, concat_axis=1, tiled=True)
    vel_phys = jnp.einsum("qp,cplb->cqlb", inverse, vel_lines, preferred_element_type=jnp.float32)
    vort_phys = jnp.einsum("qp,cplb->cqlb", inverse, vort_lines, preferred_element_type=jnp.float32)
    lamb_field = lamb_vector(vel_phys, vort_phys).astype(jnp.bfloat16)
    nonlin_lines = jnp.einsum(
        "pq,cqlb->cplb", forward, lamb_field, preferred_element_type=jnp.float32
    ).astype(jnp.bfloat16)
    interior_point_velocity = (
        (LAMBDA_TIMESTEP * velocity[:, :, 1:, :])
        .astype(jnp.bfloat16)
        .reshape(components, planes_dev, -1)
    )
    lifted_velocity = jnp.einsum(
        "hf,vqf->qvh", lift, interior_point_velocity, preferred_element_type=jnp.float32
    )
    nonlin = lax.all_to_all(nonlin_lines, "mode", split_axis=1, concat_axis=2, tiled=True)
    inner_nonlinear_term = nonlin[:, :, 1:, :].reshape(components, planes_dev, -1)
    condensed = lifted_velocity + jnp.einsum(
        "hf,vqf->qvh", lift, inner_nonlinear_term, preferred_element_type=jnp.float32
    )
    halfway_offsets = jnp.concatenate(
        [jnp.zeros((point_total,), jnp.int32), jnp.full((point_total,), point_total, jnp.int32)]
    )
    row_order = node_map[0] + halfway_offsets
    inverse_order = jnp.argsort(row_order)
    line_zero_rhs = jnp.swapaxes(
        LAMBDA_TIMESTEP * velocity[:, :, 0, :] + nonlin[:, :, 0, :].astype(jnp.float32), 0, 1
    )
    cond_line = condensed[:, :, row_order]
    rhs_left = cond_line[:, :, :point_total] + line_zero_rhs
    right_part = cond_line[:, :, point_total:]
    slab_index = lax.axis_index("slab")
    slab_count = lax.axis_size("slab")
    leading_flag = slab_index == 0
    elimination_coefficient = interface_chain_factors[0]
    back_factor = interface_chain_factors[1]
    identity_blocks = jnp.broadcast_to(
        jnp.eye(point_total, dtype=jnp.float32), elimination_coefficient.shape
    )
    zero_blocks = jnp.zeros_like(elimination_coefficient)
    upper_rows = jnp.concatenate([-elimination_coefficient, identity_blocks], axis=2)
    lower_rows = jnp.concatenate([zero_blocks, zero_blocks], axis=2)
    advance_matrix = jnp.where(leading_flag, 0.0, jnp.concatenate([upper_rows, lower_rows], axis=1))
    advance_offset = jnp.concatenate([jnp.where(leading_flag, 0.0, rhs_left), right_part], axis=2)
    wide_identity = jnp.broadcast_to(
        jnp.eye(2 * point_total, dtype=jnp.float32), advance_matrix.shape
    )
    leading_part = prefix(
        (advance_matrix, advance_offset),
        "slab",
        chain_maps,
        (wide_identity, jnp.zeros_like(advance_offset)),
        False,
    )
    carried = leading_part[1]
    previous_entry = carried[:, :, :point_total]
    previous_rows = carried[:, :, point_total:]
    forward_results = jnp.where(
        leading_flag,
        0.0,
        rhs_left + previous_rows - mapping_application(elimination_coefficient, previous_entry),
    )
    pivot_term = mapping_application(pivot_inverse, forward_results)
    is_last = slab_index == slab_count - 1
    back_matrix = jnp.where(is_last, 0.0, -back_factor)
    suffix = prefix(
        (back_matrix, pivot_term),
        "slab",
        chain_maps,
        (identity_blocks, jnp.zeros_like(pivot_term)),
        True,
    )
    right_values = suffix[1]
    left_solved = pivot_term - mapping_application(back_factor, right_values)
    left_values = jnp.where(leading_flag, 0.0, left_solved)
    boundary_line = jnp.concatenate([left_values, right_values], axis=2)
    local_boundary_rows = boundary_line[:, :, inverse_order].astype(jnp.bfloat16)
    extension = jnp.einsum(
        "hg,dog->odh", extend, local_boundary_rows, preferred_element_type=jnp.float32
    )
    extension = extension.reshape(components, planes_dev, line_count - 1, point_total)
    inner_rhs = LAMBDA_TIMESTEP * velocity[:, :, 1:, :] + nonlin[:, :, 1:, :].astype(jnp.float32)
    new_inner = extension + inner_rhs / (interior_diag[None, None] + shifts[None, :, None, None])
    line_zero = jnp.swapaxes(left_values, 0, 1)
    return jnp.concatenate([line_zero[:, :, None, :], new_inner], axis=2)


def solution(mesh):
    in_specs = (
        P(None, "mode", "slab", None),
        P(None, "mode", "slab", None),
        P("slab", None),
        P("slab", None),
        P(None, "mode", "slab", None),
        P("mode", "slab", None),
        P("slab", None),
        P("slab", None),
    )
    out_specs = P(None, "mode", "slab", None)
    return jax.shard_map(
        on_device, mesh=mesh, in_specs=in_specs, out_specs=out_specs, check_vma=False
    )
```

profile of v0, /device:TPU:1, one launch (start us, length us, event | category | flops | bytes accessed | tf_op | source)
XLA Modules:
  0.0 234.7 jit_solution(18005431540662967177)
XLA Ops:
  11.4 7.6 %all-to-all-start = ((bf16[3,4,16,128]{3,1,0,2:T(4,128)(2,1)}), bf16[3,4,16,128]{3,1,0,2:T(4,128)(2,1)S(1)}, u32[]{:S(2)}, u32[]{:S(2)}) async-start(bf16[3,4,16,128]{3,1,0,2:T(4,128)(2,1)} %copy.87), calls=%async_computation | async-start | bytes 98304 | tf_op jit(solution)/shard_map/all_to_all | solution.py:88
  19.2 3.2 %sort.17 = (s32[256]{0:T(256)}, s32[256]{0:T(256)S(1)}) sort(s32[256]{0:T(256)S(1)} %bitcast.169, s32[256]{0:T(256)S(1)} %iota.51), dimensions={0}, to_apply=%region_4.5 | sort | flops 2048 | bytes 4096 | tf_op jit(solution)/shard_map/jit(argsort)/sort | solution.py:113
  25.4 4.8 %all-to-all-start.1 = ((bf16[3,4,16,128]{3,1,0,2:T(4,128)(2,1)}), bf16[3,4,16,128]{3,1,0,2:T(4,128)(2,1)S(1)}, u32[]{:S(2)}, u32[]{:S(2)}) async-start(bf16[3,4,16,128]{3,1,0,2:T(4,128)(2,1)} %copy.49), calls=%async_computation.1 | async-start | bytes 98304 | tf_op jit(solution)/shard_map/all_to_all | solution.py:89
  30.3 6.4 %all-to-all-done.1 = bf16[3,4,16,128]{3,1,0,2:T(4,128)(2,1)S(1)} async-done(((bf16[3,4,16,128]{3,1,0,2:T(4,128)(2,1)}), bf16[3,4,16,128]{3,1,0,2:T(4,128)(2,1)S(1)}, u32[]{:S(2)}, u32[]{:S(2)}) %all-to-all-start.1) | async-done | bytes 49184 | tf_op jit(solution)/shard_map/all_to_all | solution.py:89
  38.6 3.5 %all-to-all-start.2 = ((bf16[3,64,1,128]{3,0,2,1:T(4,128)(2,1)}), bf16[3,64,1,128]{3,0,2,1:T(4,128)(2,1)S(1)}, u32[]{:S(2)}, u32[]{:S(2)}) async-start(bf16[3,64,1,128]{3,0,2,1:T(4,128)(2,1)} %copy.55), calls=%async_computation.2 | async-start | bytes 131072 | tf_op jit(solution)/shard_map/all_to_all | solution.py:104
  42.2 6.4 %all-to-all-done.2 = bf16[3,64,1,128]{3,0,2,1:T(4,128)(2,1)S(1)} async-done(((bf16[3,64,1,128]{3,0,2,1:T(4,128)(2,1)}), bf16[3,64,1,128]{3,0,2,1:T(4,128)(2,1)S(1)}, u32[]{:S(2)}, u32[]{:S(2)}) %all-to-all-start.2) | async-done | bytes 49184 | tf_op jit(solution)/shard_map/all_to_all | solution.py:104
  50.6 24.6 %all-gather = f32[64,3,256]{2,1,0:T(4,128)S(1)} all-gather(f32[4,3,256]{2,1,0:T(4,128)S(1)} %pad_maximum_fusion.1), channel_id=2, replica_groups=mesh['mode'=16,'slab'=16] {'slab'}, dimensions={0}, use_global_device_ids=true | all-gather | bytes 208896 | tf_op jit(solution)/shard_map/all_gather | solution.py:15
  75.3 4.6 %rev.7 = f32[16,4,128,128]{3,2,1,0:T(8,128)} reverse(f32[16,4,128,128]{3,2,1,0:T(8,128)} %all-gather.6.cloned.1.call-done), dimensions={0} | reverse | bytes 8388608 | tf_op jit(solution)/shard_map/rev | solution.py:17
  79.9 71.9 %all-gather.8.cloned.1.call-done = f32[64,256,256]{2,1,0:T(8,128)} async-done(((f32[4,256,256]{2,1,0:T(8,128)}), f32[64,256,256]{2,1,0:T(8,128)}) %all-gather.8.cloned.1.call-update) | async-done | bytes 16777232 | tf_op jit(solution)/shard_map/all_gather | solution.py:15
  151.8 33.4 %while.28 = (s32[]{:T(128)}, f32[4,3,256]{2,1,0:T(4,128)S(1)}, s32[]{:T(128)}, f32[16,4,3,256]{3,2,1,0:T(4,128)S(1)}, f32[16,4,256,256]{3,2,1,0:T(8,128)}, /*index=5*/s32[]{:T(128)}, s32[]{:T(128)}) while((s32[]{:T(128)}, f32[4,3,256]{2,1,0:T(4,128)S(1)}, s32[]{:T(128)}, f32[16,4,3,256]{3,2,1,0:T(4,128)S(1)}, ...), condition=%wide.region_1.2_spmd.clone, body=%wide.region_0.1_spmd.clone.sunk | while | flops 9449476 | bytes 1137247 | solution.py:27
  154.0 2.2 fusion.103
  156.3 2.2 fusion.103
  158.5 2.2 fusion.103
  160.7 2.2 fusion.103
  163.0 2.2 fusion.103
  165.2 2.2 fusion.103
  167.4 2.2 fusion.103
  169.6 2.2 fusion.103
  171.9 2.2 fusion.103
  174.1 2.2 fusion.103
  178.6 2.2 fusion.103
  180.8 2.2 fusion.103
  186.3 15.9 %all-gather.2 = f32[64,3,128]{2,1,0:T(4,128)S(1)} all-gather(f32[4,3,128]{2,1,0:T(4,128)S(1)} %fusion.86), channel_id=4, replica_groups=mesh['mode'=16,'slab'=16] {'slab'}, dimensions={0}, use_global_device_ids=true | all-gather | bytes 104448 | tf_op jit(solution)/shard_map/all_gather | solution.py:15
  202.2 22.3 %while.29 = (s32[]{:T(128)}, f32[4,3,128]{2,1,0:T(4,128)S(1)}, s32[]{:T(128)}, f32[16,4,3,128]{3,2,1,0:T(4,128)S(1)}, f32[16,4,128,128]{3,2,1,0:T(8,128)}, /*index=5*/s32[]{:T(128)}, s32[]{:T(128)}) while((s32[]{:T(128)}, f32[4,3,128]{2,1,0:T(4,128)S(1)}, s32[]{:T(128)}, f32[16,4,3,128]{3,2,1,0:T(4,128)S(1)}, ...), condition=%wide.region_3.4_spmd.clone, body=%wide.region_2.3_spmd.clone.sunk | while | flops 2365444 | bytes 307807 | solution.py:27
  (127 shorter events, 45.2 us)
Async XLA Ops:
  6.5 220.0 %copy-start = (bf16[1920,256]{1,0:T(8,128)(2,1)S(1)}, bf16[1920,256]{1,0:T(8,128)(2,1)}, u32[]{:S(2)}) copy-start(bf16[1920,256]{1,0:T(8,128)(2,1)} %param.15) | copy-start | bytes 2949124
  6.5 12.6 %copy-start.8 = (s32[1,256]{1,0:T(1,128)S(1)}, s32[1,256]{1,0:T(1,128)}, u32[]{:S(2)}) copy-start(s32[1,256]{1,0:T(1,128)} %constant.133.clone.1) | copy-start | bytes 3076
  6.5 4.1 %copy-start.3 = (f32[3,4,16,128]{3,2,1,0:T(8,128)S(1)}, f32[3,4,16,128]{3,2,1,0:T(8,128)}, u32[]{:S(2)}) copy-start(f32[3,4,16,128]{3,2,1,0:T(8,128)} %param.12) | copy-start | bytes 294916
  6.5 12.6 %copy-start.7 = (s32[1,256]{1,0:T(1,128)S(1)}, s32[1,256]{1,0:T(1,128)}, u32[]{:S(2)}) copy-start(s32[1,256]{1,0:T(1,128)} %param.19) | copy-start | bytes 3076
  6.5 15.9 %copy-start.6 = (f32[15,128]{1,0:T(8,128)S(1)}, f32[15,128]{1,0:T(8,128)}, u32[]{:S(2)}) copy-start(f32[15,128]{1,0:T(8,128)} %param.18) | copy-start | bytes 23044
  6.5 16.0 %copy-start.1 = (bf16[256,1920]{1,0:T(8,128)(2,1)S(1)}, bf16[256,1920]{1,0:T(8,128)(2,1)}, u32[]{:S(2)}) copy-start(bf16[256,1920]{1,0:T(8,128)(2,1)} %param.14) | copy-start | bytes 2949124
  6.6 16.4 %copy-start.5 = (bf16[3,4,16,128]{3,2,1,0:T(8,128)(2,1)S(1)}, bf16[3,4,16,128]{3,2,1,0:T(8,128)(2,1)}, u32[]{:S(2)}) copy-start(bf16[3,4,16,128]{3,2,1,0:T(8,128)(2,1)} %param.13) | copy-start | bytes 147460
  6.6 68.7 %all-gather.6.cloned.1.call-start = ((), (), s32[]{:S(2)}) async-start(), calls=%async_computation.3 | async-start | bytes 4456448 | tf_op jit(solution)/shard_map/all_gather | solution.py:15
  8.5 143.3 %all-gather.8.cloned.1.call-start = ((), (), s32[]{:S(2)}) async-start(), calls=%async_computation.4 | async-start | bytes 17825792 | tf_op jit(solution)/shard_map/all_gather | solution.py:15
  11.4 14.1 %all-to-all-start = ((bf16[3,4,16,128]{3,1,0,2:T(4,128)(2,1)}), bf16[3,4,16,128]{3,1,0,2:T(4,128)(2,1)S(1)}, u32[]{:S(2)}, u32[]{:S(2)}) async-start(bf16[3,4,16,128]{3,1,0,2:T(4,128)(2,1)} %copy.87), calls=%async_computation | async-start | bytes 98304 | tf_op jit(solution)/shard_map/all_to_all | solution.py:88
  25.4 11.3 %all-to-all-start.1 = ((bf16[3,4,16,128]{3,1,0,2:T(4,128)(2,1)}), bf16[3,4,16,128]{3,1,0,2:T(4,128)(2,1)S(1)}, u32[]{:S(2)}, u32[]{:S(2)}) async-start(bf16[3,4,16,128]{3,1,0,2:T(4,128)(2,1)} %copy.49), calls=%async_computation.1 | async-start | bytes 98304 | tf_op jit(solution)/shard_map/all_to_all | solution.py:89
  38.6 10.0 %all-to-all-start.2 = ((bf16[3,64,1,128]{3,0,2,1:T(4,128)(2,1)}), bf16[3,64,1,128]{3,0,2,1:T(4,128)(2,1)S(1)}, u32[]{:S(2)}, u32[]{:S(2)}) async-start(bf16[3,64,1,128]{3,0,2,1:T(4,128)(2,1)} %copy.55), calls=%async_computation.2 | async-start | bytes 131072 | tf_op jit(solution)/shard_map/all_to_all | solution.py:104
  79.9 105.3 %copy-start.2 = (f32[2,4,128,128]{3,2,1,0:T(8,128)S(1)}, f32[2,4,128,128]{3,2,1,0:T(8,128)}, u32[]{:S(2)}) copy-start(f32[2,4,128,128]{3,2,1,0:T(8,128)} %param.16) | copy-start | bytes 1572868
  79.9 105.9 %copy-start.4 = (f32[4,128,128]{2,1,0:T(8,128)S(1)}, f32[4,128,128]{2,1,0:T(8,128)}, u32[]{:S(2)}) copy-start(f32[4,128,128]{2,1,0:T(8,128)} %param.17) | copy-start | bytes 786436
Sparse Core Ops, SparseCore 0:
  9.2 46.7 all-gather.5
  57.9 93.8 all-gather.7
where the time goes:
time: 236 us; the launch traced here: 235 us
  waiting for transfers between devices  86.6 us (37%)
  matrix products  59.2 us (25%)
  blocking collectives  40.6 us (17%)
  starting transfers between devices  16 us (7%)
  between operations  13.8 us (6%)
  local copies, waits for them, and re-layouts  10.7 us (5%)
  other arithmetic  7.61 us (3%)
    all_gather x2, waiting for transfers between devices, prefix(): pieces = jax.tree.map(lambda part: lax.all_gather(part, axis), value)  71.9 us
    dot_general x33, matrix products, mapping_application(): jnp.einsum('pab,pcb->pca', matrix, vectors, precision=lax.Precision.HIGHEST)  56.9 us
    all_gather x2, blocking collectives, prefix(): pieces = jax.tree.map(lambda part: lax.all_gather(part, axis), value)  40.6 us
    all_to_all x1, starting transfers between devices, on_device(): lax.all_to_all(velocity_half, 'mode', split_axis=2, concat_axis=1, tiled=...  7.58 us
    all_to_all x1, waiting for transfers between devices, on_device(): lax.all_to_all(vorticity, 'mode', split_axis=2, concat_axis=1, tiled=True)  6.42 us
    all_to_all x1, waiting for transfers between devices, on_device(): lax.all_to_all(nonlin_lines, 'mode', split_axis=1, concat_axis=2, tiled=T...  6.41 us
    all_to_all x1, starting transfers between devices, on_device(): lax.all_to_all(vorticity, 'mode', split_axis=2, concat_axis=1, tiled=True)  4.81 us
  transfers between devices with their start and end apart: 5, of which 4 were waited for; matrix products, arithmetic and copies ran while one was open for 7% of the time, Pallas kernels for 0%

commit v1 on v0

v1 whole, which is shorter than its diff:
```python
import jax
import jax.numpy as jnp
from jax import lax
from jax.sharding import PartitionSpec as P

PLANES = 64


LAMBDA_TIMESTEP = 0.5
WAVE_BASE = 0.125
HIGHEST = lax.Precision.HIGHEST


def plane_numbers(planes):
    index_plane = jnp.arange(planes, dtype=jnp.int32)
    return jnp.where(index_plane == 1, planes // 2, index_plane // 2)


def plane_shift(wavenum):
    return LAMBDA_TIMESTEP + (wavenum.astype(jnp.float32) * WAVE_BASE) ** 2


def spectral_tables(planes, quad_points):
    wavenum = plane_numbers(planes)
    station = jnp.arange(quad_points, dtype=jnp.int32)
    phases = station[:, None] * wavenum[None, :] % quad_points
    angles = phases.astype(jnp.float32) * (2.0 * jnp.pi / quad_points)
    index_plane = jnp.arange(planes, dtype=jnp.int32)
    odd_plane = (index_plane % 2 == 1) & (index_plane != 1)
    inverse = jnp.where(odd_plane[None, :], -jnp.sin(angles), jnp.cos(angles))
    weights = jnp.where(index_plane == 0, 1.0, 2.0).astype(jnp.float32) / quad_points
    forward = weights[:, None] * inverse.T
    return (inverse.astype(jnp.bfloat16), forward.astype(jnp.bfloat16))


def lamb_vector(velocity_phys, vorticity_phys):
    first = velocity_phys[1] * vorticity_phys[2] - velocity_phys[2] * vorticity_phys[1]
    second = velocity_phys[2] * vorticity_phys[0] - velocity_phys[0] * vorticity_phys[2]
    third = velocity_phys[0] * vorticity_phys[1] - velocity_phys[1] * vorticity_phys[0]
    return jnp.stack([first, second, third])


def mapping_application(matrix, vectors):
    return jnp.einsum("pab,pcb->pca", matrix, vectors, precision=HIGHEST)


def chain_stack(factors, start, first, last, step):
    count = factors.shape[0]
    slots = jnp.arange(count, dtype=jnp.int32)[:, None, None, None]
    eye = jnp.eye(factors.shape[-1], dtype=factors.dtype)
    stack = jnp.where((slots == start) & (start >= first) & (start <= last), eye, 0.0)
    stack = jnp.broadcast_to(stack, factors.shape)
    running = jnp.broadcast_to(eye, factors.shape[1:])

    def body(distance, carry):
        running, stack = carry
        target = start + step * distance
        factor = lax.dynamic_index_in_dim(
            factors, jnp.clip(target - step, 0, count - 1), 0, keepdims=False
        )
        running = jnp.einsum("pab,pbd->pad", running, factor, precision=HIGHEST)
        valid = (target >= first) & (target <= last)
        current = lax.dynamic_index_in_dim(stack, jnp.clip(target, 0, count - 1), 0, keepdims=False)
        stack = lax.dynamic_update_index_in_dim(
            stack, jnp.where(valid, running, current), jnp.clip(target, 0, count - 1), 0
        )
        return running, stack

    return lax.fori_loop(1, count, body, (running, stack))[1]


def on_device(
    velocity,
    vorticity,
    lift,
    extend,
    interface_chain_factors,
    pivot_inverse,
    interior_diag,
    node_map,
):
    components, planes_dev, line_count, point_total = velocity.shape
    quad_points = 3 * PLANES // 2
    slab_index = lax.axis_index("slab")
    slab_count = lax.axis_size("slab")

    factors = lax.all_gather(interface_chain_factors, "slab", axis=1)
    elimination_all = -factors[0]
    back_all = -factors[1]
    upstream = chain_stack(elimination_all, slab_index, 1, slab_count - 1, -1)
    downstream = chain_stack(back_all, slab_index + 1, 1, slab_count - 1, 1)

    halfway_offsets = jnp.concatenate(
        [jnp.zeros((point_total,), jnp.int32), jnp.full((point_total,), point_total, jnp.int32)]
    )
    row_order = node_map[0] + halfway_offsets
    one_hot = (
        row_order[:, None] == jnp.arange(2 * point_total, dtype=jnp.int32)[None, :]
    ).astype(jnp.bfloat16)
    lift_rows = jnp.einsum(
        "ir,rf->if", one_hot, lift, preferred_element_type=jnp.float32
    ).astype(jnp.bfloat16)
    extend_cols = jnp.einsum(
        "hr,ir->hi", extend, one_hot, preferred_element_type=jnp.float32
    ).astype(jnp.bfloat16)

    inverse, forward = spectral_tables(PLANES, quad_points)
    wavenum = lax.dynamic_slice_in_dim(
        plane_numbers(PLANES), lax.axis_index("mode") * planes_dev, planes_dev
    )
    shifts = plane_shift(wavenum)
    velocity_half = velocity.astype(jnp.bfloat16)
    both_fields = jnp.concatenate([velocity_half, vorticity], axis=0)
    field_lines = lax.all_to_all(both_fields, "mode", split_axis=2, concat_axis=1, tiled=True)
    phys = jnp.einsum("qp,cplb->cqlb", inverse, field_lines, preferred_element_type=jnp.float32)
    lamb_field = lamb_vector(phys[:components], phys[components:]).astype(jnp.bfloat16)
    nonlin_lines = jnp.einsum(
        "pq,cqlb->cplb", forward, lamb_field, preferred_element_type=jnp.float32
    ).astype(jnp.bfloat16)
    interior_point_velocity = (
        (LAMBDA_TIMESTEP * velocity[:, :, 1:, :])
        .astype(jnp.bfloat16)
        .reshape(components, planes_dev, -1)
    )
    lifted_velocity = jnp.einsum(
        "hf,vqf->qvh", lift_rows, interior_point_velocity, preferred_element_type=jnp.float32
    )
    nonlin = lax.all_to_all(nonlin_lines, "mode", split_axis=1, concat_axis=2, tiled=True)
    inner_nonlinear_term = nonlin[:, :, 1:, :].reshape(components, planes_dev, -1)
    cond_line = lifted_velocity + jnp.einsum(
        "hf,vqf->qvh", lift_rows, inner_nonlinear_term, preferred_element_type=jnp.float32
    )
    line_zero_rhs = jnp.swapaxes(
        LAMBDA_TIMESTEP * velocity[:, :, 0, :] + nonlin[:, :, 0, :].astype(jnp.float32), 0, 1
    )
    rhs_left = cond_line[:, :, :point_total] + line_zero_rhs
    right_part = cond_line[:, :, point_total:]

    sides = lax.all_gather(jnp.stack([rhs_left, right_part]), "slab")
    previous_right = jnp.concatenate([jnp.zeros_like(sides[:1, 1]), sides[:-1, 1]], axis=0)
    interface_rhs = sides[:, 0] + previous_right
    forward_results = jnp.einsum("kpab,kpcb->pca", upstream, interface_rhs, precision=HIGHEST)
    pivot_term = mapping_application(pivot_inverse, forward_results)

    pivots = lax.all_gather(pivot_term, "slab")
    right_values = jnp.einsum("kpab,kpcb->pca", downstream, pivots, precision=HIGHEST)
    left_solved = pivot_term - mapping_application(interface_chain_factors[1], right_values)
    leading_flag = slab_index == 0
    left_values = jnp.where(leading_flag, 0.0, left_solved)

    boundary_line = jnp.concatenate([left_values, right_values], axis=2).astype(jnp.bfloat16)
    extension = jnp.einsum(
        "hg,dog->odh", extend_cols, boundary_line, preferred_element_type=jnp.float32
    )
    extension = extension.reshape(components, planes_dev, line_count - 1, point_total)
    inner_rhs = LAMBDA_TIMESTEP * velocity[:, :, 1:, :] + nonlin[:, :, 1:, :].astype(jnp.float32)
    new_inner = extension + inner_rhs / (interior_diag[None, None] + shifts[None, :, None, None])
    line_zero = jnp.swapaxes(left_values, 0, 1)
    return jnp.concatenate([line_zero[:, :, None, :], new_inner], axis=2)


def solution(mesh):
    in_specs = (
        P(None, "mode", "slab", None),
        P(None, "mode", "slab", None),
        P("slab", None),
        P("slab", None),
        P(None, "mode", "slab", None),
        P("mode", "slab", None),
        P("slab", None),
        P("slab", None),
    )
    out_specs = P(None, "mode", "slab", None)
    return jax.shard_map(
        on_device, mesh=mesh, in_specs=in_specs, out_specs=out_specs, check_vma=False
    )
```

time: 236 us -> 223 us (0.945)
  waiting for transfers between devices: 86.6 us -> 19.4 us
  local copies, waits for them, and re-layouts: 10.7 us -> 51.3 us
  matrix products: 59.2 us -> 71.9 us
  starting transfers between devices: 16 us -> 11.2 us
  other arithmetic: 7.61 us -> 12.3 us
    all_gather x2 -> x1, waiting for transfers between devices: 71.9 us -> 9.96 us  [on_device(): factors = lax.all_gather(interface_chain_factors, 'slab', axis=1)]
    dynamic_slice x0 -> x30, local copies, waits for them, and re-layouts: none -> 29.3 us  [body(): lax.dynamic_index_in_dim(stack, jnp.clip(target, 0, count - 1), 0, keepdi...]
    dot_general x38 -> x39, matrix products: 58.9 us -> 71.5 us  [the longest x30 62 us: body(): running = jnp.einsum('pab,pbd->pad', running, factor, precision=HIGHEST)]
    neg x0 -> x2, local copies, waits for them, and re-layouts: none -> 11.2 us  [the longest x1 5.6 us: on_device(): back_all = -factors[1]]
    neg x1, other arithmetic: 0.97 us -> 8.35 us  [on_device(): back_all = -factors[1]]
    broadcast_in_dim x1 -> x4, local copies, waits for them, and re-layouts: 0.02 us -> 6.33 us  [the longest x2 6.3 us: chain_stack(): stack = jnp.broadcast_to(stack, factors.shape)]
    all_to_all x2 -> x1, waiting for transfers between devices: 8.27 us -> 3.05 us  [on_device(): lax.all_to_all(both_fields, 'mode', split_axis=2, concat_axis=1, tiled=True)]
    all_to_all x2 -> x1, starting transfers between devices: 12.4 us -> 7.58 us  [on_device(): lax.all_to_all(both_fields, 'mode', split_axis=2, concat_axis=1, tiled=True)]
  transfers between devices with their start and end apart: 5 -> 3, of which waited for: 4 -> 3; matrix products, arithmetic and copies ran while one was open for 7% -> 4% of each run, Pallas kernels for 0% -> 0%
where the time goes in v1:
time: 223 us; the launch traced here: 220 us
  matrix products  71.9 us (32%)
  local copies, waits for them, and re-layouts  51.3 us (23%)
  blocking collectives  40.2 us (18%)
  waiting for transfers between devices  19.4 us (9%)
  between operations  13.6 us (6%)
  other arithmetic  12.3 us (6%)
  starting transfers between devices  11.2 us (5%)
    dot_general x30, matrix products, body(): running = jnp.einsum('pab,pbd->pad', running, factor, precision=HIGHEST)  62 us
    dynamic_slice x30, local copies, waits for them, and re-layouts, body(): lax.dynamic_index_in_dim(stack, jnp.clip(target, 0, count - 1), 0, keepdi...  29.3 us
    all_gather x1, blocking collectives, on_device(): sides = lax.all_gather(jnp.stack([rhs_left, right_part]), 'slab')  24.1 us
    all_gather x1, blocking collectives, on_device(): pivots = lax.all_gather(pivot_term, 'slab')  16.2 us
    all_gather x1, waiting for transfers between devices, on_device(): factors = lax.all_gather(interface_chain_factors, 'slab', axis=1)  9.96 us
    neg x1, other arithmetic, on_device(): back_all = -factors[1]  8.35 us
    all_to_all x1, starting transfers between devices, on_device(): lax.all_to_all(both_fields, 'mode', split_axis=2, concat_axis=1, tiled=True)  7.58 us
    broadcast_in_dim x2, local copies, waits for them, and re-layouts, chain_stack(): stack = jnp.broadcast_to(stack, factors.shape)  6.3 us
  transfers between devices with their start and end apart: 3, of which 3 were waited for; matrix products, arithmetic and copies ran while one was open for 4% of the time, Pallas kernels for 0%

profile of v1, /device:TPU:1, one launch (start us, length us, event | category | flops | bytes accessed | tf_op | source)
XLA Modules:
  0.0 220.1 jit_solution(16786617440290350302)
XLA Ops:
  9.7 7.6 %all-to-all-start = ((bf16[6,4,16,128]{3,0,1,2:T(8,128)(2,1)}), bf16[6,4,16,128]{3,0,1,2:T(8,128)(2,1)S(1)}, u32[]{:S(2)}, u32[]{:S(2)}) async-start(bf16[6,4,16,128]{3,0,1,2:T(8,128)(2,1)} %copy.124), calls=%async_computation | async-start | bytes 262144 | tf_op jit(solution)/shard_map/all_to_all | solution.py:114
  21.1 3.0 %all-to-all-done = bf16[6,4,16,128]{3,0,1,2:T(8,128)(2,1)S(1)} async-done(((bf16[6,4,16,128]{3,0,1,2:T(8,128)(2,1)}), bf16[6,4,16,128]{3,0,1,2:T(8,128)(2,1)S(1)}, u32[]{:S(2)}, u32[]{:S(2)}) %all-to-all-start) | async-done | bytes 98336 | tf_op jit(solution)/shard_map/all_to_all | solution.py:114
  25.7 3.6 %all-to-all-start.1 = ((bf16[3,64,1,128]{3,0,2,1:T(4,128)(2,1)}), bf16[3,64,1,128]{3,0,2,1:T(4,128)(2,1)S(1)}, u32[]{:S(2)}, u32[]{:S(2)}) async-start(bf16[3,64,1,128]{3,0,2,1:T(4,128)(2,1)} %copy.134), calls=%async_computation.1 | async-start | bytes 131072 | tf_op jit(solution)/shard_map/all_to_all | solution.py:128
  30.2 5.7 %all-to-all-done.1 = bf16[3,64,1,128]{3,0,2,1:T(4,128)(2,1)S(1)} async-done(((bf16[3,64,1,128]{3,0,2,1:T(4,128)(2,1)}), bf16[3,64,1,128]{3,0,2,1:T(4,128)(2,1)S(1)}, u32[]{:S(2)}, u32[]{:S(2)}) %all-to-all-start.1) | async-done | bytes 49184 | tf_op jit(solution)/shard_map/all_to_all | solution.py:128
  36.4 24.1 %all-gather = f32[32,4,3,128]{3,1,2,0:T(4,128)S(1)} all-gather(f32[2,4,3,128]{3,1,2,0:T(4,128)S(1)} %pad_maximum_fusion.2), channel_id=2, replica_groups=mesh['mode'=16,'slab'=16] {'slab'}, dimensions={0}, use_global_device_ids=true | all-gather | bytes 208896 | tf_op jit(solution)/shard_map/all_gather | solution.py:139
  60.5 10.0 %all-gather.5.cloned.1.call-done = f32[2,64,128,128]{3,2,1,0:T(8,128)} async-done(((f32[2,4,128,128]{3,2,1,0:T(8,128)}), f32[2,64,128,128]{3,2,1,0:T(8,128)}) %all-gather.5.cloned.1.call-update) | async-done | bytes 8388624 | tf_op jit(solution)/shard_map/all_gather | solution.py:87
  70.5 8.3 %slice_negate_fusion = (f32[1,64,128,128]{3,2,1,0:T(8,128)}, f32[1,64,128,128]{3,2,1,0:T(8,128)}) fusion(f32[2,64,128,128]{3,2,1,0:T(8,128)} %all-gather.5.cloned.1.call-done), kind=kLoop, calls=%fused_computation.14 | loop fusion | flops 2097152 | bytes 16777216 | tf_op jit(solution)/shard_map/neg | solution.py:89
  78.8 5.6 %copy.143 = f32[1,64,128,128]{2,3,1,0:T(8,128)} copy(f32[1,64,128,128]{3,2,1,0:T(8,128)} %get-tuple-element.295) | data formatting | bytes 8388608 | tf_op jit(solution)/shard_map/neg | solution.py:89
  84.4 3.7 %broadcast_in_dim.115 = f32[16,4,128,128]{2,3,1,0:T(8,128)} broadcast(f32[16,128,128]{1,2,0:T(8,128)} %get-tuple-element.299), dimensions={0,2,3} | broadcast | bytes 5242880 | tf_op jit(solution)/shard_map/broadcast_in_dim | solution.py:52
  88.2 46.0 %while.35 = (s32[]{:T(128)}, f32[4,128,128]{1,2,0:T(8,128)S(1)}, f32[16,4,128,128]{2,3,1,0:T(8,128)}, s32[]{:T(128)}, f32[16,4,128,128]{2,3,1,0:T(8,128)}, /*index=5*/s32[]{:T(128)}, s32[]{:T(128)}, s32[]{:T(128)}, s32[]{:T(128)}) while((s32[]{:T(128)}, f32[4,128,128]{1,2,0:T(8,128)S(1)}, f32[16,4,128,128]{2,3,1,0:T(8,128)}, s32[]{:T(128)}, ...), condition=%wide.region_3.4_spmd, body=%wide.region_2.3_spmd.sunk | while | flops 100728840 | bytes 2359495 | solution.py:69
  104.5 2.1 bitcast_dynamic-update-slice_fusion.5
  110.6 2.1 bitcast_dynamic-update-slice_fusion.5
  122.8 2.1 bitcast_dynamic-update-slice_fusion.5
  125.9 2.1 bitcast_dynamic-update-slice_fusion.5
  129.0 2.1 bitcast_dynamic-update-slice_fusion.5
  132.1 2.1 bitcast_dynamic-update-slice_fusion.5
  134.2 5.6 %copy.141 = f32[1,64,128,128]{2,3,1,0:T(8,128)} copy(f32[1,64,128,128]{3,2,1,0:T(8,128)} %get-tuple-element.296) | data formatting | bytes 8388608 | tf_op jit(solution)/shard_map/neg | solution.py:88
  139.8 2.6 %broadcast_in_dim.113.clone = f32[16,4,128,128]{2,3,0,1:T(8,128)} broadcast(f32[16,128,128]{1,2,0:T(8,128)S(1)} %get-tuple-element.300), dimensions={0,2,3} | broadcast | bytes 5242880 | tf_op jit(solution)/shard_map/broadcast_in_dim | solution.py:52
  142.3 46.1 %while.34 = (s32[]{:T(128)}, f32[4,128,128]{1,2,0:T(8,128)S(1)}, f32[16,4,128,128]{2,3,0,1:T(8,128)}, s32[]{:T(128)}, f32[16,4,128,128]{2,3,1,0:T(8,128)}, /*index=5*/s32[]{:T(128)}, s32[]{:T(128)}, s32[]{:T(128)}, s32[]{:T(128)}) while((s32[]{:T(128)}, f32[4,128,128]{1,2,0:T(8,128)S(1)}, f32[16,4,128,128]{2,3,0,1:T(8,128)}, s32[]{:T(128)}, ...), condition=%wide.region_1.2_spmd, body=%wide.region_0.1_spmd.sunk | while | flops 100728840 | bytes 2359507 | solution.py:69
  158.7 2.1 bitcast_dynamic-update-slice_fusion.4
  161.8 2.1 bitcast_dynamic-update-slice_fusion.4
  188.4 4.1 %convolution_bitcast_fusion.4 = f32[4,3,128]{2,1,0:T(4,128)S(1)} fusion(f32[16,4,128,128]{2,3,0,1:T(8,128)} %get-tuple-element.269, f32[16,1,4,3,128]{4,2,3,1,0:T(4,128)S(1)} %slice.96, f32[15,4,3,128]{3,2,0,1:T(4,128)S(1)} %bitcast.185), kind=kOutput, calls=%fused_computation.26 | convolution fusion | flops 37773312 | bytes 4390912 | tf_op jit(solution)/shard_map/kpab,kpcb->pca/dot_general | solution.py:142
  193.0 16.2 %all-gather.2 = f32[64,3,128]{2,1,0:T(4,128)S(1)} all-gather(f32[4,3,128]{2,1,0:T(4,128)S(1)} %fusion.81), channel_id=4, replica_groups=mesh['mode'=16,'slab'=16] {'slab'}, dimensions={0}, use_global_device_ids=true | all-gather | bytes 104448 | tf_op jit(solution)/shard_map/all_gather | solution.py:145
  209.2 2.1 convolution_bitcast_fusion.3
  (135 shorter events, 87.5 us)
Async XLA Ops:
  6.5 12.4 %copy-start = (bf16[256,1920]{1,0:T(8,128)(2,1)S(1)}, bf16[256,1920]{1,0:T(8,128)(2,1)}, u32[]{:S(2)}) copy-start(bf16[256,1920]{1,0:T(8,128)(2,1)} %param.14) | copy-start | bytes 2949124
  6.5 63.9 %all-gather.5.cloned.1.call-start = ((), (), s32[]{:S(2)}) async-start(), calls=%async_computation.2 | async-start | bytes 8912896 | tf_op jit(solution)/shard_map/all_gather | solution.py:87
  7.3 22.1 %copy-start.5 = (f32[15,128]{1,0:T(8,128)S(1)}, f32[15,128]{1,0:T(8,128)}, u32[]{:S(2)}) copy-start(f32[15,128]{1,0:T(8,128)} %param.18) | copy-start | bytes 23044
  9.7 14.5 %all-to-all-start = ((bf16[6,4,16,128]{3,0,1,2:T(8,128)(2,1)}), bf16[6,4,16,128]{3,0,1,2:T(8,128)(2,1)S(1)}, u32[]{:S(2)}, u32[]{:S(2)}) async-start(bf16[6,4,16,128]{3,0,1,2:T(8,128)(2,1)} %copy.124), calls=%async_computation | async-start | bytes 262144 | tf_op jit(solution)/shard_map/all_to_all | solution.py:114
  25.7 10.2 %all-to-all-start.1 = ((bf16[3,64,1,128]{3,0,2,1:T(4,128)(2,1)}), bf16[3,64,1,128]{3,0,2,1:T(4,128)(2,1)S(1)}, u32[]{:S(2)}, u32[]{:S(2)}) async-start(bf16[3,64,1,128]{3,0,2,1:T(4,128)(2,1)} %copy.134), calls=%async_computation.1 | async-start | bytes 131072 | tf_op jit(solution)/shard_map/all_to_all | solution.py:128
  188.4 4.1 %copy-start.4 = (f32[4,128,128]{2,1,0:T(8,128)S(1)}, f32[4,128,128]{2,1,0:T(8,128)}, u32[]{:S(2)}) copy-start(f32[4,128,128]{2,1,0:T(8,128)} %param.17) | copy-start | bytes 786436
  188.4 20.8 %copy-start.1 = (f32[16,4,128,128]{2,3,1,0:T(8,128)S(1)}, f32[16,4,128,128]{2,3,1,0:T(8,128)}, u32[]{:S(2)}) copy-start(f32[16,4,128,128]{2,3,1,0:T(8,128)} %get-tuple-element.270) | copy-start | bytes 12582916
  188.4 22.9 %copy-start.2 = (f32[2,4,128,128]{3,2,1,0:T(8,128)S(1)}, f32[2,4,128,128]{3,2,1,0:T(8,128)}, u32[]{:S(2)}) copy-start(f32[2,4,128,128]{3,2,1,0:T(8,128)} %param.16) | copy-start | bytes 1572868
  188.4 23.4 %copy-start.3 = (bf16[1920,256]{1,0:T(8,128)(2,1)S(1)}, bf16[1920,256]{1,0:T(8,128)(2,1)}, u32[]{:S(2)}) copy-start(bf16[1920,256]{1,0:T(8,128)(2,1)} %param.15) | copy-start | bytes 2949124
Sparse Core Ops, SparseCore 0:
  9.2 61.2 all-gather.4

commit v2 on v1

--- a/solution.py
+++ b/solution.py
@@ -1,3 +1,5 @@
+import functools
+
 import jax
 import jax.numpy as jnp
 from jax import lax
@@ -40,33 +42,19 @@
     return jnp.stack([first, second, third])
 
 
-def mapping_application(matrix, vectors):
-    return jnp.einsum("pab,pcb->pca", matrix, vectors, precision=HIGHEST)
-
-
-def chain_stack(factors, start, first, last, step):
-    count = factors.shape[0]
-    slots = jnp.arange(count, dtype=jnp.int32)[:, None, None, None]
-    eye = jnp.eye(factors.shape[-1], dtype=factors.dtype)
-    stack = jnp.where((slots == start) & (start >= first) & (start <= last), eye, 0.0)
-    stack = jnp.broadcast_to(stack, factors.shape)
-    running = jnp.broadcast_to(eye, factors.shape[1:])
-
-    def body(distance, carry):
-        running, stack = carry
-        target = start + step * distance
-        factor = lax.dynamic_index_in_dim(
-            factors, jnp.clip(target - step, 0, count - 1), 0, keepdims=False
-        )
-        running = jnp.einsum("pab,pbd->pad", running, factor, precision=HIGHEST)
-        valid = (target >= first) & (target <= last)
-        current = lax.dynamic_index_in_dim(stack, jnp.clip(target, 0, count - 1), 0, keepdims=False)
-        stack = lax.dynamic_update_index_in_dim(
-            stack, jnp.where(valid, running, current), jnp.clip(target, 0, count - 1), 0
-        )
-        return running, stack
-
-    return lax.fori_loop(1, count, body, (running, stack))[1]
+def owner_solve(blocks, sides, slab_count):
+    zero = jnp.zeros_like(sides[0, 0])
+    forward_values = [zero]
+    for k in range(1, slab_count):
+        source = sides[k, 0] + sides[k - 1, 1]
+        applied = jnp.einsum("ab,cb->ca", blocks[k, 0], forward_values[-1], precision=HIGHEST)
+        forward_values.append(source - applied)
+    solved = [zero] * (slab_count + 1)
+    for k in range(slab_count - 1, 0, -1):
+        pivot = jnp.einsum("ab,cb->ca", blocks[k, 2], forward_values[k], precision=HIGHEST)
+        back = jnp.einsum("ab,cb->ca", blocks[k, 1], solved[k + 1], precision=HIGHEST)
+        solved[k] = pivot - back
+    return jnp.stack(solved)
 
 
 def on_device(
@@ -78,17 +66,39 @@
     pivot_inverse,
     interior_diag,
     node_map,
+    *,
+    slab_count,
 ):
     components, planes_dev, line_count, point_total = velocity.shape
     quad_points = 3 * PLANES // 2
     slab_index = lax.axis_index("slab")
-    slab_count = lax.axis_size("slab")
+    group_size = planes_dev
+    group_count = slab_count // group_size
+    position = slab_index % group_size
+    owners = [plane * group_size + plane for plane in range(planes_dev)]
 
-    factors = lax.all_gather(interface_chain_factors, "slab", axis=1)
-    elimination_all = -factors[0]
-    back_all = -factors[1]
-    upstream = chain_stack(elimination_all, slab_index, 1, slab_count - 1, -1)
-    downstream = chain_stack(back_all, slab_index + 1, 1, slab_count - 1, 1)
+    blocks = jnp.stack(
+        [interface_chain_factors[0], interface_chain_factors[1], pivot_inverse], axis=1
+    )
+    within = [blocks[position]]
+    for offset in range(1, group_size):
+        pairs = [
+            (group * group_size + spot, group * group_size + (spot - offset) % group_size)
+            for group in range(group_count)
+            for spot in range(group_size)
+        ]
+        within.append(lax.ppermute(blocks[(position - offset) % group_size], "slab", pairs))
+    group_blocks = jnp.roll(jnp.stack(within), position, axis=0)
+    across = [group_blocks]
+    for offset in range(1, group_count):
+        pairs = [
+            (((plane + offset) % group_count) * group_size + plane, owners[plane])
+            for plane in range(planes_dev)
+        ]
+        across.append(lax.ppermute(group_blocks, "slab", pairs))
+    plane_blocks = jnp.roll(jnp.stack(across), position, axis=0).reshape(
+        (slab_count,) + blocks.shape[1:]
+    )
 
     halfway_offsets = jnp.concatenate(
         [jnp.zeros((point_total,), jnp.int32), jnp.full((point_total,), point_total, jnp.int32)]
@@ -136,17 +146,19 @@
     rhs_left = cond_line[:, :, :point_total] + line_zero_rhs
     right_part = cond_line[:, :, point_total:]
 
-    sides = lax.all_gather(jnp.stack([rhs_left, right_part]), "slab")
-    previous_right = jnp.concatenate([jnp.zeros_like(sides[:1, 1]), sides[:-1, 1]], axis=0)
-    interface_rhs = sides[:, 0] + previous_right
-    forward_results = jnp.einsum("kpab,kpcb->pca", upstream, interface_rhs, precision=HIGHEST)
-    pivot_term = mapping_application(pivot_inverse, forward_results)
-
-    pivots = lax.all_gather(pivot_term, "slab")
-    right_values = jnp.einsum("kpab,kpcb->pca", downstream, pivots, precision=HIGHEST)
-    left_solved = pivot_term - mapping_application(interface_chain_factors[1], right_values)
-    leading_flag = slab_index == 0
-    left_values = jnp.where(leading_flag, 0.0, left_solved)
+    sides = jnp.stack([rhs_left, right_part], axis=1)
+    destination_plane = jnp.asarray(
+        [owners.index(slab) if slab in owners else 0 for slab in range(slab_count)], jnp.int32
+    )
+    to_owner = lax.all_to_all(
+        sides[destination_plane], "slab", split_axis=0, concat_axis=0, tiled=True
+    )
+    solved = owner_solve(plane_blocks, to_owner, slab_count)
+    both_sides = jnp.stack([solved[:-1], solved[1:]], axis=1)
+    from_owner = lax.all_to_all(both_sides, "slab", split_axis=0, concat_axis=0, tiled=True)
+    mine = from_owner[jnp.asarray(owners)]
+    left_values = mine[:, 0]
+    right_values = mine[:, 1]
 
     boundary_line = jnp.concatenate([left_values, right_values], axis=2).astype(jnp.bfloat16)
     extension = jnp.einsum(
@@ -172,5 +184,5 @@
     )
     out_specs = P(None, "mode", "slab", None)
     return jax.shard_map(
-        on_device, mesh=mesh, in_specs=in_specs, out_specs=out_specs, check_vma=False
+        functools.partial(on_device, slab_count=mesh.shape["slab"]), mesh=mesh, in_specs=in_specs, out_specs=out_specs, check_vma=False
     )

time: 223 us -> 168 us (0.75)
  starting transfers between devices: 11.2 us -> 53.2 us
  blocking collectives: 40.2 us -> 0 us
  matrix products: 71.9 us -> 45 us
  local copies, waits for them, and re-layouts: 51.3 us -> 28 us
  waiting for transfers between devices: 19.4 us -> 33.6 us
  between operations: 13.6 us -> 0.54 us
  other arithmetic: 12.3 us -> 5.49 us
    all_gather x2 -> x0, blocking collectives: 40.2 us -> none  [the longest x1 24.1 us: on_device(): sides = lax.all_gather(jnp.stack([rhs_left, right_part]), 'slab')]
    all_to_all x0 -> x2, starting transfers between devices: none -> 30.7 us  [the longest x1 20.1 us: on_device(): lax.all_to_all(both_sides, 'slab', split_axis=0, concat_axis=0, tiled=True)]
    dot_general x34 -> x45, matrix products: 69.2 us -> 41 us  [the longest x15 15.9 us: owner_solve(): jnp.einsum('ab,cb->ca', blocks[k, 1], solved[k + 1], precision=HIGHEST)]
    dynamic_slice x30 -> x1, local copies, waits for them, and re-layouts: 29.3 us -> 2.09 us  [on_device(): jnp.roll(jnp.stack(across), position, axis=0)]
    all_to_all x0 -> x2, waiting for transfers between devices: none -> 25.7 us  [the longest x1 18.2 us: on_device(): lax.all_to_all(sides[destination_plane], 'slab', split_axis=0, concat_axi...]
    unnamed x13 -> x50, local copies, waits for them, and re-layouts: 0.06 us -> 13.9 us
    ppermute x0 -> x6, starting transfers between devices: none -> 11.9 us  [the longest x3 7.05 us: on_device(): across.append(lax.ppermute(group_blocks, 'slab', pairs))]
    neg x2 -> x0, local copies, waits for them, and re-layouts: 11.2 us -> none  [the longest x1 5.6 us: on_device(): back_all = -factors[1]]
  transfers between devices with their start and end apart: 3 -> 10, of which waited for: 3 -> 4; matrix products, arithmetic and copies ran while one was open for 4% -> 10% of each run, Pallas kernels for 0% -> 0%
where the time goes in v2:
time: 168 us; the launch traced here: 166 us
  starting transfers between devices  53.2 us (32%)
  matrix products  45 us (27%)
  waiting for transfers between devices  33.6 us (20%)
  local copies, waits for them, and re-layouts  28 us (17%)
  other arithmetic  5.49 us (3%)
    all_to_all x1, starting transfers between devices, on_device(): lax.all_to_all(both_sides, 'slab', split_axis=0, concat_axis=0, tiled=True)  20.1 us
    all_to_all x1, waiting for transfers between devices, on_device(): lax.all_to_all(sides[destination_plane], 'slab', split_axis=0, concat_axi...  18.2 us
    dot_general x15, matrix products, owner_solve(): jnp.einsum('ab,cb->ca', blocks[k, 1], solved[k + 1], precision=HIGHEST)  15.9 us
    unnamed x50, local copies, waits for them, and re-layouts  13.9 us
    dot_general x15, matrix products, owner_solve(): jnp.einsum('ab,cb->ca', blocks[k, 2], forward_values[k], precision=HIGHEST)  12.5 us
    dot_general x15, matrix products, owner_solve(): jnp.einsum('ab,cb->ca', blocks[k, 0], forward_values[-1], precision=HIGHEST)  12.5 us
    all_to_all x1, starting transfers between devices, on_device(): lax.all_to_all(sides[destination_plane], 'slab', split_axis=0, concat_axi...  10.5 us
    all_to_all x1, waiting for transfers between devices, on_device(): lax.all_to_all(both_sides, 'slab', split_axis=0, concat_axis=0, tiled=True)  7.47 us
  transfers between devices with their start and end apart: 10, of which 4 were waited for; matrix products, arithmetic and copies ran while one was open for 10% of the time, Pallas kernels for 0%

profile of v2, /device:TPU:1, one launch (start us, length us, event | category | flops | bytes accessed | tf_op | source)
XLA Modules:
  0.0 165.7 jit_solution(11577417159479648792)
XLA Ops:
  0.1 1.1 slice_bitcast_fusion.1
  3.2 3.2 %collective-permute-start = (f32[3,128,128]{2,1,0:T(8,128)}, f32[3,128,128]{2,1,0:T(8,128)S(1)}, u32[]{:S(2)}, u32[]{:S(2)}) collective-permute-start(f32[3,128,128]{2,1,0:T(8,128)} %get-tuple-element.10), channel_id=1, source_target_pairs={{0,3},{1,0},{2,1},{3,2},{4,7},{5,4},{6,5},{7,6},{8,11},{9,8},{10,9... | collective-permute-start | bytes 589832 | tf_op jit(solution)/shard_map/ppermute | solution.py:90
  6.4 1.6 collective-permute-start.2
  8.8 6.4 %all-to-all-start = ((bf16[6,4,16,128]{3,0,1,2:T(8,128)(2,1)}), bf16[6,4,16,128]{3,0,1,2:T(8,128)(2,1)}, u32[]{:S(2)}, u32[]{:S(2)}) async-start(bf16[6,4,16,128]{3,0,1,2:T(8,128)(2,1)} %copy.155), calls=%async_computation | async-start | bytes 262144 | tf_op jit(solution)/shard_map/all_to_all | solution.py:124
  18.6 1.4 broadcast_add_fusion
  20.5 2.5 %all-to-all-done = bf16[6,4,16,128]{3,0,1,2:T(8,128)(2,1)} async-done(((bf16[6,4,16,128]{3,0,1,2:T(8,128)(2,1)}), bf16[6,4,16,128]{3,0,1,2:T(8,128)(2,1)}, u32[]{:S(2)}, u32[]{:S(2)}) %all-to-all-start) | async-done | bytes 98336 | tf_op jit(solution)/shard_map/all_to_all | solution.py:124
  23.9 1.1 fusion.54
  26.7 4.2 %all-to-all-start.1 = ((bf16[3,64,1,128]{3,0,2,1:T(4,128)(2,1)}), bf16[3,64,1,128]{3,0,2,1:T(4,128)(2,1)}, u32[]{:S(2)}, u32[]{:S(2)}) async-start(bf16[3,64,1,128]{3,0,2,1:T(4,128)(2,1)} %copy.165), calls=%async_computation.1 | async-start | bytes 131072 | tf_op jit(solution)/shard_map/all_to_all | solution.py:138
  32.1 5.4 %all-to-all-done.1 = bf16[3,64,1,128]{3,0,2,1:T(4,128)(2,1)} async-done(((bf16[3,64,1,128]{3,0,2,1:T(4,128)(2,1)}), bf16[3,64,1,128]{3,0,2,1:T(4,128)(2,1)}, u32[]{:S(2)}, u32[]{:S(2)}) %all-to-all-start.1) | async-done | bytes 49184 | tf_op jit(solution)/shard_map/all_to_all | solution.py:138
  43.7 2.1 %bitcast_dynamic-update-slice_fusion.6 = (f32[8,4,3,128,128]{4,3,2,1,0:T(8,128)}, f32[4,3,128,128]{3,2,1,0:T(8,128)S(1)}) fusion(f32[8,3,128,128]{3,2,1,0:T(8,128)} %bitcast_dynamic-update-slice_fusion.9, s32[]{:T(128)S(6)} %select_n.139), kind=kLoop, calls=%fused_computation.49 | loop fusion | bytes 2359300
  46.6 1.3 gather_fusion
  47.9 10.5 %all-to-all-start.2 = ((f32[16,2,3,128]{3,1,2,0:T(2,128)}), f32[16,2,3,128]{3,1,2,0:T(2,128)S(1)}, u32[]{:S(2)}, u32[]{:S(2)}) async-start(f32[16,2,3,128]{3,1,2,0:T(2,128)} %gather_fusion), calls=%async_computation.2 | async-start | bytes 98304 | tf_op jit(solution)/shard_map/all_to_all | solution.py:153
  59.2 5.7 %collective-permute-start.5 = (f32[4,3,128,128]{3,2,1,0:T(8,128)S(1)}, f32[4,3,128,128]{3,2,1,0:T(8,128)}, u32[]{:S(2)}, u32[]{:S(2)}) collective-permute-start(f32[4,3,128,128]{3,2,1,0:T(8,128)S(1)} %get-tuple-element.6), channel_id=1, source_target_pairs={{12,0},{1,5},{6,10},{11,15},{28,16},{17,21},{22,26},{27,31},{44,32... | collective-permute-start | bytes 2359304 | tf_op jit(solution)/shard_map/ppermute | solution.py:98
  64.9 18.2 %all-to-all-done.2 = f32[16,2,3,128]{3,1,2,0:T(2,128)S(1)} async-done(((f32[16,2,3,128]{3,1,2,0:T(2,128)}), f32[16,2,3,128]{3,1,2,0:T(2,128)S(1)}, u32[]{:S(2)}, u32[]{:S(2)}) %all-to-all-start.2) | async-done | bytes 49184 | tf_op jit(solution)/shard_map/all_to_all | solution.py:153
  85.1 2.1 %bitcast_dynamic-update-slice_fusion = f32[8,4,3,128,128]{4,3,2,1,0:T(8,128)} fusion(f32[8,4,3,128,128]{4,3,2,1,0:T(8,128)} %bitcast_dynamic-update-slice_fusion.2, f32[4,3,128,128]{3,2,1,0:T(8,128)} %collective-permute-done.5), kind=kLoop, calls=%fused_computation.43 | loop fusion | bytes 1572864
  90.0 2.1 %bitcast_dynamic-update-slice_fusion.1 = f32[8,4,3,128,128]{4,3,2,1,0:T(8,128)} fusion(f32[8,4,3,128,128]{4,3,2,1,0:T(8,128)} %bitcast_dynamic-update-slice_fusion.3, f32[4,3,128,128]{3,2,1,0:T(8,128)} %collective-permute-done.5), kind=kLoop, calls=%fused_computation.44 | loop fusion | bytes 1572864 | tf_op jit(solution)/shard_map/jit(_roll_dynamic)/concatenate | solution.py:99
  92.1 2.1 %constant_dynamic-slice_fusion = f32[4,4,3,128,128]{4,3,2,1,0:T(8,128)S(1)} fusion(f32[8,4,3,128,128]{4,3,2,1,0:T(8,128)} %bitcast_dynamic-update-slice_fusion.1, s32[]{:T(128)S(6)} %select_n.139), kind=kLoop, calls=%fused_computation.268 | loop fusion | bytes 6291460 | tf_op jit(solution)/shard_map/jit(_roll_dynamic)/dynamic_slice | solution.py:99
  96.0 1.1 convolution_subtract_fusion.25
  100.2 1.1 convolution_subtract_fusion.23
  104.4 1.1 convolution_subtract_fusion.21
  108.7 1.1 convolution_subtract_fusion.19
  134.2 1.1 constant_dynamic-update-slice_fusion.14
  136.1 20.1 %all-to-all-start.3 = ((f32[16,2,3,128]{3,1,2,0:T(2,128)}), f32[16,2,3,128]{3,1,2,0:T(2,128)S(1)}, u32[]{:S(2)}, u32[]{:S(2)}) async-start(f32[16,2,3,128]{3,1,2,0:T(2,128)} %copy.201), calls=%async_computation.3 | async-start | bytes 98304 | tf_op jit(solution)/shard_map/all_to_all | solution.py:158
  156.3 7.5 %all-to-all-done.3 = f32[16,2,3,128]{3,1,2,0:T(2,128)S(1)} async-done(((f32[16,2,3,128]{3,1,2,0:T(2,128)}), f32[16,2,3,128]{3,1,2,0:T(2,128)S(1)}, u32[]{:S(2)}, u32[]{:S(2)}) %all-to-all-start.3) | async-done | bytes 49184 | tf_op jit(solution)/shard_map/all_to_all | solution.py:158
  (139 shorter events, 61.2 us)
Async XLA Ops:
  0.0 16.9 %copy-start = (bf16[256,1920]{1,0:T(8,128)(2,1)S(1)}, bf16[256,1920]{1,0:T(8,128)(2,1)}, u32[]{:S(2)}) copy-start(bf16[256,1920]{1,0:T(8,128)(2,1)} %param.12) | copy-start | bytes 2949124
  0.0 16.3 %copy-start.10 = (s32[16]{0:T(128)S(1)}, s32[16]{0:T(128)}, u32[]{:S(2)}) copy-start(s32[16]{0:T(128)} %constant.162) | copy-start | bytes 196
  0.0 16.9 %copy-start.9 = (s32[1,256]{1,0:T(1,128)S(1)}, s32[1,256]{1,0:T(1,128)}, u32[]{:S(2)}) copy-start(s32[1,256]{1,0:T(1,128)} %constant.129.clone.1) | copy-start | bytes 3076
  0.0 8.1 %copy-start.3 = (f32[3,4,16,128]{3,2,1,0:T(8,128)S(1)}, f32[3,4,16,128]{3,2,1,0:T(8,128)}, u32[]{:S(2)}) copy-start(f32[3,4,16,128]{3,2,1,0:T(8,128)} %param.10) | copy-start | bytes 294916
  0.0 8.1 %copy-start.5 = (bf16[3,4,16,128]{3,2,1,0:T(8,128)(2,1)S(1)}, bf16[3,4,16,128]{3,2,1,0:T(8,128)(2,1)}, u32[]{:S(2)}) copy-start(bf16[3,4,16,128]{3,2,1,0:T(8,128)(2,1)} %param.11) | copy-start | bytes 147460
  0.0 16.9 %copy-start.8 = (s32[1,256]{1,0:T(1,128)S(1)}, s32[1,256]{1,0:T(1,128)}, u32[]{:S(2)}) copy-start(s32[1,256]{1,0:T(1,128)} %param.17) | copy-start | bytes 3076
  3.2 35.6 %collective-permute-start = (f32[3,128,128]{2,1,0:T(8,128)}, f32[3,128,128]{2,1,0:T(8,128)S(1)}, u32[]{:S(2)}, u32[]{:S(2)}) collective-permute-start(f32[3,128,128]{2,1,0:T(8,128)} %get-tuple-element.10), channel_id=1, source_target_pairs={{0,3},{1,0},{2,1},{3,2},{4,7},{5,4},{6,5},{7,6},{8,11},{9,8},{10,9... | collective-permute-start | bytes 589832 | tf_op jit(solution)/shard_map/ppermute | solution.py:90
  6.4 33.1 %collective-permute-start.1 = (f32[3,128,128]{2,1,0:T(8,128)}, f32[3,128,128]{2,1,0:T(8,128)S(1)}, u32[]{:S(2)}, u32[]{:S(2)}) collective-permute-start(f32[3,128,128]{2,1,0:T(8,128)} %get-tuple-element.9), channel_id=1, source_target_pairs={{0,2},{1,3},{2,0},{3,1},{4,6},{5,7},{6,4},{7,5},{8,10},{9,11},{10,... | collective-permute-start | bytes 589832 | tf_op jit(solution)/shard_map/ppermute | solution.py:90
  6.4 33.8 %collective-permute-start.2 = (f32[3,128,128]{2,1,0:T(8,128)}, f32[3,128,128]{2,1,0:T(8,128)S(1)}, u32[]{:S(2)}, u32[]{:S(2)}) collective-permute-start(f32[3,128,128]{2,1,0:T(8,128)} %get-tuple-element.7), channel_id=1, source_target_pairs={{0,1},{1,2},{2,3},{3,0},{4,5},{5,6},{6,7},{7,4},{8,9},{9,10},{10,1... | collective-permute-start | bytes 589832 | tf_op jit(solution)/shard_map/ppermute | solution.py:90
  8.8 14.1 %all-to-all-start = ((bf16[6,4,16,128]{3,0,1,2:T(8,128)(2,1)}), bf16[6,4,16,128]{3,0,1,2:T(8,128)(2,1)}, u32[]{:S(2)}, u32[]{:S(2)}) async-start(bf16[6,4,16,128]{3,0,1,2:T(8,128)(2,1)} %copy.155), calls=%async_computation | async-start | bytes 262144 | tf_op jit(solution)/shard_map/all_to_all | solution.py:124
  26.7 10.8 %all-to-all-start.1 = ((bf16[3,64,1,128]{3,0,2,1:T(4,128)(2,1)}), bf16[3,64,1,128]{3,0,2,1:T(4,128)(2,1)}, u32[]{:S(2)}, u32[]{:S(2)}) async-start(bf16[3,64,1,128]{3,0,2,1:T(4,128)(2,1)} %copy.165), calls=%async_computation.1 | async-start | bytes 131072 | tf_op jit(solution)/shard_map/all_to_all | solution.py:138
  37.5 9.0 %copy-start.7 = (f32[3,4,1,128]{3,2,1,0:T(1,128)S(1)}, f32[3,4,1,128]{3,2,1,0:T(1,128)}, u32[]{:S(2)}) copy-start(f32[3,4,1,128]{3,2,1,0:T(1,128)} %slice.301) | copy-start | bytes 18436
  45.8 37.3 %collective-permute-start.3 = (f32[4,3,128,128]{3,2,1,0:T(8,128)S(1)}, f32[4,3,128,128]{3,2,1,0:T(8,128)S(1)}, u32[]{:S(2)}, u32[]{:S(2)}) collective-permute-start(f32[4,3,128,128]{3,2,1,0:T(8,128)S(1)} %get-tuple-element.6), channel_id=1, source_target_pairs={{4,0},{9,5},{14,10},{3,15},{20,16},{25,21},{30,26},{19,31},{36,32}... | collective-permute-start | bytes 2359304 | tf_op jit(solution)/shard_map/ppermute | solution.py:98
  47.9 35.2 %all-to-all-start.2 = ((f32[16,2,3,128]{3,1,2,0:T(2,128)}), f32[16,2,3,128]{3,1,2,0:T(2,128)S(1)}, u32[]{:S(2)}, u32[]{:S(2)}) async-start(f32[16,2,3,128]{3,1,2,0:T(2,128)} %gather_fusion), calls=%async_computation.2 | async-start | bytes 98304 | tf_op jit(solution)/shard_map/all_to_all | solution.py:153
  58.5 25.6 %collective-permute-start.4 = (f32[4,3,128,128]{3,2,1,0:T(8,128)S(1)}, f32[4,3,128,128]{3,2,1,0:T(8,128)S(1)}, u32[]{:S(2)}, u32[]{:S(2)}) collective-permute-start(f32[4,3,128,128]{3,2,1,0:T(8,128)S(1)} %get-tuple-element.6), channel_id=1, source_target_pairs={{8,0},{13,5},{2,10},{7,15},{24,16},{29,21},{18,26},{23,31},{40,32}... | collective-permute-start | bytes 2359304 | tf_op jit(solution)/shard_map/ppermute | solution.py:98
  59.2 25.9 %collective-permute-start.5 = (f32[4,3,128,128]{3,2,1,0:T(8,128)S(1)}, f32[4,3,128,128]{3,2,1,0:T(8,128)}, u32[]{:S(2)}, u32[]{:S(2)}) collective-permute-start(f32[4,3,128,128]{3,2,1,0:T(8,128)S(1)} %get-tuple-element.6), channel_id=1, source_target_pairs={{12,0},{1,5},{6,10},{11,15},{28,16},{17,21},{22,26},{27,31},{44,32... | collective-permute-start | bytes 2359304 | tf_op jit(solution)/shard_map/ppermute | solution.py:98
  94.2 1.8 %copy-start.1 = (f32[4,4,3,128,128]{4,3,2,1,0:T(8,128)}, f32[4,4,3,128,128]{4,3,2,1,0:T(8,128)S(1)}, u32[]{:S(2)}) copy-start(f32[4,4,3,128,128]{4,3,2,1,0:T(8,128)S(1)} %constant_dynamic-slice_fusion) | copy-start | bytes 9437188
  94.2 40.0 %copy-start.6 = (f32[16,3,128]{2,1,0:T(4,128)S(1)}, f32[16,3,128]{2,1,0:T(4,128)}, u32[]{:S(2)}) copy-start(f32[16,3,128]{2,1,0:T(4,128)} %constant_dynamic-update-slice_fusion.15) | copy-start | bytes 73732
  94.2 70.2 %copy-start.2 = (bf16[1920,256]{1,0:T(8,128)(2,1)S(1)}, bf16[1920,256]{1,0:T(8,128)(2,1)}, u32[]{:S(2)}) copy-start(bf16[1920,256]{1,0:T(8,128)(2,1)} %param.13) | copy-start | bytes 2949124
  94.2 70.8 %copy-start.4 = (f32[4,15,128]{2,0,1:T(4,128)S(1)}, f32[4,15,128]{2,0,1:T(4,128)}, u32[]{:S(2)}) copy-start(f32[4,15,128]{2,0,1:T(4,128)} %broadcast_add_fusion) | copy-start | bytes 92164
  136.1 27.6 %all-to-all-start.3 = ((f32[16,2,3,128]{3,1,2,0:T(2,128)}), f32[16,2,3,128]{3,1,2,0:T(2,128)S(1)}, u32[]{:S(2)}, u32[]{:S(2)}) async-start(f32[16,2,3,128]{3,1,2,0:T(2,128)} %copy.201), calls=%async_computation.3 | async-start | bytes 98304 | tf_op jit(solution)/shard_map/all_to_all | solution.py:158

commit v3 on v2

--- a/solution.py
+++ b/solution.py
@@ -3,6 +3,8 @@
 import jax
 import jax.numpy as jnp
 from jax import lax
+from jax.experimental import pallas as pl
+from jax.experimental.pallas import tpu as pltpu
 from jax.sharding import PartitionSpec as P
 
 PLANES = 64
@@ -42,19 +44,38 @@
     return jnp.stack([first, second, third])
 
 
-def owner_solve(blocks, sides, slab_count):
-    zero = jnp.zeros_like(sides[0, 0])
+def chain_kernel(position_ref, blocks_ref, sides_ref, out_ref, *, group_size):
+    slab_count = sides_ref.shape[0]
+    position = position_ref[0]
+
+    def slot(slab):
+        group_slot = (slab // group_size - position + group_size) % group_size
+        spot_slot = (slab % group_size - position + group_size) % group_size
+        return group_slot * group_size + spot_slot
+
+    def apply(matrix, vectors):
+        return lax.dot_general(
+            vectors,
+            matrix,
+            (((1,), (1,)), ((), ())),
+            precision=HIGHEST,
+            preferred_element_type=jnp.float32,
+        )
+
+    zero = jnp.zeros(sides_ref.shape[2:], jnp.float32)
     forward_values = [zero]
     for k in range(1, slab_count):
-        source = sides[k, 0] + sides[k - 1, 1]
-        applied = jnp.einsum("ab,cb->ca", blocks[k, 0], forward_values[-1], precision=HIGHEST)
-        forward_values.append(source - applied)
-    solved = [zero] * (slab_count + 1)
+        source = sides_ref[k, 0] + sides_ref[k - 1, 1]
+        forward_values.append(source - apply(blocks_ref[slot(k), 0], forward_values[-1]))
+    after = zero
     for k in range(slab_count - 1, 0, -1):
-        pivot = jnp.einsum("ab,cb->ca", blocks[k, 2], forward_values[k], precision=HIGHEST)
-        back = jnp.einsum("ab,cb->ca", blocks[k, 1], solved[k + 1], precision=HIGHEST)
-        solved[k] = pivot - back
-    return jnp.stack(solved)
+        blocks = blocks_ref[slot(k)]
+        solved = apply(blocks[2], forward_values[k]) - apply(blocks[1], after)
+        out_ref[k, 0] = solved
+        out_ref[k, 1] = after
+        after = solved
+    out_ref[0, 0] = zero
+    out_ref[0, 1] = after
 
 
 def on_device(
@@ -88,7 +109,7 @@
             for spot in range(group_size)
         ]
         within.append(lax.ppermute(blocks[(position - offset) % group_size], "slab", pairs))
-    group_blocks = jnp.roll(jnp.stack(within), position, axis=0)
+    group_blocks = jnp.stack(within)
     across = [group_blocks]
     for offset in range(1, group_count):
         pairs = [
@@ -96,9 +117,7 @@
             for plane in range(planes_dev)
         ]
         across.append(lax.ppermute(group_blocks, "slab", pairs))
-    plane_blocks = jnp.roll(jnp.stack(across), position, axis=0).reshape(
-        (slab_count,) + blocks.shape[1:]
-    )
+    plane_blocks = jnp.concatenate(across, axis=0)
 
     halfway_offsets = jnp.concatenate(
         [jnp.zeros((point_total,), jnp.int32), jnp.full((point_total,), point_total, jnp.int32)]
@@ -153,8 +172,16 @@
     to_owner = lax.all_to_all(
         sides[destination_plane], "slab", split_axis=0, concat_axis=0, tiled=True
     )
-    solved = owner_solve(plane_blocks, to_owner, slab_count)
-    both_sides = jnp.stack([solved[:-1], solved[1:]], axis=1)
+    both_sides = pl.pallas_call(
+        functools.partial(chain_kernel, group_size=group_size),
+        out_shape=jax.ShapeDtypeStruct(to_owner.shape, jnp.float32),
+        in_specs=[
+            pl.BlockSpec(memory_space=pltpu.SMEM),
+            pl.BlockSpec(memory_space=pltpu.VMEM),
+            pl.BlockSpec(memory_space=pltpu.VMEM),
+        ],
+        out_specs=pl.BlockSpec(memory_space=pltpu.VMEM),
+    )(position.astype(jnp.int32).reshape(1), plane_blocks, to_owner)
     from_owner = lax.all_to_all(both_sides, "slab", split_axis=0, concat_axis=0, tiled=True)
     mine = from_owner[jnp.asarray(owners)]
     left_values = mine[:, 0]

time: 168 us -> 120 us (0.71); the launches traced: 166 us -> 120 us
  matrix products: 45 us -> 2.67 us
  local copies, waits for them, and re-layouts: 28 us -> 15.4 us
  Pallas kernels: 0 us -> 11 us
  other arithmetic: 5.49 us -> 1.43 us
  waiting for transfers between devices: 33.6 us -> 36.8 us
    dot_general x45 -> x0, matrix products: 41 us -> none  [the longest x15 15.9 us: owner_solve(): jnp.einsum('ab,cb->ca', blocks[k, 1], solved[k + 1], precision=HIGHEST)]
    pallas_call x0 -> x1, Pallas kernels: none -> 11 us  [on_device(): pl.pallas_call(functools.partial(chain_kernel, group_size=group_size), ou...]
    unnamed x50 -> x22, local copies, waits for them, and re-layouts: 13.9 us -> 5.28 us
    all_to_all x1, waiting for transfers between devices: 2.46 us -> 6.45 us  [on_device(): lax.all_to_all(both_fields, 'mode', split_axis=2, concat_axis=1, tiled=True)]
    dynamic_slice x1 -> x0, local copies, waits for them, and re-layouts: 2.09 us -> none  [on_device(): jnp.roll(jnp.stack(across), position, axis=0)]
    all_to_all x1, waiting for transfers between devices: 18.2 us -> 16.5 us  [on_device(): lax.all_to_all(sides[destination_plane], 'slab', split_axis=0, concat_axi...]
  transfers between devices with their start and end apart: 10 -> 10, of which waited for: 4 -> 4; matrix products, arithmetic and copies ran while one was open for 10% -> 9% of each run, Pallas kernels for 0% -> 0%
where the time goes in v3:
time: 120 us
  starting transfers between devices  51.7 us (43%)
  waiting for transfers between devices  36.8 us (31%)
  local copies, waits for them, and re-layouts  15.4 us (13%)
  Pallas kernels  11 us (9%)
  matrix products  2.67 us (2%)
  other arithmetic  1.43 us (1%)
    all_to_all x1, starting transfers between devices, on_device(): lax.all_to_all(both_sides, 'slab', split_axis=0, concat_axis=0, tiled=True)  19.2 us
    all_to_all x1, waiting for transfers between devices, on_device(): lax.all_to_all(sides[destination_plane], 'slab', split_axis=0, concat_axi...  16.5 us
    pallas_call x1, Pallas kernels, on_device(): pl.pallas_call(functools.partial(chain_kernel, group_size=group_size), ou...  11 us
    all_to_all x1, starting transfers between devices, on_device(): lax.all_to_all(sides[destination_plane], 'slab', split_axis=0, concat_axi...  10.7 us
    all_to_all x1, waiting for transfers between devices, on_device(): lax.all_to_all(both_sides, 'slab', split_axis=0, concat_axis=0, tiled=True)  7.47 us
    ppermute x3, starting transfers between devices, on_device(): across.append(lax.ppermute(group_blocks, 'slab', pairs))  7.08 us
    all_to_all x1, waiting for transfers between devices, on_device(): lax.all_to_all(both_fields, 'mode', split_axis=2, concat_axis=1, tiled=True)  6.45 us
    all_to_all x1, waiting for transfers between devices, on_device(): lax.all_to_all(nonlin_lines, 'mode', split_axis=1, concat_axis=2, tiled=T...  6.43 us
  transfers between devices with their start and end apart: 10, of which 4 were waited for; matrix products, arithmetic and copies ran while one was open for 9% of the time, Pallas kernels for 0%

profile of v3, /device:TPU:1, one launch (start us, length us, event | category | flops | bytes accessed | tf_op | source)
XLA Modules:
  0.0 119.6 jit_solution(12250581981301668352)
XLA Ops:
  0.1 1.1 slice_bitcast_fusion.1
  1.3 1.0 pad_maximum_fusion
  2.3 0.9 dynamic-slice_bitcast_fusion
  3.2 3.2 %collective-permute-start = (f32[3,128,128]{2,1,0:T(8,128)}, f32[3,128,128]{2,1,0:T(8,128)S(1)}, u32[]{:S(2)}, u32[]{:S(2)}) collective-permute-start(f32[3,128,128]{2,1,0:T(8,128)} %get-tuple-element.9), channel_id=1, source_target_pairs={{0,3},{1,0},{2,1},{3,2},{4,7},{5,4},{6,5},{7,6},{8,11},{9,8},{10,9... | collective-permute-start | bytes 589832 | tf_op jit(solution)/shard_map/ppermute | solution.py:111
  6.4 1.6 %collective-permute-start.2 = (f32[3,128,128]{2,1,0:T(8,128)S(1)}, f32[3,128,128]{2,1,0:T(8,128)S(1)}, u32[]{:S(2)}, u32[]{:S(2)}) collective-permute-start(f32[3,128,128]{2,1,0:T(8,128)S(1)} %get-tuple-element.7), channel_id=1, source_target_pairs={{0,1},{1,2},{2,3},{3,0},{4,5},{5,6},{6,7},{7,4},{8,9},{9,10},{10,1... | collective-permute-start | bytes 589832 | tf_op jit(solution)/shard_map/ppermute | solution.py:111
  8.1 0.7 copy.123
  8.8 6.4 %all-to-all-start = ((bf16[6,4,16,128]{3,0,1,2:T(8,128)(2,1)}), bf16[6,4,16,128]{3,0,1,2:T(8,128)(2,1)S(1)}, u32[]{:S(2)}, u32[]{:S(2)}) async-start(bf16[6,4,16,128]{3,0,1,2:T(8,128)(2,1)} %copy.123), calls=%async_computation | async-start | bytes 262144 | tf_op jit(solution)/shard_map/all_to_all | solution.py:143
  16.4 6.5 %all-to-all-done = bf16[6,4,16,128]{3,0,1,2:T(8,128)(2,1)S(1)} async-done(((bf16[6,4,16,128]{3,0,1,2:T(8,128)(2,1)}), bf16[6,4,16,128]{3,0,1,2:T(8,128)(2,1)S(1)}, u32[]{:S(2)}, u32[]{:S(2)}) %all-to-all-start) | async-done | bytes 98336 | tf_op jit(solution)/shard_map/all_to_all | solution.py:143
  24.4 3.5 %all-to-all-start.1 = ((bf16[3,64,1,128]{3,0,2,1:T(4,128)(2,1)}), bf16[3,64,1,128]{3,0,2,1:T(4,128)(2,1)S(1)}, u32[]{:S(2)}, u32[]{:S(2)}) async-start(bf16[3,64,1,128]{3,0,2,1:T(4,128)(2,1)} %copy.133), calls=%async_computation.1 | async-start | bytes 131072 | tf_op jit(solution)/shard_map/all_to_all | solution.py:157
  27.9 6.4 %all-to-all-done.1 = bf16[3,64,1,128]{3,0,2,1:T(4,128)(2,1)S(1)} async-done(((bf16[3,64,1,128]{3,0,2,1:T(4,128)(2,1)}), bf16[3,64,1,128]{3,0,2,1:T(4,128)(2,1)S(1)}, u32[]{:S(2)}, u32[]{:S(2)}) %all-to-all-start.1) | async-done | bytes 49184 | tf_op jit(solution)/shard_map/all_to_all | solution.py:157
  34.9 0.7 collective-permute-start.3
  35.7 1.2 %gather_fusion = f32[16,2,3,128]{3,1,2,0:T(2,128)} fusion(f32[4,2,3,128]{3,1,2,0:T(2,128)S(1)} %copy.138, s32[1024]{0:T(1024)S(1)} %pad_clamp_fusion.1), kind=kCustom, calls=%fused_computation | custom fusion | bytes 98368 | tf_op jit(solution)/shard_map/gather | solution.py:173
  36.9 10.7 %all-to-all-start.2 = ((f32[16,2,3,128]{3,1,2,0:T(2,128)}), f32[16,2,3,128]{3,1,2,0:T(2,128)S(1)}, u32[]{:S(2)}, u32[]{:S(2)}) async-start(f32[16,2,3,128]{3,1,2,0:T(2,128)} %gather_fusion), calls=%async_computation.2 | async-start | bytes 98304 | tf_op jit(solution)/shard_map/all_to_all | solution.py:172
  47.6 1.5 %collective-permute-start.4 = (f32[4,3,128,128]{3,2,1,0:T(8,128)S(1)}, f32[4,3,128,128]{3,2,1,0:T(8,128)}, u32[]{:S(2)}, u32[]{:S(2)}) collective-permute-start(f32[4,3,128,128]{3,2,1,0:T(8,128)S(1)} %pad_maximum_fusion.1), channel_id=1, source_target_pairs={{8,0},{13,5},{2,10},{7,15},{24,16},{29,21},{18,26},{23,31},{40,32}... | collective-permute-start | bytes 2359304 | tf_op jit(solution)/shard_map/ppermute | solution.py:119
  49.1 4.8 %collective-permute-start.5 = (f32[4,3,128,128]{3,2,1,0:T(8,128)S(1)}, f32[4,3,128,128]{3,2,1,0:T(8,128)}, u32[]{:S(2)}, u32[]{:S(2)}) collective-permute-start(f32[4,3,128,128]{3,2,1,0:T(8,128)S(1)} %pad_maximum_fusion.1), channel_id=1, source_target_pairs={{12,0},{1,5},{6,10},{11,15},{28,16},{17,21},{22,26},{27,31},{44,32... | collective-permute-start | bytes 2359304 | tf_op jit(solution)/shard_map/ppermute | solution.py:119
  54.6 0.7 constant_dynamic-update-slice_fusion.4
  56.0 16.5 %all-to-all-done.2 = f32[16,2,3,128]{3,1,2,0:T(2,128)S(1)} async-done(((f32[16,2,3,128]{3,1,2,0:T(2,128)}), f32[16,2,3,128]{3,1,2,0:T(2,128)S(1)}, u32[]{:S(2)}, u32[]{:S(2)}) %all-to-all-start.2) | async-done | bytes 49184 | tf_op jit(solution)/shard_map/all_to_all | solution.py:172
  73.1 1.0 constant_dynamic-update-slice_fusion.2
  74.1 2.2 %constant_dynamic-update-slice_fusion.1 = f32[16,3,128,128]{3,2,1,0:T(8,128)} fusion(f32[16,3,128,128]{3,2,1,0:T(8,128)} %constant_dynamic-update-slice_fusion.2, f32[4,3,128,128]{3,2,1,0:T(8,128)} %collective-permute-done.4), kind=kLoop, calls=%fused_computation.81 | loop fusion | bytes 1572864
  76.3 2.1 %constant_dynamic-update-slice_fusion.blocks_ref = f32[16,3,128,128]{3,2,1,0:T(8,128)} fusion(f32[16,3,128,128]{3,2,1,0:T(8,128)} %constant_dynamic-update-slice_fusion.1, f32[4,3,128,128]{3,2,1,0:T(8,128)} %collective-permute-done.5), kind=kLoop, calls=%fused_computation.80 | loop fusion | bytes 1572864 | tf_op jit(solution)/shard_map/concatenate | solution.py:120
  78.4 11.0 %shard_map.100 = f32[16,2,3,128]{3,2,1,0:T(4,128)} custom-call(s32[1]{0:T(128)} %bitcast.position_ref, f32[16,3,128,128]{3,2,1,0:T(8,128)} %constant_dynamic-update-slice_fusion.blocks_ref, f32[16,2,3,128]{3,2,1,0:T(4,128)} %copy.139.sides_ref), custom_call_target="tpu_custom_call" | custom-call | tf_op jit(solution)/shard_map/pallas_call | solution.py:175
  89.4 1.5 %copy.140 = f32[16,2,3,128]{3,1,2,0:T(2,128)} copy(f32[16,2,3,128]{3,2,1,0:T(4,128)} %shard_map.100) | data formatting | bytes 98304 | tf_op jit(solution)/shard_map/pallas_call | solution.py:175
  90.9 19.2 %all-to-all-start.3 = ((f32[16,2,3,128]{3,1,2,0:T(2,128)}), f32[16,2,3,128]{3,1,2,0:T(2,128)S(1)}, u32[]{:S(2)}, u32[]{:S(2)}) async-start(f32[16,2,3,128]{3,1,2,0:T(2,128)} %copy.140), calls=%async_computation.3 | async-start | bytes 98304 | tf_op jit(solution)/shard_map/all_to_all | solution.py:185
  110.1 7.5 %all-to-all-done.3 = f32[16,2,3,128]{3,1,2,0:T(2,128)S(1)} async-done(((f32[16,2,3,128]{3,1,2,0:T(2,128)}), f32[16,2,3,128]{3,1,2,0:T(2,128)S(1)}, u32[]{:S(2)}, u32[]{:S(2)}) %all-to-all-start.3) | async-done | bytes 49184 | tf_op jit(solution)/shard_map/all_to_all | solution.py:185
  (62 shorter events, 7.2 us)
Async XLA Ops:
  0.0 15.3 %copy-start = (bf16[256,1920]{1,0:T(8,128)(2,1)S(1)}, bf16[256,1920]{1,0:T(8,128)(2,1)}, u32[]{:S(2)}) copy-start(bf16[256,1920]{1,0:T(8,128)(2,1)} %param.12) | copy-start | bytes 2949124
  0.0 15.2 %copy-start.7 = (s32[16]{0:T(128)S(1)}, s32[16]{0:T(128)}, u32[]{:S(2)}) copy-start(s32[16]{0:T(128)} %constant.133) | copy-start | bytes 196
  0.0 15.3 %copy-start.6 = (s32[1,256]{1,0:T(1,128)S(1)}, s32[1,256]{1,0:T(1,128)}, u32[]{:S(2)}) copy-start(s32[1,256]{1,0:T(1,128)} %constant.108.clone.1) | copy-start | bytes 3076
  0.0 8.0 %copy-start.2 = (f32[3,4,16,128]{3,2,1,0:T(8,128)S(1)}, f32[3,4,16,128]{3,2,1,0:T(8,128)}, u32[]{:S(2)}) copy-start(f32[3,4,16,128]{3,2,1,0:T(8,128)} %param.10) | copy-start | bytes 294916
  0.0 8.0 %copy-start.3 = (bf16[3,4,16,128]{3,2,1,0:T(8,128)(2,1)S(1)}, bf16[3,4,16,128]{3,2,1,0:T(8,128)(2,1)}, u32[]{:S(2)}) copy-start(bf16[3,4,16,128]{3,2,1,0:T(8,128)(2,1)} %param.11) | copy-start | bytes 147460
  0.0 15.2 %copy-start.5 = (s32[1,256]{1,0:T(1,128)S(1)}, s32[1,256]{1,0:T(1,128)}, u32[]{:S(2)}) copy-start(s32[1,256]{1,0:T(1,128)} %param.17) | copy-start | bytes 3076
  2.3 14.0 %copy-start.4 = (f32[15,128]{1,0:T(8,128)S(1)}, f32[15,128]{1,0:T(8,128)}, u32[]{:S(2)}) copy-start(f32[15,128]{1,0:T(8,128)} %param.16) | copy-start | bytes 23044
  3.2 31.7 %collective-permute-start = (f32[3,128,128]{2,1,0:T(8,128)}, f32[3,128,128]{2,1,0:T(8,128)S(1)}, u32[]{:S(2)}, u32[]{:S(2)}) collective-permute-start(f32[3,128,128]{2,1,0:T(8,128)} %get-tuple-element.9), channel_id=1, source_target_pairs={{0,3},{1,0},{2,1},{3,2},{4,7},{5,4},{6,5},{7,6},{8,11},{9,8},{10,9... | collective-permute-start | bytes 589832 | tf_op jit(solution)/shard_map/ppermute | solution.py:111
  6.4 28.4 %collective-permute-start.1 = (f32[3,128,128]{2,1,0:T(8,128)}, f32[3,128,128]{2,1,0:T(8,128)S(1)}, u32[]{:S(2)}, u32[]{:S(2)}) collective-permute-start(f32[3,128,128]{2,1,0:T(8,128)} %get-tuple-element.8), channel_id=1, source_target_pairs={{0,2},{1,3},{2,0},{3,1},{4,6},{5,7},{6,4},{7,5},{8,10},{9,11},{10,... | collective-permute-start | bytes 589832 | tf_op jit(solution)/shard_map/ppermute | solution.py:111
  6.4 28.4 %collective-permute-start.2 = (f32[3,128,128]{2,1,0:T(8,128)S(1)}, f32[3,128,128]{2,1,0:T(8,128)S(1)}, u32[]{:S(2)}, u32[]{:S(2)}) collective-permute-start(f32[3,128,128]{2,1,0:T(8,128)S(1)} %get-tuple-element.7), channel_id=1, source_target_pairs={{0,1},{1,2},{2,3},{3,0},{4,5},{5,6},{6,7},{7,4},{8,9},{9,10},{10,1... | collective-permute-start | bytes 589832 | tf_op jit(solution)/shard_map/ppermute | solution.py:111
  8.8 14.0 %all-to-all-start = ((bf16[6,4,16,128]{3,0,1,2:T(8,128)(2,1)}), bf16[6,4,16,128]{3,0,1,2:T(8,128)(2,1)S(1)}, u32[]{:S(2)}, u32[]{:S(2)}) async-start(bf16[6,4,16,128]{3,0,1,2:T(8,128)(2,1)} %copy.123), calls=%async_computation | async-start | bytes 262144 | tf_op jit(solution)/shard_map/all_to_all | solution.py:143
  24.4 10.0 %all-to-all-start.1 = ((bf16[3,64,1,128]{3,0,2,1:T(4,128)(2,1)}), bf16[3,64,1,128]{3,0,2,1:T(4,128)(2,1)S(1)}, u32[]{:S(2)}, u32[]{:S(2)}) async-start(bf16[3,64,1,128]{3,0,2,1:T(4,128)(2,1)} %copy.133), calls=%async_computation.1 | async-start | bytes 131072 | tf_op jit(solution)/shard_map/all_to_all | solution.py:157
  34.9 38.2 %collective-permute-start.3 = (f32[4,3,128,128]{3,2,1,0:T(8,128)S(1)}, f32[4,3,128,128]{3,2,1,0:T(8,128)S(1)}, u32[]{:S(2)}, u32[]{:S(2)}) collective-permute-start(f32[4,3,128,128]{3,2,1,0:T(8,128)S(1)} %pad_maximum_fusion.1), channel_id=1, source_target_pairs={{4,0},{9,5},{14,10},{3,15},{20,16},{25,21},{30,26},{19,31},{36,32}... | collective-permute-start | bytes 2359304 | tf_op jit(solution)/shard_map/ppermute | solution.py:119
  36.9 35.6 %all-to-all-start.2 = ((f32[16,2,3,128]{3,1,2,0:T(2,128)}), f32[16,2,3,128]{3,1,2,0:T(2,128)S(1)}, u32[]{:S(2)}, u32[]{:S(2)}) async-start(f32[16,2,3,128]{3,1,2,0:T(2,128)} %gather_fusion), calls=%async_computation.2 | async-start | bytes 98304 | tf_op jit(solution)/shard_map/all_to_all | solution.py:172
  47.6 26.6 %collective-permute-start.4 = (f32[4,3,128,128]{3,2,1,0:T(8,128)S(1)}, f32[4,3,128,128]{3,2,1,0:T(8,128)}, u32[]{:S(2)}, u32[]{:S(2)}) collective-permute-start(f32[4,3,128,128]{3,2,1,0:T(8,128)S(1)} %pad_maximum_fusion.1), channel_id=1, source_target_pairs={{8,0},{13,5},{2,10},{7,15},{24,16},{29,21},{18,26},{23,31},{40,32}... | collective-permute-start | bytes 2359304 | tf_op jit(solution)/shard_map/ppermute | solution.py:119
  49.1 27.2 %collective-permute-start.5 = (f32[4,3,128,128]{3,2,1,0:T(8,128)S(1)}, f32[4,3,128,128]{3,2,1,0:T(8,128)}, u32[]{:S(2)}, u32[]{:S(2)}) collective-permute-start(f32[4,3,128,128]{3,2,1,0:T(8,128)S(1)} %pad_maximum_fusion.1), channel_id=1, source_target_pairs={{12,0},{1,5},{6,10},{11,15},{28,16},{17,21},{22,26},{27,31},{44,32... | collective-permute-start | bytes 2359304 | tf_op jit(solution)/shard_map/ppermute | solution.py:119
  74.1 44.1 %copy-start.1 = (bf16[1920,256]{1,0:T(8,128)(2,1)S(1)}, bf16[1920,256]{1,0:T(8,128)(2,1)}, u32[]{:S(2)}) copy-start(bf16[1920,256]{1,0:T(8,128)(2,1)} %param.13) | copy-start | bytes 2949124
  90.9 26.7 %all-to-all-start.3 = ((f32[16,2,3,128]{3,1,2,0:T(2,128)}), f32[16,2,3,128]{3,1,2,0:T(2,128)S(1)}, u32[]{:S(2)}, u32[]{:S(2)}) async-start(f32[16,2,3,128]{3,1,2,0:T(2,128)} %copy.140), calls=%async_computation.3 | async-start | bytes 98304 | tf_op jit(solution)/shard_map/all_to_all | solution.py:185

commit v4 on v3

--- a/solution.py
+++ b/solution.py
@@ -110,6 +110,30 @@
         ]
         within.append(lax.ppermute(blocks[(position - offset) % group_size], "slab", pairs))
     group_blocks = jnp.stack(within)
+
+    halfway_offsets = jnp.concatenate(
+        [jnp.zeros((point_total,), jnp.int32), jnp.full((point_total,), point_total, jnp.int32)]
+    )
+    row_order = node_map[0] + halfway_offsets
+    one_hot = (
+        row_order[:, None] == jnp.arange(2 * point_total, dtype=jnp.int32)[None, :]
+    ).astype(jnp.bfloat16)
+    lift_rows = jnp.einsum(
+        "ir,rf->if", one_hot, lift, preferred_element_type=jnp.float32
+    ).astype(jnp.bfloat16)
+    extend_cols = jnp.einsum(
+        "hr,ir->hi", extend, one_hot, preferred_element_type=jnp.float32
+    ).astype(jnp.bfloat16)
+
+    inverse, forward = spectral_tables(PLANES, quad_points)
+    wavenum = lax.dynamic_slice_in_dim(
+        plane_numbers(PLANES), lax.axis_index("mode") * planes_dev, planes_dev
+    )
+    shifts = plane_shift(wavenum)
+    velocity_half = velocity.astype(jnp.bfloat16)
+    both_fields = jnp.concatenate([velocity_half, vorticity], axis=0)
+    field_lines = lax.all_to_all(both_fields, "mode", split_axis=2, concat_axis=1, tiled=True)
+    group_blocks, field_lines = lax.optimization_barrier((group_blocks, field_lines))
     across = [group_blocks]
     for offset in range(1, group_count):
         pairs = [
@@ -118,29 +142,6 @@
         ]
         across.append(lax.ppermute(group_blocks, "slab", pairs))
     plane_blocks = jnp.concatenate(across, axis=0)
-
-    halfway_offsets = jnp.concatenate(
-        [jnp.zeros((point_total,), jnp.int32), jnp.full((point_total,), point_total, jnp.int32)]
-    )
-    row_order = node_map[0] + halfway_offsets
-    one_hot = (
-        row_order[:, None] == jnp.arange(2 * point_total, dtype=jnp.int32)[None, :]
-    ).astype(jnp.bfloat16)
-    lift_rows = jnp.einsum(
-        "ir,rf->if", one_hot, lift, preferred_element_type=jnp.float32
-    ).astype(jnp.bfloat16)
-    extend_cols = jnp.einsum(
-        "hr,ir->hi", extend, one_hot, preferred_element_type=jnp.float32
-    ).astype(jnp.bfloat16)
-
-    inverse, forward = spectral_tables(PLANES, quad_points)
-    wavenum = lax.dynamic_slice_in_dim(
-        plane_numbers(PLANES), lax.axis_index("mode") * planes_dev, planes_dev
-    )
-    shifts = plane_shift(wavenum)
-    velocity_half = velocity.astype(jnp.bfloat16)
-    both_fields = jnp.concatenate([velocity_half, vorticity], axis=0)
-    field_lines = lax.all_to_all(both_fields, "mode", split_axis=2, concat_axis=1, tiled=True)
     phys = jnp.einsum("qp,cplb->cqlb", inverse, field_lines, preferred_element_type=jnp.float32)
     lamb_field = lamb_vector(phys[:components], phys[components:]).astype(jnp.bfloat16)
     nonlin_lines = jnp.einsum(

time: 120 us -> 101 us (0.84)
  starting transfers between devices: 51.7 us -> 38 us
  local copies, waits for them, and re-layouts: 15.4 us -> 7.34 us
  other arithmetic: 1.43 us -> 6.75 us
  waiting for transfers between devices: 36.8 us -> 33.9 us
    all_to_all x1, starting transfers between devices: 19.2 us -> 5.96 us  [on_device(): lax.all_to_all(both_sides, 'slab', split_axis=0, concat_axis=0, tiled=True)]
    unnamed x22 -> x19, local copies, waits for them, and re-layouts: 5.28 us -> 0.04 us
    concatenate x0 -> x1, other arithmetic: none -> 3.68 us  [on_device(): plane_blocks = jnp.concatenate(across, axis=0)]
    concatenate x1 -> x0, local copies, waits for them, and re-layouts: 2.07 us -> none  [on_device(): plane_blocks = jnp.concatenate(across, axis=0)]
    ppermute x3, starting transfers between devices: 7.08 us -> 8.91 us  [on_device(): across.append(lax.ppermute(group_blocks, 'slab', pairs))]
    all_to_all x1, waiting for transfers between devices: 16.5 us -> 14.6 us  [on_device(): lax.all_to_all(sides[destination_plane], 'slab', split_axis=0, concat_axi...]
    all_to_all x1, waiting for transfers between devices: 6.45 us -> 5.07 us  [on_device(): lax.all_to_all(both_fields, 'mode', split_axis=2, concat_axis=1, tiled=True)]
    all_to_all x1, starting transfers between devices: 10.7 us -> 9.3 us  [on_device(): lax.all_to_all(sides[destination_plane], 'slab', split_axis=0, concat_axi...]
  transfers between devices with their start and end apart: 10 -> 10, of which waited for: 4 -> 4; matrix products, arithmetic and copies ran while one was open for 9% -> 6% of each run, Pallas kernels for 0% -> 0%
where the time goes in v4:
time: 101 us; the launch traced here: 100 us
  starting transfers between devices  38 us (38%)
  waiting for transfers between devices  33.9 us (34%)
  Pallas kernels  11.1 us (11%)
  local copies, waits for them, and re-layouts  7.34 us (7%)
  other arithmetic  6.75 us (7%)
  matrix products  2.67 us (3%)
    all_to_all x1, waiting for transfers between devices, on_device(): lax.all_to_all(sides[destination_plane], 'slab', split_axis=0, concat_axi...  14.6 us
    pallas_call x1, Pallas kernels, on_device(): pl.pallas_call(functools.partial(chain_kernel, group_size=group_size), ou...  11.1 us
    all_to_all x1, starting transfers between devices, on_device(): lax.all_to_all(sides[destination_plane], 'slab', split_axis=0, concat_axi...  9.3 us
    ppermute x3, starting transfers between devices, on_device(): across.append(lax.ppermute(group_blocks, 'slab', pairs))  8.91 us
    all_to_all x1, waiting for transfers between devices, on_device(): lax.all_to_all(both_sides, 'slab', split_axis=0, concat_axis=0, tiled=True)  7.47 us
    all_to_all x1, waiting for transfers between devices, on_device(): lax.all_to_all(nonlin_lines, 'mode', split_axis=1, concat_axis=2, tiled=T...  6.66 us
    all_to_all x1, starting transfers between devices, on_device(): lax.all_to_all(both_sides, 'slab', split_axis=0, concat_axis=0, tiled=True)  5.96 us
    all_to_all x1, starting transfers between devices, on_device(): lax.all_to_all(both_fields, 'mode', split_axis=2, concat_axis=1, tiled=True)  5.69 us
  transfers between devices with their start and end apart: 10, of which 4 were waited for; matrix products, arithmetic and copies ran while one was open for 6% of the time, Pallas kernels for 0%

profile of v4, /device:TPU:1, one launch (start us, length us, event | category | flops | bytes accessed | tf_op | source)
XLA Modules:
  0.0 100.2 jit_solution(481843532247104600)
XLA Ops:
  0.1 1.1 %slice_bitcast_fusion.1 = (f32[4,1,128,128]{3,2,1,0:T(8,128)S(1)}, f32[4,1,128,128]{3,2,1,0:T(8,128)S(1)}) fusion(f32[2,4,128,128]{3,2,1,0:T(8,128)} %param.14), kind=kLoop, calls=%fused_computation.16 | loop fusion | bytes 1048576 | tf_op jit(solution)/shard_map/stack;squeeze | solution.py:101
  1.3 1.0 %pad_maximum_fusion.1 = f32[4,3,128,128]{3,2,1,0:T(8,128)S(1)} fusion(f32[4,1,128,128]{3,2,1,0:T(8,128)} %bitcast.134, f32[4,1,128,128]{3,2,1,0:T(8,128)S(1)} %get-tuple-element.14, f32[4,1,128,128]{3,2,1,0:T(8,128)S(1)} %get-tuple-element.13), kind=kLoop, calls=%fused_computation.12 | loop fusion | flops 393216 | bytes 1572864 | tf_op jit(solution)/shard_map/stack | solution.py:101
  2.4 3.1 %collective-permute-start.2 = (f32[3,128,128]{2,1,0:T(8,128)S(1)}, f32[3,128,128]{2,1,0:T(8,128)S(1)}, u32[]{:S(2)}, u32[]{:S(2)}) collective-permute-start(f32[3,128,128]{2,1,0:T(8,128)S(1)} %get-tuple-element.10), channel_id=1, source_target_pairs={{0,1},{1,2},{2,3},{3,0},{4,5},{5,6},{6,7},{7,4},{8,9},{9,10},{10,1... | collective-permute-start | bytes 589832 | tf_op jit(solution)/shard_map/ppermute | solution.py:111
  5.5 1.6 %collective-permute-start.1 = (f32[3,128,128]{2,1,0:T(8,128)S(1)}, f32[3,128,128]{2,1,0:T(8,128)}, u32[]{:S(2)}, u32[]{:S(2)}) collective-permute-start(f32[3,128,128]{2,1,0:T(8,128)S(1)} %get-tuple-element.11), channel_id=1, source_target_pairs={{0,2},{1,3},{2,0},{3,1},{4,6},{5,7},{6,4},{7,5},{8,10},{9,11},{10,... | collective-permute-start | bytes 589832 | tf_op jit(solution)/shard_map/ppermute | solution.py:111
  7.1 0.7 copy.120
  7.8 5.7 %all-to-all-start = ((bf16[6,4,16,128]{3,0,1,2:T(8,128)(2,1)}), bf16[6,4,16,128]{3,0,1,2:T(8,128)(2,1)S(1)}, u32[]{:S(2)}, u32[]{:S(2)}) async-start(bf16[6,4,16,128]{3,0,1,2:T(8,128)(2,1)} %copy.120), calls=%async_computation | async-start | bytes 262144 | tf_op jit(solution)/shard_map/all_to_all | solution.py:135
  14.6 0.7 broadcast_add_fusion
  15.3 5.1 %all-to-all-done = bf16[6,4,16,128]{3,0,1,2:T(8,128)(2,1)S(1)} async-done(((bf16[6,4,16,128]{3,0,1,2:T(8,128)(2,1)}), bf16[6,4,16,128]{3,0,1,2:T(8,128)(2,1)S(1)}, u32[]{:S(2)}, u32[]{:S(2)}) %all-to-all-start) | async-done | bytes 98336 | tf_op jit(solution)/shard_map/all_to_all | solution.py:135
  20.4 1.1 %pad_maximum_fusion.2 = f32[4,3,128,128]{3,2,1,0:T(8,128)S(1)} fusion(f32[1,3,128,128]{3,2,1,0:T(8,128)S(1)} %bitcast.135, f32[1,3,128,128]{3,2,1,0:T(8,128)} %bitcast.7, f32[1,3,128,128]{3,2,1,0:T(8,128)} %bitcast.5, f32[1,3,128,128]{3,2,1,0:T(8,128)S(1)} %get-tuple-element.9), kind=kLoop, calls=%fused_computation.13 | loop fusion | flops 589824 | bytes 1572864 | tf_op jit(solution)/shard_map/stack | solution.py:112
  21.5 5.8 %collective-permute-start.5 = (f32[4,3,128,128]{3,2,1,0:T(8,128)S(1)}, f32[4,3,128,128]{3,2,1,0:T(8,128)}, u32[]{:S(2)}, u32[]{:S(2)}) collective-permute-start(f32[4,3,128,128]{3,2,1,0:T(8,128)S(1)} %pad_maximum_fusion.2), channel_id=1, source_target_pairs={{12,0},{1,5},{6,10},{11,15},{28,16},{17,21},{22,26},{27,31},{44,32... | collective-permute-start | bytes 2359304 | tf_op jit(solution)/shard_map/ppermute | solution.py:143
  27.3 1.5 %collective-permute-start.4 = (f32[4,3,128,128]{3,2,1,0:T(8,128)S(1)}, f32[4,3,128,128]{3,2,1,0:T(8,128)}, u32[]{:S(2)}, u32[]{:S(2)}) collective-permute-start(f32[4,3,128,128]{3,2,1,0:T(8,128)S(1)} %pad_maximum_fusion.2), channel_id=1, source_target_pairs={{8,0},{13,5},{2,10},{7,15},{24,16},{29,21},{18,26},{23,31},{40,32}... | collective-permute-start | bytes 2359304 | tf_op jit(solution)/shard_map/ppermute | solution.py:143
  28.9 1.6 %collective-permute-start.3 = (f32[4,3,128,128]{3,2,1,0:T(8,128)S(1)}, f32[4,3,128,128]{3,2,1,0:T(8,128)}, u32[]{:S(2)}, u32[]{:S(2)}) collective-permute-start(f32[4,3,128,128]{3,2,1,0:T(8,128)S(1)} %pad_maximum_fusion.2), channel_id=1, source_target_pairs={{4,0},{9,5},{14,10},{3,15},{20,16},{25,21},{30,26},{19,31},{36,32}... | collective-permute-start | bytes 2359304 | tf_op jit(solution)/shard_map/ppermute | solution.py:143
  31.3 0.7 copy.132
  31.9 3.5 %all-to-all-start.1 = ((bf16[3,64,1,128]{3,0,2,1:T(4,128)(2,1)}), bf16[3,64,1,128]{3,0,2,1:T(4,128)(2,1)S(1)}, u32[]{:S(2)}, u32[]{:S(2)}) async-start(bf16[3,64,1,128]{3,0,2,1:T(4,128)(2,1)} %copy.132), calls=%async_computation.1 | async-start | bytes 131072 | tf_op jit(solution)/shard_map/all_to_all | solution.py:158
  35.5 6.7 %all-to-all-done.1 = bf16[3,64,1,128]{3,0,2,1:T(4,128)(2,1)S(1)} async-done(((bf16[3,64,1,128]{3,0,2,1:T(4,128)(2,1)}), bf16[3,64,1,128]{3,0,2,1:T(4,128)(2,1)S(1)}, u32[]{:S(2)}, u32[]{:S(2)}) %all-to-all-start.1) | async-done | bytes 49184 | tf_op jit(solution)/shard_map/all_to_all | solution.py:158
  42.6 1.2 %gather_fusion = f32[16,2,3,128]{3,1,2,0:T(2,128)} fusion(f32[4,2,3,128]{3,1,2,0:T(2,128)S(1)} %copy.137, s32[1024]{0:T(1024)S(1)} %pad_clamp_fusion.1), kind=kCustom, calls=%fused_computation | custom fusion | bytes 98368 | tf_op jit(solution)/shard_map/gather | solution.py:174
  43.9 9.3 %all-to-all-start.2 = ((f32[16,2,3,128]{3,1,2,0:T(2,128)}), f32[16,2,3,128]{3,1,2,0:T(2,128)S(1)}, u32[]{:S(2)}, u32[]{:S(2)}) async-start(f32[16,2,3,128]{3,1,2,0:T(2,128)} %gather_fusion), calls=%async_computation.2 | async-start | bytes 98304 | tf_op jit(solution)/shard_map/all_to_all | solution.py:173
  53.2 14.6 %all-to-all-done.2 = f32[16,2,3,128]{3,1,2,0:T(2,128)S(1)} async-done(((f32[16,2,3,128]{3,1,2,0:T(2,128)}), f32[16,2,3,128]{3,1,2,0:T(2,128)S(1)}, u32[]{:S(2)}, u32[]{:S(2)}) %all-to-all-start.2) | async-done | bytes 49184 | tf_op jit(solution)/shard_map/all_to_all | solution.py:173
  68.5 3.7 %pad_maximum_fusion.blocks_ref = f32[16,3,128,128]{3,2,1,0:T(8,128)} fusion(f32[4,3,128,128]{3,2,1,0:T(8,128)} %collective-permute-done.5, f32[4,3,128,128]{3,2,1,0:T(8,128)} %collective-permute-done.4, f32[4,3,128,128]{3,2,1,0:T(8,128)} %collective-permute-done.3, f32[4,3,128,128]{3,2,1,0:T(8,128)S(1)} %pad_maximum_fusion.2), kind=kLoop, calls=%fused_computation.2 | loop fusion | flops 2359296 | bytes 6291456 | tf_op jit(solution)/shard_map/concatenate | solution.py:144
  72.1 11.1 %shard_map.100 = f32[16,2,3,128]{3,2,1,0:T(4,128)} custom-call(s32[1]{0:T(128)} %bitcast.position_ref, f32[16,3,128,128]{3,2,1,0:T(8,128)} %pad_maximum_fusion.blocks_ref, f32[16,2,3,128]{3,2,1,0:T(4,128)} %copy.138.sides_ref), custom_call_target="tpu_custom_call" | custom-call | tf_op jit(solution)/shard_map/pallas_call | solution.py:176
  83.3 1.5 %copy.139 = f32[16,2,3,128]{3,1,2,0:T(2,128)} copy(f32[16,2,3,128]{3,2,1,0:T(4,128)} %shard_map.100) | data formatting | bytes 98304 | tf_op jit(solution)/shard_map/pallas_call | solution.py:176
  84.8 6.0 %all-to-all-start.3 = ((f32[16,2,3,128]{3,1,2,0:T(2,128)}), f32[16,2,3,128]{3,1,2,0:T(2,128)S(1)}, u32[]{:S(2)}, u32[]{:S(2)}) async-start(f32[16,2,3,128]{3,1,2,0:T(2,128)} %copy.139), calls=%async_computation.3 | async-start | bytes 98304 | tf_op jit(solution)/shard_map/all_to_all | solution.py:186
  90.7 7.5 %all-to-all-done.3 = f32[16,2,3,128]{3,1,2,0:T(2,128)S(1)} async-done(((f32[16,2,3,128]{3,1,2,0:T(2,128)}), f32[16,2,3,128]{3,1,2,0:T(2,128)S(1)}, u32[]{:S(2)}, u32[]{:S(2)}) %all-to-all-start.3) | async-done | bytes 49184 | tf_op jit(solution)/shard_map/all_to_all | solution.py:186
  99.6 0.6 copy.143
  (59 shorter events, 4.4 us)
Async XLA Ops:
  0.0 13.6 %copy-start = (bf16[256,1920]{1,0:T(8,128)(2,1)S(1)}, bf16[256,1920]{1,0:T(8,128)(2,1)}, u32[]{:S(2)}) copy-start(bf16[256,1920]{1,0:T(8,128)(2,1)} %param.12) | copy-start | bytes 2949124
  0.0 13.5 %copy-start.7 = (s32[1,256]{1,0:T(1,128)S(1)}, s32[1,256]{1,0:T(1,128)}, u32[]{:S(2)}) copy-start(s32[1,256]{1,0:T(1,128)} %constant.108.clone.1) | copy-start | bytes 3076
  0.0 7.0 %copy-start.2 = (f32[3,4,16,128]{3,2,1,0:T(8,128)S(1)}, f32[3,4,16,128]{3,2,1,0:T(8,128)}, u32[]{:S(2)}) copy-start(f32[3,4,16,128]{3,2,1,0:T(8,128)} %param.10) | copy-start | bytes 294916
  0.0 7.1 %copy-start.4 = (bf16[3,4,16,128]{3,2,1,0:T(8,128)(2,1)S(1)}, bf16[3,4,16,128]{3,2,1,0:T(8,128)(2,1)}, u32[]{:S(2)}) copy-start(bf16[3,4,16,128]{3,2,1,0:T(8,128)(2,1)} %param.11) | copy-start | bytes 147460
  0.0 13.5 %copy-start.6 = (s32[1,256]{1,0:T(1,128)S(1)}, s32[1,256]{1,0:T(1,128)}, u32[]{:S(2)}) copy-start(s32[1,256]{1,0:T(1,128)} %param.17) | copy-start | bytes 3076
  2.3 12.3 %copy-start.5 = (f32[15,128]{1,0:T(8,128)S(1)}, f32[15,128]{1,0:T(8,128)}, u32[]{:S(2)}) copy-start(f32[15,128]{1,0:T(8,128)} %param.16) | copy-start | bytes 23044
  2.4 18.0 %collective-permute-start.2 = (f32[3,128,128]{2,1,0:T(8,128)S(1)}, f32[3,128,128]{2,1,0:T(8,128)S(1)}, u32[]{:S(2)}, u32[]{:S(2)}) collective-permute-start(f32[3,128,128]{2,1,0:T(8,128)S(1)} %get-tuple-element.10), channel_id=1, source_target_pairs={{0,1},{1,2},{2,3},{3,0},{4,5},{5,6},{6,7},{7,4},{8,9},{9,10},{10,1... | collective-permute-start | bytes 589832 | tf_op jit(solution)/shard_map/ppermute | solution.py:111
  5.5 14.9 %collective-permute-start.1 = (f32[3,128,128]{2,1,0:T(8,128)S(1)}, f32[3,128,128]{2,1,0:T(8,128)}, u32[]{:S(2)}, u32[]{:S(2)}) collective-permute-start(f32[3,128,128]{2,1,0:T(8,128)S(1)} %get-tuple-element.11), channel_id=1, source_target_pairs={{0,2},{1,3},{2,0},{3,1},{4,6},{5,7},{6,4},{7,5},{8,10},{9,11},{10,... | collective-permute-start | bytes 589832 | tf_op jit(solution)/shard_map/ppermute | solution.py:111
  7.0 13.4 %collective-permute-start = (f32[3,128,128]{2,1,0:T(8,128)S(1)}, f32[3,128,128]{2,1,0:T(8,128)}, u32[]{:S(2)}, u32[]{:S(2)}) collective-permute-start(f32[3,128,128]{2,1,0:T(8,128)S(1)} %get-tuple-element.12), channel_id=1, source_target_pairs={{0,3},{1,0},{2,1},{3,2},{4,7},{5,4},{6,5},{7,6},{8,11},{9,8},{10,9... | collective-permute-start | bytes 589832 | tf_op jit(solution)/shard_map/ppermute | solution.py:111
  7.8 12.5 %all-to-all-start = ((bf16[6,4,16,128]{3,0,1,2:T(8,128)(2,1)}), bf16[6,4,16,128]{3,0,1,2:T(8,128)(2,1)S(1)}, u32[]{:S(2)}, u32[]{:S(2)}) async-start(bf16[6,4,16,128]{3,0,1,2:T(8,128)(2,1)} %copy.120), calls=%async_computation | async-start | bytes 262144 | tf_op jit(solution)/shard_map/all_to_all | solution.py:135
  13.6 21.9 %copy-start.8 = (s32[16]{0:T(128)S(1)}, s32[16]{0:T(128)}, u32[]{:S(2)}) copy-start(s32[16]{0:T(128)} %constant.133) | copy-start | bytes 196
  21.5 46.9 %collective-permute-start.5 = (f32[4,3,128,128]{3,2,1,0:T(8,128)S(1)}, f32[4,3,128,128]{3,2,1,0:T(8,128)}, u32[]{:S(2)}, u32[]{:S(2)}) collective-permute-start(f32[4,3,128,128]{3,2,1,0:T(8,128)S(1)} %pad_maximum_fusion.2), channel_id=1, source_target_pairs={{12,0},{1,5},{6,10},{11,15},{28,16},{17,21},{22,26},{27,31},{44,32... | collective-permute-start | bytes 2359304 | tf_op jit(solution)/shard_map/ppermute | solution.py:143
  27.3 41.1 %collective-permute-start.4 = (f32[4,3,128,128]{3,2,1,0:T(8,128)S(1)}, f32[4,3,128,128]{3,2,1,0:T(8,128)}, u32[]{:S(2)}, u32[]{:S(2)}) collective-permute-start(f32[4,3,128,128]{3,2,1,0:T(8,128)S(1)} %pad_maximum_fusion.2), channel_id=1, source_target_pairs={{8,0},{13,5},{2,10},{7,15},{24,16},{29,21},{18,26},{23,31},{40,32}... | collective-permute-start | bytes 2359304 | tf_op jit(solution)/shard_map/ppermute | solution.py:143
  28.9 39.6 %collective-permute-start.3 = (f32[4,3,128,128]{3,2,1,0:T(8,128)S(1)}, f32[4,3,128,128]{3,2,1,0:T(8,128)}, u32[]{:S(2)}, u32[]{:S(2)}) collective-permute-start(f32[4,3,128,128]{3,2,1,0:T(8,128)S(1)} %pad_maximum_fusion.2), channel_id=1, source_target_pairs={{4,0},{9,5},{14,10},{3,15},{20,16},{25,21},{30,26},{19,31},{36,32}... | collective-permute-start | bytes 2359304 | tf_op jit(solution)/shard_map/ppermute | solution.py:143
  31.9 10.2 %all-to-all-start.1 = ((bf16[3,64,1,128]{3,0,2,1:T(4,128)(2,1)}), bf16[3,64,1,128]{3,0,2,1:T(4,128)(2,1)S(1)}, u32[]{:S(2)}, u32[]{:S(2)}) async-start(bf16[3,64,1,128]{3,0,2,1:T(4,128)(2,1)} %copy.132), calls=%async_computation.1 | async-start | bytes 131072 | tf_op jit(solution)/shard_map/all_to_all | solution.py:158
  43.9 23.9 %all-to-all-start.2 = ((f32[16,2,3,128]{3,1,2,0:T(2,128)}), f32[16,2,3,128]{3,1,2,0:T(2,128)S(1)}, u32[]{:S(2)}, u32[]{:S(2)}) async-start(f32[16,2,3,128]{3,1,2,0:T(2,128)} %gather_fusion), calls=%async_computation.2 | async-start | bytes 98304 | tf_op jit(solution)/shard_map/all_to_all | solution.py:173
  72.1 26.7 %copy-start.1 = (bf16[1920,256]{1,0:T(8,128)(2,1)S(1)}, bf16[1920,256]{1,0:T(8,128)(2,1)}, u32[]{:S(2)}) copy-start(bf16[1920,256]{1,0:T(8,128)(2,1)} %param.13) | copy-start | bytes 2949124
  72.1 27.3 %copy-start.3 = (f32[4,15,128]{2,0,1:T(4,128)S(1)}, f32[4,15,128]{2,0,1:T(4,128)}, u32[]{:S(2)}) copy-start(f32[4,15,128]{2,0,1:T(4,128)} %broadcast_add_fusion) | copy-start | bytes 92164
  84.8 13.4 %all-to-all-start.3 = ((f32[16,2,3,128]{3,1,2,0:T(2,128)}), f32[16,2,3,128]{3,1,2,0:T(2,128)S(1)}, u32[]{:S(2)}, u32[]{:S(2)}) async-start(f32[16,2,3,128]{3,1,2,0:T(2,128)} %copy.139), calls=%async_computation.3 | async-start | bytes 98304 | tf_op jit(solution)/shard_map/all_to_all | solution.py:186

commit v5 on v4

--- a/solution.py
+++ b/solution.py
@@ -44,14 +44,10 @@
     return jnp.stack([first, second, third])
 
 
-def chain_kernel(position_ref, blocks_ref, sides_ref, out_ref, *, group_size):
+def chain_kernel(position_ref, *refs, group_size):
+    group_refs = refs[:group_size]
+    sides_ref, out_ref = refs[group_size:]
     slab_count = sides_ref.shape[0]
-    position = position_ref[0]
-
-    def slot(slab):
-        group_slot = (slab // group_size - position + group_size) % group_size
-        spot_slot = (slab % group_size - position + group_size) % group_size
-        return group_slot * group_size + spot_slot
 
     def apply(matrix, vectors):
         return lax.dot_general(
@@ -62,20 +58,29 @@
             preferred_element_type=jnp.float32,
         )
 
-    zero = jnp.zeros(sides_ref.shape[2:], jnp.float32)
-    forward_values = [zero]
-    for k in range(1, slab_count):
-        source = sides_ref[k, 0] + sides_ref[k - 1, 1]
-        forward_values.append(source - apply(blocks_ref[slot(k), 0], forward_values[-1]))
-    after = zero
-    for k in range(slab_count - 1, 0, -1):
-        blocks = blocks_ref[slot(k)]
-        solved = apply(blocks[2], forward_values[k]) - apply(blocks[1], after)
-        out_ref[k, 0] = solved
-        out_ref[k, 1] = after
-        after = solved
-    out_ref[0, 0] = zero
-    out_ref[0, 1] = after
+    def solve(position):
+        def blocks_of(slab):
+            group_slot = (slab // group_size - position) % group_size
+            spot_slot = (slab % group_size - position) % group_size
+            return group_refs[group_slot].at[spot_slot]
+
+        zero = jnp.zeros(sides_ref.shape[2:], jnp.float32)
+        forward_values = [zero]
+        for k in range(1, slab_count):
+            source = sides_ref[k, 0] + sides_ref[k - 1, 1]
+            forward_values.append(source - apply(blocks_of(k)[0], forward_values[-1]))
+        after = zero
+        for k in range(slab_count - 1, 0, -1):
+            blocks = blocks_of(k)
+            solved = apply(blocks[2], forward_values[k]) - apply(blocks[1], after)
+            out_ref[k, 0] = solved
+            out_ref[k, 1] = after
+            after = solved
+        out_ref[0, 0] = zero
+        out_ref[0, 1] = after
+
+    for position in range(group_size):
+        pl.when(position_ref[0] == position)(functools.partial(solve, position))
 
 
 def on_device(
@@ -141,7 +146,6 @@
             for plane in range(planes_dev)
         ]
         across.append(lax.ppermute(group_blocks, "slab", pairs))
-    plane_blocks = jnp.concatenate(across, axis=0)
     phys = jnp.einsum("qp,cplb->cqlb", inverse, field_lines, preferred_element_type=jnp.float32)
     lamb_field = lamb_vector(phys[:components], phys[components:]).astype(jnp.bfloat16)
     nonlin_lines = jnp.einsum(
@@ -176,13 +180,10 @@
     both_sides = pl.pallas_call(
         functools.partial(chain_kernel, group_size=group_size),
         out_shape=jax.ShapeDtypeStruct(to_owner.shape, jnp.float32),
-        in_specs=[
-            pl.BlockSpec(memory_space=pltpu.SMEM),
-            pl.BlockSpec(memory_space=pltpu.VMEM),
-            pl.BlockSpec(memory_space=pltpu.VMEM),
-        ],
+        in_specs=[pl.BlockSpec(memory_space=pltpu.SMEM)]
+        + [pl.BlockSpec(memory_space=pltpu.VMEM)] * (group_size + 1),
         out_specs=pl.BlockSpec(memory_space=pltpu.VMEM),
-    )(position.astype(jnp.int32).reshape(1), plane_blocks, to_owner)
+    )(position.astype(jnp.int32).reshape(1), *across, to_owner)
     from_owner = lax.all_to_all(both_sides, "slab", split_axis=0, concat_axis=0, tiled=True)
     mine = from_owner[jnp.asarray(owners)]
     left_values = mine[:, 0]

time: 101 us -> 95.5 us (0.946)
  other arithmetic: 6.75 us -> 3.08 us
  starting transfers between devices: 38 us -> 34.6 us
  waiting for transfers between devices: 33.9 us -> 35.4 us
    concatenate x1 -> x0, other arithmetic: 3.68 us -> none  [on_device(): plane_blocks = jnp.concatenate(across, axis=0)]
    all_to_all x1, waiting for transfers between devices: 14.6 us -> 16.7 us  [on_device(): lax.all_to_all(sides[destination_plane], 'slab', split_axis=0, concat_axi...]
    all_to_all x1, starting transfers between devices: 9.3 us -> 7.33 us  [on_device(): lax.all_to_all(sides[destination_plane], 'slab', split_axis=0, concat_axi...]
    all_to_all x1, starting transfers between devices: 5.96 us -> 4.08 us  [on_device(): lax.all_to_all(both_sides, 'slab', split_axis=0, concat_axis=0, tiled=True)]
  transfers between devices with their start and end apart: 10 -> 10, of which waited for: 4 -> 4; matrix products, arithmetic and copies ran while one was open for 6% -> 7% of each run, Pallas kernels for 0% -> 0%
where the time goes in v5:
time: 95.5 us; the launch traced here: 95 us
  waiting for transfers between devices  35.4 us (37%)
  starting transfers between devices  34.6 us (36%)
  Pallas kernels  11.1 us (12%)
  local copies, waits for them, and re-layouts  7.59 us (8%)
  other arithmetic  3.08 us (3%)
  matrix products  2.67 us (3%)
    all_to_all x1, waiting for transfers between devices, on_device(): lax.all_to_all(sides[destination_plane], 'slab', split_axis=0, concat_axi...  16.7 us
    pallas_call x1, Pallas kernels, on_device(): pl.pallas_call(functools.partial(chain_kernel, group_size=group_size), ou...  11.1 us
    ppermute x3, starting transfers between devices, on_device(): across.append(lax.ppermute(group_blocks, 'slab', pairs))  8.38 us
    all_to_all x1, waiting for transfers between devices, on_device(): lax.all_to_all(both_sides, 'slab', split_axis=0, concat_axis=0, tiled=True)  7.47 us
    all_to_all x1, starting transfers between devices, on_device(): lax.all_to_all(sides[destination_plane], 'slab', split_axis=0, concat_axi...  7.33 us
    all_to_all x1, waiting for transfers between devices, on_device(): lax.all_to_all(nonlin_lines, 'mode', split_axis=1, concat_axis=2, tiled=T...  6.66 us
    all_to_all x1, starting transfers between devices, on_device(): lax.all_to_all(both_fields, 'mode', split_axis=2, concat_axis=1, tiled=True)  6.27 us
    ppermute x3, starting transfers between devices, on_device(): lax.ppermute(blocks[(position - offset) % group_size], 'slab', pairs)  5.05 us
  transfers between devices with their start and end apart: 10, of which 4 were waited for; matrix products, arithmetic and copies ran while one was open for 7% of the time, Pallas kernels for 0%

profile of v5, /device:TPU:1, one launch (start us, length us, event | category | flops | bytes accessed | tf_op | source)
XLA Modules:
  0.0 95.0 jit_solution(14654973007296698019)
XLA Ops:
  0.0 1.2 %slice_bitcast_fusion.1 = (f32[4,1,128,128]{3,2,1,0:T(8,128)S(1)}, f32[4,1,128,128]{3,2,1,0:T(8,128)S(1)}) fusion(f32[2,4,128,128]{3,2,1,0:T(8,128)} %param.14), kind=kLoop, calls=%fused_computation.15 | loop fusion | bytes 1048576 | tf_op jit(solution)/shard_map/stack;squeeze | solution.py:106
  1.4 3.3 %collective-permute-start = (f32[3,128,128]{2,1,0:T(8,128)S(1)}, f32[3,128,128]{2,1,0:T(8,128)S(1)}, u32[]{:S(2)}, u32[]{:S(2)}) collective-permute-start(f32[3,128,128]{2,1,0:T(8,128)S(1)} %get-tuple-element.12), channel_id=1, source_target_pairs={{0,3},{1,0},{2,1},{3,2},{4,7},{5,4},{6,5},{7,6},{8,11},{9,8},{10,9... | collective-permute-start | bytes 589832 | tf_op jit(solution)/shard_map/ppermute | solution.py:116
  4.7 1.7 %collective-permute-start.2 = (f32[3,128,128]{2,1,0:T(8,128)S(1)}, f32[3,128,128]{2,1,0:T(8,128)}, u32[]{:S(2)}, u32[]{:S(2)}) collective-permute-start(f32[3,128,128]{2,1,0:T(8,128)S(1)} %get-tuple-element.10), channel_id=1, source_target_pairs={{0,1},{1,2},{2,3},{3,0},{4,5},{5,6},{6,7},{7,4},{8,9},{9,10},{10,1... | collective-permute-start | bytes 589832 | tf_op jit(solution)/shard_map/ppermute | solution.py:116
  6.5 0.7 copy.120
  7.2 6.3 %all-to-all-start = ((bf16[6,4,16,128]{3,0,1,2:T(8,128)(2,1)}), bf16[6,4,16,128]{3,0,1,2:T(8,128)(2,1)S(1)}, u32[]{:S(2)}, u32[]{:S(2)}) async-start(bf16[6,4,16,128]{3,0,1,2:T(8,128)(2,1)} %copy.120), calls=%async_computation | async-start | bytes 262144 | tf_op jit(solution)/shard_map/all_to_all | solution.py:140
  14.8 0.7 broadcast_add_fusion
  16.5 4.6 %all-to-all-done = bf16[6,4,16,128]{3,0,1,2:T(8,128)(2,1)S(1)} async-done(((bf16[6,4,16,128]{3,0,1,2:T(8,128)(2,1)}), bf16[6,4,16,128]{3,0,1,2:T(8,128)(2,1)S(1)}, u32[]{:S(2)}, u32[]{:S(2)}) %all-to-all-start) | async-done | bytes 98336 | tf_op jit(solution)/shard_map/all_to_all | solution.py:140
  21.2 1.0 %pad_maximum_fusion.1.refs_0_ = f32[4,3,128,128]{3,2,1,0:T(8,128)S(1)} fusion(f32[1,3,128,128]{3,2,1,0:T(8,128)} %bitcast.9, f32[1,3,128,128]{3,2,1,0:T(8,128)S(1)} %bitcast.136, f32[1,3,128,128]{3,2,1,0:T(8,128)S(1)} %bitcast.135, f32[1,3,128,128]{3,2,1,0:T(8,128)S(1)} %get-tuple-element.9), kind=kLoop, calls=%fused_computation.12 | loop fusion | flops 589824 | bytes 1572864 | tf_op jit(solution)/shard_map/stack | solution.py:117
  22.8 1.6 %collective-permute-start.3 = (f32[4,3,128,128]{3,2,1,0:T(8,128)S(1)}, f32[4,3,128,128]{3,2,1,0:T(8,128)}, u32[]{:S(2)}, u32[]{:S(2)}) collective-permute-start(f32[4,3,128,128]{3,2,1,0:T(8,128)S(1)} %pad_maximum_fusion.1.refs_0_), channel_id=1, source_target_pairs={{4,0},{9,5},{14,10},{3,15},{20,16},{25,21},{30,26},{19,31},{36,32}... | collective-permute-start | bytes 2359304 | tf_op jit(solution)/shard_map/ppermute | solution.py:148
  24.4 1.6 %collective-permute-start.4 = (f32[4,3,128,128]{3,2,1,0:T(8,128)S(1)}, f32[4,3,128,128]{3,2,1,0:T(8,128)}, u32[]{:S(2)}, u32[]{:S(2)}) collective-permute-start(f32[4,3,128,128]{3,2,1,0:T(8,128)S(1)} %pad_maximum_fusion.1.refs_0_), channel_id=1, source_target_pairs={{8,0},{13,5},{2,10},{7,15},{24,16},{29,21},{18,26},{23,31},{40,32}... | collective-permute-start | bytes 2359304 | tf_op jit(solution)/shard_map/ppermute | solution.py:148
  25.9 5.2 %collective-permute-start.5 = (f32[4,3,128,128]{3,2,1,0:T(8,128)S(1)}, f32[4,3,128,128]{3,2,1,0:T(8,128)}, u32[]{:S(2)}, u32[]{:S(2)}) collective-permute-start(f32[4,3,128,128]{3,2,1,0:T(8,128)S(1)} %pad_maximum_fusion.1.refs_0_), channel_id=1, source_target_pairs={{12,0},{1,5},{6,10},{11,15},{28,16},{17,21},{22,26},{27,31},{44,32... | collective-permute-start | bytes 2359304 | tf_op jit(solution)/shard_map/ppermute | solution.py:148
  31.5 0.7 copy.132
  32.2 3.5 %all-to-all-start.1 = ((bf16[3,64,1,128]{3,0,2,1:T(4,128)(2,1)}), bf16[3,64,1,128]{3,0,2,1:T(4,128)(2,1)S(1)}, u32[]{:S(2)}, u32[]{:S(2)}) async-start(bf16[3,64,1,128]{3,0,2,1:T(4,128)(2,1)} %copy.132), calls=%async_computation.1 | async-start | bytes 131072 | tf_op jit(solution)/shard_map/all_to_all | solution.py:162
  35.7 6.7 %all-to-all-done.1 = bf16[3,64,1,128]{3,0,2,1:T(4,128)(2,1)S(1)} async-done(((bf16[3,64,1,128]{3,0,2,1:T(4,128)(2,1)}), bf16[3,64,1,128]{3,0,2,1:T(4,128)(2,1)S(1)}, u32[]{:S(2)}, u32[]{:S(2)}) %all-to-all-start.1) | async-done | bytes 49184 | tf_op jit(solution)/shard_map/all_to_all | solution.py:162
  42.9 1.2 %gather_fusion = f32[16,2,3,128]{3,1,2,0:T(2,128)} fusion(f32[4,2,3,128]{3,1,2,0:T(2,128)S(1)} %copy.137, s32[1024]{0:T(1024)S(1)} %pad_clamp_fusion.1), kind=kCustom, calls=%fused_computation | custom fusion | bytes 98368 | tf_op jit(solution)/shard_map/gather | solution.py:178
  44.1 7.3 %all-to-all-start.2 = ((f32[16,2,3,128]{3,1,2,0:T(2,128)}), f32[16,2,3,128]{3,1,2,0:T(2,128)S(1)}, u32[]{:S(2)}, u32[]{:S(2)}) async-start(f32[16,2,3,128]{3,1,2,0:T(2,128)} %gather_fusion), calls=%async_computation.2 | async-start | bytes 98304 | tf_op jit(solution)/shard_map/all_to_all | solution.py:177
  51.4 16.7 %all-to-all-done.2 = f32[16,2,3,128]{3,1,2,0:T(2,128)S(1)} async-done(((f32[16,2,3,128]{3,1,2,0:T(2,128)}), f32[16,2,3,128]{3,1,2,0:T(2,128)S(1)}, u32[]{:S(2)}, u32[]{:S(2)}) %all-to-all-start.2) | async-done | bytes 49184 | tf_op jit(solution)/shard_map/all_to_all | solution.py:177
  68.1 0.6 copy.138.refs_4_
  68.8 11.1 %shard_map.100 = f32[16,2,3,128]{3,2,1,0:T(4,128)} custom-call(s32[1]{0:T(128)} %bitcast.position_ref, f32[4,3,128,128]{3,2,1,0:T(8,128)} %copy-done.1, f32[4,3,128,128]{3,2,1,0:T(8,128)} %collective-permute-done.3.refs_1_, f32[4,3,128,128]{3,2,1,0:T(8,128)} %collective-permute-done.4.refs_2_, f32[4,3,128,128]{3,2,1,0:T(8,128)} %collective-permute-done.5.refs_3_, ...), custom_call_target="tpu_custom_call" | custom-call | tf_op jit(solution)/shard_map/pallas_call | solution.py:180
  79.9 1.5 %copy.139 = f32[16,2,3,128]{3,1,2,0:T(2,128)} copy(f32[16,2,3,128]{3,2,1,0:T(4,128)} %shard_map.100) | data formatting | bytes 98304 | tf_op jit(solution)/shard_map/pallas_call | solution.py:180
  81.4 4.1 %all-to-all-start.3 = ((f32[16,2,3,128]{3,1,2,0:T(2,128)}), f32[16,2,3,128]{3,1,2,0:T(2,128)S(1)}, u32[]{:S(2)}, u32[]{:S(2)}) async-start(f32[16,2,3,128]{3,1,2,0:T(2,128)} %copy.139), calls=%async_computation.3 | async-start | bytes 98304 | tf_op jit(solution)/shard_map/all_to_all | solution.py:187
  85.5 7.5 %all-to-all-done.3 = f32[16,2,3,128]{3,1,2,0:T(2,128)S(1)} async-done(((f32[16,2,3,128]{3,1,2,0:T(2,128)}), f32[16,2,3,128]{3,1,2,0:T(2,128)S(1)}, u32[]{:S(2)}, u32[]{:S(2)}) %all-to-all-start.3) | async-done | bytes 49184 | tf_op jit(solution)/shard_map/all_to_all | solution.py:187
  93.6 0.6 convolution_bitcast_fusion
  94.3 0.6 copy.143
  (70 shorter events, 4.5 us)
Async XLA Ops:
  0.0 13.6 %copy-start = (bf16[256,1920]{1,0:T(8,128)(2,1)S(1)}, bf16[256,1920]{1,0:T(8,128)(2,1)}, u32[]{:S(2)}) copy-start(bf16[256,1920]{1,0:T(8,128)(2,1)} %param.12) | copy-start | bytes 2949124
  0.0 1.2 %copy-start.4 = (f32[4,128,128]{2,1,0:T(8,128)S(1)}, f32[4,128,128]{2,1,0:T(8,128)}, u32[]{:S(2)}) copy-start(f32[4,128,128]{2,1,0:T(8,128)} %param.15) | copy-start | bytes 786436
  1.3 5.2 %copy-start.3 = (f32[3,4,16,128]{3,2,1,0:T(8,128)S(1)}, f32[3,4,16,128]{3,2,1,0:T(8,128)}, u32[]{:S(2)}) copy-start(f32[3,4,16,128]{3,2,1,0:T(8,128)} %param.10) | copy-start | bytes 294916
  1.3 5.2 %copy-start.6 = (bf16[3,4,16,128]{3,2,1,0:T(8,128)(2,1)S(1)}, bf16[3,4,16,128]{3,2,1,0:T(8,128)(2,1)}, u32[]{:S(2)}) copy-start(bf16[3,4,16,128]{3,2,1,0:T(8,128)(2,1)} %param.11) | copy-start | bytes 147460
  1.3 12.2 %copy-start.8 = (s32[1,256]{1,0:T(1,128)S(1)}, s32[1,256]{1,0:T(1,128)}, u32[]{:S(2)}) copy-start(s32[1,256]{1,0:T(1,128)} %param.17) | copy-start | bytes 3076
  1.3 12.2 %copy-start.9 = (s32[1,256]{1,0:T(1,128)S(1)}, s32[1,256]{1,0:T(1,128)}, u32[]{:S(2)}) copy-start(s32[1,256]{1,0:T(1,128)} %constant.108.clone.1) | copy-start | bytes 3076
  1.4 19.8 %collective-permute-start = (f32[3,128,128]{2,1,0:T(8,128)S(1)}, f32[3,128,128]{2,1,0:T(8,128)S(1)}, u32[]{:S(2)}, u32[]{:S(2)}) collective-permute-start(f32[3,128,128]{2,1,0:T(8,128)S(1)} %get-tuple-element.12), channel_id=1, source_target_pairs={{0,3},{1,0},{2,1},{3,2},{4,7},{5,4},{6,5},{7,6},{8,11},{9,8},{10,9... | collective-permute-start | bytes 589832 | tf_op jit(solution)/shard_map/ppermute | solution.py:116
  4.7 16.5 %collective-permute-start.1 = (f32[3,128,128]{2,1,0:T(8,128)S(1)}, f32[3,128,128]{2,1,0:T(8,128)S(1)}, u32[]{:S(2)}, u32[]{:S(2)}) collective-permute-start(f32[3,128,128]{2,1,0:T(8,128)S(1)} %get-tuple-element.11), channel_id=1, source_target_pairs={{0,2},{1,3},{2,0},{3,1},{4,6},{5,7},{6,4},{7,5},{8,10},{9,11},{10,... | collective-permute-start | bytes 589832 | tf_op jit(solution)/shard_map/ppermute | solution.py:116
  4.7 16.5 %collective-permute-start.2 = (f32[3,128,128]{2,1,0:T(8,128)S(1)}, f32[3,128,128]{2,1,0:T(8,128)}, u32[]{:S(2)}, u32[]{:S(2)}) collective-permute-start(f32[3,128,128]{2,1,0:T(8,128)S(1)} %get-tuple-element.10), channel_id=1, source_target_pairs={{0,1},{1,2},{2,3},{3,0},{4,5},{5,6},{6,7},{7,4},{8,9},{9,10},{10,1... | collective-permute-start | bytes 589832 | tf_op jit(solution)/shard_map/ppermute | solution.py:116
  7.2 14.0 %all-to-all-start = ((bf16[6,4,16,128]{3,0,1,2:T(8,128)(2,1)}), bf16[6,4,16,128]{3,0,1,2:T(8,128)(2,1)S(1)}, u32[]{:S(2)}, u32[]{:S(2)}) async-start(bf16[6,4,16,128]{3,0,1,2:T(8,128)(2,1)} %copy.120), calls=%async_computation | async-start | bytes 262144 | tf_op jit(solution)/shard_map/all_to_all | solution.py:140
  13.5 1.0 %copy-start.10 = (s32[64]{0:T(128)}, s32[64]{0:T(128)S(1)}, u32[]{:S(2)}) copy-start(s32[64]{0:T(128)S(1)} %compare_select_fusion.2) | copy-start | bytes 772
  21.2 1.1 %copy-start.11 = (s32[64]{0:T(128)S(1)}, s32[64]{0:T(128)}, u32[]{:S(2)}) copy-start(s32[64]{0:T(128)} %copy-done.10) | copy-start | bytes 772
  21.2 1.1 %copy-start.12 = (pred[64]{0:T(512)(128)(4,1)S(1)}, pred[64]{0:T(512)(128)(4,1)}, u32[]{:S(2)}) copy-start(pred[64]{0:T(512)(128)(4,1)} %compare_and_fusion) | copy-start | bytes 196
  21.2 9.9 %copy-start.14 = (f32[64]{0:T(128)S(1)}, f32[64]{0:T(128)}, u32[]{:S(2)}) copy-start(f32[64]{0:T(128)} %fusion.59) | copy-start | bytes 772
  22.2 20.6 %copy-start.1 = (f32[4,3,128,128]{3,2,1,0:T(8,128)}, f32[4,3,128,128]{3,2,1,0:T(8,128)S(1)}, u32[]{:S(2)}) copy-start(f32[4,3,128,128]{3,2,1,0:T(8,128)S(1)} %pad_maximum_fusion.1.refs_0_) | copy-start | bytes 2359300
  22.2 13.4 %copy-start.13 = (s32[16]{0:T(128)S(1)}, s32[16]{0:T(128)}, u32[]{:S(2)}) copy-start(s32[16]{0:T(128)} %constant.133) | copy-start | bytes 196
  22.8 46.0 %collective-permute-start.3 = (f32[4,3,128,128]{3,2,1,0:T(8,128)S(1)}, f32[4,3,128,128]{3,2,1,0:T(8,128)}, u32[]{:S(2)}, u32[]{:S(2)}) collective-permute-start(f32[4,3,128,128]{3,2,1,0:T(8,128)S(1)} %pad_maximum_fusion.1.refs_0_), channel_id=1, source_target_pairs={{4,0},{9,5},{14,10},{3,15},{20,16},{25,21},{30,26},{19,31},{36,32}... | collective-permute-start | bytes 2359304 | tf_op jit(solution)/shard_map/ppermute | solution.py:148
  24.4 44.4 %collective-permute-start.4 = (f32[4,3,128,128]{3,2,1,0:T(8,128)S(1)}, f32[4,3,128,128]{3,2,1,0:T(8,128)}, u32[]{:S(2)}, u32[]{:S(2)}) collective-permute-start(f32[4,3,128,128]{3,2,1,0:T(8,128)S(1)} %pad_maximum_fusion.1.refs_0_), channel_id=1, source_target_pairs={{8,0},{13,5},{2,10},{7,15},{24,16},{29,21},{18,26},{23,31},{40,32}... | collective-permute-start | bytes 2359304 | tf_op jit(solution)/shard_map/ppermute | solution.py:148
  25.9 42.8 %collective-permute-start.5 = (f32[4,3,128,128]{3,2,1,0:T(8,128)S(1)}, f32[4,3,128,128]{3,2,1,0:T(8,128)}, u32[]{:S(2)}, u32[]{:S(2)}) collective-permute-start(f32[4,3,128,128]{3,2,1,0:T(8,128)S(1)} %pad_maximum_fusion.1.refs_0_), channel_id=1, source_target_pairs={{12,0},{1,5},{6,10},{11,15},{28,16},{17,21},{22,26},{27,31},{44,32... | collective-permute-start | bytes 2359304 | tf_op jit(solution)/shard_map/ppermute | solution.py:148
  32.2 10.2 %all-to-all-start.1 = ((bf16[3,64,1,128]{3,0,2,1:T(4,128)(2,1)}), bf16[3,64,1,128]{3,0,2,1:T(4,128)(2,1)S(1)}, u32[]{:S(2)}, u32[]{:S(2)}) async-start(bf16[3,64,1,128]{3,0,2,1:T(4,128)(2,1)} %copy.132), calls=%async_computation.1 | async-start | bytes 131072 | tf_op jit(solution)/shard_map/all_to_all | solution.py:162
  44.1 24.0 %all-to-all-start.2 = ((f32[16,2,3,128]{3,1,2,0:T(2,128)}), f32[16,2,3,128]{3,1,2,0:T(2,128)S(1)}, u32[]{:S(2)}, u32[]{:S(2)}) async-start(f32[16,2,3,128]{3,1,2,0:T(2,128)} %gather_fusion), calls=%async_computation.2 | async-start | bytes 98304 | tf_op jit(solution)/shard_map/all_to_all | solution.py:177
  68.8 24.8 %copy-start.2 = (bf16[1920,256]{1,0:T(8,128)(2,1)S(1)}, bf16[1920,256]{1,0:T(8,128)(2,1)}, u32[]{:S(2)}) copy-start(bf16[1920,256]{1,0:T(8,128)(2,1)} %param.13) | copy-start | bytes 2949124
  79.9 14.3 %copy-start.5 = (f32[4,15,128]{2,0,1:T(4,128)S(1)}, f32[4,15,128]{2,0,1:T(4,128)}, u32[]{:S(2)}) copy-start(f32[4,15,128]{2,0,1:T(4,128)} %broadcast_add_fusion) | copy-start | bytes 92164
  81.4 11.6 %all-to-all-start.3 = ((f32[16,2,3,128]{3,1,2,0:T(2,128)}), f32[16,2,3,128]{3,1,2,0:T(2,128)S(1)}, u32[]{:S(2)}, u32[]{:S(2)}) async-start(f32[16,2,3,128]{3,1,2,0:T(2,128)} %copy.139), calls=%async_computation.3 | async-start | bytes 98304 | tf_op jit(solution)/shard_map/all_to_all | solution.py:187
  (1 other events, 0.7 us)

commit v6 on v5

--- a/solution.py
+++ b/solution.py
@@ -137,8 +137,8 @@
     shifts = plane_shift(wavenum)
     velocity_half = velocity.astype(jnp.bfloat16)
     both_fields = jnp.concatenate([velocity_half, vorticity], axis=0)
+    group_blocks, both_fields = lax.optimization_barrier((group_blocks, both_fields))
     field_lines = lax.all_to_all(both_fields, "mode", split_axis=2, concat_axis=1, tiled=True)
-    group_blocks, field_lines = lax.optimization_barrier((group_blocks, field_lines))
     across = [group_blocks]
     for offset in range(1, group_count):
         pairs = [

time: 95.5 us -> 95.1 us (level)
  starting transfers between devices: 34.6 us -> 41.1 us
  waiting for transfers between devices: 35.4 us -> 30.1 us
  other arithmetic: 3.08 us -> 1.49 us
    all_to_all x1, waiting for transfers between devices: 16.7 us -> 10.3 us  [on_device(): lax.all_to_all(sides[destination_plane], 'slab', split_axis=0, concat_axi...]
    ppermute x3, waiting for transfers between devices: 0.01 us -> 5.62 us  [on_device(): lax.ppermute(blocks[(position - offset) % group_size], 'slab', pairs)]
    all_to_all x1, waiting for transfers between devices: 4.62 us -> 0.01 us  [on_device(): lax.all_to_all(both_fields, 'mode', split_axis=2, concat_axis=1, tiled=True)]
    all_to_all x1, starting transfers between devices: 3.5 us -> 6.65 us  [on_device(): lax.all_to_all(nonlin_lines, 'mode', split_axis=1, concat_axis=2, tiled=T...]
    all_to_all x1, starting transfers between devices: 7.33 us -> 9.98 us  [on_device(): lax.all_to_all(sides[destination_plane], 'slab', split_axis=0, concat_axi...]
  transfers between devices with their start and end apart: 10 -> 10, of which waited for: 4 -> 6; matrix products, arithmetic and copies ran while one was open for 7% -> 5% of each run, Pallas kernels for 0% -> 0%
where the time goes in v6:
time: 95.1 us; the launch traced here: 94.6 us
  starting transfers between devices  41.1 us (43%)
  waiting for transfers between devices  30.1 us (32%)
  Pallas kernels  11.1 us (12%)
  local copies, waits for them, and re-layouts  7.68 us (8%)
  matrix products  2.67 us (3%)
  other arithmetic  1.49 us (2%)
    pallas_call x1, Pallas kernels, on_device(): pl.pallas_call(functools.partial(chain_kernel, group_size=group_size), ou...  11.1 us
    all_to_all x1, waiting for transfers between devices, on_device(): lax.all_to_all(sides[destination_plane], 'slab', split_axis=0, concat_axi...  10.3 us
    all_to_all x1, starting transfers between devices, on_device(): lax.all_to_all(sides[destination_plane], 'slab', split_axis=0, concat_axi...  9.98 us
    ppermute x3, starting transfers between devices, on_device(): across.append(lax.ppermute(group_blocks, 'slab', pairs))  8.38 us
    all_to_all x1, waiting for transfers between devices, on_device(): lax.all_to_all(both_sides, 'slab', split_axis=0, concat_axis=0, tiled=True)  7.47 us
    all_to_all x1, starting transfers between devices, on_device(): lax.all_to_all(both_fields, 'mode', split_axis=2, concat_axis=1, tiled=True)  6.95 us
    all_to_all x1, waiting for transfers between devices, on_device(): lax.all_to_all(nonlin_lines, 'mode', split_axis=1, concat_axis=2, tiled=T...  6.7 us
    all_to_all x1, starting transfers between devices, on_device(): lax.all_to_all(nonlin_lines, 'mode', split_axis=1, concat_axis=2, tiled=T...  6.65 us
  transfers between devices with their start and end apart: 10, of which 6 were waited for; matrix products, arithmetic and copies ran while one was open for 5% of the time, Pallas kernels for 0%

profile of v6, /device:TPU:1, one launch (start us, length us, event | category | flops | bytes accessed | tf_op | source)
XLA Modules:
  0.0 94.6 jit_solution(9865803786456787078)
XLA Ops:
  0.0 1.2 %slice_bitcast_fusion.1 = (f32[4,1,128,128]{3,2,1,0:T(8,128)S(1)}, f32[4,1,128,128]{3,2,1,0:T(8,128)S(1)}) fusion(f32[2,4,128,128]{3,2,1,0:T(8,128)} %param.14), kind=kLoop, calls=%fused_computation.15 | loop fusion | bytes 1048576 | tf_op jit(solution)/shard_map/stack;squeeze | solution.py:106
  1.4 3.3 %collective-permute-start = (f32[3,128,128]{2,1,0:T(8,128)S(1)}, f32[3,128,128]{2,1,0:T(8,128)S(1)}, u32[]{:S(2)}, u32[]{:S(2)}) collective-permute-start(f32[3,128,128]{2,1,0:T(8,128)S(1)} %get-tuple-element.12), channel_id=1, source_target_pairs={{0,3},{1,0},{2,1},{3,2},{4,7},{5,4},{6,5},{7,6},{8,11},{9,8},{10,9... | collective-permute-start | bytes 589832 | tf_op jit(solution)/shard_map/ppermute | solution.py:116
  4.7 1.7 %collective-permute-start.2 = (f32[3,128,128]{2,1,0:T(8,128)S(1)}, f32[3,128,128]{2,1,0:T(8,128)}, u32[]{:S(2)}, u32[]{:S(2)}) collective-permute-start(f32[3,128,128]{2,1,0:T(8,128)S(1)} %get-tuple-element.10), channel_id=1, source_target_pairs={{0,1},{1,2},{2,3},{3,0},{4,5},{5,6},{6,7},{7,4},{8,9},{9,10},{10,1... | collective-permute-start | bytes 589832 | tf_op jit(solution)/shard_map/ppermute | solution.py:116
  7.8 0.7 collective-permute-done
  8.5 3.2 %collective-permute-done.1 = f32[3,128,128]{2,1,0:T(8,128)S(1)} collective-permute-done((f32[3,128,128]{2,1,0:T(8,128)S(1)}, f32[3,128,128]{2,1,0:T(8,128)S(1)}, u32[]{:S(2)}, u32[]{:S(2)}) %collective-permute-start.1) | collective-permute-done | bytes 196640 | tf_op jit(solution)/shard_map/ppermute | solution.py:116
  11.7 1.8 %collective-permute-done.2 = f32[3,128,128]{2,1,0:T(8,128)} collective-permute-done((f32[3,128,128]{2,1,0:T(8,128)S(1)}, f32[3,128,128]{2,1,0:T(8,128)}, u32[]{:S(2)}, u32[]{:S(2)}) %collective-permute-start.2) | collective-permute-done | bytes 196640 | tf_op jit(solution)/shard_map/ppermute | solution.py:116
  13.5 1.1 %pad_maximum_fusion.1.refs_0_ = f32[4,3,128,128]{3,2,1,0:T(8,128)S(1)} fusion(f32[1,3,128,128]{3,2,1,0:T(8,128)} %bitcast.9, f32[1,3,128,128]{3,2,1,0:T(8,128)} %bitcast.134, f32[1,3,128,128]{3,2,1,0:T(8,128)S(1)} %bitcast.133, f32[1,3,128,128]{3,2,1,0:T(8,128)S(1)} %get-tuple-element.9), kind=kLoop, calls=%fused_computation.12 | loop fusion | flops 589824 | bytes 1572864 | tf_op jit(solution)/shard_map/stack | solution.py:117
  14.6 0.8 copy.123
  15.4 7.0 %all-to-all-start = ((bf16[6,4,16,128]{3,0,1,2:T(8,128)(2,1)}), bf16[6,4,16,128]{3,0,1,2:T(8,128)(2,1)S(1)}, u32[]{:S(2)}, u32[]{:S(2)}) async-start(bf16[6,4,16,128]{3,0,1,2:T(8,128)(2,1)} %copy.123), calls=%async_computation | async-start | bytes 262144 | tf_op jit(solution)/shard_map/all_to_all | solution.py:141
  22.4 1.6 %collective-permute-start.3 = (f32[4,3,128,128]{3,2,1,0:T(8,128)S(1)}, f32[4,3,128,128]{3,2,1,0:T(8,128)}, u32[]{:S(2)}, u32[]{:S(2)}) collective-permute-start(f32[4,3,128,128]{3,2,1,0:T(8,128)S(1)} %pad_maximum_fusion.1.refs_0_), channel_id=1, source_target_pairs={{4,0},{9,5},{14,10},{3,15},{20,16},{25,21},{30,26},{19,31},{36,32}... | collective-permute-start | bytes 2359304 | tf_op jit(solution)/shard_map/ppermute | solution.py:148
  24.0 1.6 %collective-permute-start.4 = (f32[4,3,128,128]{3,2,1,0:T(8,128)S(1)}, f32[4,3,128,128]{3,2,1,0:T(8,128)}, u32[]{:S(2)}, u32[]{:S(2)}) collective-permute-start(f32[4,3,128,128]{3,2,1,0:T(8,128)S(1)} %pad_maximum_fusion.1.refs_0_), channel_id=1, source_target_pairs={{8,0},{13,5},{2,10},{7,15},{24,16},{29,21},{18,26},{23,31},{40,32}... | collective-permute-start | bytes 2359304 | tf_op jit(solution)/shard_map/ppermute | solution.py:148
  25.5 5.2 %collective-permute-start.5 = (f32[4,3,128,128]{3,2,1,0:T(8,128)S(1)}, f32[4,3,128,128]{3,2,1,0:T(8,128)}, u32[]{:S(2)}, u32[]{:S(2)}) collective-permute-start(f32[4,3,128,128]{3,2,1,0:T(8,128)S(1)} %pad_maximum_fusion.1.refs_0_), channel_id=1, source_target_pairs={{12,0},{1,5},{6,10},{11,15},{28,16},{17,21},{22,26},{27,31},{44,32... | collective-permute-start | bytes 2359304 | tf_op jit(solution)/shard_map/ppermute | solution.py:148
  31.6 0.7 copy.133
  32.3 6.7 %all-to-all-start.1 = ((bf16[3,64,1,128]{3,0,2,1:T(4,128)(2,1)}), bf16[3,64,1,128]{3,0,2,1:T(4,128)(2,1)S(1)}, u32[]{:S(2)}, u32[]{:S(2)}) async-start(bf16[3,64,1,128]{3,0,2,1:T(4,128)(2,1)} %copy.133), calls=%async_computation.1 | async-start | bytes 131072 | tf_op jit(solution)/shard_map/all_to_all | solution.py:162
  39.0 6.7 %all-to-all-done.1 = bf16[3,64,1,128]{3,0,2,1:T(4,128)(2,1)S(1)} async-done(((bf16[3,64,1,128]{3,0,2,1:T(4,128)(2,1)}), bf16[3,64,1,128]{3,0,2,1:T(4,128)(2,1)S(1)}, u32[]{:S(2)}, u32[]{:S(2)}) %all-to-all-start.1) | async-done | bytes 49184 | tf_op jit(solution)/shard_map/all_to_all | solution.py:162
  46.2 1.2 %gather_fusion = f32[16,2,3,128]{3,1,2,0:T(2,128)} fusion(f32[4,2,3,128]{3,1,2,0:T(2,128)S(1)} %copy.138, s32[1024]{0:T(1024)S(1)} %pad_clamp_fusion.1), kind=kCustom, calls=%fused_computation | custom fusion | bytes 98368 | tf_op jit(solution)/shard_map/gather | solution.py:178
  47.4 10.0 %all-to-all-start.2 = ((f32[16,2,3,128]{3,1,2,0:T(2,128)}), f32[16,2,3,128]{3,1,2,0:T(2,128)S(1)}, u32[]{:S(2)}, u32[]{:S(2)}) async-start(f32[16,2,3,128]{3,1,2,0:T(2,128)} %gather_fusion), calls=%async_computation.2 | async-start | bytes 98304 | tf_op jit(solution)/shard_map/all_to_all | solution.py:177
  57.4 10.3 %all-to-all-done.2 = f32[16,2,3,128]{3,1,2,0:T(2,128)S(1)} async-done(((f32[16,2,3,128]{3,1,2,0:T(2,128)}), f32[16,2,3,128]{3,1,2,0:T(2,128)S(1)}, u32[]{:S(2)}, u32[]{:S(2)}) %all-to-all-start.2) | async-done | bytes 49184 | tf_op jit(solution)/shard_map/all_to_all | solution.py:177
  67.7 0.6 copy.139.refs_4_
  68.4 11.1 %shard_map.100 = f32[16,2,3,128]{3,2,1,0:T(4,128)} custom-call(s32[1]{0:T(128)} %bitcast.position_ref, f32[4,3,128,128]{3,2,1,0:T(8,128)} %copy-done.1, f32[4,3,128,128]{3,2,1,0:T(8,128)} %collective-permute-done.3.refs_1_, f32[4,3,128,128]{3,2,1,0:T(8,128)} %collective-permute-done.4.refs_2_, f32[4,3,128,128]{3,2,1,0:T(8,128)} %collective-permute-done.5.refs_3_, ...), custom_call_target="tpu_custom_call" | custom-call | tf_op jit(solution)/shard_map/pallas_call | solution.py:180
  79.5 1.5 %copy.140 = f32[16,2,3,128]{3,1,2,0:T(2,128)} copy(f32[16,2,3,128]{3,2,1,0:T(4,128)} %shard_map.100) | data formatting | bytes 98304 | tf_op jit(solution)/shard_map/pallas_call | solution.py:180
  81.0 4.1 %all-to-all-start.3 = ((f32[16,2,3,128]{3,1,2,0:T(2,128)}), f32[16,2,3,128]{3,1,2,0:T(2,128)S(1)}, u32[]{:S(2)}, u32[]{:S(2)}) async-start(f32[16,2,3,128]{3,1,2,0:T(2,128)} %copy.140), calls=%async_computation.3 | async-start | bytes 98304 | tf_op jit(solution)/shard_map/all_to_all | solution.py:187
  85.1 7.5 %all-to-all-done.3 = f32[16,2,3,128]{3,1,2,0:T(2,128)S(1)} async-done(((f32[16,2,3,128]{3,1,2,0:T(2,128)}), f32[16,2,3,128]{3,1,2,0:T(2,128)S(1)}, u32[]{:S(2)}, u32[]{:S(2)}) %all-to-all-start.3) | async-done | bytes 49184 | tf_op jit(solution)/shard_map/all_to_all | solution.py:187
  93.9 0.6 copy.144
  (62 shorter events, 4.1 us)
Async XLA Ops:
  0.0 6.6 %copy-start = (bf16[256,1920]{1,0:T(8,128)(2,1)S(1)}, bf16[256,1920]{1,0:T(8,128)(2,1)}, u32[]{:S(2)}) copy-start(bf16[256,1920]{1,0:T(8,128)(2,1)} %param.12) | copy-start | bytes 2949124
  0.0 1.2 %copy-start.4 = (f32[4,128,128]{2,1,0:T(8,128)S(1)}, f32[4,128,128]{2,1,0:T(8,128)}, u32[]{:S(2)}) copy-start(f32[4,128,128]{2,1,0:T(8,128)} %param.15) | copy-start | bytes 786436
  1.3 5.2 %copy-start.3 = (f32[3,4,16,128]{3,2,1,0:T(8,128)S(1)}, f32[3,4,16,128]{3,2,1,0:T(8,128)}, u32[]{:S(2)}) copy-start(f32[3,4,16,128]{3,2,1,0:T(8,128)} %param.10) | copy-start | bytes 294916
  1.3 5.2 %copy-start.6 = (bf16[3,4,16,128]{3,2,1,0:T(8,128)(2,1)S(1)}, bf16[3,4,16,128]{3,2,1,0:T(8,128)(2,1)}, u32[]{:S(2)}) copy-start(bf16[3,4,16,128]{3,2,1,0:T(8,128)(2,1)} %param.11) | copy-start | bytes 147460
  1.3 5.2 %copy-start.8 = (s32[1,256]{1,0:T(1,128)S(1)}, s32[1,256]{1,0:T(1,128)}, u32[]{:S(2)}) copy-start(s32[1,256]{1,0:T(1,128)} %param.17) | copy-start | bytes 3076
  1.3 5.2 %copy-start.9 = (s32[1,256]{1,0:T(1,128)S(1)}, s32[1,256]{1,0:T(1,128)}, u32[]{:S(2)}) copy-start(s32[1,256]{1,0:T(1,128)} %constant.108.clone.1) | copy-start | bytes 3076
  1.4 7.1 %collective-permute-start = (f32[3,128,128]{2,1,0:T(8,128)S(1)}, f32[3,128,128]{2,1,0:T(8,128)S(1)}, u32[]{:S(2)}, u32[]{:S(2)}) collective-permute-start(f32[3,128,128]{2,1,0:T(8,128)S(1)} %get-tuple-element.12), channel_id=1, source_target_pairs={{0,3},{1,0},{2,1},{3,2},{4,7},{5,4},{6,5},{7,6},{8,11},{9,8},{10,9... | collective-permute-start | bytes 589832 | tf_op jit(solution)/shard_map/ppermute | solution.py:116
  4.7 7.0 %collective-permute-start.1 = (f32[3,128,128]{2,1,0:T(8,128)S(1)}, f32[3,128,128]{2,1,0:T(8,128)S(1)}, u32[]{:S(2)}, u32[]{:S(2)}) collective-permute-start(f32[3,128,128]{2,1,0:T(8,128)S(1)} %get-tuple-element.11), channel_id=1, source_target_pairs={{0,2},{1,3},{2,0},{3,1},{4,6},{5,7},{6,4},{7,5},{8,10},{9,11},{10,... | collective-permute-start | bytes 589832 | tf_op jit(solution)/shard_map/ppermute | solution.py:116
  4.7 8.7 %collective-permute-start.2 = (f32[3,128,128]{2,1,0:T(8,128)S(1)}, f32[3,128,128]{2,1,0:T(8,128)}, u32[]{:S(2)}, u32[]{:S(2)}) collective-permute-start(f32[3,128,128]{2,1,0:T(8,128)S(1)} %get-tuple-element.10), channel_id=1, source_target_pairs={{0,1},{1,2},{2,3},{3,0},{4,5},{5,6},{6,7},{7,4},{8,9},{9,10},{10,1... | collective-permute-start | bytes 589832 | tf_op jit(solution)/shard_map/ppermute | solution.py:116
  7.1 0.7 copy-start.7
  11.7 1.8 %copy-start.5 = (f32[3,128,128]{2,1,0:T(8,128)}, f32[3,128,128]{2,1,0:T(8,128)S(1)}, u32[]{:S(2)}) copy-start(f32[3,128,128]{2,1,0:T(8,128)S(1)} %collective-permute-done.1) | copy-start | bytes 589828
  14.5 17.1 %copy-start.1 = (f32[4,3,128,128]{3,2,1,0:T(8,128)}, f32[4,3,128,128]{3,2,1,0:T(8,128)S(1)}, u32[]{:S(2)}) copy-start(f32[4,3,128,128]{3,2,1,0:T(8,128)S(1)} %pad_maximum_fusion.1.refs_0_) | copy-start | bytes 2359300
  15.4 23.6 %copy-start.10 = (s32[16]{0:T(128)S(1)}, s32[16]{0:T(128)}, u32[]{:S(2)}) copy-start(s32[16]{0:T(128)} %constant.133) | copy-start | bytes 196
  15.4 15.4 %all-to-all-start = ((bf16[6,4,16,128]{3,0,1,2:T(8,128)(2,1)}), bf16[6,4,16,128]{3,0,1,2:T(8,128)(2,1)S(1)}, u32[]{:S(2)}, u32[]{:S(2)}) async-start(bf16[6,4,16,128]{3,0,1,2:T(8,128)(2,1)} %copy.123), calls=%async_computation | async-start | bytes 262144 | tf_op jit(solution)/shard_map/all_to_all | solution.py:141
  22.4 46.0 %collective-permute-start.3 = (f32[4,3,128,128]{3,2,1,0:T(8,128)S(1)}, f32[4,3,128,128]{3,2,1,0:T(8,128)}, u32[]{:S(2)}, u32[]{:S(2)}) collective-permute-start(f32[4,3,128,128]{3,2,1,0:T(8,128)S(1)} %pad_maximum_fusion.1.refs_0_), channel_id=1, source_target_pairs={{4,0},{9,5},{14,10},{3,15},{20,16},{25,21},{30,26},{19,31},{36,32}... | collective-permute-start | bytes 2359304 | tf_op jit(solution)/shard_map/ppermute | solution.py:148
  24.0 44.4 %collective-permute-start.4 = (f32[4,3,128,128]{3,2,1,0:T(8,128)S(1)}, f32[4,3,128,128]{3,2,1,0:T(8,128)}, u32[]{:S(2)}, u32[]{:S(2)}) collective-permute-start(f32[4,3,128,128]{3,2,1,0:T(8,128)S(1)} %pad_maximum_fusion.1.refs_0_), channel_id=1, source_target_pairs={{8,0},{13,5},{2,10},{7,15},{24,16},{29,21},{18,26},{23,31},{40,32}... | collective-permute-start | bytes 2359304 | tf_op jit(solution)/shard_map/ppermute | solution.py:148
  25.5 42.8 %collective-permute-start.5 = (f32[4,3,128,128]{3,2,1,0:T(8,128)S(1)}, f32[4,3,128,128]{3,2,1,0:T(8,128)}, u32[]{:S(2)}, u32[]{:S(2)}) collective-permute-start(f32[4,3,128,128]{3,2,1,0:T(8,128)S(1)} %pad_maximum_fusion.1.refs_0_), channel_id=1, source_target_pairs={{12,0},{1,5},{6,10},{11,15},{28,16},{17,21},{22,26},{27,31},{44,32... | collective-permute-start | bytes 2359304 | tf_op jit(solution)/shard_map/ppermute | solution.py:148
  32.3 13.4 %all-to-all-start.1 = ((bf16[3,64,1,128]{3,0,2,1:T(4,128)(2,1)}), bf16[3,64,1,128]{3,0,2,1:T(4,128)(2,1)S(1)}, u32[]{:S(2)}, u32[]{:S(2)}) async-start(bf16[3,64,1,128]{3,0,2,1:T(4,128)(2,1)} %copy.133), calls=%async_computation.1 | async-start | bytes 131072 | tf_op jit(solution)/shard_map/all_to_all | solution.py:162
  47.4 20.3 %all-to-all-start.2 = ((f32[16,2,3,128]{3,1,2,0:T(2,128)}), f32[16,2,3,128]{3,1,2,0:T(2,128)S(1)}, u32[]{:S(2)}, u32[]{:S(2)}) async-start(f32[16,2,3,128]{3,1,2,0:T(2,128)} %gather_fusion), calls=%async_computation.2 | async-start | bytes 98304 | tf_op jit(solution)/shard_map/all_to_all | solution.py:177
  68.4 24.8 %copy-start.2 = (bf16[1920,256]{1,0:T(8,128)(2,1)S(1)}, bf16[1920,256]{1,0:T(8,128)(2,1)}, u32[]{:S(2)}) copy-start(bf16[1920,256]{1,0:T(8,128)(2,1)} %param.13) | copy-start | bytes 2949124
  81.0 11.6 %all-to-all-start.3 = ((f32[16,2,3,128]{3,1,2,0:T(2,128)}), f32[16,2,3,128]{3,1,2,0:T(2,128)S(1)}, u32[]{:S(2)}, u32[]{:S(2)}) async-start(f32[16,2,3,128]{3,1,2,0:T(2,128)} %copy.140), calls=%async_computation.3 | async-start | bytes 98304 | tf_op jit(solution)/shard_map/all_to_all | solution.py:187

commit v7 on v5

--- a/solution.py
+++ b/solution.py
@@ -171,6 +171,7 @@
     right_part = cond_line[:, :, point_total:]
 
     sides = jnp.stack([rhs_left, right_part], axis=1)
+    across, sides = lax.optimization_barrier((across, sides))
     destination_plane = jnp.asarray(
         [owners.index(slab) if slab in owners else 0 for slab in range(slab_count)], jnp.int32
     )

time: 95.5 us -> 107 us (1.12)
  starting transfers between devices: 34.6 us -> 54.9 us
  waiting for transfers between devices: 35.4 us -> 26.3 us
    all_to_all x1, starting transfers between devices: 7.33 us -> 28.1 us  [on_device(): lax.all_to_all(sides[destination_plane], 'slab', split_axis=0, concat_axi...]
    all_to_all x1, waiting for transfers between devices: 16.7 us -> 7.51 us  [on_device(): lax.all_to_all(sides[destination_plane], 'slab', split_axis=0, concat_axi...]
  transfers between devices with their start and end apart: 10 -> 10, of which waited for: 4 -> 4; matrix products, arithmetic and copies ran while one was open for 7% -> 5% of each run, Pallas kernels for 0% -> 0%
where the time goes in v7:
time: 107 us; the launch traced here: 106 us
  starting transfers between devices  54.9 us (51%)
  waiting for transfers between devices  26.3 us (25%)
  Pallas kernels  11.1 us (10%)
  local copies, waits for them, and re-layouts  7.59 us (7%)
  other arithmetic  3.08 us (3%)
  matrix products  2.67 us (2%)
    all_to_all x1, starting transfers between devices, on_device(): lax.all_to_all(sides[destination_plane], 'slab', split_axis=0, concat_axi...  28.1 us
    pallas_call x1, Pallas kernels, on_device(): pl.pallas_call(functools.partial(chain_kernel, group_size=group_size), ou...  11.1 us
    ppermute x3, starting transfers between devices, on_device(): across.append(lax.ppermute(group_blocks, 'slab', pairs))  8.38 us
    all_to_all x1, waiting for transfers between devices, on_device(): lax.all_to_all(sides[destination_plane], 'slab', split_axis=0, concat_axi...  7.51 us
    all_to_all x1, waiting for transfers between devices, on_device(): lax.all_to_all(both_sides, 'slab', split_axis=0, concat_axis=0, tiled=True)  7.51 us
    all_to_all x1, waiting for transfers between devices, on_device(): lax.all_to_all(nonlin_lines, 'mode', split_axis=1, concat_axis=2, tiled=T...  6.66 us
    all_to_all x1, starting transfers between devices, on_device(): lax.all_to_all(both_fields, 'mode', split_axis=2, concat_axis=1, tiled=True)  6.27 us
    ppermute x3, starting transfers between devices, on_device(): lax.ppermute(blocks[(position - offset) % group_size], 'slab', pairs)  5.05 us
  transfers between devices with their start and end apart: 10, of which 4 were waited for; matrix products, arithmetic and copies ran while one was open for 5% of the time, Pallas kernels for 0%

profile of v7, /device:TPU:1, one launch (start us, length us, event | category | flops | bytes accessed | tf_op | source)
XLA Modules:
  0.0 106.2 jit_solution(4398841854236418783)
XLA Ops:
  0.0 1.2 %slice_bitcast_fusion.1 = (f32[4,1,128,128]{3,2,1,0:T(8,128)S(1)}, f32[4,1,128,128]{3,2,1,0:T(8,128)S(1)}) fusion(f32[2,4,128,128]{3,2,1,0:T(8,128)} %param.14), kind=kLoop, calls=%fused_computation.15 | loop fusion | bytes 1048576 | tf_op jit(solution)/shard_map/stack;squeeze | solution.py:106
  1.4 3.3 %collective-permute-start = (f32[3,128,128]{2,1,0:T(8,128)S(1)}, f32[3,128,128]{2,1,0:T(8,128)S(1)}, u32[]{:S(2)}, u32[]{:S(2)}) collective-permute-start(f32[3,128,128]{2,1,0:T(8,128)S(1)} %get-tuple-element.22), channel_id=1, source_target_pairs={{0,3},{1,0},{2,1},{3,2},{4,7},{5,4},{6,5},{7,6},{8,11},{9,8},{10,9... | collective-permute-start | bytes 589832 | tf_op jit(solution)/shard_map/ppermute | solution.py:116
  4.7 1.7 %collective-permute-start.2 = (f32[3,128,128]{2,1,0:T(8,128)S(1)}, f32[3,128,128]{2,1,0:T(8,128)}, u32[]{:S(2)}, u32[]{:S(2)}) collective-permute-start(f32[3,128,128]{2,1,0:T(8,128)S(1)} %get-tuple-element.20), channel_id=1, source_target_pairs={{0,1},{1,2},{2,3},{3,0},{4,5},{5,6},{6,7},{7,4},{8,9},{9,10},{10,1... | collective-permute-start | bytes 589832 | tf_op jit(solution)/shard_map/ppermute | solution.py:116
  6.5 0.7 copy.120
  7.2 6.3 %all-to-all-start = ((bf16[6,4,16,128]{3,0,1,2:T(8,128)(2,1)}), bf16[6,4,16,128]{3,0,1,2:T(8,128)(2,1)S(1)}, u32[]{:S(2)}, u32[]{:S(2)}) async-start(bf16[6,4,16,128]{3,0,1,2:T(8,128)(2,1)} %copy.120), calls=%async_computation | async-start | bytes 262144 | tf_op jit(solution)/shard_map/all_to_all | solution.py:140
  14.8 0.7 broadcast_add_fusion
  16.5 4.6 %all-to-all-done = bf16[6,4,16,128]{3,0,1,2:T(8,128)(2,1)S(1)} async-done(((bf16[6,4,16,128]{3,0,1,2:T(8,128)(2,1)}), bf16[6,4,16,128]{3,0,1,2:T(8,128)(2,1)S(1)}, u32[]{:S(2)}, u32[]{:S(2)}) %all-to-all-start) | async-done | bytes 98336 | tf_op jit(solution)/shard_map/all_to_all | solution.py:140
  21.2 1.0 pad_maximum_fusion.1.refs_0_
  22.8 1.6 %collective-permute-start.3 = (f32[4,3,128,128]{3,2,1,0:T(8,128)S(1)}, f32[4,3,128,128]{3,2,1,0:T(8,128)}, u32[]{:S(2)}, u32[]{:S(2)}) collective-permute-start(f32[4,3,128,128]{3,2,1,0:T(8,128)S(1)} %pad_maximum_fusion.1.refs_0_), channel_id=1, source_target_pairs={{4,0},{9,5},{14,10},{3,15},{20,16},{25,21},{30,26},{19,31},{36,32}... | collective-permute-start | bytes 2359304 | tf_op jit(solution)/shard_map/ppermute | solution.py:148
  24.4 1.6 %collective-permute-start.4 = (f32[4,3,128,128]{3,2,1,0:T(8,128)S(1)}, f32[4,3,128,128]{3,2,1,0:T(8,128)}, u32[]{:S(2)}, u32[]{:S(2)}) collective-permute-start(f32[4,3,128,128]{3,2,1,0:T(8,128)S(1)} %pad_maximum_fusion.1.refs_0_), channel_id=1, source_target_pairs={{8,0},{13,5},{2,10},{7,15},{24,16},{29,21},{18,26},{23,31},{40,32}... | collective-permute-start | bytes 2359304 | tf_op jit(solution)/shard_map/ppermute | solution.py:148
  25.9 5.2 %collective-permute-start.5 = (f32[4,3,128,128]{3,2,1,0:T(8,128)S(1)}, f32[4,3,128,128]{3,2,1,0:T(8,128)}, u32[]{:S(2)}, u32[]{:S(2)}) collective-permute-start(f32[4,3,128,128]{3,2,1,0:T(8,128)S(1)} %pad_maximum_fusion.1.refs_0_), channel_id=1, source_target_pairs={{12,0},{1,5},{6,10},{11,15},{28,16},{17,21},{22,26},{27,31},{44,32... | collective-permute-start | bytes 2359304 | tf_op jit(solution)/shard_map/ppermute | solution.py:148
  31.5 0.7 copy.132
  32.2 3.5 %all-to-all-start.1 = ((bf16[3,64,1,128]{3,0,2,1:T(4,128)(2,1)}), bf16[3,64,1,128]{3,0,2,1:T(4,128)(2,1)S(1)}, u32[]{:S(2)}, u32[]{:S(2)}) async-start(bf16[3,64,1,128]{3,0,2,1:T(4,128)(2,1)} %copy.132), calls=%async_computation.1 | async-start | bytes 131072 | tf_op jit(solution)/shard_map/all_to_all | solution.py:162
  35.7 6.7 %all-to-all-done.1 = bf16[3,64,1,128]{3,0,2,1:T(4,128)(2,1)S(1)} async-done(((bf16[3,64,1,128]{3,0,2,1:T(4,128)(2,1)}), bf16[3,64,1,128]{3,0,2,1:T(4,128)(2,1)S(1)}, u32[]{:S(2)}, u32[]{:S(2)}) %all-to-all-start.1) | async-done | bytes 49184 | tf_op jit(solution)/shard_map/all_to_all | solution.py:162
  42.9 1.2 %gather_fusion = f32[16,2,3,128]{3,1,2,0:T(2,128)} fusion(f32[4,2,3,128]{3,1,2,0:T(2,128)S(1)} %copy.137, s32[1024]{0:T(1024)S(1)} %pad_clamp_fusion.1), kind=kCustom, calls=%fused_computation | custom fusion | bytes 98368 | tf_op jit(solution)/shard_map/gather | solution.py:179
  44.1 28.1 %all-to-all-start.2 = ((f32[16,2,3,128]{3,1,2,0:T(2,128)}), f32[16,2,3,128]{3,1,2,0:T(2,128)S(1)}, u32[]{:S(2)}, u32[]{:S(2)}) async-start(f32[16,2,3,128]{3,1,2,0:T(2,128)} %gather_fusion), calls=%async_computation.2 | async-start | bytes 98304 | tf_op jit(solution)/shard_map/all_to_all | solution.py:178
  72.2 7.5 %all-to-all-done.2 = f32[16,2,3,128]{3,1,2,0:T(2,128)S(1)} async-done(((f32[16,2,3,128]{3,1,2,0:T(2,128)}), f32[16,2,3,128]{3,1,2,0:T(2,128)S(1)}, u32[]{:S(2)}, u32[]{:S(2)}) %all-to-all-start.2) | async-done | bytes 49184 | tf_op jit(solution)/shard_map/all_to_all | solution.py:178
  79.7 0.6 copy.138.refs_4_
  80.4 11.1 %shard_map.100 = f32[16,2,3,128]{3,2,1,0:T(4,128)} custom-call(s32[1]{0:T(128)} %bitcast.position_ref, f32[4,3,128,128]{3,2,1,0:T(8,128)} %copy-done.1, f32[4,3,128,128]{3,2,1,0:T(8,128)} %collective-permute-done.3.refs_1_, f32[4,3,128,128]{3,2,1,0:T(8,128)} %collective-permute-done.4.refs_2_, f32[4,3,128,128]{3,2,1,0:T(8,128)} %collective-permute-done.5.refs_3_, ...), custom_call_target="tpu_custom_call" | custom-call | tf_op jit(solution)/shard_map/pallas_call | solution.py:181
  91.5 1.5 %copy.139 = f32[16,2,3,128]{3,1,2,0:T(2,128)} copy(f32[16,2,3,128]{3,2,1,0:T(4,128)} %shard_map.100) | data formatting | bytes 98304 | tf_op jit(solution)/shard_map/pallas_call | solution.py:181
  93.0 3.6 %all-to-all-start.3 = ((f32[16,2,3,128]{3,1,2,0:T(2,128)}), f32[16,2,3,128]{3,1,2,0:T(2,128)S(1)}, u32[]{:S(2)}, u32[]{:S(2)}) async-start(f32[16,2,3,128]{3,1,2,0:T(2,128)} %copy.139), calls=%async_computation.3 | async-start | bytes 98304 | tf_op jit(solution)/shard_map/all_to_all | solution.py:188
  96.7 7.5 %all-to-all-done.3 = f32[16,2,3,128]{3,1,2,0:T(2,128)S(1)} async-done(((f32[16,2,3,128]{3,1,2,0:T(2,128)}), f32[16,2,3,128]{3,1,2,0:T(2,128)S(1)}, u32[]{:S(2)}, u32[]{:S(2)}) %all-to-all-start.3) | async-done | bytes 49184 | tf_op jit(solution)/shard_map/all_to_all | solution.py:188
  104.8 0.6 convolution_bitcast_fusion
  105.5 0.6 copy.143
  (70 shorter events, 4.5 us)
Async XLA Ops:
  0.0 13.6 %copy-start = (bf16[256,1920]{1,0:T(8,128)(2,1)S(1)}, bf16[256,1920]{1,0:T(8,128)(2,1)}, u32[]{:S(2)}) copy-start(bf16[256,1920]{1,0:T(8,128)(2,1)} %param.12) | copy-start | bytes 2949124
  0.0 1.2 %copy-start.4 = (f32[4,128,128]{2,1,0:T(8,128)S(1)}, f32[4,128,128]{2,1,0:T(8,128)}, u32[]{:S(2)}) copy-start(f32[4,128,128]{2,1,0:T(8,128)} %param.15) | copy-start | bytes 786436
  1.3 5.2 %copy-start.3 = (f32[3,4,16,128]{3,2,1,0:T(8,128)S(1)}, f32[3,4,16,128]{3,2,1,0:T(8,128)}, u32[]{:S(2)}) copy-start(f32[3,4,16,128]{3,2,1,0:T(8,128)} %param.10) | copy-start | bytes 294916
  1.3 5.2 %copy-start.6 = (bf16[3,4,16,128]{3,2,1,0:T(8,128)(2,1)S(1)}, bf16[3,4,16,128]{3,2,1,0:T(8,128)(2,1)}, u32[]{:S(2)}) copy-start(bf16[3,4,16,128]{3,2,1,0:T(8,128)(2,1)} %param.11) | copy-start | bytes 147460
  1.3 12.2 %copy-start.8 = (s32[1,256]{1,0:T(1,128)S(1)}, s32[1,256]{1,0:T(1,128)}, u32[]{:S(2)}) copy-start(s32[1,256]{1,0:T(1,128)} %param.17) | copy-start | bytes 3076
  1.3 12.2 %copy-start.9 = (s32[1,256]{1,0:T(1,128)S(1)}, s32[1,256]{1,0:T(1,128)}, u32[]{:S(2)}) copy-start(s32[1,256]{1,0:T(1,128)} %constant.108.clone.1) | copy-start | bytes 3076
  1.4 19.8 %collective-permute-start = (f32[3,128,128]{2,1,0:T(8,128)S(1)}, f32[3,128,128]{2,1,0:T(8,128)S(1)}, u32[]{:S(2)}, u32[]{:S(2)}) collective-permute-start(f32[3,128,128]{2,1,0:T(8,128)S(1)} %get-tuple-element.22), channel_id=1, source_target_pairs={{0,3},{1,0},{2,1},{3,2},{4,7},{5,4},{6,5},{7,6},{8,11},{9,8},{10,9... | collective-permute-start | bytes 589832 | tf_op jit(solution)/shard_map/ppermute | solution.py:116
  4.7 16.5 %collective-permute-start.1 = (f32[3,128,128]{2,1,0:T(8,128)S(1)}, f32[3,128,128]{2,1,0:T(8,128)S(1)}, u32[]{:S(2)}, u32[]{:S(2)}) collective-permute-start(f32[3,128,128]{2,1,0:T(8,128)S(1)} %get-tuple-element.21), channel_id=1, source_target_pairs={{0,2},{1,3},{2,0},{3,1},{4,6},{5,7},{6,4},{7,5},{8,10},{9,11},{10,... | collective-permute-start | bytes 589832 | tf_op jit(solution)/shard_map/ppermute | solution.py:116
  4.7 16.5 %collective-permute-start.2 = (f32[3,128,128]{2,1,0:T(8,128)S(1)}, f32[3,128,128]{2,1,0:T(8,128)}, u32[]{:S(2)}, u32[]{:S(2)}) collective-permute-start(f32[3,128,128]{2,1,0:T(8,128)S(1)} %get-tuple-element.20), channel_id=1, source_target_pairs={{0,1},{1,2},{2,3},{3,0},{4,5},{5,6},{6,7},{7,4},{8,9},{9,10},{10,1... | collective-permute-start | bytes 589832 | tf_op jit(solution)/shard_map/ppermute | solution.py:116
  7.2 14.0 %all-to-all-start = ((bf16[6,4,16,128]{3,0,1,2:T(8,128)(2,1)}), bf16[6,4,16,128]{3,0,1,2:T(8,128)(2,1)S(1)}, u32[]{:S(2)}, u32[]{:S(2)}) async-start(bf16[6,4,16,128]{3,0,1,2:T(8,128)(2,1)} %copy.120), calls=%async_computation | async-start | bytes 262144 | tf_op jit(solution)/shard_map/all_to_all | solution.py:140
  13.5 1.0 copy-start.10
  21.2 1.1 %copy-start.11 = (s32[64]{0:T(128)S(1)}, s32[64]{0:T(128)}, u32[]{:S(2)}) copy-start(s32[64]{0:T(128)} %copy-done.10) | copy-start | bytes 772
  21.2 1.1 %copy-start.12 = (pred[64]{0:T(512)(128)(4,1)S(1)}, pred[64]{0:T(512)(128)(4,1)}, u32[]{:S(2)}) copy-start(pred[64]{0:T(512)(128)(4,1)} %compare_and_fusion) | copy-start | bytes 196
  21.2 9.9 %copy-start.14 = (f32[64]{0:T(128)S(1)}, f32[64]{0:T(128)}, u32[]{:S(2)}) copy-start(f32[64]{0:T(128)} %fusion.59) | copy-start | bytes 772
  22.2 20.6 %copy-start.1 = (f32[4,3,128,128]{3,2,1,0:T(8,128)}, f32[4,3,128,128]{3,2,1,0:T(8,128)S(1)}, u32[]{:S(2)}) copy-start(f32[4,3,128,128]{3,2,1,0:T(8,128)S(1)} %pad_maximum_fusion.1.refs_0_) | copy-start | bytes 2359300
  22.2 13.4 %copy-start.13 = (s32[16]{0:T(128)S(1)}, s32[16]{0:T(128)}, u32[]{:S(2)}) copy-start(s32[16]{0:T(128)} %constant.133) | copy-start | bytes 196
  22.8 20.1 %collective-permute-start.3 = (f32[4,3,128,128]{3,2,1,0:T(8,128)S(1)}, f32[4,3,128,128]{3,2,1,0:T(8,128)}, u32[]{:S(2)}, u32[]{:S(2)}) collective-permute-start(f32[4,3,128,128]{3,2,1,0:T(8,128)S(1)} %pad_maximum_fusion.1.refs_0_), channel_id=1, source_target_pairs={{4,0},{9,5},{14,10},{3,15},{20,16},{25,21},{30,26},{19,31},{36,32}... | collective-permute-start | bytes 2359304 | tf_op jit(solution)/shard_map/ppermute | solution.py:148
  24.4 18.5 %collective-permute-start.4 = (f32[4,3,128,128]{3,2,1,0:T(8,128)S(1)}, f32[4,3,128,128]{3,2,1,0:T(8,128)}, u32[]{:S(2)}, u32[]{:S(2)}) collective-permute-start(f32[4,3,128,128]{3,2,1,0:T(8,128)S(1)} %pad_maximum_fusion.1.refs_0_), channel_id=1, source_target_pairs={{8,0},{13,5},{2,10},{7,15},{24,16},{29,21},{18,26},{23,31},{40,32}... | collective-permute-start | bytes 2359304 | tf_op jit(solution)/shard_map/ppermute | solution.py:148
  25.9 16.9 %collective-permute-start.5 = (f32[4,3,128,128]{3,2,1,0:T(8,128)S(1)}, f32[4,3,128,128]{3,2,1,0:T(8,128)}, u32[]{:S(2)}, u32[]{:S(2)}) collective-permute-start(f32[4,3,128,128]{3,2,1,0:T(8,128)S(1)} %pad_maximum_fusion.1.refs_0_), channel_id=1, source_target_pairs={{12,0},{1,5},{6,10},{11,15},{28,16},{17,21},{22,26},{27,31},{44,32... | collective-permute-start | bytes 2359304 | tf_op jit(solution)/shard_map/ppermute | solution.py:148
  32.2 10.2 %all-to-all-start.1 = ((bf16[3,64,1,128]{3,0,2,1:T(4,128)(2,1)}), bf16[3,64,1,128]{3,0,2,1:T(4,128)(2,1)S(1)}, u32[]{:S(2)}, u32[]{:S(2)}) async-start(bf16[3,64,1,128]{3,0,2,1:T(4,128)(2,1)} %copy.132), calls=%async_computation.1 | async-start | bytes 131072 | tf_op jit(solution)/shard_map/all_to_all | solution.py:162
  44.1 35.6 %all-to-all-start.2 = ((f32[16,2,3,128]{3,1,2,0:T(2,128)}), f32[16,2,3,128]{3,1,2,0:T(2,128)S(1)}, u32[]{:S(2)}, u32[]{:S(2)}) async-start(f32[16,2,3,128]{3,1,2,0:T(2,128)} %gather_fusion), calls=%async_computation.2 | async-start | bytes 98304 | tf_op jit(solution)/shard_map/all_to_all | solution.py:178
  80.4 24.4 %copy-start.2 = (bf16[1920,256]{1,0:T(8,128)(2,1)S(1)}, bf16[1920,256]{1,0:T(8,128)(2,1)}, u32[]{:S(2)}) copy-start(bf16[1920,256]{1,0:T(8,128)(2,1)} %param.13) | copy-start | bytes 2949124
  91.5 13.9 %copy-start.5 = (f32[4,15,128]{2,0,1:T(4,128)S(1)}, f32[4,15,128]{2,0,1:T(4,128)}, u32[]{:S(2)}) copy-start(f32[4,15,128]{2,0,1:T(4,128)} %broadcast_add_fusion) | copy-start | bytes 92164
  93.0 11.2 %all-to-all-start.3 = ((f32[16,2,3,128]{3,1,2,0:T(2,128)}), f32[16,2,3,128]{3,1,2,0:T(2,128)S(1)}, u32[]{:S(2)}, u32[]{:S(2)}) async-start(f32[16,2,3,128]{3,1,2,0:T(2,128)} %copy.139), calls=%async_computation.3 | async-start | bytes 98304 | tf_op jit(solution)/shard_map/all_to_all | solution.py:188
  (1 other events, 0.7 us)

commit v8 on v5

--- a/solution.py
+++ b/solution.py
@@ -60,8 +60,8 @@
 
     def solve(position):
         def blocks_of(slab):
-            group_slot = (slab // group_size - position) % group_size
-            spot_slot = (slab % group_size - position) % group_size
+            group_slot = (slab % group_size - position) % group_size
+            spot_slot = (slab // group_size - position) % group_size
             return group_refs[group_slot].at[spot_slot]
 
         zero = jnp.zeros(sides_ref.shape[2:], jnp.float32)
@@ -100,20 +100,20 @@
     slab_index = lax.axis_index("slab")
     group_size = planes_dev
     group_count = slab_count // group_size
-    position = slab_index % group_size
+    position = slab_index // group_size
     owners = [plane * group_size + plane for plane in range(planes_dev)]
 
     blocks = jnp.stack(
         [interface_chain_factors[0], interface_chain_factors[1], pivot_inverse], axis=1
     )
     within = [blocks[position]]
-    for offset in range(1, group_size):
+    for offset in range(1, group_count):
         pairs = [
-            (group * group_size + spot, group * group_size + (spot - offset) % group_size)
-            for group in range(group_count)
-            for spot in range(group_size)
+            (rest + group_size * rank, rest + group_size * ((rank - offset) % group_count))
+            for rest in range(group_size)
+            for rank in range(group_count)
         ]
-        within.append(lax.ppermute(blocks[(position - offset) % group_size], "slab", pairs))
+        within.append(lax.ppermute(blocks[(position - offset) % group_count], "slab", pairs))
     group_blocks = jnp.stack(within)
 
     halfway_offsets = jnp.concatenate(
@@ -140,9 +140,9 @@
     field_lines = lax.all_to_all(both_fields, "mode", split_axis=2, concat_axis=1, tiled=True)
     group_blocks, field_lines = lax.optimization_barrier((group_blocks, field_lines))
     across = [group_blocks]
-    for offset in range(1, group_count):
+    for offset in range(1, group_size):
         pairs = [
-            (((plane + offset) % group_count) * group_size + plane, owners[plane])
+            (plane * group_size + (plane + offset) % group_size, owners[plane])
             for plane in range(planes_dev)
         ]
         across.append(lax.ppermute(group_blocks, "slab", pairs))

time: 95.5 us -> 95.5 us (level)
  starting transfers between devices: 34.6 us -> 44.8 us
  waiting for transfers between devices: 35.4 us -> 25.3 us
    all_to_all x1, waiting for transfers between devices: 16.7 us -> 7.48 us  [on_device(): lax.all_to_all(sides[destination_plane], 'slab', split_axis=0, concat_axi...]
    ppermute x3, starting transfers between devices: 5.05 us -> 10.2 us  [on_device(): lax.ppermute(blocks[(position - offset) % group_count], 'slab', pairs)]
    all_to_all x1, starting transfers between devices: 7.33 us -> 11.4 us  [on_device(): lax.all_to_all(sides[destination_plane], 'slab', split_axis=0, concat_axi...]
where the time goes in v8:
time: 95.5 us; the launch traced here: 95 us
  starting transfers between devices  44.8 us (47%)
  waiting for transfers between devices  25.3 us (26%)
  Pallas kernels  11.2 us (12%)
  local copies, waits for them, and re-layouts  7.59 us (8%)
  other arithmetic  3.08 us (3%)
  matrix products  2.67 us (3%)
    all_to_all x1, starting transfers between devices, on_device(): lax.all_to_all(sides[destination_plane], 'slab', split_axis=0, concat_axi...  11.4 us
    pallas_call x1, Pallas kernels, on_device(): pl.pallas_call(functools.partial(chain_kernel, group_size=group_size), ou...  11.2 us
    ppermute x3, starting transfers between devices, on_device(): lax.ppermute(blocks[(position - offset) % group_count], 'slab', pairs)  10.2 us
    ppermute x3, starting transfers between devices, on_device(): across.append(lax.ppermute(group_blocks, 'slab', pairs))  8.89 us
    all_to_all x1, waiting for transfers between devices, on_device(): lax.all_to_all(both_sides, 'slab', split_axis=0, concat_axis=0, tiled=True)  7.51 us
    all_to_all x1, waiting for transfers between devices, on_device(): lax.all_to_all(sides[destination_plane], 'slab', split_axis=0, concat_axi...  7.48 us
    all_to_all x1, starting transfers between devices, on_device(): lax.all_to_all(both_fields, 'mode', split_axis=2, concat_axis=1, tiled=True)  6.75 us
    all_to_all x1, waiting for transfers between devices, on_device(): lax.all_to_all(nonlin_lines, 'mode', split_axis=1, concat_axis=2, tiled=T...  6.48 us
  transfers between devices with their start and end apart: 10, of which 4 were waited for; matrix products, arithmetic and copies ran while one was open for 7% of the time, Pallas kernels for 0%

profile of v8, /device:TPU:1, one launch (start us, length us, event | category | flops | bytes accessed | tf_op | source)
XLA Modules:
  0.0 95.0 jit_solution(17869112536244772845)
XLA Ops:
  0.0 1.2 %slice_bitcast_fusion.1 = (f32[4,1,128,128]{3,2,1,0:T(8,128)S(1)}, f32[4,1,128,128]{3,2,1,0:T(8,128)S(1)}) fusion(f32[2,4,128,128]{3,2,1,0:T(8,128)} %param.14), kind=kLoop, calls=%fused_computation.15 | loop fusion | bytes 1048576 | tf_op jit(solution)/shard_map/stack;squeeze | solution.py:106
  1.4 6.9 %collective-permute-start = (f32[3,128,128]{2,1,0:T(8,128)S(1)}, f32[3,128,128]{2,1,0:T(8,128)S(1)}, u32[]{:S(2)}, u32[]{:S(2)}) collective-permute-start(f32[3,128,128]{2,1,0:T(8,128)S(1)} %get-tuple-element.12), channel_id=1, source_target_pairs={{0,12},{4,0},{8,4},{12,8},{1,13},{5,1},{9,5},{13,9},{2,14},{6,2},{... | collective-permute-start | bytes 589832 | tf_op jit(solution)/shard_map/ppermute | solution.py:116
  8.3 1.0 %collective-permute-start.1 = (f32[3,128,128]{2,1,0:T(8,128)S(1)}, f32[3,128,128]{2,1,0:T(8,128)S(1)}, u32[]{:S(2)}, u32[]{:S(2)}) collective-permute-start(f32[3,128,128]{2,1,0:T(8,128)S(1)} %get-tuple-element.11), channel_id=1, source_target_pairs={{0,8},{4,12},{8,0},{12,4},{1,9},{5,13},{9,1},{13,5},{2,10},{6,14},... | collective-permute-start | bytes 589832 | tf_op jit(solution)/shard_map/ppermute | solution.py:116
  9.3 2.3 %collective-permute-start.2 = (f32[3,128,128]{2,1,0:T(8,128)S(1)}, f32[3,128,128]{2,1,0:T(8,128)}, u32[]{:S(2)}, u32[]{:S(2)}) collective-permute-start(f32[3,128,128]{2,1,0:T(8,128)S(1)} %get-tuple-element.10), channel_id=1, source_target_pairs={{0,4},{4,8},{8,12},{12,0},{1,5},{5,9},{9,13},{13,1},{2,6},{6,10},{... | collective-permute-start | bytes 589832 | tf_op jit(solution)/shard_map/ppermute | solution.py:116
  11.6 0.7 copy.120
  12.3 6.8 %all-to-all-start = ((bf16[6,4,16,128]{3,0,1,2:T(8,128)(2,1)}), bf16[6,4,16,128]{3,0,1,2:T(8,128)(2,1)S(1)}, u32[]{:S(2)}, u32[]{:S(2)}) async-start(bf16[6,4,16,128]{3,0,1,2:T(8,128)(2,1)} %copy.120), calls=%async_computation | async-start | bytes 262144 | tf_op jit(solution)/shard_map/all_to_all | solution.py:140
  20.4 0.7 broadcast_add_fusion
  22.2 3.8 %all-to-all-done = bf16[6,4,16,128]{3,0,1,2:T(8,128)(2,1)S(1)} async-done(((bf16[6,4,16,128]{3,0,1,2:T(8,128)(2,1)}), bf16[6,4,16,128]{3,0,1,2:T(8,128)(2,1)S(1)}, u32[]{:S(2)}, u32[]{:S(2)}) %all-to-all-start) | async-done | bytes 98336 | tf_op jit(solution)/shard_map/all_to_all | solution.py:140
  26.0 1.0 %pad_maximum_fusion.1.refs_0_ = f32[4,3,128,128]{3,2,1,0:T(8,128)S(1)} fusion(f32[1,3,128,128]{3,2,1,0:T(8,128)} %bitcast.9, f32[1,3,128,128]{3,2,1,0:T(8,128)S(1)} %bitcast.136, f32[1,3,128,128]{3,2,1,0:T(8,128)S(1)} %bitcast.135, f32[1,3,128,128]{3,2,1,0:T(8,128)S(1)} %get-tuple-element.9), kind=kLoop, calls=%fused_computation.12 | loop fusion | flops 589824 | bytes 1572864 | tf_op jit(solution)/shard_map/stack | solution.py:117
  27.5 5.8 %collective-permute-start.3 = (f32[4,3,128,128]{3,2,1,0:T(8,128)S(1)}, f32[4,3,128,128]{3,2,1,0:T(8,128)}, u32[]{:S(2)}, u32[]{:S(2)}) collective-permute-start(f32[4,3,128,128]{3,2,1,0:T(8,128)S(1)} %pad_maximum_fusion.1.refs_0_), channel_id=1, source_target_pairs={{1,0},{6,5},{11,10},{12,15},{17,16},{22,21},{27,26},{28,31},{33,32... | collective-permute-start | bytes 2359304 | tf_op jit(solution)/shard_map/ppermute | solution.py:148
  33.3 1.6 %collective-permute-start.4 = (f32[4,3,128,128]{3,2,1,0:T(8,128)S(1)}, f32[4,3,128,128]{3,2,1,0:T(8,128)}, u32[]{:S(2)}, u32[]{:S(2)}) collective-permute-start(f32[4,3,128,128]{3,2,1,0:T(8,128)S(1)} %pad_maximum_fusion.1.refs_0_), channel_id=1, source_target_pairs={{2,0},{7,5},{8,10},{13,15},{18,16},{23,21},{24,26},{29,31},{34,32}... | collective-permute-start | bytes 2359304 | tf_op jit(solution)/shard_map/ppermute | solution.py:148
  34.9 1.5 %collective-permute-start.5 = (f32[4,3,128,128]{3,2,1,0:T(8,128)S(1)}, f32[4,3,128,128]{3,2,1,0:T(8,128)}, u32[]{:S(2)}, u32[]{:S(2)}) collective-permute-start(f32[4,3,128,128]{3,2,1,0:T(8,128)S(1)} %pad_maximum_fusion.1.refs_0_), channel_id=1, source_target_pairs={{3,0},{4,5},{9,10},{14,15},{19,16},{20,21},{25,26},{30,31},{35,32}... | collective-permute-start | bytes 2359304 | tf_op jit(solution)/shard_map/ppermute | solution.py:148
  36.8 0.7 copy.132
  37.5 3.9 %all-to-all-start.1 = ((bf16[3,64,1,128]{3,0,2,1:T(4,128)(2,1)}), bf16[3,64,1,128]{3,0,2,1:T(4,128)(2,1)S(1)}, u32[]{:S(2)}, u32[]{:S(2)}) async-start(bf16[3,64,1,128]{3,0,2,1:T(4,128)(2,1)} %copy.132), calls=%async_computation.1 | async-start | bytes 131072 | tf_op jit(solution)/shard_map/all_to_all | solution.py:162
  41.4 6.5 %all-to-all-done.1 = bf16[3,64,1,128]{3,0,2,1:T(4,128)(2,1)S(1)} async-done(((bf16[3,64,1,128]{3,0,2,1:T(4,128)(2,1)}), bf16[3,64,1,128]{3,0,2,1:T(4,128)(2,1)S(1)}, u32[]{:S(2)}, u32[]{:S(2)}) %all-to-all-start.1) | async-done | bytes 49184 | tf_op jit(solution)/shard_map/all_to_all | solution.py:162
  48.4 1.2 %gather_fusion = f32[16,2,3,128]{3,1,2,0:T(2,128)} fusion(f32[4,2,3,128]{3,1,2,0:T(2,128)S(1)} %copy.137, s32[1024]{0:T(1024)S(1)} %pad_clamp_fusion.1), kind=kCustom, calls=%fused_computation | custom fusion | bytes 98368 | tf_op jit(solution)/shard_map/gather | solution.py:178
  49.6 11.4 %all-to-all-start.2 = ((f32[16,2,3,128]{3,1,2,0:T(2,128)}), f32[16,2,3,128]{3,1,2,0:T(2,128)S(1)}, u32[]{:S(2)}, u32[]{:S(2)}) async-start(f32[16,2,3,128]{3,1,2,0:T(2,128)} %gather_fusion), calls=%async_computation.2 | async-start | bytes 98304 | tf_op jit(solution)/shard_map/all_to_all | solution.py:177
  61.0 7.5 %all-to-all-done.2 = f32[16,2,3,128]{3,1,2,0:T(2,128)S(1)} async-done(((f32[16,2,3,128]{3,1,2,0:T(2,128)}), f32[16,2,3,128]{3,1,2,0:T(2,128)S(1)}, u32[]{:S(2)}, u32[]{:S(2)}) %all-to-all-start.2) | async-done | bytes 49184 | tf_op jit(solution)/shard_map/all_to_all | solution.py:177
  68.5 0.6 copy.138.refs_4_
  69.2 11.2 %shard_map.100 = f32[16,2,3,128]{3,2,1,0:T(4,128)} custom-call(s32[1]{0:T(128)} %bitcast.position_ref, f32[4,3,128,128]{3,2,1,0:T(8,128)} %copy-done.1, f32[4,3,128,128]{3,2,1,0:T(8,128)} %collective-permute-done.3.refs_1_, f32[4,3,128,128]{3,2,1,0:T(8,128)} %collective-permute-done.4.refs_2_, f32[4,3,128,128]{3,2,1,0:T(8,128)} %collective-permute-done.5.refs_3_, ...), custom_call_target="tpu_custom_call" | custom-call | tf_op jit(solution)/shard_map/pallas_call | solution.py:180
  80.3 1.5 %copy.139 = f32[16,2,3,128]{3,1,2,0:T(2,128)} copy(f32[16,2,3,128]{3,2,1,0:T(4,128)} %shard_map.100) | data formatting | bytes 98304 | tf_op jit(solution)/shard_map/pallas_call | solution.py:180
  81.8 3.6 %all-to-all-start.3 = ((f32[16,2,3,128]{3,1,2,0:T(2,128)}), f32[16,2,3,128]{3,1,2,0:T(2,128)S(1)}, u32[]{:S(2)}, u32[]{:S(2)}) async-start(f32[16,2,3,128]{3,1,2,0:T(2,128)} %copy.139), calls=%async_computation.3 | async-start | bytes 98304 | tf_op jit(solution)/shard_map/all_to_all | solution.py:187
  85.5 7.5 %all-to-all-done.3 = f32[16,2,3,128]{3,1,2,0:T(2,128)S(1)} async-done(((f32[16,2,3,128]{3,1,2,0:T(2,128)}), f32[16,2,3,128]{3,1,2,0:T(2,128)S(1)}, u32[]{:S(2)}, u32[]{:S(2)}) %all-to-all-start.3) | async-done | bytes 49184 | tf_op jit(solution)/shard_map/all_to_all | solution.py:187
  94.3 0.6 copy.143
  (70 shorter events, 5.1 us)
Async XLA Ops:
  0.0 19.2 %copy-start = (bf16[256,1920]{1,0:T(8,128)(2,1)S(1)}, bf16[256,1920]{1,0:T(8,128)(2,1)}, u32[]{:S(2)}) copy-start(bf16[256,1920]{1,0:T(8,128)(2,1)} %param.12) | copy-start | bytes 2949124
  0.0 1.2 %copy-start.4 = (f32[4,128,128]{2,1,0:T(8,128)S(1)}, f32[4,128,128]{2,1,0:T(8,128)}, u32[]{:S(2)}) copy-start(f32[4,128,128]{2,1,0:T(8,128)} %param.15) | copy-start | bytes 786436
  1.3 10.3 %copy-start.3 = (f32[3,4,16,128]{3,2,1,0:T(8,128)S(1)}, f32[3,4,16,128]{3,2,1,0:T(8,128)}, u32[]{:S(2)}) copy-start(f32[3,4,16,128]{3,2,1,0:T(8,128)} %param.10) | copy-start | bytes 294916
  1.3 10.3 %copy-start.6 = (bf16[3,4,16,128]{3,2,1,0:T(8,128)(2,1)S(1)}, bf16[3,4,16,128]{3,2,1,0:T(8,128)(2,1)}, u32[]{:S(2)}) copy-start(bf16[3,4,16,128]{3,2,1,0:T(8,128)(2,1)} %param.11) | copy-start | bytes 147460
  1.3 17.9 %copy-start.8 = (s32[1,256]{1,0:T(1,128)S(1)}, s32[1,256]{1,0:T(1,128)}, u32[]{:S(2)}) copy-start(s32[1,256]{1,0:T(1,128)} %param.17) | copy-start | bytes 3076
  1.3 17.9 %copy-start.9 = (s32[1,256]{1,0:T(1,128)S(1)}, s32[1,256]{1,0:T(1,128)}, u32[]{:S(2)}) copy-start(s32[1,256]{1,0:T(1,128)} %constant.116.clone.1) | copy-start | bytes 3076
  1.4 24.6 %collective-permute-start = (f32[3,128,128]{2,1,0:T(8,128)S(1)}, f32[3,128,128]{2,1,0:T(8,128)S(1)}, u32[]{:S(2)}, u32[]{:S(2)}) collective-permute-start(f32[3,128,128]{2,1,0:T(8,128)S(1)} %get-tuple-element.12), channel_id=1, source_target_pairs={{0,12},{4,0},{8,4},{12,8},{1,13},{5,1},{9,5},{13,9},{2,14},{6,2},{... | collective-permute-start | bytes 589832 | tf_op jit(solution)/shard_map/ppermute | solution.py:116
  8.3 17.7 %collective-permute-start.1 = (f32[3,128,128]{2,1,0:T(8,128)S(1)}, f32[3,128,128]{2,1,0:T(8,128)S(1)}, u32[]{:S(2)}, u32[]{:S(2)}) collective-permute-start(f32[3,128,128]{2,1,0:T(8,128)S(1)} %get-tuple-element.11), channel_id=1, source_target_pairs={{0,8},{4,12},{8,0},{12,4},{1,9},{5,13},{9,1},{13,5},{2,10},{6,14},... | collective-permute-start | bytes 589832 | tf_op jit(solution)/shard_map/ppermute | solution.py:116
  9.3 16.7 %collective-permute-start.2 = (f32[3,128,128]{2,1,0:T(8,128)S(1)}, f32[3,128,128]{2,1,0:T(8,128)}, u32[]{:S(2)}, u32[]{:S(2)}) collective-permute-start(f32[3,128,128]{2,1,0:T(8,128)S(1)} %get-tuple-element.10), channel_id=1, source_target_pairs={{0,4},{4,8},{8,12},{12,0},{1,5},{5,9},{9,13},{13,1},{2,6},{6,10},{... | collective-permute-start | bytes 589832 | tf_op jit(solution)/shard_map/ppermute | solution.py:116
  12.3 13.6 %all-to-all-start = ((bf16[6,4,16,128]{3,0,1,2:T(8,128)(2,1)}), bf16[6,4,16,128]{3,0,1,2:T(8,128)(2,1)S(1)}, u32[]{:S(2)}, u32[]{:S(2)}) async-start(bf16[6,4,16,128]{3,0,1,2:T(8,128)(2,1)} %copy.120), calls=%async_computation | async-start | bytes 262144 | tf_op jit(solution)/shard_map/all_to_all | solution.py:140
  19.1 1.0 %copy-start.10 = (s32[64]{0:T(128)}, s32[64]{0:T(128)S(1)}, u32[]{:S(2)}) copy-start(s32[64]{0:T(128)S(1)} %compare_select_fusion.2) | copy-start | bytes 772
  25.9 1.1 %copy-start.11 = (s32[64]{0:T(128)S(1)}, s32[64]{0:T(128)}, u32[]{:S(2)}) copy-start(s32[64]{0:T(128)} %copy-done.10) | copy-start | bytes 772
  25.9 1.1 %copy-start.12 = (pred[64]{0:T(512)(128)(4,1)S(1)}, pred[64]{0:T(512)(128)(4,1)}, u32[]{:S(2)}) copy-start(pred[64]{0:T(512)(128)(4,1)} %compare_and_fusion) | copy-start | bytes 196
  26.0 10.4 %copy-start.14 = (f32[64]{0:T(128)S(1)}, f32[64]{0:T(128)}, u32[]{:S(2)}) copy-start(f32[64]{0:T(128)} %fusion.59) | copy-start | bytes 772
  27.0 21.3 %copy-start.1 = (f32[4,3,128,128]{3,2,1,0:T(8,128)}, f32[4,3,128,128]{3,2,1,0:T(8,128)S(1)}, u32[]{:S(2)}) copy-start(f32[4,3,128,128]{3,2,1,0:T(8,128)S(1)} %pad_maximum_fusion.1.refs_0_) | copy-start | bytes 2359300
  27.0 14.3 %copy-start.13 = (s32[16]{0:T(128)S(1)}, s32[16]{0:T(128)}, u32[]{:S(2)}) copy-start(s32[16]{0:T(128)} %constant.139) | copy-start | bytes 196
  27.5 41.6 %collective-permute-start.3 = (f32[4,3,128,128]{3,2,1,0:T(8,128)S(1)}, f32[4,3,128,128]{3,2,1,0:T(8,128)}, u32[]{:S(2)}, u32[]{:S(2)}) collective-permute-start(f32[4,3,128,128]{3,2,1,0:T(8,128)S(1)} %pad_maximum_fusion.1.refs_0_), channel_id=1, source_target_pairs={{1,0},{6,5},{11,10},{12,15},{17,16},{22,21},{27,26},{28,31},{33,32... | collective-permute-start | bytes 2359304 | tf_op jit(solution)/shard_map/ppermute | solution.py:148
  33.3 35.8 %collective-permute-start.4 = (f32[4,3,128,128]{3,2,1,0:T(8,128)S(1)}, f32[4,3,128,128]{3,2,1,0:T(8,128)}, u32[]{:S(2)}, u32[]{:S(2)}) collective-permute-start(f32[4,3,128,128]{3,2,1,0:T(8,128)S(1)} %pad_maximum_fusion.1.refs_0_), channel_id=1, source_target_pairs={{2,0},{7,5},{8,10},{13,15},{18,16},{23,21},{24,26},{29,31},{34,32}... | collective-permute-start | bytes 2359304 | tf_op jit(solution)/shard_map/ppermute | solution.py:148
  34.9 34.3 %collective-permute-start.5 = (f32[4,3,128,128]{3,2,1,0:T(8,128)S(1)}, f32[4,3,128,128]{3,2,1,0:T(8,128)}, u32[]{:S(2)}, u32[]{:S(2)}) collective-permute-start(f32[4,3,128,128]{3,2,1,0:T(8,128)S(1)} %pad_maximum_fusion.1.refs_0_), channel_id=1, source_target_pairs={{3,0},{4,5},{9,10},{14,15},{19,16},{20,21},{25,26},{30,31},{35,32}... | collective-permute-start | bytes 2359304 | tf_op jit(solution)/shard_map/ppermute | solution.py:148
  37.5 10.4 %all-to-all-start.1 = ((bf16[3,64,1,128]{3,0,2,1:T(4,128)(2,1)}), bf16[3,64,1,128]{3,0,2,1:T(4,128)(2,1)S(1)}, u32[]{:S(2)}, u32[]{:S(2)}) async-start(bf16[3,64,1,128]{3,0,2,1:T(4,128)(2,1)} %copy.132), calls=%async_computation.1 | async-start | bytes 131072 | tf_op jit(solution)/shard_map/all_to_all | solution.py:162
  49.6 18.9 %all-to-all-start.2 = ((f32[16,2,3,128]{3,1,2,0:T(2,128)}), f32[16,2,3,128]{3,1,2,0:T(2,128)S(1)}, u32[]{:S(2)}, u32[]{:S(2)}) async-start(f32[16,2,3,128]{3,1,2,0:T(2,128)} %gather_fusion), calls=%async_computation.2 | async-start | bytes 98304 | tf_op jit(solution)/shard_map/all_to_all | solution.py:177
  69.2 24.5 %copy-start.2 = (bf16[1920,256]{1,0:T(8,128)(2,1)S(1)}, bf16[1920,256]{1,0:T(8,128)(2,1)}, u32[]{:S(2)}) copy-start(bf16[1920,256]{1,0:T(8,128)(2,1)} %param.13) | copy-start | bytes 2949124
  80.3 13.9 %copy-start.5 = (f32[4,15,128]{2,0,1:T(4,128)S(1)}, f32[4,15,128]{2,0,1:T(4,128)}, u32[]{:S(2)}) copy-start(f32[4,15,128]{2,0,1:T(4,128)} %broadcast_add_fusion) | copy-start | bytes 92164
  81.8 11.2 %all-to-all-start.3 = ((f32[16,2,3,128]{3,1,2,0:T(2,128)}), f32[16,2,3,128]{3,1,2,0:T(2,128)S(1)}, u32[]{:S(2)}, u32[]{:S(2)}) async-start(f32[16,2,3,128]{3,1,2,0:T(2,128)} %copy.139), calls=%async_computation.3 | async-start | bytes 98304 | tf_op jit(solution)/shard_map/all_to_all | solution.py:187
  (1 other events, 0.7 us)

commit v9 on v8

--- a/solution.py
+++ b/solution.py
@@ -54,7 +54,7 @@
             vectors,
             matrix,
             (((1,), (1,)), ((), ())),
-            precision=HIGHEST,
+            precision=lax.Precision.HIGH,
             preferred_element_type=jnp.float32,
         )
 
@@ -171,12 +171,9 @@
     right_part = cond_line[:, :, point_total:]
 
     sides = jnp.stack([rhs_left, right_part], axis=1)
-    destination_plane = jnp.asarray(
-        [owners.index(slab) if slab in owners else 0 for slab in range(slab_count)], jnp.int32
-    )
-    to_owner = lax.all_to_all(
-        sides[destination_plane], "slab", split_axis=0, concat_axis=0, tiled=True
-    )
+    destination_plane = [owners.index(slab) if slab in owners else 0 for slab in range(slab_count)]
+    outgoing = jnp.stack([sides[plane] for plane in destination_plane])
+    to_owner = lax.all_to_all(outgoing, "slab", split_axis=0, concat_axis=0, tiled=True)
     both_sides = pl.pallas_call(
         functools.partial(chain_kernel, group_size=group_size),
         out_shape=jax.ShapeDtypeStruct(to_owner.shape, jnp.float32),
@@ -185,7 +182,7 @@
         out_specs=pl.BlockSpec(memory_space=pltpu.VMEM),
     )(position.astype(jnp.int32).reshape(1), *across, to_owner)
     from_owner = lax.all_to_all(both_sides, "slab", split_axis=0, concat_axis=0, tiled=True)
-    mine = from_owner[jnp.asarray(owners)]
+    mine = jnp.stack([from_owner[owner] for owner in owners])
     left_values = mine[:, 0]
     right_values = mine[:, 1]
 

time: 95.5 us -> 90.7 us (0.950)
  Pallas kernels: 11.2 us -> 8.03 us
  waiting for transfers between devices: 25.3 us -> 27 us
  other arithmetic: 3.08 us -> 1.41 us
  local copies, waits for them, and re-layouts: 7.59 us -> 6.31 us
    all_to_all x1, waiting for transfers between devices: 6.48 us -> 0.01 us  [on_device(): lax.all_to_all(nonlin_lines, 'mode', split_axis=1, concat_axis=2, tiled=T...]
    all_to_all x1, waiting for transfers between devices: 7.48 us -> 13.3 us  [on_device(): lax.all_to_all(outgoing, 'slab', split_axis=0, concat_axis=0, tiled=True)]
    pallas_call x1, Pallas kernels: 11.2 us -> 8.03 us  [on_device(): pl.pallas_call(functools.partial(chain_kernel, group_size=group_size), ou...]
    all_to_all x1, waiting for transfers between devices: 3.78 us -> 6.25 us  [on_device(): lax.all_to_all(both_fields, 'mode', split_axis=2, concat_axis=1, tiled=True)]
    gather x2 -> x0, local copies, waits for them, and re-layouts: 1.8 us -> none  [the longest x1 1.23 us: on_device(): sides[destination_plane]]
    all_to_all x1, starting transfers between devices: 11.4 us -> 10.2 us  [on_device(): lax.all_to_all(outgoing, 'slab', split_axis=0, concat_axis=0, tiled=True)]
  transfers between devices with their start and end apart: 10 -> 10, of which waited for: 4 -> 3; matrix products, arithmetic and copies ran while one was open for 7% -> 4% of each run, Pallas kernels for 0% -> 0%
where the time goes in v9:
time: 90.7 us; the launch traced here: 90.1 us
  starting transfers between devices  44.3 us (49%)
  waiting for transfers between devices  27 us (30%)
  Pallas kernels  8.03 us (9%)
  local copies, waits for them, and re-layouts  6.31 us (7%)
  matrix products  2.66 us (3%)
  other arithmetic  1.41 us (2%)
    all_to_all x1, waiting for transfers between devices, on_device(): lax.all_to_all(outgoing, 'slab', split_axis=0, concat_axis=0, tiled=True)  13.3 us
    all_to_all x1, starting transfers between devices, on_device(): lax.all_to_all(outgoing, 'slab', split_axis=0, concat_axis=0, tiled=True)  10.2 us
    ppermute x3, starting transfers between devices, on_device(): lax.ppermute(blocks[(position - offset) % group_count], 'slab', pairs)  10.2 us
    ppermute x3, starting transfers between devices, on_device(): across.append(lax.ppermute(group_blocks, 'slab', pairs))  9.25 us
    pallas_call x1, Pallas kernels, on_device(): pl.pallas_call(functools.partial(chain_kernel, group_size=group_size), ou...  8.03 us
    all_to_all x1, waiting for transfers between devices, on_device(): lax.all_to_all(both_sides, 'slab', split_axis=0, concat_axis=0, tiled=True)  7.43 us
    all_to_all x1, starting transfers between devices, on_device(): lax.all_to_all(both_fields, 'mode', split_axis=2, concat_axis=1, tiled=True)  6.75 us
    all_to_all x1, waiting for transfers between devices, on_device(): lax.all_to_all(both_fields, 'mode', split_axis=2, concat_axis=1, tiled=True)  6.25 us
  transfers between devices with their start and end apart: 10, of which 3 were waited for; matrix products, arithmetic and copies ran while one was open for 4% of the time, Pallas kernels for 0%

profile of v9, /device:TPU:1, one launch (start us, length us, event | category | flops | bytes accessed | tf_op | source)
XLA Modules:
  0.0 90.1 jit_solution(1007788546632870034)
XLA Ops:
  0.0 1.2 %slice_bitcast_fusion.1 = (f32[4,1,128,128]{3,2,1,0:T(8,128)S(1)}, f32[4,1,128,128]{3,2,1,0:T(8,128)S(1)}) fusion(f32[2,4,128,128]{3,2,1,0:T(8,128)} %param.12), kind=kLoop, calls=%fused_computation.13 | loop fusion | bytes 1048576 | tf_op jit(solution)/shard_map/stack;squeeze | solution.py:106
  1.4 6.9 %collective-permute-start = (f32[3,128,128]{2,1,0:T(8,128)S(1)}, f32[3,128,128]{2,1,0:T(8,128)S(1)}, u32[]{:S(2)}, u32[]{:S(2)}) collective-permute-start(f32[3,128,128]{2,1,0:T(8,128)S(1)} %get-tuple-element.12), channel_id=1, source_target_pairs={{0,12},{4,0},{8,4},{12,8},{1,13},{5,1},{9,5},{13,9},{2,14},{6,2},{... | collective-permute-start | bytes 589832 | tf_op jit(solution)/shard_map/ppermute | solution.py:116
  8.3 1.0 %collective-permute-start.1 = (f32[3,128,128]{2,1,0:T(8,128)S(1)}, f32[3,128,128]{2,1,0:T(8,128)S(1)}, u32[]{:S(2)}, u32[]{:S(2)}) collective-permute-start(f32[3,128,128]{2,1,0:T(8,128)S(1)} %get-tuple-element.11), channel_id=1, source_target_pairs={{0,8},{4,12},{8,0},{12,4},{1,9},{5,13},{9,1},{13,5},{2,10},{6,14},... | collective-permute-start | bytes 589832 | tf_op jit(solution)/shard_map/ppermute | solution.py:116
  9.3 2.3 %collective-permute-start.2 = (f32[3,128,128]{2,1,0:T(8,128)S(1)}, f32[3,128,128]{2,1,0:T(8,128)}, u32[]{:S(2)}, u32[]{:S(2)}) collective-permute-start(f32[3,128,128]{2,1,0:T(8,128)S(1)} %get-tuple-element.10), channel_id=1, source_target_pairs={{0,4},{4,8},{8,12},{12,0},{1,5},{5,9},{9,13},{13,1},{2,6},{6,10},{... | collective-permute-start | bytes 589832 | tf_op jit(solution)/shard_map/ppermute | solution.py:116
  11.6 0.7 copy.126
  12.3 6.8 %all-to-all-start = ((bf16[6,4,16,128]{3,0,1,2:T(8,128)(2,1)}), bf16[6,4,16,128]{3,0,1,2:T(8,128)(2,1)S(1)}, u32[]{:S(2)}, u32[]{:S(2)}) async-start(bf16[6,4,16,128]{3,0,1,2:T(8,128)(2,1)} %copy.126), calls=%async_computation | async-start | bytes 262144 | tf_op jit(solution)/shard_map/all_to_all | solution.py:140
  19.2 0.5 fusion
  19.7 6.3 %all-to-all-done = bf16[6,4,16,128]{3,0,1,2:T(8,128)(2,1)S(1)} async-done(((bf16[6,4,16,128]{3,0,1,2:T(8,128)(2,1)}), bf16[6,4,16,128]{3,0,1,2:T(8,128)(2,1)S(1)}, u32[]{:S(2)}, u32[]{:S(2)}) %all-to-all-start) | async-done | bytes 98336 | tf_op jit(solution)/shard_map/all_to_all | solution.py:140
  26.0 1.0 %pad_maximum_fusion.1.refs_0_ = f32[4,3,128,128]{3,2,1,0:T(8,128)S(1)} fusion(f32[1,3,128,128]{3,2,1,0:T(8,128)} %bitcast.9, f32[1,3,128,128]{3,2,1,0:T(8,128)S(1)} %bitcast.135, f32[1,3,128,128]{3,2,1,0:T(8,128)S(1)} %bitcast.134, f32[1,3,128,128]{3,2,1,0:T(8,128)S(1)} %get-tuple-element.9), kind=kLoop, calls=%fused_computation.10 | loop fusion | flops 589824 | bytes 1572864 | tf_op jit(solution)/shard_map/stack | solution.py:117
  27.8 0.7 copy.138
  28.5 3.8 %all-to-all-start.1 = ((bf16[3,64,1,128]{3,0,2,1:T(4,128)(2,1)}), bf16[3,64,1,128]{3,0,2,1:T(4,128)(2,1)S(1)}, u32[]{:S(2)}, u32[]{:S(2)}) async-start(bf16[3,64,1,128]{3,0,2,1:T(4,128)(2,1)} %copy.138), calls=%async_computation.1 | async-start | bytes 131072 | tf_op jit(solution)/shard_map/all_to_all | solution.py:162
  32.8 6.1 %collective-permute-start.3 = (f32[4,3,128,128]{3,2,1,0:T(8,128)S(1)}, f32[4,3,128,128]{3,2,1,0:T(8,128)}, u32[]{:S(2)}, u32[]{:S(2)}) collective-permute-start(f32[4,3,128,128]{3,2,1,0:T(8,128)S(1)} %pad_maximum_fusion.1.refs_0_), channel_id=1, source_target_pairs={{1,0},{6,5},{11,10},{12,15},{17,16},{22,21},{27,26},{28,31},{33,32... | collective-permute-start | bytes 2359304 | tf_op jit(solution)/shard_map/ppermute | solution.py:148
  38.9 1.6 %collective-permute-start.4 = (f32[4,3,128,128]{3,2,1,0:T(8,128)S(1)}, f32[4,3,128,128]{3,2,1,0:T(8,128)}, u32[]{:S(2)}, u32[]{:S(2)}) collective-permute-start(f32[4,3,128,128]{3,2,1,0:T(8,128)S(1)} %pad_maximum_fusion.1.refs_0_), channel_id=1, source_target_pairs={{2,0},{7,5},{8,10},{13,15},{18,16},{23,21},{24,26},{29,31},{34,32}... | collective-permute-start | bytes 2359304 | tf_op jit(solution)/shard_map/ppermute | solution.py:148
  40.5 1.5 %collective-permute-start.5 = (f32[4,3,128,128]{3,2,1,0:T(8,128)S(1)}, f32[4,3,128,128]{3,2,1,0:T(8,128)}, u32[]{:S(2)}, u32[]{:S(2)}) collective-permute-start(f32[4,3,128,128]{3,2,1,0:T(8,128)S(1)} %pad_maximum_fusion.1.refs_0_), channel_id=1, source_target_pairs={{3,0},{4,5},{9,10},{14,15},{19,16},{20,21},{25,26},{30,31},{35,32}... | collective-permute-start | bytes 2359304 | tf_op jit(solution)/shard_map/ppermute | solution.py:148
  42.6 0.6 copy.143
  43.3 10.2 %all-to-all-start.2 = ((f32[16,2,3,128]{3,1,2,0:T(2,128)}), f32[16,2,3,128]{3,1,2,0:T(2,128)S(1)}, u32[]{:S(2)}, u32[]{:S(2)}) async-start(f32[16,2,3,128]{3,1,2,0:T(2,128)} %copy.143), calls=%async_computation.2 | async-start | bytes 98304 | tf_op jit(solution)/shard_map/all_to_all | solution.py:176
  53.6 13.3 %all-to-all-done.2 = f32[16,2,3,128]{3,1,2,0:T(2,128)S(1)} async-done(((f32[16,2,3,128]{3,1,2,0:T(2,128)}), f32[16,2,3,128]{3,1,2,0:T(2,128)S(1)}, u32[]{:S(2)}, u32[]{:S(2)}) %all-to-all-start.2) | async-done | bytes 49184 | tf_op jit(solution)/shard_map/all_to_all | solution.py:176
  66.9 0.6 copy.144.refs_4_
  67.5 8.0 %shard_map.82 = f32[16,2,3,128]{3,2,1,0:T(4,128)} custom-call(s32[1]{0:T(128)} %bitcast.position_ref, f32[4,3,128,128]{3,2,1,0:T(8,128)} %copy-done.1, f32[4,3,128,128]{3,2,1,0:T(8,128)} %collective-permute-done.3.refs_1_, f32[4,3,128,128]{3,2,1,0:T(8,128)} %collective-permute-done.4.refs_2_, f32[4,3,128,128]{3,2,1,0:T(8,128)} %collective-permute-done.5.refs_3_, ...), custom_call_target="tpu_custom_call" | custom-call | tf_op jit(solution)/shard_map/pallas_call | solution.py:177
  75.6 1.5 %copy.145 = f32[16,2,3,128]{3,1,2,0:T(2,128)} copy(f32[16,2,3,128]{3,2,1,0:T(4,128)} %shard_map.82) | data formatting | bytes 98304 | tf_op jit(solution)/shard_map/pallas_call | solution.py:177
  77.1 4.1 %all-to-all-start.3 = ((f32[16,2,3,128]{3,1,2,0:T(2,128)}), f32[16,2,3,128]{3,1,2,0:T(2,128)S(1)}, u32[]{:S(2)}, u32[]{:S(2)}) async-start(f32[16,2,3,128]{3,1,2,0:T(2,128)} %copy.145), calls=%async_computation.3 | async-start | bytes 98304 | tf_op jit(solution)/shard_map/all_to_all | solution.py:184
  81.3 7.4 %all-to-all-done.3 = f32[16,2,3,128]{3,1,2,0:T(2,128)S(1)} async-done(((f32[16,2,3,128]{3,1,2,0:T(2,128)}), f32[16,2,3,128]{3,1,2,0:T(2,128)S(1)}, u32[]{:S(2)}, u32[]{:S(2)}) %all-to-all-start.3) | async-done | bytes 49184 | tf_op jit(solution)/shard_map/all_to_all | solution.py:184
  88.8 0.6 convolution_bitcast_fusion
  89.5 0.6 copy.151
  (59 shorter events, 2.4 us)
Async XLA Ops:
  0.0 19.2 %copy-start = (bf16[256,1920]{1,0:T(8,128)(2,1)S(1)}, bf16[256,1920]{1,0:T(8,128)(2,1)}, u32[]{:S(2)}) copy-start(bf16[256,1920]{1,0:T(8,128)(2,1)} %param.10) | copy-start | bytes 2949124
  0.0 1.2 %copy-start.4 = (f32[4,128,128]{2,1,0:T(8,128)S(1)}, f32[4,128,128]{2,1,0:T(8,128)}, u32[]{:S(2)}) copy-start(f32[4,128,128]{2,1,0:T(8,128)} %param.13) | copy-start | bytes 786436
  1.3 10.3 %copy-start.3 = (f32[3,4,16,128]{3,2,1,0:T(8,128)S(1)}, f32[3,4,16,128]{3,2,1,0:T(8,128)}, u32[]{:S(2)}) copy-start(f32[3,4,16,128]{3,2,1,0:T(8,128)} %param.8) | copy-start | bytes 294916
  1.3 10.3 %copy-start.5 = (bf16[3,4,16,128]{3,2,1,0:T(8,128)(2,1)S(1)}, bf16[3,4,16,128]{3,2,1,0:T(8,128)(2,1)}, u32[]{:S(2)}) copy-start(bf16[3,4,16,128]{3,2,1,0:T(8,128)(2,1)} %param.9) | copy-start | bytes 147460
  1.3 17.8 %copy-start.7 = (s32[1,256]{1,0:T(1,128)S(1)}, s32[1,256]{1,0:T(1,128)}, u32[]{:S(2)}) copy-start(s32[1,256]{1,0:T(1,128)} %param.15) | copy-start | bytes 3076
  1.3 17.8 %copy-start.8 = (s32[1,256]{1,0:T(1,128)S(1)}, s32[1,256]{1,0:T(1,128)}, u32[]{:S(2)}) copy-start(s32[1,256]{1,0:T(1,128)} %constant.107.clone.1) | copy-start | bytes 3076
  1.4 24.6 %collective-permute-start = (f32[3,128,128]{2,1,0:T(8,128)S(1)}, f32[3,128,128]{2,1,0:T(8,128)S(1)}, u32[]{:S(2)}, u32[]{:S(2)}) collective-permute-start(f32[3,128,128]{2,1,0:T(8,128)S(1)} %get-tuple-element.12), channel_id=1, source_target_pairs={{0,12},{4,0},{8,4},{12,8},{1,13},{5,1},{9,5},{13,9},{2,14},{6,2},{... | collective-permute-start | bytes 589832 | tf_op jit(solution)/shard_map/ppermute | solution.py:116
  8.3 17.7 %collective-permute-start.1 = (f32[3,128,128]{2,1,0:T(8,128)S(1)}, f32[3,128,128]{2,1,0:T(8,128)S(1)}, u32[]{:S(2)}, u32[]{:S(2)}) collective-permute-start(f32[3,128,128]{2,1,0:T(8,128)S(1)} %get-tuple-element.11), channel_id=1, source_target_pairs={{0,8},{4,12},{8,0},{12,4},{1,9},{5,13},{9,1},{13,5},{2,10},{6,14},... | collective-permute-start | bytes 589832 | tf_op jit(solution)/shard_map/ppermute | solution.py:116
  9.3 16.7 %collective-permute-start.2 = (f32[3,128,128]{2,1,0:T(8,128)S(1)}, f32[3,128,128]{2,1,0:T(8,128)}, u32[]{:S(2)}, u32[]{:S(2)}) collective-permute-start(f32[3,128,128]{2,1,0:T(8,128)S(1)} %get-tuple-element.10), channel_id=1, source_target_pairs={{0,4},{4,8},{8,12},{12,0},{1,5},{5,9},{9,13},{13,1},{2,6},{6,10},{... | collective-permute-start | bytes 589832 | tf_op jit(solution)/shard_map/ppermute | solution.py:116
  12.3 13.6 %all-to-all-start = ((bf16[6,4,16,128]{3,0,1,2:T(8,128)(2,1)}), bf16[6,4,16,128]{3,0,1,2:T(8,128)(2,1)S(1)}, u32[]{:S(2)}, u32[]{:S(2)}) async-start(bf16[6,4,16,128]{3,0,1,2:T(8,128)(2,1)} %copy.126), calls=%async_computation | async-start | bytes 262144 | tf_op jit(solution)/shard_map/all_to_all | solution.py:140
  27.0 13.5 %copy-start.1 = (f32[4,3,128,128]{3,2,1,0:T(8,128)}, f32[4,3,128,128]{3,2,1,0:T(8,128)S(1)}, u32[]{:S(2)}) copy-start(f32[4,3,128,128]{3,2,1,0:T(8,128)S(1)} %pad_maximum_fusion.1.refs_0_) | copy-start | bytes 2359300
  28.5 13.5 %all-to-all-start.1 = ((bf16[3,64,1,128]{3,0,2,1:T(4,128)(2,1)}), bf16[3,64,1,128]{3,0,2,1:T(4,128)(2,1)S(1)}, u32[]{:S(2)}, u32[]{:S(2)}) async-start(bf16[3,64,1,128]{3,0,2,1:T(4,128)(2,1)} %copy.138), calls=%async_computation.1 | async-start | bytes 131072 | tf_op jit(solution)/shard_map/all_to_all | solution.py:162
  32.8 34.7 %collective-permute-start.3 = (f32[4,3,128,128]{3,2,1,0:T(8,128)S(1)}, f32[4,3,128,128]{3,2,1,0:T(8,128)}, u32[]{:S(2)}, u32[]{:S(2)}) collective-permute-start(f32[4,3,128,128]{3,2,1,0:T(8,128)S(1)} %pad_maximum_fusion.1.refs_0_), channel_id=1, source_target_pairs={{1,0},{6,5},{11,10},{12,15},{17,16},{22,21},{27,26},{28,31},{33,32... | collective-permute-start | bytes 2359304 | tf_op jit(solution)/shard_map/ppermute | solution.py:148
  38.9 28.6 %collective-permute-start.4 = (f32[4,3,128,128]{3,2,1,0:T(8,128)S(1)}, f32[4,3,128,128]{3,2,1,0:T(8,128)}, u32[]{:S(2)}, u32[]{:S(2)}) collective-permute-start(f32[4,3,128,128]{3,2,1,0:T(8,128)S(1)} %pad_maximum_fusion.1.refs_0_), channel_id=1, source_target_pairs={{2,0},{7,5},{8,10},{13,15},{18,16},{23,21},{24,26},{29,31},{34,32}... | collective-permute-start | bytes 2359304 | tf_op jit(solution)/shard_map/ppermute | solution.py:148
  40.5 27.0 %collective-permute-start.5 = (f32[4,3,128,128]{3,2,1,0:T(8,128)S(1)}, f32[4,3,128,128]{3,2,1,0:T(8,128)}, u32[]{:S(2)}, u32[]{:S(2)}) collective-permute-start(f32[4,3,128,128]{3,2,1,0:T(8,128)S(1)} %pad_maximum_fusion.1.refs_0_), channel_id=1, source_target_pairs={{3,0},{4,5},{9,10},{14,15},{19,16},{20,21},{25,26},{30,31},{35,32}... | collective-permute-start | bytes 2359304 | tf_op jit(solution)/shard_map/ppermute | solution.py:148
  43.3 23.6 %all-to-all-start.2 = ((f32[16,2,3,128]{3,1,2,0:T(2,128)}), f32[16,2,3,128]{3,1,2,0:T(2,128)S(1)}, u32[]{:S(2)}, u32[]{:S(2)}) async-start(f32[16,2,3,128]{3,1,2,0:T(2,128)} %copy.143), calls=%async_computation.2 | async-start | bytes 98304 | tf_op jit(solution)/shard_map/all_to_all | solution.py:176
  67.5 13.6 %copy-start.6 = (f32[15,128]{1,0:T(8,128)S(1)}, f32[15,128]{1,0:T(8,128)}, u32[]{:S(2)}) copy-start(f32[15,128]{1,0:T(8,128)} %param.14) | copy-start | bytes 23044
  67.5 21.2 %copy-start.2 = (bf16[1920,256]{1,0:T(8,128)(2,1)S(1)}, bf16[1920,256]{1,0:T(8,128)(2,1)}, u32[]{:S(2)}) copy-start(bf16[1920,256]{1,0:T(8,128)(2,1)} %param.11) | copy-start | bytes 2949124
  77.1 11.6 %all-to-all-start.3 = ((f32[16,2,3,128]{3,1,2,0:T(2,128)}), f32[16,2,3,128]{3,1,2,0:T(2,128)S(1)}, u32[]{:S(2)}, u32[]{:S(2)}) async-start(f32[16,2,3,128]{3,1,2,0:T(2,128)} %copy.145), calls=%async_computation.3 | async-start | bytes 98304 | tf_op jit(solution)/shard_map/all_to_all | solution.py:184

commit v10 on v9

--- a/solution.py
+++ b/solution.py
@@ -60,8 +60,9 @@
 
     def solve(position):
         def blocks_of(slab):
-            group_slot = (slab % group_size - position) % group_size
-            spot_slot = (slab // group_size - position) % group_size
+            label = (slab + 1) % slab_count
+            group_slot = (label % group_size - 1) % group_size
+            spot_slot = (label // group_size - position) % group_size
             return group_refs[group_slot].at[spot_slot]
 
         zero = jnp.zeros(sides_ref.shape[2:], jnp.float32)
@@ -100,8 +101,12 @@
     slab_index = lax.axis_index("slab")
     group_size = planes_dev
     group_count = slab_count // group_size
-    position = slab_index // group_size
-    owners = [plane * group_size + plane for plane in range(planes_dev)]
+    position = ((slab_index + 1) % slab_count) // group_size
+
+    def slab_of(label):
+        return (label - 1) % slab_count
+
+    owners = [slab_of(plane * group_size + 1) for plane in range(planes_dev)]
 
     blocks = jnp.stack(
         [interface_chain_factors[0], interface_chain_factors[1], pivot_inverse], axis=1
@@ -109,7 +114,10 @@
     within = [blocks[position]]
     for offset in range(1, group_count):
         pairs = [
-            (rest + group_size * rank, rest + group_size * ((rank - offset) % group_count))
+            (
+                slab_of(rest + group_size * rank),
+                slab_of(rest + group_size * ((rank - offset) % group_count)),
+            )
             for rest in range(group_size)
             for rank in range(group_count)
         ]
@@ -142,7 +150,7 @@
     across = [group_blocks]
     for offset in range(1, group_size):
         pairs = [
-            (plane * group_size + (plane + offset) % group_size, owners[plane])
+            (slab_of(plane * group_size + (1 + offset) % group_size), owners[plane])
             for plane in range(planes_dev)
         ]
         across.append(lax.ppermute(group_blocks, "slab", pairs))

time: 90.7 us -> 84.3 us (0.929)
  waiting for transfers between devices: 27 us -> 21.1 us
    all_to_all x1, waiting for transfers between devices: 13.3 us -> 7.4 us  [on_device(): lax.all_to_all(outgoing, 'slab', split_axis=0, concat_axis=0, tiled=True)]
where the time goes in v10:
time: 84.3 us; the launch traced here: 83.8 us
  starting transfers between devices  43.9 us (52%)
  waiting for transfers between devices  21.1 us (25%)
  Pallas kernels  8.03 us (10%)
  local copies, waits for them, and re-layouts  6.31 us (7%)
  matrix products  2.66 us (3%)
  other arithmetic  1.41 us (2%)
    all_to_all x1, starting transfers between devices, on_device(): lax.all_to_all(outgoing, 'slab', split_axis=0, concat_axis=0, tiled=True)  10.2 us
    ppermute x3, starting transfers between devices, on_device(): lax.ppermute(blocks[(position - offset) % group_count], 'slab', pairs)  10.2 us
    ppermute x3, starting transfers between devices, on_device(): across.append(lax.ppermute(group_blocks, 'slab', pairs))  9.25 us
    pallas_call x1, Pallas kernels, on_device(): pl.pallas_call(functools.partial(chain_kernel, group_size=group_size), ou...  8.03 us
    all_to_all x1, waiting for transfers between devices, on_device(): lax.all_to_all(both_sides, 'slab', split_axis=0, concat_axis=0, tiled=True)  7.43 us
    all_to_all x1, waiting for transfers between devices, on_device(): lax.all_to_all(outgoing, 'slab', split_axis=0, concat_axis=0, tiled=True)  7.4 us
    all_to_all x1, starting transfers between devices, on_device(): lax.all_to_all(both_fields, 'mode', split_axis=2, concat_axis=1, tiled=True)  6.75 us
    all_to_all x1, waiting for transfers between devices, on_device(): lax.all_to_all(both_fields, 'mode', split_axis=2, concat_axis=1, tiled=True)  6.25 us
  transfers between devices with their start and end apart: 10, of which 3 were waited for; matrix products, arithmetic and copies ran while one was open for 4% of the time, Pallas kernels for 0%

profile of v10, /device:TPU:1, one launch (start us, length us, event | category | flops | bytes accessed | tf_op | source)
XLA Modules:
  0.0 83.8 jit_solution(12573458176665052146)
XLA Ops:
  0.0 1.2 %slice_bitcast_fusion.1 = (f32[4,1,128,128]{3,2,1,0:T(8,128)S(1)}, f32[4,1,128,128]{3,2,1,0:T(8,128)S(1)}) fusion(f32[2,4,128,128]{3,2,1,0:T(8,128)} %param.12), kind=kLoop, calls=%fused_computation.13 | loop fusion | bytes 1048576 | tf_op jit(solution)/shard_map/stack;squeeze | solution.py:111
  1.4 6.9 %collective-permute-start = (f32[3,128,128]{2,1,0:T(8,128)S(1)}, f32[3,128,128]{2,1,0:T(8,128)S(1)}, u32[]{:S(2)}, u32[]{:S(2)}) collective-permute-start(f32[3,128,128]{2,1,0:T(8,128)S(1)} %get-tuple-element.12), channel_id=1, source_target_pairs={{15,11},{3,15},{7,3},{11,7},{0,12},{4,0},{8,4},{12,8},{1,13},{5,1}... | collective-permute-start | bytes 589832 | tf_op jit(solution)/shard_map/ppermute | solution.py:124
  8.3 1.0 %collective-permute-start.1 = (f32[3,128,128]{2,1,0:T(8,128)S(1)}, f32[3,128,128]{2,1,0:T(8,128)S(1)}, u32[]{:S(2)}, u32[]{:S(2)}) collective-permute-start(f32[3,128,128]{2,1,0:T(8,128)S(1)} %get-tuple-element.11), channel_id=1, source_target_pairs={{15,7},{3,11},{7,15},{11,3},{0,8},{4,12},{8,0},{12,4},{1,9},{5,13}... | collective-permute-start | bytes 589832 | tf_op jit(solution)/shard_map/ppermute | solution.py:124
  9.3 2.3 %collective-permute-start.2 = (f32[3,128,128]{2,1,0:T(8,128)S(1)}, f32[3,128,128]{2,1,0:T(8,128)}, u32[]{:S(2)}, u32[]{:S(2)}) collective-permute-start(f32[3,128,128]{2,1,0:T(8,128)S(1)} %get-tuple-element.10), channel_id=1, source_target_pairs={{15,3},{3,7},{7,11},{11,15},{0,4},{4,8},{8,12},{12,0},{1,5},{5,9},... | collective-permute-start | bytes 589832 | tf_op jit(solution)/shard_map/ppermute | solution.py:124
  11.6 0.7 copy.126
  12.3 6.8 %all-to-all-start = ((bf16[6,4,16,128]{3,0,1,2:T(8,128)(2,1)}), bf16[6,4,16,128]{3,0,1,2:T(8,128)(2,1)S(1)}, u32[]{:S(2)}, u32[]{:S(2)}) async-start(bf16[6,4,16,128]{3,0,1,2:T(8,128)(2,1)} %copy.126), calls=%async_computation | async-start | bytes 262144 | tf_op jit(solution)/shard_map/all_to_all | solution.py:148
  19.2 0.5 fusion
  19.7 6.3 %all-to-all-done = bf16[6,4,16,128]{3,0,1,2:T(8,128)(2,1)S(1)} async-done(((bf16[6,4,16,128]{3,0,1,2:T(8,128)(2,1)}), bf16[6,4,16,128]{3,0,1,2:T(8,128)(2,1)S(1)}, u32[]{:S(2)}, u32[]{:S(2)}) %all-to-all-start) | async-done | bytes 98336 | tf_op jit(solution)/shard_map/all_to_all | solution.py:148
  26.0 1.0 %pad_maximum_fusion.1.refs_0_ = f32[4,3,128,128]{3,2,1,0:T(8,128)S(1)} fusion(f32[1,3,128,128]{3,2,1,0:T(8,128)} %bitcast.9, f32[1,3,128,128]{3,2,1,0:T(8,128)S(1)} %bitcast.135, f32[1,3,128,128]{3,2,1,0:T(8,128)S(1)} %bitcast.134, f32[1,3,128,128]{3,2,1,0:T(8,128)S(1)} %get-tuple-element.9), kind=kLoop, calls=%fused_computation.10 | loop fusion | flops 589824 | bytes 1572864 | tf_op jit(solution)/shard_map/stack | solution.py:125
  27.8 0.7 copy.138
  28.5 3.8 %all-to-all-start.1 = ((bf16[3,64,1,128]{3,0,2,1:T(4,128)(2,1)}), bf16[3,64,1,128]{3,0,2,1:T(4,128)(2,1)S(1)}, u32[]{:S(2)}, u32[]{:S(2)}) async-start(bf16[3,64,1,128]{3,0,2,1:T(4,128)(2,1)} %copy.138), calls=%async_computation.1 | async-start | bytes 131072 | tf_op jit(solution)/shard_map/all_to_all | solution.py:170
  32.8 6.1 %collective-permute-start.3 = (f32[4,3,128,128]{3,2,1,0:T(8,128)S(1)}, f32[4,3,128,128]{3,2,1,0:T(8,128)}, u32[]{:S(2)}, u32[]{:S(2)}) collective-permute-start(f32[4,3,128,128]{3,2,1,0:T(8,128)S(1)} %pad_maximum_fusion.1.refs_0_), channel_id=1, source_target_pairs={{1,0},{5,4},{9,8},{13,12},{17,16},{21,20},{25,24},{29,28},{33,32},... | collective-permute-start | bytes 2359304 | tf_op jit(solution)/shard_map/ppermute | solution.py:156
  38.9 1.6 %collective-permute-start.4 = (f32[4,3,128,128]{3,2,1,0:T(8,128)S(1)}, f32[4,3,128,128]{3,2,1,0:T(8,128)}, u32[]{:S(2)}, u32[]{:S(2)}) collective-permute-start(f32[4,3,128,128]{3,2,1,0:T(8,128)S(1)} %pad_maximum_fusion.1.refs_0_), channel_id=1, source_target_pairs={{2,0},{6,4},{10,8},{14,12},{18,16},{22,20},{26,24},{30,28},{34,32}... | collective-permute-start | bytes 2359304 | tf_op jit(solution)/shard_map/ppermute | solution.py:156
  40.5 1.5 %collective-permute-start.5 = (f32[4,3,128,128]{3,2,1,0:T(8,128)S(1)}, f32[4,3,128,128]{3,2,1,0:T(8,128)}, u32[]{:S(2)}, u32[]{:S(2)}) collective-permute-start(f32[4,3,128,128]{3,2,1,0:T(8,128)S(1)} %pad_maximum_fusion.1.refs_0_), channel_id=1, source_target_pairs={{15,0},{3,4},{7,8},{11,12},{31,16},{19,20},{23,24},{27,28},{47,32}... | collective-permute-start | bytes 2359304 | tf_op jit(solution)/shard_map/ppermute | solution.py:156
  42.6 0.6 copy.143
  43.3 10.2 %all-to-all-start.2 = ((f32[16,2,3,128]{3,1,2,0:T(2,128)}), f32[16,2,3,128]{3,1,2,0:T(2,128)S(1)}, u32[]{:S(2)}, u32[]{:S(2)}) async-start(f32[16,2,3,128]{3,1,2,0:T(2,128)} %copy.143), calls=%async_computation.2 | async-start | bytes 98304 | tf_op jit(solution)/shard_map/all_to_all | solution.py:184
  53.6 7.4 %all-to-all-done.2 = f32[16,2,3,128]{3,1,2,0:T(2,128)S(1)} async-done(((f32[16,2,3,128]{3,1,2,0:T(2,128)}), f32[16,2,3,128]{3,1,2,0:T(2,128)S(1)}, u32[]{:S(2)}, u32[]{:S(2)}) %all-to-all-start.2) | async-done | bytes 49184 | tf_op jit(solution)/shard_map/all_to_all | solution.py:184
  61.0 0.6 copy.144.refs_4_
  61.7 8.0 %shard_map.82 = f32[16,2,3,128]{3,2,1,0:T(4,128)} custom-call(s32[1]{0:T(128)} %bitcast.position_ref, f32[4,3,128,128]{3,2,1,0:T(8,128)} %copy-done.1, f32[4,3,128,128]{3,2,1,0:T(8,128)} %collective-permute-done.3.refs_1_, f32[4,3,128,128]{3,2,1,0:T(8,128)} %collective-permute-done.4.refs_2_, f32[4,3,128,128]{3,2,1,0:T(8,128)} %collective-permute-done.5.refs_3_, ...), custom_call_target="tpu_custom_call" | custom-call | tf_op jit(solution)/shard_map/pallas_call | solution.py:185
  69.7 1.5 %copy.145 = f32[16,2,3,128]{3,1,2,0:T(2,128)} copy(f32[16,2,3,128]{3,2,1,0:T(4,128)} %shard_map.82) | data formatting | bytes 98304 | tf_op jit(solution)/shard_map/pallas_call | solution.py:185
  71.2 3.6 %all-to-all-start.3 = ((f32[16,2,3,128]{3,1,2,0:T(2,128)}), f32[16,2,3,128]{3,1,2,0:T(2,128)S(1)}, u32[]{:S(2)}, u32[]{:S(2)}) async-start(f32[16,2,3,128]{3,1,2,0:T(2,128)} %copy.145), calls=%async_computation.3 | async-start | bytes 98304 | tf_op jit(solution)/shard_map/all_to_all | solution.py:192
  74.9 7.4 %all-to-all-done.3 = f32[16,2,3,128]{3,1,2,0:T(2,128)S(1)} async-done(((f32[16,2,3,128]{3,1,2,0:T(2,128)}), f32[16,2,3,128]{3,1,2,0:T(2,128)S(1)}, u32[]{:S(2)}, u32[]{:S(2)}) %all-to-all-start.3) | async-done | bytes 49184 | tf_op jit(solution)/shard_map/all_to_all | solution.py:192
  82.4 0.6 convolution_bitcast_fusion
  83.1 0.6 copy.151
  (59 shorter events, 2.4 us)
Async XLA Ops:
  0.0 19.2 %copy-start = (bf16[256,1920]{1,0:T(8,128)(2,1)S(1)}, bf16[256,1920]{1,0:T(8,128)(2,1)}, u32[]{:S(2)}) copy-start(bf16[256,1920]{1,0:T(8,128)(2,1)} %param.10) | copy-start | bytes 2949124
  0.0 1.2 %copy-start.4 = (f32[4,128,128]{2,1,0:T(8,128)S(1)}, f32[4,128,128]{2,1,0:T(8,128)}, u32[]{:S(2)}) copy-start(f32[4,128,128]{2,1,0:T(8,128)} %param.13) | copy-start | bytes 786436
  1.3 10.3 %copy-start.3 = (f32[3,4,16,128]{3,2,1,0:T(8,128)S(1)}, f32[3,4,16,128]{3,2,1,0:T(8,128)}, u32[]{:S(2)}) copy-start(f32[3,4,16,128]{3,2,1,0:T(8,128)} %param.8) | copy-start | bytes 294916
  1.3 10.3 %copy-start.5 = (bf16[3,4,16,128]{3,2,1,0:T(8,128)(2,1)S(1)}, bf16[3,4,16,128]{3,2,1,0:T(8,128)(2,1)}, u32[]{:S(2)}) copy-start(bf16[3,4,16,128]{3,2,1,0:T(8,128)(2,1)} %param.9) | copy-start | bytes 147460
  1.3 17.8 %copy-start.7 = (s32[1,256]{1,0:T(1,128)S(1)}, s32[1,256]{1,0:T(1,128)}, u32[]{:S(2)}) copy-start(s32[1,256]{1,0:T(1,128)} %param.15) | copy-start | bytes 3076
  1.3 17.8 %copy-start.8 = (s32[1,256]{1,0:T(1,128)S(1)}, s32[1,256]{1,0:T(1,128)}, u32[]{:S(2)}) copy-start(s32[1,256]{1,0:T(1,128)} %constant.117.clone.1) | copy-start | bytes 3076
  1.4 24.6 %collective-permute-start = (f32[3,128,128]{2,1,0:T(8,128)S(1)}, f32[3,128,128]{2,1,0:T(8,128)S(1)}, u32[]{:S(2)}, u32[]{:S(2)}) collective-permute-start(f32[3,128,128]{2,1,0:T(8,128)S(1)} %get-tuple-element.12), channel_id=1, source_target_pairs={{15,11},{3,15},{7,3},{11,7},{0,12},{4,0},{8,4},{12,8},{1,13},{5,1}... | collective-permute-start | bytes 589832 | tf_op jit(solution)/shard_map/ppermute | solution.py:124
  8.3 17.7 %collective-permute-start.1 = (f32[3,128,128]{2,1,0:T(8,128)S(1)}, f32[3,128,128]{2,1,0:T(8,128)S(1)}, u32[]{:S(2)}, u32[]{:S(2)}) collective-permute-start(f32[3,128,128]{2,1,0:T(8,128)S(1)} %get-tuple-element.11), channel_id=1, source_target_pairs={{15,7},{3,11},{7,15},{11,3},{0,8},{4,12},{8,0},{12,4},{1,9},{5,13}... | collective-permute-start | bytes 589832 | tf_op jit(solution)/shard_map/ppermute | solution.py:124
  9.3 16.7 %collective-permute-start.2 = (f32[3,128,128]{2,1,0:T(8,128)S(1)}, f32[3,128,128]{2,1,0:T(8,128)}, u32[]{:S(2)}, u32[]{:S(2)}) collective-permute-start(f32[3,128,128]{2,1,0:T(8,128)S(1)} %get-tuple-element.10), channel_id=1, source_target_pairs={{15,3},{3,7},{7,11},{11,15},{0,4},{4,8},{8,12},{12,0},{1,5},{5,9},... | collective-permute-start | bytes 589832 | tf_op jit(solution)/shard_map/ppermute | solution.py:124
  12.3 13.6 %all-to-all-start = ((bf16[6,4,16,128]{3,0,1,2:T(8,128)(2,1)}), bf16[6,4,16,128]{3,0,1,2:T(8,128)(2,1)S(1)}, u32[]{:S(2)}, u32[]{:S(2)}) async-start(bf16[6,4,16,128]{3,0,1,2:T(8,128)(2,1)} %copy.126), calls=%async_computation | async-start | bytes 262144 | tf_op jit(solution)/shard_map/all_to_all | solution.py:148
  27.0 13.5 %copy-start.1 = (f32[4,3,128,128]{3,2,1,0:T(8,128)}, f32[4,3,128,128]{3,2,1,0:T(8,128)S(1)}, u32[]{:S(2)}) copy-start(f32[4,3,128,128]{3,2,1,0:T(8,128)S(1)} %pad_maximum_fusion.1.refs_0_) | copy-start | bytes 2359300
  28.5 13.5 %all-to-all-start.1 = ((bf16[3,64,1,128]{3,0,2,1:T(4,128)(2,1)}), bf16[3,64,1,128]{3,0,2,1:T(4,128)(2,1)S(1)}, u32[]{:S(2)}, u32[]{:S(2)}) async-start(bf16[3,64,1,128]{3,0,2,1:T(4,128)(2,1)} %copy.138), calls=%async_computation.1 | async-start | bytes 131072 | tf_op jit(solution)/shard_map/all_to_all | solution.py:170
  32.8 28.8 %collective-permute-start.3 = (f32[4,3,128,128]{3,2,1,0:T(8,128)S(1)}, f32[4,3,128,128]{3,2,1,0:T(8,128)}, u32[]{:S(2)}, u32[]{:S(2)}) collective-permute-start(f32[4,3,128,128]{3,2,1,0:T(8,128)S(1)} %pad_maximum_fusion.1.refs_0_), channel_id=1, source_target_pairs={{1,0},{5,4},{9,8},{13,12},{17,16},{21,20},{25,24},{29,28},{33,32},... | collective-permute-start | bytes 2359304 | tf_op jit(solution)/shard_map/ppermute | solution.py:156
  38.9 22.7 %collective-permute-start.4 = (f32[4,3,128,128]{3,2,1,0:T(8,128)S(1)}, f32[4,3,128,128]{3,2,1,0:T(8,128)}, u32[]{:S(2)}, u32[]{:S(2)}) collective-permute-start(f32[4,3,128,128]{3,2,1,0:T(8,128)S(1)} %pad_maximum_fusion.1.refs_0_), channel_id=1, source_target_pairs={{2,0},{6,4},{10,8},{14,12},{18,16},{22,20},{26,24},{30,28},{34,32}... | collective-permute-start | bytes 2359304 | tf_op jit(solution)/shard_map/ppermute | solution.py:156
  40.5 21.1 %collective-permute-start.5 = (f32[4,3,128,128]{3,2,1,0:T(8,128)S(1)}, f32[4,3,128,128]{3,2,1,0:T(8,128)}, u32[]{:S(2)}, u32[]{:S(2)}) collective-permute-start(f32[4,3,128,128]{3,2,1,0:T(8,128)S(1)} %pad_maximum_fusion.1.refs_0_), channel_id=1, source_target_pairs={{15,0},{3,4},{7,8},{11,12},{31,16},{19,20},{23,24},{27,28},{47,32}... | collective-permute-start | bytes 2359304 | tf_op jit(solution)/shard_map/ppermute | solution.py:156
  43.3 17.7 %all-to-all-start.2 = ((f32[16,2,3,128]{3,1,2,0:T(2,128)}), f32[16,2,3,128]{3,1,2,0:T(2,128)S(1)}, u32[]{:S(2)}, u32[]{:S(2)}) async-start(f32[16,2,3,128]{3,1,2,0:T(2,128)} %copy.143), calls=%async_computation.2 | async-start | bytes 98304 | tf_op jit(solution)/shard_map/all_to_all | solution.py:184
  61.6 13.2 %copy-start.6 = (f32[15,128]{1,0:T(8,128)S(1)}, f32[15,128]{1,0:T(8,128)}, u32[]{:S(2)}) copy-start(f32[15,128]{1,0:T(8,128)} %param.14) | copy-start | bytes 23044
  61.6 20.8 %copy-start.2 = (bf16[1920,256]{1,0:T(8,128)(2,1)S(1)}, bf16[1920,256]{1,0:T(8,128)(2,1)}, u32[]{:S(2)}) copy-start(bf16[1920,256]{1,0:T(8,128)(2,1)} %param.11) | copy-start | bytes 2949124
  71.2 11.2 %all-to-all-start.3 = ((f32[16,2,3,128]{3,1,2,0:T(2,128)}), f32[16,2,3,128]{3,1,2,0:T(2,128)S(1)}, u32[]{:S(2)}, u32[]{:S(2)}) async-start(f32[16,2,3,128]{3,1,2,0:T(2,128)} %copy.145), calls=%async_computation.3 | async-start | bytes 98304 | tf_op jit(solution)/shard_map/all_to_all | solution.py:192

commit v11 on v10

--- a/solution.py
+++ b/solution.py
@@ -65,20 +65,19 @@
             spot_slot = (label // group_size - position) % group_size
             return group_refs[group_slot].at[spot_slot]
 
-        zero = jnp.zeros(sides_ref.shape[2:], jnp.float32)
+        zero = jnp.zeros((sides_ref.shape[1], sides_ref.shape[3]), jnp.float32)
+        sides = [sides_ref[k] for k in range(slab_count)]
         forward_values = [zero]
         for k in range(1, slab_count):
-            source = sides_ref[k, 0] + sides_ref[k - 1, 1]
+            source = sides[k][:, 0] + sides[k - 1][:, 1]
             forward_values.append(source - apply(blocks_of(k)[0], forward_values[-1]))
         after = zero
         for k in range(slab_count - 1, 0, -1):
             blocks = blocks_of(k)
             solved = apply(blocks[2], forward_values[k]) - apply(blocks[1], after)
-            out_ref[k, 0] = solved
-            out_ref[k, 1] = after
+            out_ref[k] = jnp.stack([solved, after], axis=1)
             after = solved
-        out_ref[0, 0] = zero
-        out_ref[0, 1] = after
+        out_ref[0] = jnp.stack([zero, after], axis=1)
 
     for position in range(group_size):
         pl.when(position_ref[0] == position)(functools.partial(solve, position))
@@ -178,7 +177,7 @@
     rhs_left = cond_line[:, :, :point_total] + line_zero_rhs
     right_part = cond_line[:, :, point_total:]
 
-    sides = jnp.stack([rhs_left, right_part], axis=1)
+    sides = jnp.stack([rhs_left, right_part], axis=2)
     destination_plane = [owners.index(slab) if slab in owners else 0 for slab in range(slab_count)]
     outgoing = jnp.stack([sides[plane] for plane in destination_plane])
     to_owner = lax.all_to_all(outgoing, "slab", split_axis=0, concat_axis=0, tiled=True)
@@ -191,8 +190,8 @@
     )(position.astype(jnp.int32).reshape(1), *across, to_owner)
     from_owner = lax.all_to_all(both_sides, "slab", split_axis=0, concat_axis=0, tiled=True)
     mine = jnp.stack([from_owner[owner] for owner in owners])
-    left_values = mine[:, 0]
-    right_values = mine[:, 1]
+    left_values = mine[:, :, 0]
+    right_values = mine[:, :, 1]
 
     boundary_line = jnp.concatenate([left_values, right_values], axis=2).astype(jnp.bfloat16)
     extension = jnp.einsum(

time: 84.3 us -> 90.7 us (1.076)
  local copies, waits for them, and re-layouts: 6.31 us -> 10.4 us
  other arithmetic: 1.41 us -> 3.74 us
    unnamed x22 -> x30, local copies, waits for them, and re-layouts: 0.07 us -> 6.43 us
    unnamed x0 -> x4, other arithmetic: none -> 2.36 us
    pallas_call x1 -> x0, local copies, waits for them, and re-layouts: 1.48 us -> none  [on_device(): pl.pallas_call(functools.partial(chain_kernel, group_size=group_size), ou...]
  transfers between devices with their start and end apart: 10 -> 10, of which waited for: 3 -> 3; matrix products, arithmetic and copies ran while one was open for 4% -> 12% of each run, Pallas kernels for 0% -> 0%
where the time goes in v11:
time: 90.7 us; the launch traced here: 90.2 us
  starting transfers between devices  43.9 us (48%)
  waiting for transfers between devices  21.1 us (23%)
  local copies, waits for them, and re-layouts  10.4 us (11%)
  Pallas kernels  8.03 us (9%)
  other arithmetic  3.74 us (4%)
  matrix products  2.67 us (3%)
    all_to_all x1, starting transfers between devices, on_device(): lax.all_to_all(outgoing, 'slab', split_axis=0, concat_axis=0, tiled=True)  10.2 us
    ppermute x3, starting transfers between devices, on_device(): lax.ppermute(blocks[(position - offset) % group_count], 'slab', pairs)  10.2 us
    ppermute x3, starting transfers between devices, on_device(): across.append(lax.ppermute(group_blocks, 'slab', pairs))  9.25 us
    pallas_call x1, Pallas kernels, on_device(): pl.pallas_call(functools.partial(chain_kernel, group_size=group_size), ou...  8.03 us
    all_to_all x1, waiting for transfers between devices, on_device(): lax.all_to_all(both_sides, 'slab', split_axis=0, concat_axis=0, tiled=True)  7.43 us
    all_to_all x1, waiting for transfers between devices, on_device(): lax.all_to_all(outgoing, 'slab', split_axis=0, concat_axis=0, tiled=True)  7.4 us
    all_to_all x1, starting transfers between devices, on_device(): lax.all_to_all(both_fields, 'mode', split_axis=2, concat_axis=1, tiled=True)  6.75 us
    unnamed x30, local copies, waits for them, and re-layouts  6.43 us
  transfers between devices with their start and end apart: 10, of which 3 were waited for; matrix products, arithmetic and copies ran while one was open for 12% of the time, Pallas kernels for 0%

profile of v11, /device:TPU:1, one launch (start us, length us, event | category | flops | bytes accessed | tf_op | source)
XLA Modules:
  0.0 90.2 jit_solution(367807562045717452)
XLA Ops:
  0.0 1.2 %slice_bitcast_fusion.1 = (f32[4,1,128,128]{3,2,1,0:T(8,128)S(1)}, f32[4,1,128,128]{3,2,1,0:T(8,128)S(1)}) fusion(f32[2,4,128,128]{3,2,1,0:T(8,128)} %param.12), kind=kLoop, calls=%fused_computation.13 | loop fusion | bytes 1048576 | tf_op jit(solution)/shard_map/stack;squeeze | solution.py:110
  1.4 6.9 %collective-permute-start = (f32[3,128,128]{2,1,0:T(8,128)S(1)}, f32[3,128,128]{2,1,0:T(8,128)S(1)}, u32[]{:S(2)}, u32[]{:S(2)}) collective-permute-start(f32[3,128,128]{2,1,0:T(8,128)S(1)} %get-tuple-element.14), channel_id=1, source_target_pairs={{15,11},{3,15},{7,3},{11,7},{0,12},{4,0},{8,4},{12,8},{1,13},{5,1}... | collective-permute-start | bytes 589832 | tf_op jit(solution)/shard_map/ppermute | solution.py:123
  8.3 1.0 %collective-permute-start.1 = (f32[3,128,128]{2,1,0:T(8,128)S(1)}, f32[3,128,128]{2,1,0:T(8,128)S(1)}, u32[]{:S(2)}, u32[]{:S(2)}) collective-permute-start(f32[3,128,128]{2,1,0:T(8,128)S(1)} %get-tuple-element.13), channel_id=1, source_target_pairs={{15,7},{3,11},{7,15},{11,3},{0,8},{4,12},{8,0},{12,4},{1,9},{5,13}... | collective-permute-start | bytes 589832 | tf_op jit(solution)/shard_map/ppermute | solution.py:123
  9.3 2.3 %collective-permute-start.2 = (f32[3,128,128]{2,1,0:T(8,128)S(1)}, f32[3,128,128]{2,1,0:T(8,128)}, u32[]{:S(2)}, u32[]{:S(2)}) collective-permute-start(f32[3,128,128]{2,1,0:T(8,128)S(1)} %get-tuple-element.12), channel_id=1, source_target_pairs={{15,3},{3,7},{7,11},{11,15},{0,4},{4,8},{8,12},{12,0},{1,5},{5,9},... | collective-permute-start | bytes 589832 | tf_op jit(solution)/shard_map/ppermute | solution.py:123
  11.6 0.7 copy.158
  12.3 6.8 %all-to-all-start = ((bf16[6,4,16,128]{3,0,1,2:T(8,128)(2,1)}), bf16[6,4,16,128]{3,0,1,2:T(8,128)(2,1)S(1)}, u32[]{:S(2)}, u32[]{:S(2)}) async-start(bf16[6,4,16,128]{3,0,1,2:T(8,128)(2,1)} %copy.158), calls=%async_computation | async-start | bytes 262144 | tf_op jit(solution)/shard_map/all_to_all | solution.py:147
  19.7 6.3 %all-to-all-done = bf16[6,4,16,128]{3,0,1,2:T(8,128)(2,1)S(1)} async-done(((bf16[6,4,16,128]{3,0,1,2:T(8,128)(2,1)}), bf16[6,4,16,128]{3,0,1,2:T(8,128)(2,1)S(1)}, u32[]{:S(2)}, u32[]{:S(2)}) %all-to-all-start) | async-done | bytes 98336 | tf_op jit(solution)/shard_map/all_to_all | solution.py:147
  26.0 1.0 %pad_maximum_fusion.1.refs_0_ = f32[4,3,128,128]{3,2,1,0:T(8,128)S(1)} fusion(f32[1,3,128,128]{3,2,1,0:T(8,128)} %bitcast.9, f32[1,3,128,128]{3,2,1,0:T(8,128)S(1)} %bitcast.136, f32[1,3,128,128]{3,2,1,0:T(8,128)S(1)} %bitcast.135, f32[1,3,128,128]{3,2,1,0:T(8,128)S(1)} %get-tuple-element.11), kind=kLoop, calls=%fused_computation.10 | loop fusion | flops 589824 | bytes 1572864 | tf_op jit(solution)/shard_map/stack | solution.py:124
  27.8 0.7 copy.170
  28.5 3.8 %all-to-all-start.1 = ((bf16[3,64,1,128]{3,0,2,1:T(4,128)(2,1)}), bf16[3,64,1,128]{3,0,2,1:T(4,128)(2,1)S(1)}, u32[]{:S(2)}, u32[]{:S(2)}) async-start(bf16[3,64,1,128]{3,0,2,1:T(4,128)(2,1)} %copy.170), calls=%async_computation.1 | async-start | bytes 131072 | tf_op jit(solution)/shard_map/all_to_all | solution.py:169
  32.8 6.2 %collective-permute-start.3 = (f32[4,3,128,128]{3,2,1,0:T(8,128)S(1)}, f32[4,3,128,128]{3,2,1,0:T(8,128)}, u32[]{:S(2)}, u32[]{:S(2)}) collective-permute-start(f32[4,3,128,128]{3,2,1,0:T(8,128)S(1)} %pad_maximum_fusion.1.refs_0_), channel_id=1, source_target_pairs={{1,0},{5,4},{9,8},{13,12},{17,16},{21,20},{25,24},{29,28},{33,32},... | collective-permute-start | bytes 2359304 | tf_op jit(solution)/shard_map/ppermute | solution.py:155
  38.9 1.6 %collective-permute-start.4 = (f32[4,3,128,128]{3,2,1,0:T(8,128)S(1)}, f32[4,3,128,128]{3,2,1,0:T(8,128)}, u32[]{:S(2)}, u32[]{:S(2)}) collective-permute-start(f32[4,3,128,128]{3,2,1,0:T(8,128)S(1)} %pad_maximum_fusion.1.refs_0_), channel_id=1, source_target_pairs={{2,0},{6,4},{10,8},{14,12},{18,16},{22,20},{26,24},{30,28},{34,32}... | collective-permute-start | bytes 2359304 | tf_op jit(solution)/shard_map/ppermute | solution.py:155
  40.5 1.5 %collective-permute-start.5 = (f32[4,3,128,128]{3,2,1,0:T(8,128)S(1)}, f32[4,3,128,128]{3,2,1,0:T(8,128)}, u32[]{:S(2)}, u32[]{:S(2)}) collective-permute-start(f32[4,3,128,128]{3,2,1,0:T(8,128)S(1)} %pad_maximum_fusion.1.refs_0_), channel_id=1, source_target_pairs={{15,0},{3,4},{7,8},{11,12},{31,16},{19,20},{23,24},{27,28},{47,32}... | collective-permute-start | bytes 2359304 | tf_op jit(solution)/shard_map/ppermute | solution.py:155
  42.5 0.6 constant_dynamic-update-slice_fusion.14
  44.3 0.6 constant_dynamic-update-slice_fusion.11
  46.6 0.6 constant_dynamic-update-slice_fusion.7
  51.3 10.2 %all-to-all-start.2 = ((f32[16,3,2,128]{3,2,1,0:T(2,128)}), f32[16,3,2,128]{3,2,1,0:T(2,128)S(1)}, u32[]{:S(2)}, u32[]{:S(2)}) async-start(f32[16,3,2,128]{3,2,1,0:T(2,128)} %constant_dynamic-update-slice_fusion), calls=%async_computation.2 | async-start | bytes 98304 | tf_op jit(solution)/shard_map/all_to_all | solution.py:183
  61.6 7.4 %all-to-all-done.2.refs_4_ = f32[16,3,2,128]{3,2,1,0:T(2,128)S(1)} async-done(((f32[16,3,2,128]{3,2,1,0:T(2,128)}), f32[16,3,2,128]{3,2,1,0:T(2,128)S(1)}, u32[]{:S(2)}, u32[]{:S(2)}) %all-to-all-start.2) | async-done | bytes 49184 | tf_op jit(solution)/shard_map/all_to_all | solution.py:183
  69.0 0.6 copy-done.5
  69.6 8.0 %shard_map.82 = f32[16,3,2,128]{3,2,1,0:T(2,128)} custom-call(s32[1]{0:T(128)} %bitcast.position_ref, f32[4,3,128,128]{3,2,1,0:T(8,128)} %copy-done.1, f32[4,3,128,128]{3,2,1,0:T(8,128)} %collective-permute-done.3.refs_1_, f32[4,3,128,128]{3,2,1,0:T(8,128)} %collective-permute-done.4.refs_2_, f32[4,3,128,128]{3,2,1,0:T(8,128)} %collective-permute-done.5.refs_3_, ...), custom_call_target="tpu_custom_call" | custom-call | tf_op jit(solution)/shard_map/pallas_call | solution.py:184
  77.6 3.6 %all-to-all-start.3 = ((f32[16,3,2,128]{3,2,1,0:T(2,128)}), f32[16,3,2,128]{3,2,1,0:T(2,128)S(1)}, u32[]{:S(2)}, u32[]{:S(2)}) async-start(f32[16,3,2,128]{3,2,1,0:T(2,128)} %shard_map.82), calls=%async_computation.3 | async-start | bytes 98304 | tf_op jit(solution)/shard_map/all_to_all | solution.py:191
  81.3 7.4 %all-to-all-done.3 = f32[16,3,2,128]{3,2,1,0:T(2,128)S(1)} async-done(((f32[16,3,2,128]{3,2,1,0:T(2,128)}), f32[16,3,2,128]{3,2,1,0:T(2,128)S(1)}, u32[]{:S(2)}, u32[]{:S(2)}) %all-to-all-start.3) | async-done | bytes 49184 | tf_op jit(solution)/shard_map/all_to_all | solution.py:191
  88.8 0.6 convolution_bitcast_fusion
  89.6 0.6 copy.180
  (70 shorter events, 9.7 us)
Async XLA Ops:
  0.0 19.2 %copy-start = (bf16[256,1920]{1,0:T(8,128)(2,1)S(1)}, bf16[256,1920]{1,0:T(8,128)(2,1)}, u32[]{:S(2)}) copy-start(bf16[256,1920]{1,0:T(8,128)(2,1)} %param.10) | copy-start | bytes 2949124
  0.0 1.2 %copy-start.4 = (f32[4,128,128]{2,1,0:T(8,128)S(1)}, f32[4,128,128]{2,1,0:T(8,128)}, u32[]{:S(2)}) copy-start(f32[4,128,128]{2,1,0:T(8,128)} %param.13) | copy-start | bytes 786436
  1.3 10.3 %copy-start.3 = (f32[3,4,16,128]{3,2,1,0:T(8,128)S(1)}, f32[3,4,16,128]{3,2,1,0:T(8,128)}, u32[]{:S(2)}) copy-start(f32[3,4,16,128]{3,2,1,0:T(8,128)} %param.8) | copy-start | bytes 294916
  1.3 10.3 %copy-start.6 = (bf16[3,4,16,128]{3,2,1,0:T(8,128)(2,1)S(1)}, bf16[3,4,16,128]{3,2,1,0:T(8,128)(2,1)}, u32[]{:S(2)}) copy-start(bf16[3,4,16,128]{3,2,1,0:T(8,128)(2,1)} %param.9) | copy-start | bytes 147460
  1.3 17.8 %copy-start.8 = (s32[1,256]{1,0:T(1,128)S(1)}, s32[1,256]{1,0:T(1,128)}, u32[]{:S(2)}) copy-start(s32[1,256]{1,0:T(1,128)} %param.15) | copy-start | bytes 3076
  1.3 17.8 %copy-start.9 = (s32[1,256]{1,0:T(1,128)S(1)}, s32[1,256]{1,0:T(1,128)}, u32[]{:S(2)}) copy-start(s32[1,256]{1,0:T(1,128)} %constant.117.clone.1) | copy-start | bytes 3076
  1.4 24.6 %collective-permute-start = (f32[3,128,128]{2,1,0:T(8,128)S(1)}, f32[3,128,128]{2,1,0:T(8,128)S(1)}, u32[]{:S(2)}, u32[]{:S(2)}) collective-permute-start(f32[3,128,128]{2,1,0:T(8,128)S(1)} %get-tuple-element.14), channel_id=1, source_target_pairs={{15,11},{3,15},{7,3},{11,7},{0,12},{4,0},{8,4},{12,8},{1,13},{5,1}... | collective-permute-start | bytes 589832 | tf_op jit(solution)/shard_map/ppermute | solution.py:123
  8.3 17.7 %collective-permute-start.1 = (f32[3,128,128]{2,1,0:T(8,128)S(1)}, f32[3,128,128]{2,1,0:T(8,128)S(1)}, u32[]{:S(2)}, u32[]{:S(2)}) collective-permute-start(f32[3,128,128]{2,1,0:T(8,128)S(1)} %get-tuple-element.13), channel_id=1, source_target_pairs={{15,7},{3,11},{7,15},{11,3},{0,8},{4,12},{8,0},{12,4},{1,9},{5,13}... | collective-permute-start | bytes 589832 | tf_op jit(solution)/shard_map/ppermute | solution.py:123
  9.3 16.7 %collective-permute-start.2 = (f32[3,128,128]{2,1,0:T(8,128)S(1)}, f32[3,128,128]{2,1,0:T(8,128)}, u32[]{:S(2)}, u32[]{:S(2)}) collective-permute-start(f32[3,128,128]{2,1,0:T(8,128)S(1)} %get-tuple-element.12), channel_id=1, source_target_pairs={{15,3},{3,7},{7,11},{11,15},{0,4},{4,8},{8,12},{12,0},{1,5},{5,9},... | collective-permute-start | bytes 589832 | tf_op jit(solution)/shard_map/ppermute | solution.py:123
  12.3 13.6 %all-to-all-start = ((bf16[6,4,16,128]{3,0,1,2:T(8,128)(2,1)}), bf16[6,4,16,128]{3,0,1,2:T(8,128)(2,1)S(1)}, u32[]{:S(2)}, u32[]{:S(2)}) async-start(bf16[6,4,16,128]{3,0,1,2:T(8,128)(2,1)} %copy.158), calls=%async_computation | async-start | bytes 262144 | tf_op jit(solution)/shard_map/all_to_all | solution.py:147
  27.0 13.5 %copy-start.1 = (f32[4,3,128,128]{3,2,1,0:T(8,128)}, f32[4,3,128,128]{3,2,1,0:T(8,128)S(1)}, u32[]{:S(2)}) copy-start(f32[4,3,128,128]{3,2,1,0:T(8,128)S(1)} %pad_maximum_fusion.1.refs_0_) | copy-start | bytes 2359300
  28.5 13.5 %all-to-all-start.1 = ((bf16[3,64,1,128]{3,0,2,1:T(4,128)(2,1)}), bf16[3,64,1,128]{3,0,2,1:T(4,128)(2,1)S(1)}, u32[]{:S(2)}, u32[]{:S(2)}) async-start(bf16[3,64,1,128]{3,0,2,1:T(4,128)(2,1)} %copy.170), calls=%async_computation.1 | async-start | bytes 131072 | tf_op jit(solution)/shard_map/all_to_all | solution.py:169
  32.8 36.2 %collective-permute-start.3 = (f32[4,3,128,128]{3,2,1,0:T(8,128)S(1)}, f32[4,3,128,128]{3,2,1,0:T(8,128)}, u32[]{:S(2)}, u32[]{:S(2)}) collective-permute-start(f32[4,3,128,128]{3,2,1,0:T(8,128)S(1)} %pad_maximum_fusion.1.refs_0_), channel_id=1, source_target_pairs={{1,0},{5,4},{9,8},{13,12},{17,16},{21,20},{25,24},{29,28},{33,32},... | collective-permute-start | bytes 2359304 | tf_op jit(solution)/shard_map/ppermute | solution.py:155
  38.9 30.0 %collective-permute-start.4 = (f32[4,3,128,128]{3,2,1,0:T(8,128)S(1)}, f32[4,3,128,128]{3,2,1,0:T(8,128)}, u32[]{:S(2)}, u32[]{:S(2)}) collective-permute-start(f32[4,3,128,128]{3,2,1,0:T(8,128)S(1)} %pad_maximum_fusion.1.refs_0_), channel_id=1, source_target_pairs={{2,0},{6,4},{10,8},{14,12},{18,16},{22,20},{26,24},{30,28},{34,32}... | collective-permute-start | bytes 2359304 | tf_op jit(solution)/shard_map/ppermute | solution.py:155
  40.5 28.5 %collective-permute-start.5 = (f32[4,3,128,128]{3,2,1,0:T(8,128)S(1)}, f32[4,3,128,128]{3,2,1,0:T(8,128)}, u32[]{:S(2)}, u32[]{:S(2)}) collective-permute-start(f32[4,3,128,128]{3,2,1,0:T(8,128)S(1)} %pad_maximum_fusion.1.refs_0_), channel_id=1, source_target_pairs={{15,0},{3,4},{7,8},{11,12},{31,16},{19,20},{23,24},{27,28},{47,32}... | collective-permute-start | bytes 2359304 | tf_op jit(solution)/shard_map/ppermute | solution.py:155
  51.3 17.7 %all-to-all-start.2 = ((f32[16,3,2,128]{3,2,1,0:T(2,128)}), f32[16,3,2,128]{3,2,1,0:T(2,128)S(1)}, u32[]{:S(2)}, u32[]{:S(2)}) async-start(f32[16,3,2,128]{3,2,1,0:T(2,128)} %constant_dynamic-update-slice_fusion), calls=%async_computation.2 | async-start | bytes 98304 | tf_op jit(solution)/shard_map/all_to_all | solution.py:183
  69.0 0.6 copy-start.5
  69.6 11.7 %copy-start.7 = (f32[15,128]{1,0:T(8,128)S(1)}, f32[15,128]{1,0:T(8,128)}, u32[]{:S(2)}) copy-start(f32[15,128]{1,0:T(8,128)} %param.14) | copy-start | bytes 23044
  69.6 19.3 %copy-start.2 = (bf16[1920,256]{1,0:T(8,128)(2,1)S(1)}, bf16[1920,256]{1,0:T(8,128)(2,1)}, u32[]{:S(2)}) copy-start(bf16[1920,256]{1,0:T(8,128)(2,1)} %param.11) | copy-start | bytes 2949124
  77.6 11.2 %all-to-all-start.3 = ((f32[16,3,2,128]{3,2,1,0:T(2,128)}), f32[16,3,2,128]{3,2,1,0:T(2,128)S(1)}, u32[]{:S(2)}, u32[]{:S(2)}) async-start(f32[16,3,2,128]{3,2,1,0:T(2,128)} %shard_map.82), calls=%async_computation.3 | async-start | bytes 98304 | tf_op jit(solution)/shard_map/all_to_all | solution.py:191

commit v12 on v11

--- a/solution.py
+++ b/solution.py
@@ -178,8 +178,8 @@
     right_part = cond_line[:, :, point_total:]
 
     sides = jnp.stack([rhs_left, right_part], axis=2)
-    destination_plane = [owners.index(slab) if slab in owners else 0 for slab in range(slab_count)]
-    outgoing = jnp.stack([sides[plane] for plane in destination_plane])
+    assert all(owner // group_size == plane for plane, owner in enumerate(owners))
+    outgoing = jnp.repeat(sides, group_size, axis=0)
     to_owner = lax.all_to_all(outgoing, "slab", split_axis=0, concat_axis=0, tiled=True)
     both_sides = pl.pallas_call(
         functools.partial(chain_kernel, group_size=group_size),

time: 90.7 us -> 88.8 us (0.979)
  waiting for transfers between devices: 21.1 us -> 27.2 us
  local copies, waits for them, and re-layouts: 10.4 us -> 4.67 us
  other arithmetic: 3.74 us -> 1.39 us
    all_to_all x1, waiting for transfers between devices: 0.01 us -> 6.08 us  [on_device(): lax.all_to_all(nonlin_lines, 'mode', split_axis=1, concat_axis=2, tiled=T...]
    unnamed x30 -> x20, local copies, waits for them, and re-layouts: 6.43 us -> 0.65 us
    unnamed x4 -> x0, other arithmetic: 2.36 us -> none
  transfers between devices with their start and end apart: 10 -> 10, of which waited for: 3 -> 4; matrix products, arithmetic and copies ran while one was open for 12% -> 4% of each run, Pallas kernels for 0% -> 0%
where the time goes in v12:
time: 88.8 us; the launch traced here: 88.3 us
  starting transfers between devices  44 us (50%)
  waiting for transfers between devices  27.2 us (31%)
  Pallas kernels  8.03 us (9%)
  local copies, waits for them, and re-layouts  4.67 us (5%)
  matrix products  2.66 us (3%)
  other arithmetic  1.39 us (2%)
    all_to_all x1, starting transfers between devices, on_device(): lax.all_to_all(outgoing, 'slab', split_axis=0, concat_axis=0, tiled=True)  10.6 us
    ppermute x3, starting transfers between devices, on_device(): lax.ppermute(blocks[(position - offset) % group_count], 'slab', pairs)  10.2 us
    ppermute x3, starting transfers between devices, on_device(): across.append(lax.ppermute(group_blocks, 'slab', pairs))  8.89 us
    pallas_call x1, Pallas kernels, on_device(): pl.pallas_call(functools.partial(chain_kernel, group_size=group_size), ou...  8.03 us
    all_to_all x1, waiting for transfers between devices, on_device(): lax.all_to_all(both_sides, 'slab', split_axis=0, concat_axis=0, tiled=True)  7.43 us
    all_to_all x1, waiting for transfers between devices, on_device(): lax.all_to_all(outgoing, 'slab', split_axis=0, concat_axis=0, tiled=True)  7.4 us
    all_to_all x1, starting transfers between devices, on_device(): lax.all_to_all(both_fields, 'mode', split_axis=2, concat_axis=1, tiled=True)  6.75 us
    all_to_all x1, waiting for transfers between devices, on_device(): lax.all_to_all(both_fields, 'mode', split_axis=2, concat_axis=1, tiled=True)  6.25 us
  transfers between devices with their start and end apart: 10, of which 4 were waited for; matrix products, arithmetic and copies ran while one was open for 4% of the time, Pallas kernels for 0%

profile of v12, /device:TPU:1, one launch (start us, length us, event | category | flops | bytes accessed | tf_op | source)
XLA Modules:
  0.0 88.3 jit_solution(14953314613911808495)
XLA Ops:
  0.0 1.2 %slice_bitcast_fusion.1 = (f32[4,1,128,128]{3,2,1,0:T(8,128)S(1)}, f32[4,1,128,128]{3,2,1,0:T(8,128)S(1)}) fusion(f32[2,4,128,128]{3,2,1,0:T(8,128)} %param.12), kind=kLoop, calls=%fused_computation.13 | loop fusion | bytes 1048576 | tf_op jit(solution)/shard_map/stack;squeeze | solution.py:110
  1.4 6.9 %collective-permute-start = (f32[3,128,128]{2,1,0:T(8,128)S(1)}, f32[3,128,128]{2,1,0:T(8,128)S(1)}, u32[]{:S(2)}, u32[]{:S(2)}) collective-permute-start(f32[3,128,128]{2,1,0:T(8,128)S(1)} %get-tuple-element.12), channel_id=1, source_target_pairs={{15,11},{3,15},{7,3},{11,7},{0,12},{4,0},{8,4},{12,8},{1,13},{5,1}... | collective-permute-start | bytes 589832 | tf_op jit(solution)/shard_map/ppermute | solution.py:123
  8.3 1.0 %collective-permute-start.1 = (f32[3,128,128]{2,1,0:T(8,128)S(1)}, f32[3,128,128]{2,1,0:T(8,128)S(1)}, u32[]{:S(2)}, u32[]{:S(2)}) collective-permute-start(f32[3,128,128]{2,1,0:T(8,128)S(1)} %get-tuple-element.11), channel_id=1, source_target_pairs={{15,7},{3,11},{7,15},{11,3},{0,8},{4,12},{8,0},{12,4},{1,9},{5,13}... | collective-permute-start | bytes 589832 | tf_op jit(solution)/shard_map/ppermute | solution.py:123
  9.3 2.3 %collective-permute-start.2 = (f32[3,128,128]{2,1,0:T(8,128)S(1)}, f32[3,128,128]{2,1,0:T(8,128)}, u32[]{:S(2)}, u32[]{:S(2)}) collective-permute-start(f32[3,128,128]{2,1,0:T(8,128)S(1)} %get-tuple-element.10), channel_id=1, source_target_pairs={{15,3},{3,7},{7,11},{11,15},{0,4},{4,8},{8,12},{12,0},{1,5},{5,9},... | collective-permute-start | bytes 589832 | tf_op jit(solution)/shard_map/ppermute | solution.py:123
  11.6 0.7 copy.111
  12.3 6.8 %all-to-all-start = ((bf16[6,4,16,128]{3,0,1,2:T(8,128)(2,1)}), bf16[6,4,16,128]{3,0,1,2:T(8,128)(2,1)S(1)}, u32[]{:S(2)}, u32[]{:S(2)}) async-start(bf16[6,4,16,128]{3,0,1,2:T(8,128)(2,1)} %copy.111), calls=%async_computation | async-start | bytes 262144 | tf_op jit(solution)/shard_map/all_to_all | solution.py:147
  19.2 0.5 fusion
  19.7 6.3 %all-to-all-done = bf16[6,4,16,128]{3,0,1,2:T(8,128)(2,1)S(1)} async-done(((bf16[6,4,16,128]{3,0,1,2:T(8,128)(2,1)}), bf16[6,4,16,128]{3,0,1,2:T(8,128)(2,1)S(1)}, u32[]{:S(2)}, u32[]{:S(2)}) %all-to-all-start) | async-done | bytes 98336 | tf_op jit(solution)/shard_map/all_to_all | solution.py:147
  26.0 1.0 %pad_maximum_fusion.1.refs_0_ = f32[4,3,128,128]{3,2,1,0:T(8,128)S(1)} fusion(f32[1,3,128,128]{3,2,1,0:T(8,128)} %bitcast.9, f32[1,3,128,128]{3,2,1,0:T(8,128)S(1)} %bitcast.137, f32[1,3,128,128]{3,2,1,0:T(8,128)S(1)} %bitcast.136, f32[1,3,128,128]{3,2,1,0:T(8,128)S(1)} %get-tuple-element.9), kind=kLoop, calls=%fused_computation.10 | loop fusion | flops 589824 | bytes 1572864 | tf_op jit(solution)/shard_map/stack | solution.py:124
  27.5 5.8 %collective-permute-start.3 = (f32[4,3,128,128]{3,2,1,0:T(8,128)S(1)}, f32[4,3,128,128]{3,2,1,0:T(8,128)}, u32[]{:S(2)}, u32[]{:S(2)}) collective-permute-start(f32[4,3,128,128]{3,2,1,0:T(8,128)S(1)} %pad_maximum_fusion.1.refs_0_), channel_id=1, source_target_pairs={{1,0},{5,4},{9,8},{13,12},{17,16},{21,20},{25,24},{29,28},{33,32},... | collective-permute-start | bytes 2359304 | tf_op jit(solution)/shard_map/ppermute | solution.py:155
  33.3 1.6 %collective-permute-start.4 = (f32[4,3,128,128]{3,2,1,0:T(8,128)S(1)}, f32[4,3,128,128]{3,2,1,0:T(8,128)}, u32[]{:S(2)}, u32[]{:S(2)}) collective-permute-start(f32[4,3,128,128]{3,2,1,0:T(8,128)S(1)} %pad_maximum_fusion.1.refs_0_), channel_id=1, source_target_pairs={{2,0},{6,4},{10,8},{14,12},{18,16},{22,20},{26,24},{30,28},{34,32}... | collective-permute-start | bytes 2359304 | tf_op jit(solution)/shard_map/ppermute | solution.py:155
  34.9 1.5 %collective-permute-start.5 = (f32[4,3,128,128]{3,2,1,0:T(8,128)S(1)}, f32[4,3,128,128]{3,2,1,0:T(8,128)}, u32[]{:S(2)}, u32[]{:S(2)}) collective-permute-start(f32[4,3,128,128]{3,2,1,0:T(8,128)S(1)} %pad_maximum_fusion.1.refs_0_), channel_id=1, source_target_pairs={{15,0},{3,4},{7,8},{11,12},{31,16},{19,20},{23,24},{27,28},{47,32}... | collective-permute-start | bytes 2359304 | tf_op jit(solution)/shard_map/ppermute | solution.py:155
  36.7 0.7 copy.123
  37.4 3.9 %all-to-all-start.1 = ((bf16[3,64,1,128]{3,0,2,1:T(4,128)(2,1)}), bf16[3,64,1,128]{3,0,2,1:T(4,128)(2,1)S(1)}, u32[]{:S(2)}, u32[]{:S(2)}) async-start(bf16[3,64,1,128]{3,0,2,1:T(4,128)(2,1)} %copy.123), calls=%async_computation.1 | async-start | bytes 131072 | tf_op jit(solution)/shard_map/all_to_all | solution.py:169
  41.8 6.1 %all-to-all-done.1 = bf16[3,64,1,128]{3,0,2,1:T(4,128)(2,1)S(1)} async-done(((bf16[3,64,1,128]{3,0,2,1:T(4,128)(2,1)}), bf16[3,64,1,128]{3,0,2,1:T(4,128)(2,1)S(1)}, u32[]{:S(2)}, u32[]{:S(2)}) %all-to-all-start.1) | async-done | bytes 49184 | tf_op jit(solution)/shard_map/all_to_all | solution.py:169
  48.3 0.6 broadcast_in_dim.42
  49.0 10.6 %all-to-all-start.2 = ((f32[16,3,2,128]{3,2,1,0:T(2,128)}), f32[16,3,2,128]{3,2,1,0:T(2,128)S(1)}, u32[]{:S(2)}, u32[]{:S(2)}) async-start(f32[16,3,2,128]{3,2,1,0:T(2,128)} %bitcast.43), calls=%async_computation.2 | async-start | bytes 98304 | tf_op jit(solution)/shard_map/all_to_all | solution.py:183
  59.7 7.4 %all-to-all-done.2.refs_4_ = f32[16,3,2,128]{3,2,1,0:T(2,128)S(1)} async-done(((f32[16,3,2,128]{3,2,1,0:T(2,128)}), f32[16,3,2,128]{3,2,1,0:T(2,128)S(1)}, u32[]{:S(2)}, u32[]{:S(2)}) %all-to-all-start.2) | async-done | bytes 49184 | tf_op jit(solution)/shard_map/all_to_all | solution.py:183
  67.1 0.6 copy-done.5
  67.7 8.0 %shard_map.82 = f32[16,3,2,128]{3,2,1,0:T(2,128)} custom-call(s32[1]{0:T(128)} %bitcast.position_ref, f32[4,3,128,128]{3,2,1,0:T(8,128)} %copy-done.1, f32[4,3,128,128]{3,2,1,0:T(8,128)} %collective-permute-done.3.refs_1_, f32[4,3,128,128]{3,2,1,0:T(8,128)} %collective-permute-done.4.refs_2_, f32[4,3,128,128]{3,2,1,0:T(8,128)} %collective-permute-done.5.refs_3_, ...), custom_call_target="tpu_custom_call" | custom-call | tf_op jit(solution)/shard_map/pallas_call | solution.py:184
  75.7 3.6 %all-to-all-start.3 = ((f32[16,3,2,128]{3,2,1,0:T(2,128)}), f32[16,3,2,128]{3,2,1,0:T(2,128)S(1)}, u32[]{:S(2)}, u32[]{:S(2)}) async-start(f32[16,3,2,128]{3,2,1,0:T(2,128)} %shard_map.82), calls=%async_computation.3 | async-start | bytes 98304 | tf_op jit(solution)/shard_map/all_to_all | solution.py:191
  79.5 7.4 %all-to-all-done.3 = f32[16,3,2,128]{3,2,1,0:T(2,128)S(1)} async-done(((f32[16,3,2,128]{3,2,1,0:T(2,128)}), f32[16,3,2,128]{3,2,1,0:T(2,128)S(1)}, u32[]{:S(2)}, u32[]{:S(2)}) %all-to-all-start.3) | async-done | bytes 49184 | tf_op jit(solution)/shard_map/all_to_all | solution.py:191
  87.0 0.6 convolution_bitcast_fusion
  87.7 0.6 copy.132
  (56 shorter events, 2.2 us)
Async XLA Ops:
  0.0 19.2 %copy-start = (bf16[256,1920]{1,0:T(8,128)(2,1)S(1)}, bf16[256,1920]{1,0:T(8,128)(2,1)}, u32[]{:S(2)}) copy-start(bf16[256,1920]{1,0:T(8,128)(2,1)} %param.10) | copy-start | bytes 2949124
  0.0 1.2 %copy-start.4 = (f32[4,128,128]{2,1,0:T(8,128)S(1)}, f32[4,128,128]{2,1,0:T(8,128)}, u32[]{:S(2)}) copy-start(f32[4,128,128]{2,1,0:T(8,128)} %param.13) | copy-start | bytes 786436
  1.3 10.3 %copy-start.3 = (f32[3,4,16,128]{3,2,1,0:T(8,128)S(1)}, f32[3,4,16,128]{3,2,1,0:T(8,128)}, u32[]{:S(2)}) copy-start(f32[3,4,16,128]{3,2,1,0:T(8,128)} %param.8) | copy-start | bytes 294916
  1.3 10.3 %copy-start.6 = (bf16[3,4,16,128]{3,2,1,0:T(8,128)(2,1)S(1)}, bf16[3,4,16,128]{3,2,1,0:T(8,128)(2,1)}, u32[]{:S(2)}) copy-start(bf16[3,4,16,128]{3,2,1,0:T(8,128)(2,1)} %param.9) | copy-start | bytes 147460
  1.3 17.8 %copy-start.8 = (s32[1,256]{1,0:T(1,128)S(1)}, s32[1,256]{1,0:T(1,128)}, u32[]{:S(2)}) copy-start(s32[1,256]{1,0:T(1,128)} %param.15) | copy-start | bytes 3076
  1.3 17.8 %copy-start.9 = (s32[1,256]{1,0:T(1,128)S(1)}, s32[1,256]{1,0:T(1,128)}, u32[]{:S(2)}) copy-start(s32[1,256]{1,0:T(1,128)} %constant.117.clone.1) | copy-start | bytes 3076
  1.4 24.6 %collective-permute-start = (f32[3,128,128]{2,1,0:T(8,128)S(1)}, f32[3,128,128]{2,1,0:T(8,128)S(1)}, u32[]{:S(2)}, u32[]{:S(2)}) collective-permute-start(f32[3,128,128]{2,1,0:T(8,128)S(1)} %get-tuple-element.12), channel_id=1, source_target_pairs={{15,11},{3,15},{7,3},{11,7},{0,12},{4,0},{8,4},{12,8},{1,13},{5,1}... | collective-permute-start | bytes 589832 | tf_op jit(solution)/shard_map/ppermute | solution.py:123
  8.3 17.7 %collective-permute-start.1 = (f32[3,128,128]{2,1,0:T(8,128)S(1)}, f32[3,128,128]{2,1,0:T(8,128)S(1)}, u32[]{:S(2)}, u32[]{:S(2)}) collective-permute-start(f32[3,128,128]{2,1,0:T(8,128)S(1)} %get-tuple-element.11), channel_id=1, source_target_pairs={{15,7},{3,11},{7,15},{11,3},{0,8},{4,12},{8,0},{12,4},{1,9},{5,13}... | collective-permute-start | bytes 589832 | tf_op jit(solution)/shard_map/ppermute | solution.py:123
  9.3 16.7 %collective-permute-start.2 = (f32[3,128,128]{2,1,0:T(8,128)S(1)}, f32[3,128,128]{2,1,0:T(8,128)}, u32[]{:S(2)}, u32[]{:S(2)}) collective-permute-start(f32[3,128,128]{2,1,0:T(8,128)S(1)} %get-tuple-element.10), channel_id=1, source_target_pairs={{15,3},{3,7},{7,11},{11,15},{0,4},{4,8},{8,12},{12,0},{1,5},{5,9},... | collective-permute-start | bytes 589832 | tf_op jit(solution)/shard_map/ppermute | solution.py:123
  12.3 13.6 %all-to-all-start = ((bf16[6,4,16,128]{3,0,1,2:T(8,128)(2,1)}), bf16[6,4,16,128]{3,0,1,2:T(8,128)(2,1)S(1)}, u32[]{:S(2)}, u32[]{:S(2)}) async-start(bf16[6,4,16,128]{3,0,1,2:T(8,128)(2,1)} %copy.111), calls=%async_computation | async-start | bytes 262144 | tf_op jit(solution)/shard_map/all_to_all | solution.py:147
  27.0 14.7 %copy-start.1 = (f32[4,3,128,128]{3,2,1,0:T(8,128)}, f32[4,3,128,128]{3,2,1,0:T(8,128)S(1)}, u32[]{:S(2)}) copy-start(f32[4,3,128,128]{3,2,1,0:T(8,128)S(1)} %pad_maximum_fusion.1.refs_0_) | copy-start | bytes 2359300
  27.5 39.6 %collective-permute-start.3 = (f32[4,3,128,128]{3,2,1,0:T(8,128)S(1)}, f32[4,3,128,128]{3,2,1,0:T(8,128)}, u32[]{:S(2)}, u32[]{:S(2)}) collective-permute-start(f32[4,3,128,128]{3,2,1,0:T(8,128)S(1)} %pad_maximum_fusion.1.refs_0_), channel_id=1, source_target_pairs={{1,0},{5,4},{9,8},{13,12},{17,16},{21,20},{25,24},{29,28},{33,32},... | collective-permute-start | bytes 2359304 | tf_op jit(solution)/shard_map/ppermute | solution.py:155
  33.3 33.8 %collective-permute-start.4 = (f32[4,3,128,128]{3,2,1,0:T(8,128)S(1)}, f32[4,3,128,128]{3,2,1,0:T(8,128)}, u32[]{:S(2)}, u32[]{:S(2)}) collective-permute-start(f32[4,3,128,128]{3,2,1,0:T(8,128)S(1)} %pad_maximum_fusion.1.refs_0_), channel_id=1, source_target_pairs={{2,0},{6,4},{10,8},{14,12},{18,16},{22,20},{26,24},{30,28},{34,32}... | collective-permute-start | bytes 2359304 | tf_op jit(solution)/shard_map/ppermute | solution.py:155
  34.9 32.2 %collective-permute-start.5 = (f32[4,3,128,128]{3,2,1,0:T(8,128)S(1)}, f32[4,3,128,128]{3,2,1,0:T(8,128)}, u32[]{:S(2)}, u32[]{:S(2)}) collective-permute-start(f32[4,3,128,128]{3,2,1,0:T(8,128)S(1)} %pad_maximum_fusion.1.refs_0_), channel_id=1, source_target_pairs={{15,0},{3,4},{7,8},{11,12},{31,16},{19,20},{23,24},{27,28},{47,32}... | collective-permute-start | bytes 2359304 | tf_op jit(solution)/shard_map/ppermute | solution.py:155
  37.4 10.4 %all-to-all-start.1 = ((bf16[3,64,1,128]{3,0,2,1:T(4,128)(2,1)}), bf16[3,64,1,128]{3,0,2,1:T(4,128)(2,1)S(1)}, u32[]{:S(2)}, u32[]{:S(2)}) async-start(bf16[3,64,1,128]{3,0,2,1:T(4,128)(2,1)} %copy.123), calls=%async_computation.1 | async-start | bytes 131072 | tf_op jit(solution)/shard_map/all_to_all | solution.py:169
  49.0 18.1 %all-to-all-start.2 = ((f32[16,3,2,128]{3,2,1,0:T(2,128)}), f32[16,3,2,128]{3,2,1,0:T(2,128)S(1)}, u32[]{:S(2)}, u32[]{:S(2)}) async-start(f32[16,3,2,128]{3,2,1,0:T(2,128)} %bitcast.43), calls=%async_computation.2 | async-start | bytes 98304 | tf_op jit(solution)/shard_map/all_to_all | solution.py:183
  67.1 0.6 copy-start.5
  67.7 11.7 %copy-start.7 = (f32[15,128]{1,0:T(8,128)S(1)}, f32[15,128]{1,0:T(8,128)}, u32[]{:S(2)}) copy-start(f32[15,128]{1,0:T(8,128)} %param.14) | copy-start | bytes 23044
  67.7 19.3 %copy-start.2 = (bf16[1920,256]{1,0:T(8,128)(2,1)S(1)}, bf16[1920,256]{1,0:T(8,128)(2,1)}, u32[]{:S(2)}) copy-start(bf16[1920,256]{1,0:T(8,128)(2,1)} %param.11) | copy-start | bytes 2949124
  75.7 11.2 %all-to-all-start.3 = ((f32[16,3,2,128]{3,2,1,0:T(2,128)}), f32[16,3,2,128]{3,2,1,0:T(2,128)S(1)}, u32[]{:S(2)}, u32[]{:S(2)}) async-start(f32[16,3,2,128]{3,2,1,0:T(2,128)} %shard_map.82), calls=%async_computation.3 | async-start | bytes 98304 | tf_op jit(solution)/shard_map/all_to_all | solution.py:191

commit v13 on v10

--- a/solution.py
+++ b/solution.py
@@ -179,6 +179,7 @@
     right_part = cond_line[:, :, point_total:]
 
     sides = jnp.stack([rhs_left, right_part], axis=1)
+    across, sides = lax.optimization_barrier((across, sides))
     destination_plane = [owners.index(slab) if slab in owners else 0 for slab in range(slab_count)]
     outgoing = jnp.stack([sides[plane] for plane in destination_plane])
     to_owner = lax.all_to_all(outgoing, "slab", split_axis=0, concat_axis=0, tiled=True)

time: 84.3 us -> 90.5 us (1.074)
  waiting for transfers between devices: 21.1 us -> 27.2 us
    all_to_all x1, waiting for transfers between devices: 0.01 us -> 6.08 us  [on_device(): lax.all_to_all(nonlin_lines, 'mode', split_axis=1, concat_axis=2, tiled=T...]
  transfers between devices with their start and end apart: 10 -> 10, of which waited for: 3 -> 4; matrix products, arithmetic and copies ran while one was open for 4% -> 4% of each run, Pallas kernels for 0% -> 0%
where the time goes in v13:
time: 90.5 us; the launch traced here: 90 us
  starting transfers between devices  44 us (49%)
  waiting for transfers between devices  27.2 us (30%)
  Pallas kernels  8.02 us (9%)
  local copies, waits for them, and re-layouts  6.32 us (7%)
  matrix products  2.66 us (3%)
  other arithmetic  1.4 us (2%)
    all_to_all x1, starting transfers between devices, on_device(): lax.all_to_all(outgoing, 'slab', split_axis=0, concat_axis=0, tiled=True)  10.6 us
    ppermute x3, starting transfers between devices, on_device(): lax.ppermute(blocks[(position - offset) % group_count], 'slab', pairs)  10.2 us
    ppermute x3, starting transfers between devices, on_device(): across.append(lax.ppermute(group_blocks, 'slab', pairs))  8.89 us
    pallas_call x1, Pallas kernels, on_device(): pl.pallas_call(functools.partial(chain_kernel, group_size=group_size), ou...  8.02 us
    all_to_all x1, waiting for transfers between devices, on_device(): lax.all_to_all(both_sides, 'slab', split_axis=0, concat_axis=0, tiled=True)  7.43 us
    all_to_all x1, waiting for transfers between devices, on_device(): lax.all_to_all(outgoing, 'slab', split_axis=0, concat_axis=0, tiled=True)  7.4 us
    all_to_all x1, starting transfers between devices, on_device(): lax.all_to_all(both_fields, 'mode', split_axis=2, concat_axis=1, tiled=True)  6.75 us
    all_to_all x1, waiting for transfers between devices, on_device(): lax.all_to_all(both_fields, 'mode', split_axis=2, concat_axis=1, tiled=True)  6.25 us
  transfers between devices with their start and end apart: 10, of which 4 were waited for; matrix products, arithmetic and copies ran while one was open for 4% of the time, Pallas kernels for 0%

profile of v13, /device:TPU:1, one launch (start us, length us, event | category | flops | bytes accessed | tf_op | source)
XLA Modules:
  0.0 90.0 jit_solution(12059477343137035091)
XLA Ops:
  0.0 1.2 %slice_bitcast_fusion.1 = (f32[4,1,128,128]{3,2,1,0:T(8,128)S(1)}, f32[4,1,128,128]{3,2,1,0:T(8,128)S(1)}) fusion(f32[2,4,128,128]{3,2,1,0:T(8,128)} %param.12), kind=kLoop, calls=%fused_computation.13 | loop fusion | bytes 1048576 | tf_op jit(solution)/shard_map/stack;squeeze | solution.py:111
  1.4 6.9 %collective-permute-start = (f32[3,128,128]{2,1,0:T(8,128)S(1)}, f32[3,128,128]{2,1,0:T(8,128)S(1)}, u32[]{:S(2)}, u32[]{:S(2)}) collective-permute-start(f32[3,128,128]{2,1,0:T(8,128)S(1)} %get-tuple-element.22), channel_id=1, source_target_pairs={{15,11},{3,15},{7,3},{11,7},{0,12},{4,0},{8,4},{12,8},{1,13},{5,1}... | collective-permute-start | bytes 589832 | tf_op jit(solution)/shard_map/ppermute | solution.py:124
  8.3 1.0 %collective-permute-start.1 = (f32[3,128,128]{2,1,0:T(8,128)S(1)}, f32[3,128,128]{2,1,0:T(8,128)S(1)}, u32[]{:S(2)}, u32[]{:S(2)}) collective-permute-start(f32[3,128,128]{2,1,0:T(8,128)S(1)} %get-tuple-element.21), channel_id=1, source_target_pairs={{15,7},{3,11},{7,15},{11,3},{0,8},{4,12},{8,0},{12,4},{1,9},{5,13}... | collective-permute-start | bytes 589832 | tf_op jit(solution)/shard_map/ppermute | solution.py:124
  9.3 2.3 %collective-permute-start.2 = (f32[3,128,128]{2,1,0:T(8,128)S(1)}, f32[3,128,128]{2,1,0:T(8,128)}, u32[]{:S(2)}, u32[]{:S(2)}) collective-permute-start(f32[3,128,128]{2,1,0:T(8,128)S(1)} %get-tuple-element.20), channel_id=1, source_target_pairs={{15,3},{3,7},{7,11},{11,15},{0,4},{4,8},{8,12},{12,0},{1,5},{5,9},... | collective-permute-start | bytes 589832 | tf_op jit(solution)/shard_map/ppermute | solution.py:124
  11.6 0.7 copy.126
  12.3 6.8 %all-to-all-start = ((bf16[6,4,16,128]{3,0,1,2:T(8,128)(2,1)}), bf16[6,4,16,128]{3,0,1,2:T(8,128)(2,1)S(1)}, u32[]{:S(2)}, u32[]{:S(2)}) async-start(bf16[6,4,16,128]{3,0,1,2:T(8,128)(2,1)} %copy.126), calls=%async_computation | async-start | bytes 262144 | tf_op jit(solution)/shard_map/all_to_all | solution.py:148
  19.7 6.3 %all-to-all-done = bf16[6,4,16,128]{3,0,1,2:T(8,128)(2,1)S(1)} async-done(((bf16[6,4,16,128]{3,0,1,2:T(8,128)(2,1)}), bf16[6,4,16,128]{3,0,1,2:T(8,128)(2,1)S(1)}, u32[]{:S(2)}, u32[]{:S(2)}) %all-to-all-start) | async-done | bytes 98336 | tf_op jit(solution)/shard_map/all_to_all | solution.py:148
  26.0 1.0 %pad_maximum_fusion.1.refs_0_ = f32[4,3,128,128]{3,2,1,0:T(8,128)S(1)} fusion(f32[1,3,128,128]{3,2,1,0:T(8,128)} %bitcast.9, f32[1,3,128,128]{3,2,1,0:T(8,128)S(1)} %bitcast.135, f32[1,3,128,128]{3,2,1,0:T(8,128)S(1)} %bitcast.134, f32[1,3,128,128]{3,2,1,0:T(8,128)S(1)} %get-tuple-element.19), kind=kLoop, calls=%fused_computation.10 | loop fusion | flops 589824 | bytes 1572864 | tf_op jit(solution)/shard_map/stack | solution.py:125
  27.5 5.8 %collective-permute-start.3 = (f32[4,3,128,128]{3,2,1,0:T(8,128)S(1)}, f32[4,3,128,128]{3,2,1,0:T(8,128)}, u32[]{:S(2)}, u32[]{:S(2)}) collective-permute-start(f32[4,3,128,128]{3,2,1,0:T(8,128)S(1)} %pad_maximum_fusion.1.refs_0_), channel_id=1, source_target_pairs={{1,0},{5,4},{9,8},{13,12},{17,16},{21,20},{25,24},{29,28},{33,32},... | collective-permute-start | bytes 2359304 | tf_op jit(solution)/shard_map/ppermute | solution.py:156
  33.3 1.6 %collective-permute-start.4 = (f32[4,3,128,128]{3,2,1,0:T(8,128)S(1)}, f32[4,3,128,128]{3,2,1,0:T(8,128)}, u32[]{:S(2)}, u32[]{:S(2)}) collective-permute-start(f32[4,3,128,128]{3,2,1,0:T(8,128)S(1)} %pad_maximum_fusion.1.refs_0_), channel_id=1, source_target_pairs={{2,0},{6,4},{10,8},{14,12},{18,16},{22,20},{26,24},{30,28},{34,32}... | collective-permute-start | bytes 2359304 | tf_op jit(solution)/shard_map/ppermute | solution.py:156
  34.9 1.5 %collective-permute-start.5 = (f32[4,3,128,128]{3,2,1,0:T(8,128)S(1)}, f32[4,3,128,128]{3,2,1,0:T(8,128)}, u32[]{:S(2)}, u32[]{:S(2)}) collective-permute-start(f32[4,3,128,128]{3,2,1,0:T(8,128)S(1)} %pad_maximum_fusion.1.refs_0_), channel_id=1, source_target_pairs={{15,0},{3,4},{7,8},{11,12},{31,16},{19,20},{23,24},{27,28},{47,32}... | collective-permute-start | bytes 2359304 | tf_op jit(solution)/shard_map/ppermute | solution.py:156
  36.7 0.7 copy.138
  37.4 3.9 %all-to-all-start.1 = ((bf16[3,64,1,128]{3,0,2,1:T(4,128)(2,1)}), bf16[3,64,1,128]{3,0,2,1:T(4,128)(2,1)S(1)}, u32[]{:S(2)}, u32[]{:S(2)}) async-start(bf16[3,64,1,128]{3,0,2,1:T(4,128)(2,1)} %copy.138), calls=%async_computation.1 | async-start | bytes 131072 | tf_op jit(solution)/shard_map/all_to_all | solution.py:170
  41.8 6.1 %all-to-all-done.1 = bf16[3,64,1,128]{3,0,2,1:T(4,128)(2,1)S(1)} async-done(((bf16[3,64,1,128]{3,0,2,1:T(4,128)(2,1)}), bf16[3,64,1,128]{3,0,2,1:T(4,128)(2,1)S(1)}, u32[]{:S(2)}, u32[]{:S(2)}) %all-to-all-start.1) | async-done | bytes 49184 | tf_op jit(solution)/shard_map/all_to_all | solution.py:170
  48.5 0.6 copy.143
  49.1 10.6 %all-to-all-start.2 = ((f32[16,2,3,128]{3,1,2,0:T(2,128)}), f32[16,2,3,128]{3,1,2,0:T(2,128)S(1)}, u32[]{:S(2)}, u32[]{:S(2)}) async-start(f32[16,2,3,128]{3,1,2,0:T(2,128)} %copy.143), calls=%async_computation.2 | async-start | bytes 98304 | tf_op jit(solution)/shard_map/all_to_all | solution.py:185
  59.8 7.4 %all-to-all-done.2 = f32[16,2,3,128]{3,1,2,0:T(2,128)S(1)} async-done(((f32[16,2,3,128]{3,1,2,0:T(2,128)}), f32[16,2,3,128]{3,1,2,0:T(2,128)S(1)}, u32[]{:S(2)}, u32[]{:S(2)}) %all-to-all-start.2) | async-done | bytes 49184 | tf_op jit(solution)/shard_map/all_to_all | solution.py:185
  67.2 0.6 copy.144.refs_4_
  67.9 8.0 %shard_map.82 = f32[16,2,3,128]{3,2,1,0:T(4,128)} custom-call(s32[1]{0:T(128)} %bitcast.position_ref, f32[4,3,128,128]{3,2,1,0:T(8,128)} %copy-done.1, f32[4,3,128,128]{3,2,1,0:T(8,128)} %collective-permute-done.3.refs_1_, f32[4,3,128,128]{3,2,1,0:T(8,128)} %collective-permute-done.4.refs_2_, f32[4,3,128,128]{3,2,1,0:T(8,128)} %collective-permute-done.5.refs_3_, ...), custom_call_target="tpu_custom_call" | custom-call | tf_op jit(solution)/shard_map/pallas_call | solution.py:186
  75.9 1.5 %copy.145 = f32[16,2,3,128]{3,1,2,0:T(2,128)} copy(f32[16,2,3,128]{3,2,1,0:T(4,128)} %shard_map.82) | data formatting | bytes 98304 | tf_op jit(solution)/shard_map/pallas_call | solution.py:186
  77.4 3.6 %all-to-all-start.3 = ((f32[16,2,3,128]{3,1,2,0:T(2,128)}), f32[16,2,3,128]{3,1,2,0:T(2,128)S(1)}, u32[]{:S(2)}, u32[]{:S(2)}) async-start(f32[16,2,3,128]{3,1,2,0:T(2,128)} %copy.145), calls=%async_computation.3 | async-start | bytes 98304 | tf_op jit(solution)/shard_map/all_to_all | solution.py:193
  81.1 7.4 %all-to-all-done.3 = f32[16,2,3,128]{3,1,2,0:T(2,128)S(1)} async-done(((f32[16,2,3,128]{3,1,2,0:T(2,128)}), f32[16,2,3,128]{3,1,2,0:T(2,128)S(1)}, u32[]{:S(2)}, u32[]{:S(2)}) %all-to-all-start.3) | async-done | bytes 49184 | tf_op jit(solution)/shard_map/all_to_all | solution.py:193
  88.7 0.6 convolution_bitcast_fusion
  89.4 0.6 copy.151
  (60 shorter events, 2.8 us)
Async XLA Ops:
  0.0 19.2 %copy-start = (bf16[256,1920]{1,0:T(8,128)(2,1)S(1)}, bf16[256,1920]{1,0:T(8,128)(2,1)}, u32[]{:S(2)}) copy-start(bf16[256,1920]{1,0:T(8,128)(2,1)} %param.10) | copy-start | bytes 2949124
  0.0 1.2 %copy-start.4 = (f32[4,128,128]{2,1,0:T(8,128)S(1)}, f32[4,128,128]{2,1,0:T(8,128)}, u32[]{:S(2)}) copy-start(f32[4,128,128]{2,1,0:T(8,128)} %param.13) | copy-start | bytes 786436
  1.3 10.3 %copy-start.3 = (f32[3,4,16,128]{3,2,1,0:T(8,128)S(1)}, f32[3,4,16,128]{3,2,1,0:T(8,128)}, u32[]{:S(2)}) copy-start(f32[3,4,16,128]{3,2,1,0:T(8,128)} %param.8) | copy-start | bytes 294916
  1.3 10.3 %copy-start.5 = (bf16[3,4,16,128]{3,2,1,0:T(8,128)(2,1)S(1)}, bf16[3,4,16,128]{3,2,1,0:T(8,128)(2,1)}, u32[]{:S(2)}) copy-start(bf16[3,4,16,128]{3,2,1,0:T(8,128)(2,1)} %param.9) | copy-start | bytes 147460
  1.3 17.8 %copy-start.7 = (s32[1,256]{1,0:T(1,128)S(1)}, s32[1,256]{1,0:T(1,128)}, u32[]{:S(2)}) copy-start(s32[1,256]{1,0:T(1,128)} %param.15) | copy-start | bytes 3076
  1.3 17.8 %copy-start.8 = (s32[1,256]{1,0:T(1,128)S(1)}, s32[1,256]{1,0:T(1,128)}, u32[]{:S(2)}) copy-start(s32[1,256]{1,0:T(1,128)} %constant.117.clone.1) | copy-start | bytes 3076
  1.4 24.6 %collective-permute-start = (f32[3,128,128]{2,1,0:T(8,128)S(1)}, f32[3,128,128]{2,1,0:T(8,128)S(1)}, u32[]{:S(2)}, u32[]{:S(2)}) collective-permute-start(f32[3,128,128]{2,1,0:T(8,128)S(1)} %get-tuple-element.22), channel_id=1, source_target_pairs={{15,11},{3,15},{7,3},{11,7},{0,12},{4,0},{8,4},{12,8},{1,13},{5,1}... | collective-permute-start | bytes 589832 | tf_op jit(solution)/shard_map/ppermute | solution.py:124
  8.3 17.7 %collective-permute-start.1 = (f32[3,128,128]{2,1,0:T(8,128)S(1)}, f32[3,128,128]{2,1,0:T(8,128)S(1)}, u32[]{:S(2)}, u32[]{:S(2)}) collective-permute-start(f32[3,128,128]{2,1,0:T(8,128)S(1)} %get-tuple-element.21), channel_id=1, source_target_pairs={{15,7},{3,11},{7,15},{11,3},{0,8},{4,12},{8,0},{12,4},{1,9},{5,13}... | collective-permute-start | bytes 589832 | tf_op jit(solution)/shard_map/ppermute | solution.py:124
  9.3 16.7 %collective-permute-start.2 = (f32[3,128,128]{2,1,0:T(8,128)S(1)}, f32[3,128,128]{2,1,0:T(8,128)}, u32[]{:S(2)}, u32[]{:S(2)}) collective-permute-start(f32[3,128,128]{2,1,0:T(8,128)S(1)} %get-tuple-element.20), channel_id=1, source_target_pairs={{15,3},{3,7},{7,11},{11,15},{0,4},{4,8},{8,12},{12,0},{1,5},{5,9},... | collective-permute-start | bytes 589832 | tf_op jit(solution)/shard_map/ppermute | solution.py:124
  12.3 13.6 %all-to-all-start = ((bf16[6,4,16,128]{3,0,1,2:T(8,128)(2,1)}), bf16[6,4,16,128]{3,0,1,2:T(8,128)(2,1)S(1)}, u32[]{:S(2)}, u32[]{:S(2)}) async-start(bf16[6,4,16,128]{3,0,1,2:T(8,128)(2,1)} %copy.126), calls=%async_computation | async-start | bytes 262144 | tf_op jit(solution)/shard_map/all_to_all | solution.py:148
  27.0 14.7 %copy-start.1 = (f32[4,3,128,128]{3,2,1,0:T(8,128)}, f32[4,3,128,128]{3,2,1,0:T(8,128)S(1)}, u32[]{:S(2)}) copy-start(f32[4,3,128,128]{3,2,1,0:T(8,128)S(1)} %pad_maximum_fusion.1.refs_0_) | copy-start | bytes 2359300
  27.5 20.8 %collective-permute-start.3 = (f32[4,3,128,128]{3,2,1,0:T(8,128)S(1)}, f32[4,3,128,128]{3,2,1,0:T(8,128)}, u32[]{:S(2)}, u32[]{:S(2)}) collective-permute-start(f32[4,3,128,128]{3,2,1,0:T(8,128)S(1)} %pad_maximum_fusion.1.refs_0_), channel_id=1, source_target_pairs={{1,0},{5,4},{9,8},{13,12},{17,16},{21,20},{25,24},{29,28},{33,32},... | collective-permute-start | bytes 2359304 | tf_op jit(solution)/shard_map/ppermute | solution.py:156
  33.3 15.0 %collective-permute-start.4 = (f32[4,3,128,128]{3,2,1,0:T(8,128)S(1)}, f32[4,3,128,128]{3,2,1,0:T(8,128)}, u32[]{:S(2)}, u32[]{:S(2)}) collective-permute-start(f32[4,3,128,128]{3,2,1,0:T(8,128)S(1)} %pad_maximum_fusion.1.refs_0_), channel_id=1, source_target_pairs={{2,0},{6,4},{10,8},{14,12},{18,16},{22,20},{26,24},{30,28},{34,32}... | collective-permute-start | bytes 2359304 | tf_op jit(solution)/shard_map/ppermute | solution.py:156
  34.9 13.5 %collective-permute-start.5 = (f32[4,3,128,128]{3,2,1,0:T(8,128)S(1)}, f32[4,3,128,128]{3,2,1,0:T(8,128)}, u32[]{:S(2)}, u32[]{:S(2)}) collective-permute-start(f32[4,3,128,128]{3,2,1,0:T(8,128)S(1)} %pad_maximum_fusion.1.refs_0_), channel_id=1, source_target_pairs={{15,0},{3,4},{7,8},{11,12},{31,16},{19,20},{23,24},{27,28},{47,32}... | collective-permute-start | bytes 2359304 | tf_op jit(solution)/shard_map/ppermute | solution.py:156
  37.4 10.4 %all-to-all-start.1 = ((bf16[3,64,1,128]{3,0,2,1:T(4,128)(2,1)}), bf16[3,64,1,128]{3,0,2,1:T(4,128)(2,1)S(1)}, u32[]{:S(2)}, u32[]{:S(2)}) async-start(bf16[3,64,1,128]{3,0,2,1:T(4,128)(2,1)} %copy.138), calls=%async_computation.1 | async-start | bytes 131072 | tf_op jit(solution)/shard_map/all_to_all | solution.py:170
  49.1 18.1 %all-to-all-start.2 = ((f32[16,2,3,128]{3,1,2,0:T(2,128)}), f32[16,2,3,128]{3,1,2,0:T(2,128)S(1)}, u32[]{:S(2)}, u32[]{:S(2)}) async-start(f32[16,2,3,128]{3,1,2,0:T(2,128)} %copy.143), calls=%async_computation.2 | async-start | bytes 98304 | tf_op jit(solution)/shard_map/all_to_all | solution.py:185
  67.9 13.2 %copy-start.6 = (f32[15,128]{1,0:T(8,128)S(1)}, f32[15,128]{1,0:T(8,128)}, u32[]{:S(2)}) copy-start(f32[15,128]{1,0:T(8,128)} %param.14) | copy-start | bytes 23044
  67.9 20.8 %copy-start.2 = (bf16[1920,256]{1,0:T(8,128)(2,1)S(1)}, bf16[1920,256]{1,0:T(8,128)(2,1)}, u32[]{:S(2)}) copy-start(bf16[1920,256]{1,0:T(8,128)(2,1)} %param.11) | copy-start | bytes 2949124
  77.4 11.2 %all-to-all-start.3 = ((f32[16,2,3,128]{3,1,2,0:T(2,128)}), f32[16,2,3,128]{3,1,2,0:T(2,128)S(1)}, u32[]{:S(2)}, u32[]{:S(2)}) async-start(f32[16,2,3,128]{3,1,2,0:T(2,128)} %copy.145), calls=%async_computation.3 | async-start | bytes 98304 | tf_op jit(solution)/shard_map/all_to_all | solution.py:193

commit v14 on v11

--- a/solution.py
+++ b/solution.py
@@ -65,11 +65,10 @@
             spot_slot = (label // group_size - position) % group_size
             return group_refs[group_slot].at[spot_slot]
 
-        zero = jnp.zeros((sides_ref.shape[1], sides_ref.shape[3]), jnp.float32)
-        sides = [sides_ref[k] for k in range(slab_count)]
+        zero = jnp.zeros(sides_ref.shape[2:], jnp.float32)
         forward_values = [zero]
         for k in range(1, slab_count):
-            source = sides[k][:, 0] + sides[k - 1][:, 1]
+            source = sides_ref[k, 0] + sides_ref[k - 1, 1]
             forward_values.append(source - apply(blocks_of(k)[0], forward_values[-1]))
         after = zero
         for k in range(slab_count - 1, 0, -1):
@@ -177,13 +176,15 @@
     rhs_left = cond_line[:, :, :point_total] + line_zero_rhs
     right_part = cond_line[:, :, point_total:]
 
-    sides = jnp.stack([rhs_left, right_part], axis=2)
+    sides = jnp.stack([rhs_left, right_part], axis=1)
     destination_plane = [owners.index(slab) if slab in owners else 0 for slab in range(slab_count)]
     outgoing = jnp.stack([sides[plane] for plane in destination_plane])
     to_owner = lax.all_to_all(outgoing, "slab", split_axis=0, concat_axis=0, tiled=True)
     both_sides = pl.pallas_call(
         functools.partial(chain_kernel, group_size=group_size),
-        out_shape=jax.ShapeDtypeStruct(to_owner.shape, jnp.float32),
+        out_shape=jax.ShapeDtypeStruct(
+            (slab_count, components, 2, point_total), jnp.float32
+        ),
         in_specs=[pl.BlockSpec(memory_space=pltpu.SMEM)]
         + [pl.BlockSpec(memory_space=pltpu.VMEM)] * (group_size + 1),
         out_specs=pl.BlockSpec(memory_space=pltpu.VMEM),

time: 90.7 us -> 82.8 us (0.913)
  local copies, waits for them, and re-layouts: 10.4 us -> 4.83 us
  other arithmetic: 3.74 us -> 1.41 us
    unnamed x30 -> x22, local copies, waits for them, and re-layouts: 6.43 us -> 0.07 us
    unnamed x4 -> x0, other arithmetic: 2.36 us -> none
  transfers between devices with their start and end apart: 10 -> 10, of which waited for: 3 -> 3; matrix products, arithmetic and copies ran while one was open for 12% -> 4% of each run, Pallas kernels for 0% -> 0%
where the time goes in v14:
time: 82.8 us; the launch traced here: 82.3 us
  starting transfers between devices  43.9 us (53%)
  waiting for transfers between devices  21.1 us (25%)
  Pallas kernels  8.03 us (10%)
  local copies, waits for them, and re-layouts  4.83 us (6%)
  matrix products  2.66 us (3%)
  other arithmetic  1.41 us (2%)
    all_to_all x1, starting transfers between devices, on_device(): lax.all_to_all(outgoing, 'slab', split_axis=0, concat_axis=0, tiled=True)  10.2 us
    ppermute x3, starting transfers between devices, on_device(): lax.ppermute(blocks[(position - offset) % group_count], 'slab', pairs)  10.2 us
    ppermute x3, starting transfers between devices, on_device(): across.append(lax.ppermute(group_blocks, 'slab', pairs))  9.25 us
    pallas_call x1, Pallas kernels, on_device(): pl.pallas_call(functools.partial(chain_kernel, group_size=group_size), ou...  8.03 us
    all_to_all x1, waiting for transfers between devices, on_device(): lax.all_to_all(both_sides, 'slab', split_axis=0, concat_axis=0, tiled=True)  7.43 us
    all_to_all x1, waiting for transfers between devices, on_device(): lax.all_to_all(outgoing, 'slab', split_axis=0, concat_axis=0, tiled=True)  7.4 us
    all_to_all x1, starting transfers between devices, on_device(): lax.all_to_all(both_fields, 'mode', split_axis=2, concat_axis=1, tiled=True)  6.75 us
    all_to_all x1, waiting for transfers between devices, on_device(): lax.all_to_all(both_fields, 'mode', split_axis=2, concat_axis=1, tiled=True)  6.25 us
  transfers between devices with their start and end apart: 10, of which 3 were waited for; matrix products, arithmetic and copies ran while one was open for 4% of the time, Pallas kernels for 0%

profile of v14, /device:TPU:1, one launch (start us, length us, event | category | flops | bytes accessed | tf_op | source)
XLA Modules:
  0.0 82.3 jit_solution(18149428070511581878)
XLA Ops:
  0.0 1.2 %slice_bitcast_fusion.1 = (f32[4,1,128,128]{3,2,1,0:T(8,128)S(1)}, f32[4,1,128,128]{3,2,1,0:T(8,128)S(1)}) fusion(f32[2,4,128,128]{3,2,1,0:T(8,128)} %param.12), kind=kLoop, calls=%fused_computation.13 | loop fusion | bytes 1048576 | tf_op jit(solution)/shard_map/stack;squeeze | solution.py:109
  1.4 6.9 %collective-permute-start = (f32[3,128,128]{2,1,0:T(8,128)S(1)}, f32[3,128,128]{2,1,0:T(8,128)S(1)}, u32[]{:S(2)}, u32[]{:S(2)}) collective-permute-start(f32[3,128,128]{2,1,0:T(8,128)S(1)} %get-tuple-element.12), channel_id=1, source_target_pairs={{15,11},{3,15},{7,3},{11,7},{0,12},{4,0},{8,4},{12,8},{1,13},{5,1}... | collective-permute-start | bytes 589832 | tf_op jit(solution)/shard_map/ppermute | solution.py:122
  8.3 1.0 %collective-permute-start.1 = (f32[3,128,128]{2,1,0:T(8,128)S(1)}, f32[3,128,128]{2,1,0:T(8,128)S(1)}, u32[]{:S(2)}, u32[]{:S(2)}) collective-permute-start(f32[3,128,128]{2,1,0:T(8,128)S(1)} %get-tuple-element.11), channel_id=1, source_target_pairs={{15,7},{3,11},{7,15},{11,3},{0,8},{4,12},{8,0},{12,4},{1,9},{5,13}... | collective-permute-start | bytes 589832 | tf_op jit(solution)/shard_map/ppermute | solution.py:122
  9.3 2.3 %collective-permute-start.2 = (f32[3,128,128]{2,1,0:T(8,128)S(1)}, f32[3,128,128]{2,1,0:T(8,128)}, u32[]{:S(2)}, u32[]{:S(2)}) collective-permute-start(f32[3,128,128]{2,1,0:T(8,128)S(1)} %get-tuple-element.10), channel_id=1, source_target_pairs={{15,3},{3,7},{7,11},{11,15},{0,4},{4,8},{8,12},{12,0},{1,5},{5,9},... | collective-permute-start | bytes 589832 | tf_op jit(solution)/shard_map/ppermute | solution.py:122
  11.6 0.7 copy.123
  12.3 6.8 %all-to-all-start = ((bf16[6,4,16,128]{3,0,1,2:T(8,128)(2,1)}), bf16[6,4,16,128]{3,0,1,2:T(8,128)(2,1)S(1)}, u32[]{:S(2)}, u32[]{:S(2)}) async-start(bf16[6,4,16,128]{3,0,1,2:T(8,128)(2,1)} %copy.123), calls=%async_computation | async-start | bytes 262144 | tf_op jit(solution)/shard_map/all_to_all | solution.py:146
  19.2 0.5 fusion
  19.7 6.3 %all-to-all-done = bf16[6,4,16,128]{3,0,1,2:T(8,128)(2,1)S(1)} async-done(((bf16[6,4,16,128]{3,0,1,2:T(8,128)(2,1)}), bf16[6,4,16,128]{3,0,1,2:T(8,128)(2,1)S(1)}, u32[]{:S(2)}, u32[]{:S(2)}) %all-to-all-start) | async-done | bytes 98336 | tf_op jit(solution)/shard_map/all_to_all | solution.py:146
  26.0 1.0 %pad_maximum_fusion.1.refs_0_ = f32[4,3,128,128]{3,2,1,0:T(8,128)S(1)} fusion(f32[1,3,128,128]{3,2,1,0:T(8,128)} %bitcast.9, f32[1,3,128,128]{3,2,1,0:T(8,128)S(1)} %bitcast.135, f32[1,3,128,128]{3,2,1,0:T(8,128)S(1)} %bitcast.134, f32[1,3,128,128]{3,2,1,0:T(8,128)S(1)} %get-tuple-element.9), kind=kLoop, calls=%fused_computation.10 | loop fusion | flops 589824 | bytes 1572864 | tf_op jit(solution)/shard_map/stack | solution.py:123
  27.0 0.4 fusion.7
  27.8 0.7 copy.135
  28.5 3.8 %all-to-all-start.1 = ((bf16[3,64,1,128]{3,0,2,1:T(4,128)(2,1)}), bf16[3,64,1,128]{3,0,2,1:T(4,128)(2,1)S(1)}, u32[]{:S(2)}, u32[]{:S(2)}) async-start(bf16[3,64,1,128]{3,0,2,1:T(4,128)(2,1)} %copy.135), calls=%async_computation.1 | async-start | bytes 131072 | tf_op jit(solution)/shard_map/all_to_all | solution.py:168
  32.8 6.1 %collective-permute-start.3 = (f32[4,3,128,128]{3,2,1,0:T(8,128)S(1)}, f32[4,3,128,128]{3,2,1,0:T(8,128)}, u32[]{:S(2)}, u32[]{:S(2)}) collective-permute-start(f32[4,3,128,128]{3,2,1,0:T(8,128)S(1)} %pad_maximum_fusion.1.refs_0_), channel_id=1, source_target_pairs={{1,0},{5,4},{9,8},{13,12},{17,16},{21,20},{25,24},{29,28},{33,32},... | collective-permute-start | bytes 2359304 | tf_op jit(solution)/shard_map/ppermute | solution.py:154
  38.9 1.6 %collective-permute-start.4 = (f32[4,3,128,128]{3,2,1,0:T(8,128)S(1)}, f32[4,3,128,128]{3,2,1,0:T(8,128)}, u32[]{:S(2)}, u32[]{:S(2)}) collective-permute-start(f32[4,3,128,128]{3,2,1,0:T(8,128)S(1)} %pad_maximum_fusion.1.refs_0_), channel_id=1, source_target_pairs={{2,0},{6,4},{10,8},{14,12},{18,16},{22,20},{26,24},{30,28},{34,32}... | collective-permute-start | bytes 2359304 | tf_op jit(solution)/shard_map/ppermute | solution.py:154
  40.5 1.5 %collective-permute-start.5 = (f32[4,3,128,128]{3,2,1,0:T(8,128)S(1)}, f32[4,3,128,128]{3,2,1,0:T(8,128)}, u32[]{:S(2)}, u32[]{:S(2)}) collective-permute-start(f32[4,3,128,128]{3,2,1,0:T(8,128)S(1)} %pad_maximum_fusion.1.refs_0_), channel_id=1, source_target_pairs={{15,0},{3,4},{7,8},{11,12},{31,16},{19,20},{23,24},{27,28},{47,32}... | collective-permute-start | bytes 2359304 | tf_op jit(solution)/shard_map/ppermute | solution.py:154
  42.6 0.6 copy.140
  43.3 10.2 %all-to-all-start.2 = ((f32[16,2,3,128]{3,1,2,0:T(2,128)}), f32[16,2,3,128]{3,1,2,0:T(2,128)S(1)}, u32[]{:S(2)}, u32[]{:S(2)}) async-start(f32[16,2,3,128]{3,1,2,0:T(2,128)} %copy.140), calls=%async_computation.2 | async-start | bytes 98304 | tf_op jit(solution)/shard_map/all_to_all | solution.py:182
  53.6 7.4 %all-to-all-done.2 = f32[16,2,3,128]{3,1,2,0:T(2,128)S(1)} async-done(((f32[16,2,3,128]{3,1,2,0:T(2,128)}), f32[16,2,3,128]{3,1,2,0:T(2,128)S(1)}, u32[]{:S(2)}, u32[]{:S(2)}) %all-to-all-start.2) | async-done | bytes 49184 | tf_op jit(solution)/shard_map/all_to_all | solution.py:182
  61.0 0.6 copy.141.refs_4_
  61.7 8.0 %shard_map.82 = f32[16,3,2,128]{3,2,1,0:T(2,128)} custom-call(s32[1]{0:T(128)} %bitcast.position_ref, f32[4,3,128,128]{3,2,1,0:T(8,128)} %copy-done.1, f32[4,3,128,128]{3,2,1,0:T(8,128)} %collective-permute-done.3.refs_1_, f32[4,3,128,128]{3,2,1,0:T(8,128)} %collective-permute-done.4.refs_2_, f32[4,3,128,128]{3,2,1,0:T(8,128)} %collective-permute-done.5.refs_3_, ...), custom_call_target="tpu_custom_call" | custom-call | tf_op jit(solution)/shard_map/pallas_call | solution.py:183
  69.7 3.6 %all-to-all-start.3 = ((f32[16,3,2,128]{3,2,1,0:T(2,128)}), f32[16,3,2,128]{3,2,1,0:T(2,128)S(1)}, u32[]{:S(2)}, u32[]{:S(2)}) async-start(f32[16,3,2,128]{3,2,1,0:T(2,128)} %shard_map.82), calls=%async_computation.3 | async-start | bytes 98304 | tf_op jit(solution)/shard_map/all_to_all | solution.py:192
  73.4 7.4 %all-to-all-done.3 = f32[16,3,2,128]{3,2,1,0:T(2,128)S(1)} async-done(((f32[16,3,2,128]{3,2,1,0:T(2,128)}), f32[16,3,2,128]{3,2,1,0:T(2,128)S(1)}, u32[]{:S(2)}, u32[]{:S(2)}) %all-to-all-start.3) | async-done | bytes 49184 | tf_op jit(solution)/shard_map/all_to_all | solution.py:192
  81.0 0.6 convolution_bitcast_fusion
  81.7 0.6 copy.147
  (58 shorter events, 1.9 us)
Async XLA Ops:
  0.0 19.2 %copy-start = (bf16[256,1920]{1,0:T(8,128)(2,1)S(1)}, bf16[256,1920]{1,0:T(8,128)(2,1)}, u32[]{:S(2)}) copy-start(bf16[256,1920]{1,0:T(8,128)(2,1)} %param.10) | copy-start | bytes 2949124
  0.0 1.2 %copy-start.4 = (f32[4,128,128]{2,1,0:T(8,128)S(1)}, f32[4,128,128]{2,1,0:T(8,128)}, u32[]{:S(2)}) copy-start(f32[4,128,128]{2,1,0:T(8,128)} %param.13) | copy-start | bytes 786436
  1.3 10.3 %copy-start.3 = (f32[3,4,16,128]{3,2,1,0:T(8,128)S(1)}, f32[3,4,16,128]{3,2,1,0:T(8,128)}, u32[]{:S(2)}) copy-start(f32[3,4,16,128]{3,2,1,0:T(8,128)} %param.8) | copy-start | bytes 294916
  1.3 10.3 %copy-start.5 = (bf16[3,4,16,128]{3,2,1,0:T(8,128)(2,1)S(1)}, bf16[3,4,16,128]{3,2,1,0:T(8,128)(2,1)}, u32[]{:S(2)}) copy-start(bf16[3,4,16,128]{3,2,1,0:T(8,128)(2,1)} %param.9) | copy-start | bytes 147460
  1.3 17.8 %copy-start.7 = (s32[1,256]{1,0:T(1,128)S(1)}, s32[1,256]{1,0:T(1,128)}, u32[]{:S(2)}) copy-start(s32[1,256]{1,0:T(1,128)} %param.15) | copy-start | bytes 3076
  1.3 17.8 %copy-start.8 = (s32[1,256]{1,0:T(1,128)S(1)}, s32[1,256]{1,0:T(1,128)}, u32[]{:S(2)}) copy-start(s32[1,256]{1,0:T(1,128)} %constant.117.clone.1) | copy-start | bytes 3076
  1.4 24.6 %collective-permute-start = (f32[3,128,128]{2,1,0:T(8,128)S(1)}, f32[3,128,128]{2,1,0:T(8,128)S(1)}, u32[]{:S(2)}, u32[]{:S(2)}) collective-permute-start(f32[3,128,128]{2,1,0:T(8,128)S(1)} %get-tuple-element.12), channel_id=1, source_target_pairs={{15,11},{3,15},{7,3},{11,7},{0,12},{4,0},{8,4},{12,8},{1,13},{5,1}... | collective-permute-start | bytes 589832 | tf_op jit(solution)/shard_map/ppermute | solution.py:122
  8.3 17.7 %collective-permute-start.1 = (f32[3,128,128]{2,1,0:T(8,128)S(1)}, f32[3,128,128]{2,1,0:T(8,128)S(1)}, u32[]{:S(2)}, u32[]{:S(2)}) collective-permute-start(f32[3,128,128]{2,1,0:T(8,128)S(1)} %get-tuple-element.11), channel_id=1, source_target_pairs={{15,7},{3,11},{7,15},{11,3},{0,8},{4,12},{8,0},{12,4},{1,9},{5,13}... | collective-permute-start | bytes 589832 | tf_op jit(solution)/shard_map/ppermute | solution.py:122
  9.3 16.7 %collective-permute-start.2 = (f32[3,128,128]{2,1,0:T(8,128)S(1)}, f32[3,128,128]{2,1,0:T(8,128)}, u32[]{:S(2)}, u32[]{:S(2)}) collective-permute-start(f32[3,128,128]{2,1,0:T(8,128)S(1)} %get-tuple-element.10), channel_id=1, source_target_pairs={{15,3},{3,7},{7,11},{11,15},{0,4},{4,8},{8,12},{12,0},{1,5},{5,9},... | collective-permute-start | bytes 589832 | tf_op jit(solution)/shard_map/ppermute | solution.py:122
  12.3 13.6 %all-to-all-start = ((bf16[6,4,16,128]{3,0,1,2:T(8,128)(2,1)}), bf16[6,4,16,128]{3,0,1,2:T(8,128)(2,1)S(1)}, u32[]{:S(2)}, u32[]{:S(2)}) async-start(bf16[6,4,16,128]{3,0,1,2:T(8,128)(2,1)} %copy.123), calls=%async_computation | async-start | bytes 262144 | tf_op jit(solution)/shard_map/all_to_all | solution.py:146
  27.0 13.5 %copy-start.1 = (f32[4,3,128,128]{3,2,1,0:T(8,128)}, f32[4,3,128,128]{3,2,1,0:T(8,128)S(1)}, u32[]{:S(2)}) copy-start(f32[4,3,128,128]{3,2,1,0:T(8,128)S(1)} %pad_maximum_fusion.1.refs_0_) | copy-start | bytes 2359300
  28.5 13.5 %all-to-all-start.1 = ((bf16[3,64,1,128]{3,0,2,1:T(4,128)(2,1)}), bf16[3,64,1,128]{3,0,2,1:T(4,128)(2,1)S(1)}, u32[]{:S(2)}, u32[]{:S(2)}) async-start(bf16[3,64,1,128]{3,0,2,1:T(4,128)(2,1)} %copy.135), calls=%async_computation.1 | async-start | bytes 131072 | tf_op jit(solution)/shard_map/all_to_all | solution.py:168
  32.8 28.8 %collective-permute-start.3 = (f32[4,3,128,128]{3,2,1,0:T(8,128)S(1)}, f32[4,3,128,128]{3,2,1,0:T(8,128)}, u32[]{:S(2)}, u32[]{:S(2)}) collective-permute-start(f32[4,3,128,128]{3,2,1,0:T(8,128)S(1)} %pad_maximum_fusion.1.refs_0_), channel_id=1, source_target_pairs={{1,0},{5,4},{9,8},{13,12},{17,16},{21,20},{25,24},{29,28},{33,32},... | collective-permute-start | bytes 2359304 | tf_op jit(solution)/shard_map/ppermute | solution.py:154
  38.9 22.7 %collective-permute-start.4 = (f32[4,3,128,128]{3,2,1,0:T(8,128)S(1)}, f32[4,3,128,128]{3,2,1,0:T(8,128)}, u32[]{:S(2)}, u32[]{:S(2)}) collective-permute-start(f32[4,3,128,128]{3,2,1,0:T(8,128)S(1)} %pad_maximum_fusion.1.refs_0_), channel_id=1, source_target_pairs={{2,0},{6,4},{10,8},{14,12},{18,16},{22,20},{26,24},{30,28},{34,32}... | collective-permute-start | bytes 2359304 | tf_op jit(solution)/shard_map/ppermute | solution.py:154
  40.5 21.1 %collective-permute-start.5 = (f32[4,3,128,128]{3,2,1,0:T(8,128)S(1)}, f32[4,3,128,128]{3,2,1,0:T(8,128)}, u32[]{:S(2)}, u32[]{:S(2)}) collective-permute-start(f32[4,3,128,128]{3,2,1,0:T(8,128)S(1)} %pad_maximum_fusion.1.refs_0_), channel_id=1, source_target_pairs={{15,0},{3,4},{7,8},{11,12},{31,16},{19,20},{23,24},{27,28},{47,32}... | collective-permute-start | bytes 2359304 | tf_op jit(solution)/shard_map/ppermute | solution.py:154
  43.3 17.7 %all-to-all-start.2 = ((f32[16,2,3,128]{3,1,2,0:T(2,128)}), f32[16,2,3,128]{3,1,2,0:T(2,128)S(1)}, u32[]{:S(2)}, u32[]{:S(2)}) async-start(f32[16,2,3,128]{3,1,2,0:T(2,128)} %copy.140), calls=%async_computation.2 | async-start | bytes 98304 | tf_op jit(solution)/shard_map/all_to_all | solution.py:182
  61.6 11.7 %copy-start.6 = (f32[15,128]{1,0:T(8,128)S(1)}, f32[15,128]{1,0:T(8,128)}, u32[]{:S(2)}) copy-start(f32[15,128]{1,0:T(8,128)} %param.14) | copy-start | bytes 23044
  61.6 19.3 %copy-start.2 = (bf16[1920,256]{1,0:T(8,128)(2,1)S(1)}, bf16[1920,256]{1,0:T(8,128)(2,1)}, u32[]{:S(2)}) copy-start(bf16[1920,256]{1,0:T(8,128)(2,1)} %param.11) | copy-start | bytes 2949124
  69.7 11.2 %all-to-all-start.3 = ((f32[16,3,2,128]{3,2,1,0:T(2,128)}), f32[16,3,2,128]{3,2,1,0:T(2,128)S(1)}, u32[]{:S(2)}, u32[]{:S(2)}) async-start(f32[16,3,2,128]{3,2,1,0:T(2,128)} %shard_map.82), calls=%async_computation.3 | async-start | bytes 98304 | tf_op jit(solution)/shard_map/all_to_all | solution.py:192

commit v15 on v14

--- a/solution.py
+++ b/solution.py
@@ -120,7 +120,6 @@
             for rank in range(group_count)
         ]
         within.append(lax.ppermute(blocks[(position - offset) % group_count], "slab", pairs))
-    group_blocks = jnp.stack(within)
 
     halfway_offsets = jnp.concatenate(
         [jnp.zeros((point_total,), jnp.int32), jnp.full((point_total,), point_total, jnp.int32)]
@@ -144,7 +143,8 @@
     velocity_half = velocity.astype(jnp.bfloat16)
     both_fields = jnp.concatenate([velocity_half, vorticity], axis=0)
     field_lines = lax.all_to_all(both_fields, "mode", split_axis=2, concat_axis=1, tiled=True)
-    group_blocks, field_lines = lax.optimization_barrier((group_blocks, field_lines))
+    within, field_lines = lax.optimization_barrier((tuple(within), field_lines))
+    group_blocks = jnp.stack(within)
     across = [group_blocks]
     for offset in range(1, group_size):
         pairs = [

time: 82.8 us -> 82.2 us (level)
    all_to_all x1, starting transfers between devices: 10.2 us -> 9.21 us  [on_device(): lax.all_to_all(outgoing, 'slab', split_axis=0, concat_axis=0, tiled=True)]
  transfers between devices with their start and end apart: 10 -> 10, of which waited for: 3 -> 3; matrix products, arithmetic and copies ran while one was open for 4% -> 6% of each run, Pallas kernels for 0% -> 0%
where the time goes in v15:
time: 82.2 us; the launch traced here: 81.8 us
  starting transfers between devices  43.1 us (52%)
  waiting for transfers between devices  20.7 us (25%)
  Pallas kernels  8.03 us (10%)
  local copies, waits for them, and re-layouts  5.52 us (7%)
  matrix products  2.67 us (3%)
  other arithmetic  1.41 us (2%)
    ppermute x3, starting transfers between devices, on_device(): lax.ppermute(blocks[(position - offset) % group_count], 'slab', pairs)  10.1 us
    ppermute x3, starting transfers between devices, on_device(): across.append(lax.ppermute(group_blocks, 'slab', pairs))  9.56 us
    all_to_all x1, starting transfers between devices, on_device(): lax.all_to_all(outgoing, 'slab', split_axis=0, concat_axis=0, tiled=True)  9.21 us
    pallas_call x1, Pallas kernels, on_device(): pl.pallas_call(functools.partial(chain_kernel, group_size=group_size), ou...  8.03 us
    all_to_all x1, waiting for transfers between devices, on_device(): lax.all_to_all(both_sides, 'slab', split_axis=0, concat_axis=0, tiled=True)  7.43 us
    all_to_all x1, waiting for transfers between devices, on_device(): lax.all_to_all(outgoing, 'slab', split_axis=0, concat_axis=0, tiled=True)  7.38 us
    all_to_all x1, starting transfers between devices, on_device(): lax.all_to_all(both_fields, 'mode', split_axis=2, concat_axis=1, tiled=True)  6.75 us
    all_to_all x1, waiting for transfers between devices, on_device(): lax.all_to_all(both_fields, 'mode', split_axis=2, concat_axis=1, tiled=True)  5.83 us
  transfers between devices with their start and end apart: 10, of which 3 were waited for; matrix products, arithmetic and copies ran while one was open for 6% of the time, Pallas kernels for 0%

profile of v15, /device:TPU:1, one launch (start us, length us, event | category | flops | bytes accessed | tf_op | source)
XLA Modules:
  0.0 81.8 jit_solution(6448880270142573421)
XLA Ops:
  0.0 1.2 %slice_bitcast_fusion.1 = (f32[4,1,128,128]{3,2,0,1:T(8,128)S(1)}, f32[4,1,128,128]{3,2,0,1:T(8,128)S(1)}) fusion(f32[2,4,128,128]{3,2,1,0:T(8,128)} %param.12), kind=kLoop, calls=%fused_computation.13 | loop fusion | bytes 1048576 | tf_op jit(solution)/shard_map/stack;squeeze | solution.py:109
  1.3 0.8 dynamic-slice_bitcast_fusion
  2.1 6.8 %collective-permute-start = (f32[3,128,128]{2,1,0:T(8,128)}, f32[3,128,128]{2,1,0:T(8,128)S(1)}, u32[]{:S(2)}, u32[]{:S(2)}) collective-permute-start(f32[3,128,128]{2,1,0:T(8,128)} %get-tuple-element.17), channel_id=1, source_target_pairs={{15,11},{3,15},{7,3},{11,7},{0,12},{4,0},{8,4},{12,8},{1,13},{5,1}... | collective-permute-start | bytes 589832 | tf_op jit(solution)/shard_map/ppermute | solution.py:122
  8.9 0.9 %collective-permute-start.1 = (f32[3,128,128]{2,1,0:T(8,128)S(1)}, f32[3,128,128]{2,1,0:T(8,128)S(1)}, u32[]{:S(2)}, u32[]{:S(2)}) collective-permute-start(f32[3,128,128]{2,1,0:T(8,128)S(1)} %get-tuple-element.16), channel_id=1, source_target_pairs={{15,7},{3,11},{7,15},{11,3},{0,8},{4,12},{8,0},{12,4},{1,9},{5,13}... | collective-permute-start | bytes 589832 | tf_op jit(solution)/shard_map/ppermute | solution.py:122
  9.8 2.4 %collective-permute-start.2 = (f32[3,128,128]{2,1,0:T(8,128)S(1)}, f32[3,128,128]{2,1,0:T(8,128)S(1)}, u32[]{:S(2)}, u32[]{:S(2)}) collective-permute-start(f32[3,128,128]{2,1,0:T(8,128)S(1)} %get-tuple-element.15), channel_id=1, source_target_pairs={{15,3},{3,7},{7,11},{11,15},{0,4},{4,8},{8,12},{12,0},{1,5},{5,9},... | collective-permute-start | bytes 589832 | tf_op jit(solution)/shard_map/ppermute | solution.py:122
  12.2 0.7 copy.123
  12.9 6.8 %all-to-all-start = ((bf16[6,4,16,128]{3,0,1,2:T(8,128)(2,1)}), bf16[6,4,16,128]{3,0,1,2:T(8,128)(2,1)S(1)}, u32[]{:S(2)}, u32[]{:S(2)}) async-start(bf16[6,4,16,128]{3,0,1,2:T(8,128)(2,1)} %copy.123), calls=%async_computation | async-start | bytes 262144 | tf_op jit(solution)/shard_map/all_to_all | solution.py:145
  19.8 0.5 fusion
  20.7 5.8 %all-to-all-done = bf16[6,4,16,128]{3,0,1,2:T(8,128)(2,1)S(1)} async-done(((bf16[6,4,16,128]{3,0,1,2:T(8,128)(2,1)}), bf16[6,4,16,128]{3,0,1,2:T(8,128)(2,1)S(1)}, u32[]{:S(2)}, u32[]{:S(2)}) %all-to-all-start) | async-done | bytes 98336 | tf_op jit(solution)/shard_map/all_to_all | solution.py:145
  27.5 0.7 copy.135
  28.1 3.8 %all-to-all-start.1 = ((bf16[3,64,1,128]{3,0,2,1:T(4,128)(2,1)}), bf16[3,64,1,128]{3,0,2,1:T(4,128)(2,1)S(1)}, u32[]{:S(2)}, u32[]{:S(2)}) async-start(bf16[3,64,1,128]{3,0,2,1:T(4,128)(2,1)} %copy.135), calls=%async_computation.1 | async-start | bytes 131072 | tf_op jit(solution)/shard_map/all_to_all | solution.py:168
  32.0 1.0 %pad_maximum_fusion.1.refs_0_ = f32[4,3,128,128]{3,2,1,0:T(8,128)S(1)} fusion(f32[1,3,128,128]{3,2,1,0:T(8,128)} %bitcast.140, f32[1,3,128,128]{3,2,1,0:T(8,128)S(1)} %bitcast.139, f32[1,3,128,128]{3,2,1,0:T(8,128)S(1)} %bitcast.138, f32[1,3,128,128]{3,2,1,0:T(8,128)S(1)} %bitcast.130), kind=kLoop, calls=%fused_computation.10 | loop fusion | flops 589824 | bytes 1572864 | tf_op jit(solution)/shard_map/stack | solution.py:147
  33.0 6.5 %collective-permute-start.3 = (f32[4,3,128,128]{3,2,1,0:T(8,128)S(1)}, f32[4,3,128,128]{3,2,1,0:T(8,128)}, u32[]{:S(2)}, u32[]{:S(2)}) collective-permute-start(f32[4,3,128,128]{3,2,1,0:T(8,128)S(1)} %pad_maximum_fusion.1.refs_0_), channel_id=1, source_target_pairs={{1,0},{5,4},{9,8},{13,12},{17,16},{21,20},{25,24},{29,28},{33,32},... | collective-permute-start | bytes 2359304 | tf_op jit(solution)/shard_map/ppermute | solution.py:154
  39.5 1.6 %collective-permute-start.4 = (f32[4,3,128,128]{3,2,1,0:T(8,128)S(1)}, f32[4,3,128,128]{3,2,1,0:T(8,128)}, u32[]{:S(2)}, u32[]{:S(2)}) collective-permute-start(f32[4,3,128,128]{3,2,1,0:T(8,128)S(1)} %pad_maximum_fusion.1.refs_0_), channel_id=1, source_target_pairs={{2,0},{6,4},{10,8},{14,12},{18,16},{22,20},{26,24},{30,28},{34,32}... | collective-permute-start | bytes 2359304 | tf_op jit(solution)/shard_map/ppermute | solution.py:154
  41.0 1.5 %collective-permute-start.5 = (f32[4,3,128,128]{3,2,1,0:T(8,128)S(1)}, f32[4,3,128,128]{3,2,1,0:T(8,128)}, u32[]{:S(2)}, u32[]{:S(2)}) collective-permute-start(f32[4,3,128,128]{3,2,1,0:T(8,128)S(1)} %pad_maximum_fusion.1.refs_0_), channel_id=1, source_target_pairs={{15,0},{3,4},{7,8},{11,12},{31,16},{19,20},{23,24},{27,28},{47,32}... | collective-permute-start | bytes 2359304 | tf_op jit(solution)/shard_map/ppermute | solution.py:154
  43.1 0.6 copy.140
  43.8 9.2 %all-to-all-start.2 = ((f32[16,2,3,128]{3,1,2,0:T(2,128)}), f32[16,2,3,128]{3,1,2,0:T(2,128)S(1)}, u32[]{:S(2)}, u32[]{:S(2)}) async-start(f32[16,2,3,128]{3,1,2,0:T(2,128)} %copy.140), calls=%async_computation.2 | async-start | bytes 98304 | tf_op jit(solution)/shard_map/all_to_all | solution.py:182
  53.1 7.4 %all-to-all-done.2 = f32[16,2,3,128]{3,1,2,0:T(2,128)S(1)} async-done(((f32[16,2,3,128]{3,1,2,0:T(2,128)}), f32[16,2,3,128]{3,1,2,0:T(2,128)S(1)}, u32[]{:S(2)}, u32[]{:S(2)}) %all-to-all-start.2) | async-done | bytes 49184 | tf_op jit(solution)/shard_map/all_to_all | solution.py:182
  60.5 0.6 copy.141.refs_4_
  61.1 8.0 %shard_map.82 = f32[16,3,2,128]{3,2,1,0:T(2,128)} custom-call(s32[1]{0:T(128)} %bitcast.position_ref, f32[4,3,128,128]{3,2,1,0:T(8,128)} %copy-done.1, f32[4,3,128,128]{3,2,1,0:T(8,128)} %collective-permute-done.3.refs_1_, f32[4,3,128,128]{3,2,1,0:T(8,128)} %collective-permute-done.4.refs_2_, f32[4,3,128,128]{3,2,1,0:T(8,128)} %collective-permute-done.5.refs_3_, ...), custom_call_target="tpu_custom_call" | custom-call | tf_op jit(solution)/shard_map/pallas_call | solution.py:183
  69.2 3.6 %all-to-all-start.3 = ((f32[16,3,2,128]{3,2,1,0:T(2,128)}), f32[16,3,2,128]{3,2,1,0:T(2,128)S(1)}, u32[]{:S(2)}, u32[]{:S(2)}) async-start(f32[16,3,2,128]{3,2,1,0:T(2,128)} %shard_map.82), calls=%async_computation.3 | async-start | bytes 98304 | tf_op jit(solution)/shard_map/all_to_all | solution.py:192
  72.9 7.4 %all-to-all-done.3 = f32[16,3,2,128]{3,2,1,0:T(2,128)S(1)} async-done(((f32[16,3,2,128]{3,2,1,0:T(2,128)}), f32[16,3,2,128]{3,2,1,0:T(2,128)S(1)}, u32[]{:S(2)}, u32[]{:S(2)}) %all-to-all-start.3) | async-done | bytes 49184 | tf_op jit(solution)/shard_map/all_to_all | solution.py:192
  80.4 0.6 convolution_bitcast_fusion
  81.1 0.6 copy.147
  (60 shorter events, 2.3 us)
Async XLA Ops:
  0.0 19.8 %copy-start = (bf16[256,1920]{1,0:T(8,128)(2,1)S(1)}, bf16[256,1920]{1,0:T(8,128)(2,1)}, u32[]{:S(2)}) copy-start(bf16[256,1920]{1,0:T(8,128)(2,1)} %param.10) | copy-start | bytes 2949124
  0.0 1.2 %copy-start.4 = (f32[4,128,128]{2,1,0:T(8,128)S(1)}, f32[4,128,128]{2,1,0:T(8,128)}, u32[]{:S(2)}) copy-start(f32[4,128,128]{2,1,0:T(8,128)} %param.13) | copy-start | bytes 786436
  1.3 10.9 %copy-start.3 = (f32[3,4,16,128]{3,2,1,0:T(8,128)S(1)}, f32[3,4,16,128]{3,2,1,0:T(8,128)}, u32[]{:S(2)}) copy-start(f32[3,4,16,128]{3,2,1,0:T(8,128)} %param.8) | copy-start | bytes 294916
  1.3 10.9 %copy-start.6 = (bf16[3,4,16,128]{3,2,1,0:T(8,128)(2,1)S(1)}, bf16[3,4,16,128]{3,2,1,0:T(8,128)(2,1)}, u32[]{:S(2)}) copy-start(bf16[3,4,16,128]{3,2,1,0:T(8,128)(2,1)} %param.9) | copy-start | bytes 147460
  1.3 18.5 %copy-start.8 = (s32[1,256]{1,0:T(1,128)S(1)}, s32[1,256]{1,0:T(1,128)}, u32[]{:S(2)}) copy-start(s32[1,256]{1,0:T(1,128)} %param.15) | copy-start | bytes 3076
  1.3 18.5 %copy-start.9 = (s32[1,256]{1,0:T(1,128)S(1)}, s32[1,256]{1,0:T(1,128)}, u32[]{:S(2)}) copy-start(s32[1,256]{1,0:T(1,128)} %constant.117.clone.1) | copy-start | bytes 3076
  2.1 24.5 %collective-permute-start = (f32[3,128,128]{2,1,0:T(8,128)}, f32[3,128,128]{2,1,0:T(8,128)S(1)}, u32[]{:S(2)}, u32[]{:S(2)}) collective-permute-start(f32[3,128,128]{2,1,0:T(8,128)} %get-tuple-element.17), channel_id=1, source_target_pairs={{15,11},{3,15},{7,3},{11,7},{0,12},{4,0},{8,4},{12,8},{1,13},{5,1}... | collective-permute-start | bytes 589832 | tf_op jit(solution)/shard_map/ppermute | solution.py:122
  8.9 17.7 %collective-permute-start.1 = (f32[3,128,128]{2,1,0:T(8,128)S(1)}, f32[3,128,128]{2,1,0:T(8,128)S(1)}, u32[]{:S(2)}, u32[]{:S(2)}) collective-permute-start(f32[3,128,128]{2,1,0:T(8,128)S(1)} %get-tuple-element.16), channel_id=1, source_target_pairs={{15,7},{3,11},{7,15},{11,3},{0,8},{4,12},{8,0},{12,4},{1,9},{5,13}... | collective-permute-start | bytes 589832 | tf_op jit(solution)/shard_map/ppermute | solution.py:122
  9.8 16.8 %collective-permute-start.2 = (f32[3,128,128]{2,1,0:T(8,128)S(1)}, f32[3,128,128]{2,1,0:T(8,128)S(1)}, u32[]{:S(2)}, u32[]{:S(2)}) collective-permute-start(f32[3,128,128]{2,1,0:T(8,128)S(1)} %get-tuple-element.15), channel_id=1, source_target_pairs={{15,3},{3,7},{7,11},{11,15},{0,4},{4,8},{8,12},{12,0},{1,5},{5,9},... | collective-permute-start | bytes 589832 | tf_op jit(solution)/shard_map/ppermute | solution.py:122
  12.9 13.6 %all-to-all-start = ((bf16[6,4,16,128]{3,0,1,2:T(8,128)(2,1)}), bf16[6,4,16,128]{3,0,1,2:T(8,128)(2,1)S(1)}, u32[]{:S(2)}, u32[]{:S(2)}) async-start(bf16[6,4,16,128]{3,0,1,2:T(8,128)(2,1)} %copy.123), calls=%async_computation | async-start | bytes 262144 | tf_op jit(solution)/shard_map/all_to_all | solution.py:145
  26.6 5.4 %copy-start.5 = (f32[3,128,128]{2,1,0:T(8,128)}, f32[3,128,128]{2,1,0:T(8,128)S(1)}, u32[]{:S(2)}) copy-start(f32[3,128,128]{2,1,0:T(8,128)S(1)} %collective-permute-done.2) | copy-start | bytes 589828
  28.1 14.4 %all-to-all-start.1 = ((bf16[3,64,1,128]{3,0,2,1:T(4,128)(2,1)}), bf16[3,64,1,128]{3,0,2,1:T(4,128)(2,1)S(1)}, u32[]{:S(2)}, u32[]{:S(2)}) async-start(bf16[3,64,1,128]{3,0,2,1:T(4,128)(2,1)} %copy.135), calls=%async_computation.1 | async-start | bytes 131072 | tf_op jit(solution)/shard_map/all_to_all | solution.py:168
  33.0 28.1 %copy-start.1 = (f32[4,3,128,128]{3,2,1,0:T(8,128)}, f32[4,3,128,128]{3,2,1,0:T(8,128)S(1)}, u32[]{:S(2)}) copy-start(f32[4,3,128,128]{3,2,1,0:T(8,128)S(1)} %pad_maximum_fusion.1.refs_0_) | copy-start | bytes 2359300
  33.0 28.1 %collective-permute-start.3 = (f32[4,3,128,128]{3,2,1,0:T(8,128)S(1)}, f32[4,3,128,128]{3,2,1,0:T(8,128)}, u32[]{:S(2)}, u32[]{:S(2)}) collective-permute-start(f32[4,3,128,128]{3,2,1,0:T(8,128)S(1)} %pad_maximum_fusion.1.refs_0_), channel_id=1, source_target_pairs={{1,0},{5,4},{9,8},{13,12},{17,16},{21,20},{25,24},{29,28},{33,32},... | collective-permute-start | bytes 2359304 | tf_op jit(solution)/shard_map/ppermute | solution.py:154
  39.5 21.7 %collective-permute-start.4 = (f32[4,3,128,128]{3,2,1,0:T(8,128)S(1)}, f32[4,3,128,128]{3,2,1,0:T(8,128)}, u32[]{:S(2)}, u32[]{:S(2)}) collective-permute-start(f32[4,3,128,128]{3,2,1,0:T(8,128)S(1)} %pad_maximum_fusion.1.refs_0_), channel_id=1, source_target_pairs={{2,0},{6,4},{10,8},{14,12},{18,16},{22,20},{26,24},{30,28},{34,32}... | collective-permute-start | bytes 2359304 | tf_op jit(solution)/shard_map/ppermute | solution.py:154
  41.0 20.1 %collective-permute-start.5 = (f32[4,3,128,128]{3,2,1,0:T(8,128)S(1)}, f32[4,3,128,128]{3,2,1,0:T(8,128)}, u32[]{:S(2)}, u32[]{:S(2)}) collective-permute-start(f32[4,3,128,128]{3,2,1,0:T(8,128)S(1)} %pad_maximum_fusion.1.refs_0_), channel_id=1, source_target_pairs={{15,0},{3,4},{7,8},{11,12},{31,16},{19,20},{23,24},{27,28},{47,32}... | collective-permute-start | bytes 2359304 | tf_op jit(solution)/shard_map/ppermute | solution.py:154
  43.8 16.7 %all-to-all-start.2 = ((f32[16,2,3,128]{3,1,2,0:T(2,128)}), f32[16,2,3,128]{3,1,2,0:T(2,128)S(1)}, u32[]{:S(2)}, u32[]{:S(2)}) async-start(f32[16,2,3,128]{3,1,2,0:T(2,128)} %copy.140), calls=%async_computation.2 | async-start | bytes 98304 | tf_op jit(solution)/shard_map/all_to_all | solution.py:182
  61.1 11.7 %copy-start.7 = (f32[15,128]{1,0:T(8,128)S(1)}, f32[15,128]{1,0:T(8,128)}, u32[]{:S(2)}) copy-start(f32[15,128]{1,0:T(8,128)} %param.14) | copy-start | bytes 23044
  61.1 19.3 %copy-start.2 = (bf16[1920,256]{1,0:T(8,128)(2,1)S(1)}, bf16[1920,256]{1,0:T(8,128)(2,1)}, u32[]{:S(2)}) copy-start(bf16[1920,256]{1,0:T(8,128)(2,1)} %param.11) | copy-start | bytes 2949124
  69.2 11.1 %all-to-all-start.3 = ((f32[16,3,2,128]{3,2,1,0:T(2,128)}), f32[16,3,2,128]{3,2,1,0:T(2,128)S(1)}, u32[]{:S(2)}, u32[]{:S(2)}) async-start(f32[16,3,2,128]{3,2,1,0:T(2,128)} %shard_map.82), calls=%async_computation.3 | async-start | bytes 98304 | tf_op jit(solution)/shard_map/all_to_all | solution.py:192

commit v16 on v15

--- a/solution.py
+++ b/solution.py
@@ -195,14 +195,17 @@
     right_values = mine[:, :, 1]
 
     boundary_line = jnp.concatenate([left_values, right_values], axis=2).astype(jnp.bfloat16)
+    extend_lines = jnp.pad(extend_cols, ((point_total, 0), (0, 0)))
     extension = jnp.einsum(
-        "hg,dog->odh", extend_cols, boundary_line, preferred_element_type=jnp.float32
-    )
-    extension = extension.reshape(components, planes_dev, line_count - 1, point_total)
+        "hg,dog->odh", extend_lines, boundary_line, preferred_element_type=jnp.float32
+    )
+    extension = extension.reshape(components, planes_dev, line_count, point_total)
     inner_rhs = LAMBDA_TIMESTEP * velocity[:, :, 1:, :] + nonlin[:, :, 1:, :].astype(jnp.float32)
-    new_inner = extension + inner_rhs / (interior_diag[None, None] + shifts[None, :, None, None])
+    scaled = inner_rhs / (interior_diag[None, None] + shifts[None, :, None, None])
+    interior = jnp.pad(scaled, ((0, 0), (0, 0), (1, 0), (0, 0)))
     line_zero = jnp.swapaxes(left_values, 0, 1)
-    return jnp.concatenate([line_zero[:, :, None, :], new_inner], axis=2)
+    walls = jnp.pad(line_zero[:, :, None, :], ((0, 0), (0, 0), (0, line_count - 1), (0, 0)))
+    return extension + interior + walls
 
 
 def solution(mesh):

time: 82.2 us -> 90.3 us (1.099)
  blocking collectives: 0 us -> 18.3 us
  starting transfers between devices: 43.1 us -> 33.1 us
  waiting for transfers between devices: 20.7 us -> 12.6 us
  local copies, waits for them, and re-layouts: 5.52 us -> 9.49 us
  other arithmetic: 1.41 us -> 4.03 us
  matrix products: 2.67 us -> 3.58 us
    all_to_all x0 -> x1, blocking collectives: none -> 18.3 us  [on_device(): lax.all_to_all(outgoing, 'slab', split_axis=0, concat_axis=0, tiled=True)]
    all_to_all x1 -> x0, starting transfers between devices: 9.21 us -> none  [on_device(): lax.all_to_all(outgoing, 'slab', split_axis=0, concat_axis=0, tiled=True)]
    all_to_all x1 -> x0, waiting for transfers between devices: 7.38 us -> none  [on_device(): lax.all_to_all(outgoing, 'slab', split_axis=0, concat_axis=0, tiled=True)]
    reshape x0 -> x3, local copies, waits for them, and re-layouts: none -> 2.95 us  [the longest x1 1.45 us: on_device(): nonlin[:, :, 1:, :].reshape(components, planes_dev, -1)]
    div x0 -> x1, other arithmetic: none -> 1.59 us  [on_device(): inner_rhs / (interior_diag[None, None] + shifts[None, :, None, None])]
    add x1 -> x2, other arithmetic: 0.07 us -> 1.47 us  [the longest x1 0.81 us: on_device(): LAMBDA_TIMESTEP * velocity[:, :, 0, :]]
    ppermute x3, starting transfers between devices: 9.56 us -> 8.48 us  [on_device(): across.append(lax.ppermute(group_blocks, 'slab', pairs))]
    another operation x1, other arithmetic: 0.98 us -> 0.05 us  [on_device(): group_blocks = jnp.stack(within)]
  transfers between devices with their start and end apart: 10 -> 9, of which waited for: 3 -> 2; matrix products, arithmetic and copies ran while one was open for 6% -> 13% of each run, Pallas kernels for 0% -> 0%
where the time goes in v16:
time: 90.3 us; the launch traced here: 89.6 us
  starting transfers between devices  33.1 us (37%)
  blocking collectives  18.3 us (20%)
  waiting for transfers between devices  12.6 us (14%)
  local copies, waits for them, and re-layouts  9.49 us (11%)
  Pallas kernels  8.09 us (9%)
  other arithmetic  4.03 us (4%)
  matrix products  3.58 us (4%)
    all_to_all x1, blocking collectives, on_device(): lax.all_to_all(outgoing, 'slab', split_axis=0, concat_axis=0, tiled=True)  18.3 us
    ppermute x3, starting transfers between devices, on_device(): lax.ppermute(blocks[(position - offset) % group_count], 'slab', pairs)  10.1 us
    ppermute x3, starting transfers between devices, on_device(): across.append(lax.ppermute(group_blocks, 'slab', pairs))  8.48 us
    pallas_call x1, Pallas kernels, on_device(): pl.pallas_call(functools.partial(chain_kernel, group_size=group_size), ou...  8.09 us
    all_to_all x1, waiting for transfers between devices, on_device(): lax.all_to_all(both_sides, 'slab', split_axis=0, concat_axis=0, tiled=True)  7.02 us
    all_to_all x1, starting transfers between devices, on_device(): lax.all_to_all(both_fields, 'mode', split_axis=2, concat_axis=1, tiled=True)  6.75 us
    all_to_all x1, waiting for transfers between devices, on_device(): lax.all_to_all(both_fields, 'mode', split_axis=2, concat_axis=1, tiled=True)  5.53 us
    all_to_all x1, starting transfers between devices, on_device(): lax.all_to_all(nonlin_lines, 'mode', split_axis=1, concat_axis=2, tiled=T...  4.15 us
  transfers between devices with their start and end apart: 9, of which 2 were waited for; matrix products, arithmetic and copies ran while one was open for 13% of the time, Pallas kernels for 0%

profile of v16, /device:TPU:1, one launch (start us, length us, event | category | flops | bytes accessed | tf_op | source)
XLA Modules:
  0.0 89.6 jit_solution(15753280844238649759)
XLA Ops:
  0.0 1.2 %slice_bitcast_fusion.1 = (f32[4,1,128,128]{3,2,0,1:T(8,128)S(1)}, f32[4,1,128,128]{3,2,0,1:T(8,128)S(1)}) fusion(f32[2,4,128,128]{3,2,1,0:T(8,128)} %param.12), kind=kLoop, calls=%fused_computation.15 | loop fusion | bytes 1048576 | tf_op jit(solution)/shard_map/stack;squeeze | solution.py:109
  1.3 0.7 dynamic-slice_bitcast_fusion
  2.1 6.8 %collective-permute-start = (f32[3,128,128]{2,1,0:T(8,128)}, f32[3,128,128]{2,1,0:T(8,128)S(1)}, u32[]{:S(2)}, u32[]{:S(2)}) collective-permute-start(f32[3,128,128]{2,1,0:T(8,128)} %get-tuple-element.17), channel_id=1, source_target_pairs={{15,11},{3,15},{7,3},{11,7},{0,12},{4,0},{8,4},{12,8},{1,13},{5,1}... | collective-permute-start | bytes 589832 | tf_op jit(solution)/shard_map/ppermute | solution.py:122
  8.9 0.9 collective-permute-start.1
  9.8 2.4 %collective-permute-start.2 = (f32[3,128,128]{2,1,0:T(8,128)S(1)}, f32[3,128,128]{2,1,0:T(8,128)S(1)}, u32[]{:S(2)}, u32[]{:S(2)}) collective-permute-start(f32[3,128,128]{2,1,0:T(8,128)S(1)} %get-tuple-element.15), channel_id=1, source_target_pairs={{15,3},{3,7},{7,11},{11,15},{0,4},{4,8},{8,12},{12,0},{1,5},{5,9},... | collective-permute-start | bytes 589832 | tf_op jit(solution)/shard_map/ppermute | solution.py:122
  12.2 0.7 copy.126
  12.9 6.8 %all-to-all-start = ((bf16[6,4,16,128]{3,0,1,2:T(8,128)(2,1)}), bf16[6,4,16,128]{3,0,1,2:T(8,128)(2,1)S(1)}, u32[]{:S(2)}, u32[]{:S(2)}) async-start(bf16[6,4,16,128]{3,0,1,2:T(8,128)(2,1)} %copy.126), calls=%async_computation | async-start | bytes 262144 | tf_op jit(solution)/shard_map/all_to_all | solution.py:145
  21.0 5.5 %all-to-all-done = bf16[6,4,16,128]{3,0,1,2:T(8,128)(2,1)S(1)} async-done(((bf16[6,4,16,128]{3,0,1,2:T(8,128)(2,1)}), bf16[6,4,16,128]{3,0,1,2:T(8,128)(2,1)S(1)}, u32[]{:S(2)}, u32[]{:S(2)}) %all-to-all-start) | async-done | bytes 98336 | tf_op jit(solution)/shard_map/all_to_all | solution.py:145
  27.5 0.7 copy.136
  28.1 4.2 %all-to-all-start.1 = ((bf16[3,64,1,128]{3,0,2,1:T(4,128)(2,1)}), bf16[3,64,1,128]{3,0,2,1:T(4,128)(2,1)}, u32[]{:S(2)}, u32[]{:S(2)}) async-start(bf16[3,64,1,128]{3,0,2,1:T(4,128)(2,1)} %copy.136), calls=%async_computation.1 | async-start | bytes 131072 | tf_op jit(solution)/shard_map/all_to_all | solution.py:168
  32.4 5.3 %collective-permute-start.3 = (f32[4,3,128,128]{3,2,1,0:T(8,128)S(1)}, f32[4,3,128,128]{3,2,1,0:T(8,128)S(1)}, u32[]{:S(2)}, u32[]{:S(2)}) collective-permute-start(f32[4,3,128,128]{3,2,1,0:T(8,128)S(1)} %pad_maximum_fusion.1.refs_0_), channel_id=1, source_target_pairs={{1,0},{5,4},{9,8},{13,12},{17,16},{21,20},{25,24},{29,28},{33,32},... | collective-permute-start | bytes 2359304 | tf_op jit(solution)/shard_map/ppermute | solution.py:154
  37.7 1.6 %collective-permute-start.4 = (f32[4,3,128,128]{3,2,1,0:T(8,128)S(1)}, f32[4,3,128,128]{3,2,1,0:T(8,128)}, u32[]{:S(2)}, u32[]{:S(2)}) collective-permute-start(f32[4,3,128,128]{3,2,1,0:T(8,128)S(1)} %pad_maximum_fusion.1.refs_0_), channel_id=1, source_target_pairs={{2,0},{6,4},{10,8},{14,12},{18,16},{22,20},{26,24},{30,28},{34,32}... | collective-permute-start | bytes 2359304 | tf_op jit(solution)/shard_map/ppermute | solution.py:154
  39.3 1.6 %collective-permute-start.5 = (f32[4,3,128,128]{3,2,1,0:T(8,128)S(1)}, f32[4,3,128,128]{3,2,1,0:T(8,128)}, u32[]{:S(2)}, u32[]{:S(2)}) collective-permute-start(f32[4,3,128,128]{3,2,1,0:T(8,128)S(1)} %pad_maximum_fusion.1.refs_0_), channel_id=1, source_target_pairs={{15,0},{3,4},{7,8},{11,12},{31,16},{19,20},{23,24},{27,28},{47,32}... | collective-permute-start | bytes 2359304 | tf_op jit(solution)/shard_map/ppermute | solution.py:154
  40.9 0.9 copy.155
  42.3 0.8 fusion.48
  43.2 1.6 %add_divide_fusion = (f32[3,4,15,128]{3,2,1,0:T(8,128)}, bf16[3,4,15,128]{3,2,1,0:T(8,128)(2,1)}) fusion(f32[3,4,16,128]{3,2,1,0:T(8,128)} %param.8, f32[4,15,128]{2,1,0:T(8,128)} %broadcast_add_fusion, bf16[3,4,16,128]{3,2,1,0:T(8,128)(2,1)S(1)} %bitcast.117), kind=kLoop, calls=%fused_computation.26 | loop fusion | flops 115200 | bytes 307200 | tf_op jit(solution)/shard_map/div | solution.py:204
  44.7 1.4 %reshape.126 = bf16[3,4,1920]{2,1,0:T(4,128)(2,1)} reshape(bf16[3,4,15,128]{3,2,1,0:T(8,128)(2,1)} %get-tuple-element.24) | data formatting | bytes 92160 | tf_op jit(solution)/shard_map/reshape | solution.py:163
  46.2 1.4 %reshape.128 = bf16[3,4,1920]{2,1,0:T(4,128)(2,1)} reshape(bf16[3,4,15,128]{3,2,1,0:T(8,128)(2,1)} %slice.132) | data formatting | bytes 92160 | tf_op jit(solution)/shard_map/reshape | solution.py:169
  47.6 1.2 %fusion.67 = f32[3,4,256]{2,1,0:T(4,128)S(1)} fusion(bf16[3,4,1920]{2,1,0:T(4,128)(2,1)} %reshape.126, bf16[256,1920,1]{1,0,2:T(8,128)(2,1)S(1)} %fusion), kind=kOutput, calls=%fused_computation.117 | convolution fusion | flops 11796480 | bytes 1041408 | tf_op jit(solution)/shard_map/hf,vqf->qvh/dot_general | solution.py:165
  49.4 18.3 %all_to_all.46 = f32[16,2,3,128]{3,1,2,0:T(2,128)S(1)} all-to-all(f32[16,2,3,128]{3,1,2,0:T(2,128)S(1)} %copy.139), channel_id=1, replica_groups=mesh['mode'=16,'slab'=16] {'slab'}, dimensions={0} | all-to-all | bytes 98304 | tf_op jit(solution)/shard_map/all_to_all | solution.py:182
  68.4 0.9 copy-done.3
  69.2 8.1 %shard_map.82 = f32[16,3,2,128]{3,2,1,0:T(2,128)} custom-call(s32[1]{0:T(128)} %bitcast.position_ref, f32[4,3,128,128]{3,2,1,0:T(8,128)} %copy-done.1, f32[4,3,128,128]{3,2,1,0:T(8,128)} %copy-done.3, f32[4,3,128,128]{3,2,1,0:T(8,128)} %collective-permute-done.4.refs_2_, f32[4,3,128,128]{3,2,1,0:T(8,128)} %collective-permute-done.5.refs_3_, ...), custom_call_target="tpu_custom_call" | custom-call | tf_op jit(solution)/shard_map/pallas_call | solution.py:183
  77.3 3.6 %all-to-all-start.3 = ((f32[16,3,2,128]{3,2,1,0:T(2,128)}), f32[16,3,2,128]{3,2,1,0:T(2,128)S(1)}, u32[]{:S(2)}, u32[]{:S(2)}) async-start(f32[16,3,2,128]{3,2,1,0:T(2,128)} %shard_map.82), calls=%async_computation.3 | async-start | bytes 98304 | tf_op jit(solution)/shard_map/all_to_all | solution.py:192
  81.5 7.0 %all-to-all-done.3 = f32[16,3,2,128]{3,2,1,0:T(2,128)S(1)} async-done(((f32[16,3,2,128]{3,2,1,0:T(2,128)}), f32[16,3,2,128]{3,2,1,0:T(2,128)S(1)}, u32[]{:S(2)}, u32[]{:S(2)}) %all-to-all-start.3) | async-done | bytes 49184 | tf_op jit(solution)/shard_map/all_to_all | solution.py:192
  (66 shorter events, 5.6 us)
Async XLA Ops:
  0.0 20.5 %copy-start = (bf16[256,1920]{1,0:T(8,128)(2,1)S(1)}, bf16[256,1920]{1,0:T(8,128)(2,1)}, u32[]{:S(2)}) copy-start(bf16[256,1920]{1,0:T(8,128)(2,1)} %param.10) | copy-start | bytes 2949124
  0.0 1.2 %copy-start.6 = (f32[4,128,128]{2,1,0:T(8,128)S(1)}, f32[4,128,128]{2,1,0:T(8,128)}, u32[]{:S(2)}) copy-start(f32[4,128,128]{2,1,0:T(8,128)} %param.13) | copy-start | bytes 786436
  1.3 10.9 %copy-start.4 = (f32[3,4,16,128]{3,2,1,0:T(8,128)S(1)}, f32[3,4,16,128]{3,2,1,0:T(8,128)}, u32[]{:S(2)}) copy-start(f32[3,4,16,128]{3,2,1,0:T(8,128)} %param.8) | copy-start | bytes 294916
  1.3 10.9 %copy-start.8 = (bf16[3,4,16,128]{3,2,1,0:T(8,128)(2,1)S(1)}, bf16[3,4,16,128]{3,2,1,0:T(8,128)(2,1)}, u32[]{:S(2)}) copy-start(bf16[3,4,16,128]{3,2,1,0:T(8,128)(2,1)} %param.9) | copy-start | bytes 147460
  1.3 18.5 %copy-start.9 = (f32[15,128]{1,0:T(8,128)S(1)}, f32[15,128]{1,0:T(8,128)}, u32[]{:S(2)}) copy-start(f32[15,128]{1,0:T(8,128)} %param.14) | copy-start | bytes 23044
  1.3 19.2 %copy-start.10 = (s32[1,256]{1,0:T(1,128)S(1)}, s32[1,256]{1,0:T(1,128)}, u32[]{:S(2)}) copy-start(s32[1,256]{1,0:T(1,128)} %param.15) | copy-start | bytes 3076
  1.3 19.2 %copy-start.11 = (s32[1,256]{1,0:T(1,128)S(1)}, s32[1,256]{1,0:T(1,128)}, u32[]{:S(2)}) copy-start(s32[1,256]{1,0:T(1,128)} %constant.119.clone.1) | copy-start | bytes 3076
  2.1 24.5 %collective-permute-start = (f32[3,128,128]{2,1,0:T(8,128)}, f32[3,128,128]{2,1,0:T(8,128)S(1)}, u32[]{:S(2)}, u32[]{:S(2)}) collective-permute-start(f32[3,128,128]{2,1,0:T(8,128)} %get-tuple-element.17), channel_id=1, source_target_pairs={{15,11},{3,15},{7,3},{11,7},{0,12},{4,0},{8,4},{12,8},{1,13},{5,1}... | collective-permute-start | bytes 589832 | tf_op jit(solution)/shard_map/ppermute | solution.py:122
  8.9 17.7 %collective-permute-start.1 = (f32[3,128,128]{2,1,0:T(8,128)S(1)}, f32[3,128,128]{2,1,0:T(8,128)S(1)}, u32[]{:S(2)}, u32[]{:S(2)}) collective-permute-start(f32[3,128,128]{2,1,0:T(8,128)S(1)} %get-tuple-element.16), channel_id=1, source_target_pairs={{15,7},{3,11},{7,15},{11,3},{0,8},{4,12},{8,0},{12,4},{1,9},{5,13}... | collective-permute-start | bytes 589832 | tf_op jit(solution)/shard_map/ppermute | solution.py:122
  9.8 16.8 %collective-permute-start.2 = (f32[3,128,128]{2,1,0:T(8,128)S(1)}, f32[3,128,128]{2,1,0:T(8,128)S(1)}, u32[]{:S(2)}, u32[]{:S(2)}) collective-permute-start(f32[3,128,128]{2,1,0:T(8,128)S(1)} %get-tuple-element.15), channel_id=1, source_target_pairs={{15,3},{3,7},{7,11},{11,15},{0,4},{4,8},{8,12},{12,0},{1,5},{5,9},... | collective-permute-start | bytes 589832 | tf_op jit(solution)/shard_map/ppermute | solution.py:122
  12.9 13.6 %all-to-all-start = ((bf16[6,4,16,128]{3,0,1,2:T(8,128)(2,1)}), bf16[6,4,16,128]{3,0,1,2:T(8,128)(2,1)S(1)}, u32[]{:S(2)}, u32[]{:S(2)}) async-start(bf16[6,4,16,128]{3,0,1,2:T(8,128)(2,1)} %copy.126), calls=%async_computation | async-start | bytes 262144 | tf_op jit(solution)/shard_map/all_to_all | solution.py:145
  28.1 12.7 %all-to-all-start.1 = ((bf16[3,64,1,128]{3,0,2,1:T(4,128)(2,1)}), bf16[3,64,1,128]{3,0,2,1:T(4,128)(2,1)}, u32[]{:S(2)}, u32[]{:S(2)}) async-start(bf16[3,64,1,128]{3,0,2,1:T(4,128)(2,1)} %copy.136), calls=%async_computation.1 | async-start | bytes 131072 | tf_op jit(solution)/shard_map/all_to_all | solution.py:168
  32.4 16.9 %copy-start.1 = (f32[4,3,128,128]{3,2,1,0:T(8,128)}, f32[4,3,128,128]{3,2,1,0:T(8,128)S(1)}, u32[]{:S(2)}) copy-start(f32[4,3,128,128]{3,2,1,0:T(8,128)S(1)} %pad_maximum_fusion.1.refs_0_) | copy-start | bytes 2359300
  32.4 36.0 %collective-permute-start.3 = (f32[4,3,128,128]{3,2,1,0:T(8,128)S(1)}, f32[4,3,128,128]{3,2,1,0:T(8,128)S(1)}, u32[]{:S(2)}, u32[]{:S(2)}) collective-permute-start(f32[4,3,128,128]{3,2,1,0:T(8,128)S(1)} %pad_maximum_fusion.1.refs_0_), channel_id=1, source_target_pairs={{1,0},{5,4},{9,8},{13,12},{17,16},{21,20},{25,24},{29,28},{33,32},... | collective-permute-start | bytes 2359304 | tf_op jit(solution)/shard_map/ppermute | solution.py:154
  37.7 30.7 %collective-permute-start.4 = (f32[4,3,128,128]{3,2,1,0:T(8,128)S(1)}, f32[4,3,128,128]{3,2,1,0:T(8,128)}, u32[]{:S(2)}, u32[]{:S(2)}) collective-permute-start(f32[4,3,128,128]{3,2,1,0:T(8,128)S(1)} %pad_maximum_fusion.1.refs_0_), channel_id=1, source_target_pairs={{2,0},{6,4},{10,8},{14,12},{18,16},{22,20},{26,24},{30,28},{34,32}... | collective-permute-start | bytes 2359304 | tf_op jit(solution)/shard_map/ppermute | solution.py:154
  39.3 29.1 %collective-permute-start.5 = (f32[4,3,128,128]{3,2,1,0:T(8,128)S(1)}, f32[4,3,128,128]{3,2,1,0:T(8,128)}, u32[]{:S(2)}, u32[]{:S(2)}) collective-permute-start(f32[4,3,128,128]{3,2,1,0:T(8,128)S(1)} %pad_maximum_fusion.1.refs_0_), channel_id=1, source_target_pairs={{15,0},{3,4},{7,8},{11,12},{31,16},{19,20},{23,24},{27,28},{47,32}... | collective-permute-start | bytes 2359304 | tf_op jit(solution)/shard_map/ppermute | solution.py:154
  47.6 1.2 %copy-start.7 = (bf16[3,4,1920]{2,1,0:T(4,128)(2,1)S(1)}, bf16[3,4,1920]{2,1,0:T(4,128)(2,1)}, u32[]{:S(2)}) copy-start(bf16[3,4,1920]{2,1,0:T(4,128)(2,1)} %reshape.128) | copy-start | bytes 138244
  68.4 0.9 copy-start.3
  69.2 11.7 %copy-start.2 = (bf16[1920,256]{1,0:T(8,128)(2,1)S(1)}, bf16[1920,256]{1,0:T(8,128)(2,1)}, u32[]{:S(2)}) copy-start(bf16[1920,256]{1,0:T(8,128)(2,1)} %param.11) | copy-start | bytes 2949124
  77.3 11.2 %all-to-all-start.3 = ((f32[16,3,2,128]{3,2,1,0:T(2,128)}), f32[16,3,2,128]{3,2,1,0:T(2,128)S(1)}, u32[]{:S(2)}, u32[]{:S(2)}) async-start(f32[16,3,2,128]{3,2,1,0:T(2,128)} %shard_map.82), calls=%async_computation.3 | async-start | bytes 98304 | tf_op jit(solution)/shard_map/all_to_all | solution.py:192
  81.5 7.4 %copy-start.5 = (f32[3,4,15,128]{3,2,1,0:T(8,128)S(1)}, f32[3,4,15,128]{3,2,1,0:T(8,128)}, u32[]{:S(2)}) copy-start(f32[3,4,15,128]{3,2,1,0:T(8,128)} %get-tuple-element.23) | copy-start | bytes 276484

commit v17 on v15

--- a/solution.py
+++ b/solution.py
@@ -66,14 +66,16 @@
             return group_refs[group_slot].at[spot_slot]
 
         zero = jnp.zeros(sides_ref.shape[2:], jnp.float32)
-        forward_values = [zero]
-        for k in range(1, slab_count):
+        forward_values = [zero, sides_ref[1, 0] + sides_ref[0, 1]]
+        for k in range(2, slab_count):
             source = sides_ref[k, 0] + sides_ref[k - 1, 1]
             forward_values.append(source - apply(blocks_of(k)[0], forward_values[-1]))
         after = zero
         for k in range(slab_count - 1, 0, -1):
             blocks = blocks_of(k)
-            solved = apply(blocks[2], forward_values[k]) - apply(blocks[1], after)
+            solved = apply(blocks[2], forward_values[k])
+            if k < slab_count - 1:
+                solved = solved - apply(blocks[1], after)
             out_ref[k] = jnp.stack([solved, after], axis=1)
             after = solved
         out_ref[0] = jnp.stack([zero, after], axis=1)

time: 82.2 us -> 82 us (level)
  no operation moved by 1% of the time
where the time goes in v17:
time: 82 us; the launch traced here: 81.6 us
  starting transfers between devices  43.1 us (53%)
  waiting for transfers between devices  20.7 us (25%)
  Pallas kernels  7.85 us (10%)
  local copies, waits for them, and re-layouts  5.52 us (7%)
  matrix products  2.67 us (3%)
  other arithmetic  1.41 us (2%)
    ppermute x3, starting transfers between devices, on_device(): lax.ppermute(blocks[(position - offset) % group_count], 'slab', pairs)  10.1 us
    ppermute x3, starting transfers between devices, on_device(): across.append(lax.ppermute(group_blocks, 'slab', pairs))  9.56 us
    all_to_all x1, starting transfers between devices, on_device(): lax.all_to_all(outgoing, 'slab', split_axis=0, concat_axis=0, tiled=True)  9.21 us
    pallas_call x1, Pallas kernels, on_device(): pl.pallas_call(functools.partial(chain_kernel, group_size=group_size), ou...  7.85 us
    all_to_all x1, waiting for transfers between devices, on_device(): lax.all_to_all(both_sides, 'slab', split_axis=0, concat_axis=0, tiled=True)  7.43 us
    all_to_all x1, waiting for transfers between devices, on_device(): lax.all_to_all(outgoing, 'slab', split_axis=0, concat_axis=0, tiled=True)  7.38 us
    all_to_all x1, starting transfers between devices, on_device(): lax.all_to_all(both_fields, 'mode', split_axis=2, concat_axis=1, tiled=True)  6.75 us
    all_to_all x1, waiting for transfers between devices, on_device(): lax.all_to_all(both_fields, 'mode', split_axis=2, concat_axis=1, tiled=True)  5.83 us
  transfers between devices with their start and end apart: 10, of which 3 were waited for; matrix products, arithmetic and copies ran while one was open for 6% of the time, Pallas kernels for 0%

profile of v17, /device:TPU:1, one launch (start us, length us, event | category | flops | bytes accessed | tf_op | source)
XLA Modules:
  0.0 81.6 jit_solution(15736233661529364538)
XLA Ops:
  0.0 1.2 %slice_bitcast_fusion.1 = (f32[4,1,128,128]{3,2,0,1:T(8,128)S(1)}, f32[4,1,128,128]{3,2,0,1:T(8,128)S(1)}) fusion(f32[2,4,128,128]{3,2,1,0:T(8,128)} %param.12), kind=kLoop, calls=%fused_computation.13 | loop fusion | bytes 1048576 | tf_op jit(solution)/shard_map/stack;squeeze | solution.py:111
  1.3 0.8 dynamic-slice_bitcast_fusion
  2.1 6.8 %collective-permute-start = (f32[3,128,128]{2,1,0:T(8,128)}, f32[3,128,128]{2,1,0:T(8,128)S(1)}, u32[]{:S(2)}, u32[]{:S(2)}) collective-permute-start(f32[3,128,128]{2,1,0:T(8,128)} %get-tuple-element.17), channel_id=1, source_target_pairs={{15,11},{3,15},{7,3},{11,7},{0,12},{4,0},{8,4},{12,8},{1,13},{5,1}... | collective-permute-start | bytes 589832 | tf_op jit(solution)/shard_map/ppermute | solution.py:124
  8.9 0.9 %collective-permute-start.1 = (f32[3,128,128]{2,1,0:T(8,128)S(1)}, f32[3,128,128]{2,1,0:T(8,128)S(1)}, u32[]{:S(2)}, u32[]{:S(2)}) collective-permute-start(f32[3,128,128]{2,1,0:T(8,128)S(1)} %get-tuple-element.16), channel_id=1, source_target_pairs={{15,7},{3,11},{7,15},{11,3},{0,8},{4,12},{8,0},{12,4},{1,9},{5,13}... | collective-permute-start | bytes 589832 | tf_op jit(solution)/shard_map/ppermute | solution.py:124
  9.8 2.4 %collective-permute-start.2 = (f32[3,128,128]{2,1,0:T(8,128)S(1)}, f32[3,128,128]{2,1,0:T(8,128)S(1)}, u32[]{:S(2)}, u32[]{:S(2)}) collective-permute-start(f32[3,128,128]{2,1,0:T(8,128)S(1)} %get-tuple-element.15), channel_id=1, source_target_pairs={{15,3},{3,7},{7,11},{11,15},{0,4},{4,8},{8,12},{12,0},{1,5},{5,9},... | collective-permute-start | bytes 589832 | tf_op jit(solution)/shard_map/ppermute | solution.py:124
  12.2 0.7 copy.123
  12.9 6.8 %all-to-all-start = ((bf16[6,4,16,128]{3,0,1,2:T(8,128)(2,1)}), bf16[6,4,16,128]{3,0,1,2:T(8,128)(2,1)S(1)}, u32[]{:S(2)}, u32[]{:S(2)}) async-start(bf16[6,4,16,128]{3,0,1,2:T(8,128)(2,1)} %copy.123), calls=%async_computation | async-start | bytes 262144 | tf_op jit(solution)/shard_map/all_to_all | solution.py:147
  19.8 0.5 fusion
  20.7 5.8 %all-to-all-done = bf16[6,4,16,128]{3,0,1,2:T(8,128)(2,1)S(1)} async-done(((bf16[6,4,16,128]{3,0,1,2:T(8,128)(2,1)}), bf16[6,4,16,128]{3,0,1,2:T(8,128)(2,1)S(1)}, u32[]{:S(2)}, u32[]{:S(2)}) %all-to-all-start) | async-done | bytes 98336 | tf_op jit(solution)/shard_map/all_to_all | solution.py:147
  27.5 0.7 copy.135
  28.1 3.8 %all-to-all-start.1 = ((bf16[3,64,1,128]{3,0,2,1:T(4,128)(2,1)}), bf16[3,64,1,128]{3,0,2,1:T(4,128)(2,1)S(1)}, u32[]{:S(2)}, u32[]{:S(2)}) async-start(bf16[3,64,1,128]{3,0,2,1:T(4,128)(2,1)} %copy.135), calls=%async_computation.1 | async-start | bytes 131072 | tf_op jit(solution)/shard_map/all_to_all | solution.py:170
  32.0 1.0 %pad_maximum_fusion.1.refs_0_ = f32[4,3,128,128]{3,2,1,0:T(8,128)S(1)} fusion(f32[1,3,128,128]{3,2,1,0:T(8,128)} %bitcast.140, f32[1,3,128,128]{3,2,1,0:T(8,128)S(1)} %bitcast.139, f32[1,3,128,128]{3,2,1,0:T(8,128)S(1)} %bitcast.138, f32[1,3,128,128]{3,2,1,0:T(8,128)S(1)} %bitcast.130), kind=kLoop, calls=%fused_computation.10 | loop fusion | flops 589824 | bytes 1572864 | tf_op jit(solution)/shard_map/stack | solution.py:149
  33.0 6.5 %collective-permute-start.3 = (f32[4,3,128,128]{3,2,1,0:T(8,128)S(1)}, f32[4,3,128,128]{3,2,1,0:T(8,128)}, u32[]{:S(2)}, u32[]{:S(2)}) collective-permute-start(f32[4,3,128,128]{3,2,1,0:T(8,128)S(1)} %pad_maximum_fusion.1.refs_0_), channel_id=1, source_target_pairs={{1,0},{5,4},{9,8},{13,12},{17,16},{21,20},{25,24},{29,28},{33,32},... | collective-permute-start | bytes 2359304 | tf_op jit(solution)/shard_map/ppermute | solution.py:156
  39.5 1.6 %collective-permute-start.4 = (f32[4,3,128,128]{3,2,1,0:T(8,128)S(1)}, f32[4,3,128,128]{3,2,1,0:T(8,128)}, u32[]{:S(2)}, u32[]{:S(2)}) collective-permute-start(f32[4,3,128,128]{3,2,1,0:T(8,128)S(1)} %pad_maximum_fusion.1.refs_0_), channel_id=1, source_target_pairs={{2,0},{6,4},{10,8},{14,12},{18,16},{22,20},{26,24},{30,28},{34,32}... | collective-permute-start | bytes 2359304 | tf_op jit(solution)/shard_map/ppermute | solution.py:156
  41.0 1.5 %collective-permute-start.5 = (f32[4,3,128,128]{3,2,1,0:T(8,128)S(1)}, f32[4,3,128,128]{3,2,1,0:T(8,128)}, u32[]{:S(2)}, u32[]{:S(2)}) collective-permute-start(f32[4,3,128,128]{3,2,1,0:T(8,128)S(1)} %pad_maximum_fusion.1.refs_0_), channel_id=1, source_target_pairs={{15,0},{3,4},{7,8},{11,12},{31,16},{19,20},{23,24},{27,28},{47,32}... | collective-permute-start | bytes 2359304 | tf_op jit(solution)/shard_map/ppermute | solution.py:156
  43.1 0.6 copy.140
  43.8 9.2 %all-to-all-start.2 = ((f32[16,2,3,128]{3,1,2,0:T(2,128)}), f32[16,2,3,128]{3,1,2,0:T(2,128)S(1)}, u32[]{:S(2)}, u32[]{:S(2)}) async-start(f32[16,2,3,128]{3,1,2,0:T(2,128)} %copy.140), calls=%async_computation.2 | async-start | bytes 98304 | tf_op jit(solution)/shard_map/all_to_all | solution.py:184
  53.1 7.4 %all-to-all-done.2 = f32[16,2,3,128]{3,1,2,0:T(2,128)S(1)} async-done(((f32[16,2,3,128]{3,1,2,0:T(2,128)}), f32[16,2,3,128]{3,1,2,0:T(2,128)S(1)}, u32[]{:S(2)}, u32[]{:S(2)}) %all-to-all-start.2) | async-done | bytes 49184 | tf_op jit(solution)/shard_map/all_to_all | solution.py:184
  60.5 0.6 copy.141.refs_4_
  61.1 7.8 %shard_map.82 = f32[16,3,2,128]{3,2,1,0:T(2,128)} custom-call(s32[1]{0:T(128)} %bitcast.position_ref, f32[4,3,128,128]{3,2,1,0:T(8,128)} %copy-done.1, f32[4,3,128,128]{3,2,1,0:T(8,128)} %collective-permute-done.3.refs_1_, f32[4,3,128,128]{3,2,1,0:T(8,128)} %collective-permute-done.4.refs_2_, f32[4,3,128,128]{3,2,1,0:T(8,128)} %collective-permute-done.5.refs_3_, ...), custom_call_target="tpu_custom_call" | custom-call | tf_op jit(solution)/shard_map/pallas_call | solution.py:185
  69.0 3.6 %all-to-all-start.3 = ((f32[16,3,2,128]{3,2,1,0:T(2,128)}), f32[16,3,2,128]{3,2,1,0:T(2,128)S(1)}, u32[]{:S(2)}, u32[]{:S(2)}) async-start(f32[16,3,2,128]{3,2,1,0:T(2,128)} %shard_map.82), calls=%async_computation.3 | async-start | bytes 98304 | tf_op jit(solution)/shard_map/all_to_all | solution.py:194
  72.7 7.4 %all-to-all-done.3 = f32[16,3,2,128]{3,2,1,0:T(2,128)S(1)} async-done(((f32[16,3,2,128]{3,2,1,0:T(2,128)}), f32[16,3,2,128]{3,2,1,0:T(2,128)S(1)}, u32[]{:S(2)}, u32[]{:S(2)}) %all-to-all-start.3) | async-done | bytes 49184 | tf_op jit(solution)/shard_map/all_to_all | solution.py:194
  80.2 0.6 convolution_bitcast_fusion
  80.9 0.6 copy.147
  (60 shorter events, 2.3 us)
Async XLA Ops:
  0.0 19.8 %copy-start = (bf16[256,1920]{1,0:T(8,128)(2,1)S(1)}, bf16[256,1920]{1,0:T(8,128)(2,1)}, u32[]{:S(2)}) copy-start(bf16[256,1920]{1,0:T(8,128)(2,1)} %param.10) | copy-start | bytes 2949124
  0.0 1.2 %copy-start.4 = (f32[4,128,128]{2,1,0:T(8,128)S(1)}, f32[4,128,128]{2,1,0:T(8,128)}, u32[]{:S(2)}) copy-start(f32[4,128,128]{2,1,0:T(8,128)} %param.13) | copy-start | bytes 786436
  1.3 10.9 %copy-start.3 = (f32[3,4,16,128]{3,2,1,0:T(8,128)S(1)}, f32[3,4,16,128]{3,2,1,0:T(8,128)}, u32[]{:S(2)}) copy-start(f32[3,4,16,128]{3,2,1,0:T(8,128)} %param.8) | copy-start | bytes 294916
  1.3 10.9 %copy-start.6 = (bf16[3,4,16,128]{3,2,1,0:T(8,128)(2,1)S(1)}, bf16[3,4,16,128]{3,2,1,0:T(8,128)(2,1)}, u32[]{:S(2)}) copy-start(bf16[3,4,16,128]{3,2,1,0:T(8,128)(2,1)} %param.9) | copy-start | bytes 147460
  1.3 18.5 %copy-start.8 = (s32[1,256]{1,0:T(1,128)S(1)}, s32[1,256]{1,0:T(1,128)}, u32[]{:S(2)}) copy-start(s32[1,256]{1,0:T(1,128)} %param.15) | copy-start | bytes 3076
  1.3 18.5 %copy-start.9 = (s32[1,256]{1,0:T(1,128)S(1)}, s32[1,256]{1,0:T(1,128)}, u32[]{:S(2)}) copy-start(s32[1,256]{1,0:T(1,128)} %constant.117.clone.1) | copy-start | bytes 3076
  2.1 24.5 %collective-permute-start = (f32[3,128,128]{2,1,0:T(8,128)}, f32[3,128,128]{2,1,0:T(8,128)S(1)}, u32[]{:S(2)}, u32[]{:S(2)}) collective-permute-start(f32[3,128,128]{2,1,0:T(8,128)} %get-tuple-element.17), channel_id=1, source_target_pairs={{15,11},{3,15},{7,3},{11,7},{0,12},{4,0},{8,4},{12,8},{1,13},{5,1}... | collective-permute-start | bytes 589832 | tf_op jit(solution)/shard_map/ppermute | solution.py:124
  8.9 17.7 %collective-permute-start.1 = (f32[3,128,128]{2,1,0:T(8,128)S(1)}, f32[3,128,128]{2,1,0:T(8,128)S(1)}, u32[]{:S(2)}, u32[]{:S(2)}) collective-permute-start(f32[3,128,128]{2,1,0:T(8,128)S(1)} %get-tuple-element.16), channel_id=1, source_target_pairs={{15,7},{3,11},{7,15},{11,3},{0,8},{4,12},{8,0},{12,4},{1,9},{5,13}... | collective-permute-start | bytes 589832 | tf_op jit(solution)/shard_map/ppermute | solution.py:124
  9.8 16.8 %collective-permute-start.2 = (f32[3,128,128]{2,1,0:T(8,128)S(1)}, f32[3,128,128]{2,1,0:T(8,128)S(1)}, u32[]{:S(2)}, u32[]{:S(2)}) collective-permute-start(f32[3,128,128]{2,1,0:T(8,128)S(1)} %get-tuple-element.15), channel_id=1, source_target_pairs={{15,3},{3,7},{7,11},{11,15},{0,4},{4,8},{8,12},{12,0},{1,5},{5,9},... | collective-permute-start | bytes 589832 | tf_op jit(solution)/shard_map/ppermute | solution.py:124
  12.9 13.6 %all-to-all-start = ((bf16[6,4,16,128]{3,0,1,2:T(8,128)(2,1)}), bf16[6,4,16,128]{3,0,1,2:T(8,128)(2,1)S(1)}, u32[]{:S(2)}, u32[]{:S(2)}) async-start(bf16[6,4,16,128]{3,0,1,2:T(8,128)(2,1)} %copy.123), calls=%async_computation | async-start | bytes 262144 | tf_op jit(solution)/shard_map/all_to_all | solution.py:147
  26.6 5.4 %copy-start.5 = (f32[3,128,128]{2,1,0:T(8,128)}, f32[3,128,128]{2,1,0:T(8,128)S(1)}, u32[]{:S(2)}) copy-start(f32[3,128,128]{2,1,0:T(8,128)S(1)} %collective-permute-done.2) | copy-start | bytes 589828
  28.1 14.4 %all-to-all-start.1 = ((bf16[3,64,1,128]{3,0,2,1:T(4,128)(2,1)}), bf16[3,64,1,128]{3,0,2,1:T(4,128)(2,1)S(1)}, u32[]{:S(2)}, u32[]{:S(2)}) async-start(bf16[3,64,1,128]{3,0,2,1:T(4,128)(2,1)} %copy.135), calls=%async_computation.1 | async-start | bytes 131072 | tf_op jit(solution)/shard_map/all_to_all | solution.py:170
  33.0 28.1 %copy-start.1 = (f32[4,3,128,128]{3,2,1,0:T(8,128)}, f32[4,3,128,128]{3,2,1,0:T(8,128)S(1)}, u32[]{:S(2)}) copy-start(f32[4,3,128,128]{3,2,1,0:T(8,128)S(1)} %pad_maximum_fusion.1.refs_0_) | copy-start | bytes 2359300
  33.0 28.1 %collective-permute-start.3 = (f32[4,3,128,128]{3,2,1,0:T(8,128)S(1)}, f32[4,3,128,128]{3,2,1,0:T(8,128)}, u32[]{:S(2)}, u32[]{:S(2)}) collective-permute-start(f32[4,3,128,128]{3,2,1,0:T(8,128)S(1)} %pad_maximum_fusion.1.refs_0_), channel_id=1, source_target_pairs={{1,0},{5,4},{9,8},{13,12},{17,16},{21,20},{25,24},{29,28},{33,32},... | collective-permute-start | bytes 2359304 | tf_op jit(solution)/shard_map/ppermute | solution.py:156
  39.5 21.7 %collective-permute-start.4 = (f32[4,3,128,128]{3,2,1,0:T(8,128)S(1)}, f32[4,3,128,128]{3,2,1,0:T(8,128)}, u32[]{:S(2)}, u32[]{:S(2)}) collective-permute-start(f32[4,3,128,128]{3,2,1,0:T(8,128)S(1)} %pad_maximum_fusion.1.refs_0_), channel_id=1, source_target_pairs={{2,0},{6,4},{10,8},{14,12},{18,16},{22,20},{26,24},{30,28},{34,32}... | collective-permute-start | bytes 2359304 | tf_op jit(solution)/shard_map/ppermute | solution.py:156
  41.0 20.1 %collective-permute-start.5 = (f32[4,3,128,128]{3,2,1,0:T(8,128)S(1)}, f32[4,3,128,128]{3,2,1,0:T(8,128)}, u32[]{:S(2)}, u32[]{:S(2)}) collective-permute-start(f32[4,3,128,128]{3,2,1,0:T(8,128)S(1)} %pad_maximum_fusion.1.refs_0_), channel_id=1, source_target_pairs={{15,0},{3,4},{7,8},{11,12},{31,16},{19,20},{23,24},{27,28},{47,32}... | collective-permute-start | bytes 2359304 | tf_op jit(solution)/shard_map/ppermute | solution.py:156
  43.8 16.7 %all-to-all-start.2 = ((f32[16,2,3,128]{3,1,2,0:T(2,128)}), f32[16,2,3,128]{3,1,2,0:T(2,128)S(1)}, u32[]{:S(2)}, u32[]{:S(2)}) async-start(f32[16,2,3,128]{3,1,2,0:T(2,128)} %copy.140), calls=%async_computation.2 | async-start | bytes 98304 | tf_op jit(solution)/shard_map/all_to_all | solution.py:184
  61.1 11.5 %copy-start.7 = (f32[15,128]{1,0:T(8,128)S(1)}, f32[15,128]{1,0:T(8,128)}, u32[]{:S(2)}) copy-start(f32[15,128]{1,0:T(8,128)} %param.14) | copy-start | bytes 23044
  61.1 19.1 %copy-start.2 = (bf16[1920,256]{1,0:T(8,128)(2,1)S(1)}, bf16[1920,256]{1,0:T(8,128)(2,1)}, u32[]{:S(2)}) copy-start(bf16[1920,256]{1,0:T(8,128)(2,1)} %param.11) | copy-start | bytes 2949124
  69.0 11.1 %all-to-all-start.3 = ((f32[16,3,2,128]{3,2,1,0:T(2,128)}), f32[16,3,2,128]{3,2,1,0:T(2,128)S(1)}, u32[]{:S(2)}, u32[]{:S(2)}) async-start(f32[16,3,2,128]{3,2,1,0:T(2,128)} %shard_map.82), calls=%async_computation.3 | async-start | bytes 98304 | tf_op jit(solution)/shard_map/all_to_all | solution.py:194
